TPU v7x, 32 devices: a whole 2x2x4 slice. The times are simulated.
32 devices in a mesh: rep: 4 (over x, core), dev: 8 (over z, y).
Axes of the slice: x: 2, y: 2, z: 4, core: 2. Of those that a mesh axis runs over, the one named last changes fastest.
Arguments:
- group_weights: bfloat16 [4, 160, 128, 1024], P('rep', None, 'dev'), may hold values from -6 to 6
- owner: int32 [160], replicated, may hold values from 0 to 7, as said below
- start_weights: float32 [8, 40, 128, 1024], P('dev', None, None, 'rep'), may hold values from -6 to 6
- momentum: float32 [8, 40, 128, 1024], P('dev', None, None, 'rep'), may hold values from -6 to 6
- basis: float32 [64, 1024], replicated, may hold values from -1 to 1
- vec_groups: bfloat16 [4, 13, 1024], P('rep'), may hold values from -6 to 6
- vec_start: float32 [13, 1024], replicated, may hold values from -6 to 6
- vec_momentum: float32 [13, 1024], replicated, may hold values from -6 to 6
Outputs:
- new_start: float32 [8, 40, 128, 1024], P('dev', None, None, 'rep')
- new_momentum: float32 [8, 40, 128, 1024], P('dev', None, None, 'rep')
- returned: bfloat16 [160, 128, 1024], P(None, 'dev')
- vec_new: float32 [13, 1024], replicated
- vec_new_momentum: float32 [13, 1024], replicated
Inputs may be any that keep to these rules, and one draw needn't show every extreme that they name: `owner`: each index along dev owns at most 40 blocks, and some index owns exactly 40.
All inputs are finite; a program needn't handle non-finite values.
Results may differ from a plain program's by a relative error of at most 0.012.
Values may be sent and summed in bfloat16 or wider, within the bound.
No kernel may reach another device: no remote copies, remote signals or barrier semaphores. Data moves between devices by JAX's collectives and lax.ppermute only.
A program may use at most 128 MiB of HBM per device.

v0:
```python
import jax
import jax.numpy as jnp
from jax import lax
from jax.sharding import PartitionSpec as P

EMB_FIRST = 96


outer_rate = 0.7
outer_momentum = 0.9


def body(group_weights, owner, start_weights, momentum, basis, vec_groups, vec_start, vec_momentum):
    dev_count = lax.axis_size("dev")
    rep_count = lax.axis_size("rep")
    unit_count = owner.shape[0]
    slot_count = start_weights.shape[1]
    quarter = start_weights.shape[3]
    unit_ids = jnp.arange(unit_count, dtype=jnp.int32)
    same_owner = owner[:, None] == owner[None, :]
    earlier = unit_ids[None, :] < unit_ids[:, None]
    slot_of = jnp.sum((same_owner & earlier).astype(jnp.int32), axis=1)
    target = owner * slot_count + slot_of
    positions = jnp.arange(dev_count * slot_count, dtype=jnp.int32)
    placed = target[:, None] == positions[None, :]
    filled = jnp.any(placed, axis=0)
    source_unit = jnp.sum(jnp.where(placed, unit_ids[:, None], 0), axis=0)
    own_rows = group_weights[0]
    picked = jnp.take(own_rows, source_unit, axis=0)
    picked = jnp.where(filled[:, None, None], picked, jnp.zeros((), own_rows.dtype))
    arrived = lax.all_to_all(
        picked.reshape(dev_count, slot_count, own_rows.shape[1], own_rows.shape[2]),
        "dev",
        split_axis=0,
        concat_axis=2,
        tiled=True,
    )
    summed = lax.psum_scatter(
        arrived[0].astype(jnp.float32).astype(jnp.bfloat16), "rep", scatter_dimension=2, tiled=True
    ).astype(jnp.float32)
    group_mean = summed / rep_count
    start_rows = start_weights[0]
    momentum_rows = momentum[0]
    my_slots = lax.axis_index("dev") * slot_count + jnp.arange(slot_count, dtype=jnp.int32)
    own_placed = target[:, None] == my_slots[None, :]
    is_owned = jnp.any(own_placed, axis=0)
    is_embedding = jnp.any(own_placed & (unit_ids >= EMB_FIRST)[:, None], axis=0)
    change = start_rows - group_mean
    first_column = lax.axis_index("rep") * quarter
    basis_part = lax.dynamic_slice_in_dim(basis, first_column, quarter, 1)
    coeff_terms = jnp.einsum("sbq,kq->sbk", change, basis_part, precision=lax.Precision.HIGHEST)
    vec_terms = vec_groups[0].astype(jnp.float32)
    coeffs, vec_summed = (
        lax.psum(coeff_terms.astype(jnp.bfloat16), "rep").astype(jnp.float32),
        lax.psum(vec_terms.astype(jnp.bfloat16), "rep").astype(jnp.float32),
    )
    projected = jnp.einsum("sbk,kq->sbq", coeffs, basis_part, precision=lax.Precision.HIGHEST)
    outer_grad = jnp.where(is_embedding[:, None, None], projected, change)
    fresh_momentum = outer_momentum * momentum_rows + outer_grad
    fresh_start = start_rows - outer_rate * (outer_grad + outer_momentum * fresh_momentum)
    owned_mask = is_owned[:, None, None]
    new_momentum = jnp.where(owned_mask, fresh_momentum, momentum_rows)
    new_start = jnp.where(owned_mask, fresh_start, start_rows)
    rounded = fresh_start.astype(jnp.bfloat16)
    pieces = lax.all_to_all(rounded, "dev", split_axis=1, concat_axis=0, tiled=True)
    picked = jnp.take(pieces, target, axis=0)
    returned = lax.all_gather(picked, "rep", axis=2, tiled=True)
    vec_change = vec_start - vec_summed / rep_count
    vec_new_momentum = outer_momentum * vec_momentum + vec_change
    vec_new = vec_start - outer_rate * (vec_change + outer_momentum * vec_new_momentum)
    return (new_start[None], new_momentum[None], returned, vec_new, vec_new_momentum)


def solution(mesh):
    return jax.shard_map(
        body,
        mesh=mesh,
        in_specs=(
            P("rep", None, "dev", None),
            P(),
            P("dev", None, None, "rep"),
            P("dev", None, None, "rep"),
            P(),
            P("rep", None, None),
            P(),
            P(),
        ),
        out_specs=(
            P("dev", None, None, "rep"),
            P("dev", None, None, "rep"),
            P(None, "dev", None),
            P(),
            P(),
        ),
        check_vma=False,
    )
```

profile of v0, /device:TPU:0, one launch (start us, length us, event | category | flops | bytes accessed | tf_op | source)
XLA Modules:
  0.0 537.5 jit_solution(10734063896174378784)
XLA Ops:
  7.2 0.0 copy-start
  7.2 0.0 reduce-scatter.2.cloned.1.call-start
  7.2 0.9 convert_reduce_fusion
  8.2 0.7 compare_and_fusion.2
  8.9 0.1 select_reduce_fusion
  9.0 0.1 reduce_sum.24
  9.1 0.1 fusion.7
  9.2 0.1 broadcast_in_dim.85
  9.3 13.0 %gather_fusion = bf16[320,16,1024]{2,1,0:T(8,128)(2,1)} fusion(bf16[160,16,1024]{2,1,0:T(8,128)(2,1)} %bitcast.60, s32[1024]{0:T(1024)S(1)} %pad_clamp_fusion.1), kind=kCustom, calls=%fused_computation | custom fusion | bytes 20972800 | tf_op jit(solution)/shard_map/jit(_take)/gather | solution.py:29
  22.3 6.0 %select_select_fusion = bf16[8,40,16,1024]{3,2,1,0:T(8,128)(2,1)S(1)} fusion(bf16[8,40,16,1024]{3,2,1,0:T(8,128)(2,1)} %bitcast.59, pred[8,40]{1,0:T(8,128)(4,1)S(1)} %compare_and_fusion.1, pred[8,40]{1,0:T(8,128)(4,1)S(1)} %broadcast_in_dim.85), kind=kLoop, calls=%fused_computation.2 | loop fusion | flops 10485760 | bytes 20972160 | tf_op jit(solution)/shard_map/jit(_where)/select_n | solution.py:30
  28.3 235.2 %all_to_all.33 = bf16[8,40,16,1024]{3,2,1,0:T(8,128)(2,1)} all-to-all(bf16[8,40,16,1024]{3,2,1,0:T(8,128)(2,1)S(1)} %select_select_fusion), channel_id=1, replica_groups=mesh['rep'=4,'dev'=8] {'dev'}, dimensions={0} | all-to-all | bytes 20971520 | tf_op jit(solution)/shard_map/all_to_all | solution.py:31
  263.5 10.4 %copy.24 = bf16[1,40,8,16,1024]{4,3,2,1,0:T(8,128)(2,1)} copy(bf16[1,40,8,16,1024]{4,3,1,2,0:T(8,128)(2,1)} %bitcast.58) | data formatting | bytes 20971520 | tf_op jit(solution)/shard_map/all_to_all | solution.py:31
  273.9 0.0 reduce-scatter.2.cloned.1.call-update
  273.9 0.0 all-reduce.2.cloned.1.call-start
  274.0 84.4 %reduce-scatter.2.cloned.1.call-done = bf16[40,128,256]{2,1,0:T(8,128)(2,1)} async-done(((bf16[40,128,1024]{2,1,0:T(8,128)(2,1)}), bf16[40,128,256]{2,1,0:T(8,128)(2,1)}) %reduce-scatter.2.cloned.1.call-update) | async-done | bytes 2621456 | tf_op jit(solution)/shard_map/reduce_scatter | solution.py:38
  358.4 0.0 copy-done
  358.4 0.0 copy-start.1
  358.4 9.5 %fusion.6 = bf16[40,128,64]{1,2,0:T(8,128)(2,1)} fusion(f32[1,40,128,256]{3,2,1,0:T(8,128)} %param.10, bf16[40,128,256]{2,1,0:T(8,128)(2,1)} %reduce-scatter.2.cloned.1.call-done, f32[64,1024]{1,0:T(8,128)S(1)} %copy-done, s32[]{:T(128)S(6)} %select_n.58), kind=kOutput, calls=%fused_computation.14 | convolution fusion | flops 1010892800 | bytes 8585220 | tf_op jit(solution)/shard_map/sbq,kq->sbk/dot_general | solution.py:51
  367.9 0.0 all-reduce.2.cloned.1.call-update
  368.0 0.2 fusion.14
  368.2 33.7 %all-reduce.2.cloned.1.call-done = bf16[40,128,64]{1,2,0:T(8,128)(2,1)} async-done(((bf16[40,128,64]{1,2,0:T(8,128)(2,1)}), bf16[40,128,64]{1,2,0:T(8,128)(2,1)}) %all-reduce.2.cloned.1.call-update) | async-done | bytes 655376 | tf_op jit(solution)/shard_map/psum | solution.py:54
  401.9 0.0 copy-done.1
  401.9 10.2 %fusion.1 = (f32[1,40,128,256]{3,2,1,0:T(8,128)}, f32[1,40,128,256]{3,2,1,0:T(8,128)}, bf16[40,128,256]{2,1,0:T(8,128)(2,1)S(1)}) fusion(f32[1,40,128,256]{3,2,1,0:T(8,128)} %param.11, bf16[40,128,256]{2,1,0:T(8,128)(2,1)S(1)} %copy-done.1, f32[1,40,128,256]{3,2,1,0:T(8,128)} %param.10, pred[40]{0:T(512)(128)(4,1)S(1)} %get-tuple-element.5, ...), kind=kOutput, calls=%fused_computation.6 | convolution fusion | flops 1023672320 | bytes 26936324 | tf_op jit(solution)/shard_map/sbk,kq->sbq/dot_general | solution.py:57
  412.1 3.0 copy.25
  415.0 5.5 %all-to-all-start.1 = ((bf16[40,128,256]{2,0,1:T(8,128)(2,1)}), bf16[40,128,256]{2,0,1:T(8,128)(2,1)S(1)}, u32[]{:S(2)}, u32[]{:S(2)}) async-start(bf16[40,128,256]{2,0,1:T(8,128)(2,1)} %copy.25), calls=%async_computation.2 | async-start | bytes 5242880 | tf_op jit(solution)/shard_map/all_to_all | solution.py:65
  420.6 0.0 all-gather.2.cloned.1.call-start
  420.6 58.5 %all-to-all-done.1 = bf16[40,128,256]{2,0,1:T(8,128)(2,1)S(1)} async-done(((bf16[40,128,256]{2,0,1:T(8,128)(2,1)}), bf16[40,128,256]{2,0,1:T(8,128)(2,1)S(1)}, u32[]{:S(2)}, u32[]{:S(2)}) %all-to-all-start.1) | async-done | bytes 2621472 | tf_op jit(solution)/shard_map/all_to_all | solution.py:65
  479.1 0.0 copy-start.4
  479.1 0.0 copy-start.2
  479.1 0.0 copy-start.3
  479.1 2.1 copy.27
  481.2 2.6 gather_fusion.1
  483.8 1.3 broadcast_select_fusion
  485.1 0.0 all-gather.2.cloned.1.call-update
  485.1 0.0 copy-done.4
  485.1 10.3 %psum.15 = bf16[13,1024]{1,0:T(8,128)(2,1)S(1)} all-reduce(bf16[13,1024]{1,0:T(8,128)(2,1)S(1)} %bitcast.63), channel_id=1, replica_groups=mesh['rep'=4,'dev'=8] {'rep'}, use_global_device_ids=true, to_apply=%region_7.8 | all-reduce | flops 13312 | bytes 53248 | tf_op jit(solution)/shard_map/psum | solution.py:55
  495.4 0.0 copy-done.2
  495.4 0.0 copy-done.3
  495.4 0.7 multiply_subtract_fusion
  496.1 28.9 %all-gather.2.cloned.1.call-done = bf16[160,16,1024]{2,1,0:T(8,128)(2,1)} async-done(((bf16[160,16,256]{2,1,0:T(8,128)(2,1)}), bf16[160,16,1024]{2,1,0:T(8,128)(2,1)}) %all-gather.2.cloned.1.call-update) | async-done | bytes 5242896 | tf_op jit(solution)/shard_map/all_gather | solution.py:67
  525.0 6.0 %copy.31 = bf16[160,16,1024]{2,1,0:T(8,128)(2,1)} copy(bf16[160,16,1024]{2,1,0:T(8,128)(2,1)} %all-gather.2.cloned.1.call-done) | data formatting | bytes 10485760
  (6 shorter events, 0.0 us)
Async XLA Ops:
  7.2 351.2 %copy-start = (f32[64,1024]{1,0:T(8,128)S(1)}, f32[64,1024]{1,0:T(8,128)}, u32[]{:S(2)}) copy-start(f32[64,1024]{1,0:T(8,128)} %param.12) | copy-start | bytes 786436
  7.2 351.2 %reduce-scatter.2.cloned.1.call-start = ((), (), s32[]{:S(2)}) async-start(), calls=%async_computation.3 | async-start | bytes 13107200 | tf_op jit(solution)/shard_map/reduce_scatter | solution.py:38
  273.9 128.0 %all-reduce.2.cloned.1.call-start = ((), (), s32[]{:S(2)}) async-start(), calls=%async_computation.4 | async-start | bytes 1310720 | tf_op jit(solution)/shard_map/psum | solution.py:54
  358.4 43.5 %copy-start.1 = (bf16[40,128,256]{2,1,0:T(8,128)(2,1)S(1)}, bf16[40,128,256]{2,1,0:T(8,128)(2,1)}, u32[]{:S(2)}) copy-start(bf16[40,128,256]{2,1,0:T(8,128)(2,1)} %reduce-scatter.2.cloned.1.call-done) | copy-start | bytes 7864324
  415.0 64.1 %all-to-all-start.1 = ((bf16[40,128,256]{2,0,1:T(8,128)(2,1)}), bf16[40,128,256]{2,0,1:T(8,128)(2,1)S(1)}, u32[]{:S(2)}, u32[]{:S(2)}) async-start(bf16[40,128,256]{2,0,1:T(8,128)(2,1)} %copy.25), calls=%async_computation.2 | async-start | bytes 5242880 | tf_op jit(solution)/shard_map/all_to_all | solution.py:65
  420.6 104.5 %all-gather.2.cloned.1.call-start = ((), (), s32[]{:S(2)}) async-start(), calls=%async_computation.5 | async-start | bytes 6553600 | tf_op jit(solution)/shard_map/all_gather | solution.py:67
  479.1 6.0 %copy-start.4 = (bf16[1,13,1024]{2,1,0:T(8,128)(2,1)S(1)}, bf16[1,13,1024]{2,1,0:T(8,128)(2,1)}, u32[]{:S(2)}) copy-start(bf16[1,13,1024]{2,1,0:T(8,128)(2,1)} %param.13) | copy-start | bytes 79876
  479.1 16.3 %copy-start.2 = (f32[13,1024]{1,0:T(8,128)S(1)}, f32[13,1024]{1,0:T(8,128)}, u32[]{:S(2)}) copy-start(f32[13,1024]{1,0:T(8,128)} %param.14) | copy-start | bytes 159748
  479.1 16.3 %copy-start.3 = (f32[13,1024]{1,0:T(8,128)S(1)}, f32[13,1024]{1,0:T(8,128)}, u32[]{:S(2)}) copy-start(f32[13,1024]{1,0:T(8,128)} %param.15) | copy-start | bytes 159748
Sparse Core Ops, SparseCore 0:
  274.0 84.3 reduce-scatter.1
  368.1 33.7 all-reduce.1
  485.2 39.7 all-gather.1
where the time goes:
time: 538 us
  blocking collectives  245 us (46%)
  waiting for transfers between devices  206 us (38%)
  local copies, waits for them, and re-layouts  37.2 us (7%)
  matrix products  19.7 us (4%)
  between operations  13.9 us (3%)
  other arithmetic  10 us (2%)
  starting transfers between devices  5.63 us (1%)
    all_to_all x1, blocking collectives, body(): lax.all_to_all(picked.reshape(dev_count, slot_count, own_rows.shape[1], o...  235 us
    reduce_scatter x1, waiting for transfers between devices, body(): lax.psum_scatter(arrived[0].astype(jnp.float32).astype(jnp.bfloat16), 're...  84.4 us
    all_to_all x1, waiting for transfers between devices, body(): lax.all_to_all(rounded, 'dev', split_axis=1, concat_axis=0, tiled=True)  58.5 us
    psum x1, waiting for transfers between devices, body(): lax.psum(coeff_terms.astype(jnp.bfloat16), 'rep').astype(jnp.float32)  33.7 us
    all_gather x1, waiting for transfers between devices, body(): returned = lax.all_gather(picked, 'rep', axis=2, tiled=True)  28.9 us
    gather x1, local copies, waits for them, and re-layouts, body(): picked = jnp.take(own_rows, source_unit, axis=0)  13 us
  transfers between devices with their start and end apart: 4, of which 4 were waited for; matrix products, arithmetic and copies ran while one was open for 0% of the time, Pallas kernels for 0%

commit v1 on v0

--- a/solution.py
+++ b/solution.py
@@ -23,22 +23,18 @@
     target = owner * slot_count + slot_of
     positions = jnp.arange(dev_count * slot_count, dtype=jnp.int32)
     placed = target[:, None] == positions[None, :]
-    filled = jnp.any(placed, axis=0)
     source_unit = jnp.sum(jnp.where(placed, unit_ids[:, None], 0), axis=0)
     own_rows = group_weights[0]
-    picked = jnp.take(own_rows, source_unit, axis=0)
-    picked = jnp.where(filled[:, None, None], picked, jnp.zeros((), own_rows.dtype))
+    summed = lax.psum_scatter(own_rows, "rep", scatter_dimension=2, tiled=True)
+    picked = jnp.take(summed, source_unit, axis=0)
     arrived = lax.all_to_all(
-        picked.reshape(dev_count, slot_count, own_rows.shape[1], own_rows.shape[2]),
+        picked.reshape(dev_count, slot_count, summed.shape[1], summed.shape[2]),
         "dev",
         split_axis=0,
         concat_axis=2,
         tiled=True,
     )
-    summed = lax.psum_scatter(
-        arrived[0].astype(jnp.float32).astype(jnp.bfloat16), "rep", scatter_dimension=2, tiled=True
-    ).astype(jnp.float32)
-    group_mean = summed / rep_count
+    group_mean = arrived[0].astype(jnp.float32) / rep_count
     start_rows = start_weights[0]
     momentum_rows = momentum[0]
     my_slots = lax.axis_index("dev") * slot_count + jnp.arange(slot_count, dtype=jnp.int32)
@@ -49,11 +45,11 @@
     first_column = lax.axis_index("rep") * quarter
     basis_part = lax.dynamic_slice_in_dim(basis, first_column, quarter, 1)
     coeff_terms = jnp.einsum("sbq,kq->sbk", change, basis_part, precision=lax.Precision.HIGHEST)
-    vec_terms = vec_groups[0].astype(jnp.float32)
-    coeffs, vec_summed = (
-        lax.psum(coeff_terms.astype(jnp.bfloat16), "rep").astype(jnp.float32),
-        lax.psum(vec_terms.astype(jnp.bfloat16), "rep").astype(jnp.float32),
-    )
+    vec_terms = vec_groups[0]
+    coeff_flat = coeff_terms.astype(jnp.bfloat16).reshape(-1)
+    joined = lax.psum(jnp.concatenate([coeff_flat, vec_terms.reshape(-1)]), "rep")
+    coeffs = joined[: coeff_flat.shape[0]].reshape(coeff_terms.shape).astype(jnp.float32)
+    vec_summed = joined[coeff_flat.shape[0]:].reshape(vec_terms.shape).astype(jnp.float32)
     projected = jnp.einsum("sbk,kq->sbq", coeffs, basis_part, precision=lax.Precision.HIGHEST)
     outer_grad = jnp.where(is_embedding[:, None, None], projected, change)
     fresh_momentum = outer_momentum * momentum_rows + outer_grad

time: 538 us -> 315 us (0.59)
  blocking collectives: 245 us -> 0 us
  waiting for transfers between devices: 206 us -> 245 us
  local copies, waits for them, and re-layouts: 37.2 us -> 22.5 us
  starting transfers between devices: 5.63 us -> 11.3 us
    all_to_all x1 -> x0, blocking collectives: 235 us -> none  [body(): lax.all_to_all(picked.reshape(dev_count, slot_count, own_rows.shape[1], o...]
    all_to_all x0 -> x1, waiting for transfers between devices: none -> 59.4 us  [body(): lax.all_to_all(picked.reshape(dev_count, slot_count, summed.shape[1], sum...]
    reduce_scatter x1, waiting for transfers between devices: 84.4 us -> 56.3 us  [body(): summed = lax.psum_scatter(own_rows, 'rep', scatter_dimension=2, tiled=True)]
    gather x1, local copies, waits for them, and re-layouts: 13 us -> 2.48 us  [body(): picked = jnp.take(summed, source_unit, axis=0)]
    all_to_all x1 -> x0, local copies, waits for them, and re-layouts: 10.4 us -> none  [body(): lax.all_to_all(picked.reshape(dev_count, slot_count, own_rows.shape[1], o...]
    psum x1 -> x0, blocking collectives: 10.3 us -> none  [body(): lax.psum(vec_terms.astype(jnp.bfloat16), 'rep').astype(jnp.float32)]
    all_gather x1, waiting for transfers between devices: 28.9 us -> 38.4 us  [body(): returned = lax.all_gather(picked, 'rep', axis=2, tiled=True)]
    all_to_all x0 -> x1, starting transfers between devices: none -> 5.65 us  [body(): lax.all_to_all(picked.reshape(dev_count, slot_count, summed.shape[1], sum...]
  transfers between devices with their start and end apart: 4 -> 5, of which waited for: 4 -> 5; matrix products, arithmetic and copies ran while one was open for 0% -> 1% of each run, Pallas kernels for 0% -> 0%
where the time goes in v1:
time: 315 us
  waiting for transfers between devices  245 us (78%)
  local copies, waits for them, and re-layouts  22.5 us (7%)
  matrix products  15 us (5%)
  between operations  14 us (4%)
  starting transfers between devices  11.3 us (4%)
  other arithmetic  6.64 us (2%)
    all_to_all x1, waiting for transfers between devices, body(): lax.all_to_all(picked.reshape(dev_count, slot_count, summed.shape[1], sum...  59.4 us
    all_to_all x1, waiting for transfers between devices, body(): lax.all_to_all(rounded, 'dev', split_axis=1, concat_axis=0, tiled=True)  58.6 us
    reduce_scatter x1, waiting for transfers between devices, body(): summed = lax.psum_scatter(own_rows, 'rep', scatter_dimension=2, tiled=True)  56.3 us
    all_gather x1, waiting for transfers between devices, body(): returned = lax.all_gather(picked, 'rep', axis=2, tiled=True)  38.4 us
    psum x1, waiting for transfers between devices, body(): lax.psum(jnp.concatenate([coeff_flat, vec_terms.reshape(-1)]), 'rep')  32 us
    dot_general x1, matrix products, body(): jnp.einsum('sbk,kq->sbq', coeffs, basis_part, precision=lax.Precision.HIG...  9.58 us
    unnamed x19, local copies, waits for them, and re-layouts  8.42 us
  transfers between devices with their start and end apart: 5, of which 5 were waited for; matrix products, arithmetic and copies ran while one was open for 1% of the time, Pallas kernels for 0%

profile of v1, /device:TPU:0, one launch (start us, length us, event | category | flops | bytes accessed | tf_op | source)
XLA Modules:
  0.0 314.6 jit_solution(16953501838984730410)
XLA Ops:
  7.2 0.0 copy-start
  7.2 0.0 reduce-scatter.2.cloned.1.call-start
  7.2 0.0 copy-start.6
  7.2 0.7 reduce-scatter.2.cloned.1.call-update
  7.9 0.0 copy-done.6
  7.9 0.2 convert_reduce_fusion
  8.1 0.1 select_reduce_fusion
  8.3 0.1 reduce_sum.24
  8.4 56.3 %reduce-scatter.2.cloned.1.call-done = bf16[160,16,256]{2,1,0:T(8,128)(2,1)} async-done(((bf16[160,16,1024]{2,1,0:T(8,128)(2,1)}), bf16[160,16,256]{2,1,0:T(8,128)(2,1)}) %reduce-scatter.2.cloned.1.call-update) | async-done | bytes 1310736 | tf_op jit(solution)/shard_map/reduce_scatter | solution.py:28
  64.7 2.5 gather_fusion
  67.1 1.8 broadcast_select_fusion.1
  68.9 5.6 %all-to-all-start = ((bf16[8,40,16,256]{3,2,1,0:T(8,128)(2,1)}), bf16[8,40,16,256]{3,2,1,0:T(8,128)(2,1)S(1)}, u32[]{:S(2)}, u32[]{:S(2)}) async-start(bf16[8,40,16,256]{3,2,1,0:T(8,128)(2,1)} %broadcast_select_fusion.1), calls=%async_computation.1 | async-start | bytes 5242880 | tf_op jit(solution)/shard_map/all_to_all | solution.py:30
  74.5 0.0 all-reduce.2.cloned.1.call-start
  74.6 0.0 copy-done.5
  74.7 59.4 %all-to-all-done = bf16[8,40,16,256]{3,2,1,0:T(8,128)(2,1)S(1)} async-done(((bf16[8,40,16,256]{3,2,1,0:T(8,128)(2,1)}), bf16[8,40,16,256]{3,2,1,0:T(8,128)(2,1)S(1)}, u32[]{:S(2)}, u32[]{:S(2)}) %all-to-all-start) | async-done | bytes 2621472 | tf_op jit(solution)/shard_map/all_to_all | solution.py:30
  134.0 0.7 multiply_bitcast_fusion
  134.8 0.0 slice-start.1
  134.8 0.8 copy.29
  135.6 0.0 copy-start.2
  135.6 2.3 copy-done.2
  138.0 0.0 copy-done
  138.0 0.0 slice-done
  138.0 0.0 slice-done.1
  138.0 5.4 %fusion.4 = bf16[40,128,64]{1,2,0:T(8,128)(2,1)S(1)} fusion(f32[40,128,256]{2,1,0:T(8,128)S(1)} %bitcast.55, f32[1,40,128,256]{3,2,1,0:T(8,128)S(1)} %bitcast.58, f32[64,1024]{1,0:T(8,128)S(1)} %copy-done, s32[]{:T(128)S(6)} %select_n.52), kind=kOutput, calls=%fused_computation.14 | convolution fusion | flops 1008271360 | bytes 11206660 | tf_op jit(solution)/shard_map/sbq,kq->sbk/dot_general | solution.py:47
  143.4 0.7 copy.30
  144.1 0.6 reshape.75
  144.8 0.9 pad_maximum_fusion
  145.7 0.0 all-reduce.2.cloned.1.call-update
  145.7 0.2 fusion.11
  145.9 32.0 %all-reduce.2.cloned.1.call-done = bf16[340992]{0:T(1024)(128)(2,1)} async-done(((bf16[340992]{0:T(1024)(128)(2,1)}), bf16[340992]{0:T(1024)(128)(2,1)}) %all-reduce.2.cloned.1.call-update) | async-done | bytes 682000 | tf_op jit(solution)/shard_map/psum | solution.py:50
  177.9 1.1 slice.20
  179.0 0.5 reshape.76
  179.5 9.6 %fusion.5 = (bf16[40,128,256]{2,1,0:T(8,128)(2,1)S(1)}, f32[1,40,128,256]{3,2,1,0:T(8,128)}, f32[1,40,128,256]{3,2,1,0:T(8,128)}) fusion(f32[1,40,128,256]{3,2,1,0:T(8,128)} %param.11, f32[1,40,128,256]{3,2,1,0:T(8,128)} %param.10, pred[40]{0:T(512)(128)(4,1)S(1)} %get-tuple-element.6, f32[40,128,256]{2,1,0:T(8,128)} %bitcast.56, ...), kind=kOutput, calls=%fused_computation.16 | convolution fusion | flops 1021050880 | bytes 30213124 | tf_op jit(solution)/shard_map/sbk,kq->sbq/dot_general | solution.py:53
  189.1 3.0 copy.32
  192.1 5.5 %all-to-all-start.1 = ((bf16[40,128,256]{2,0,1:T(8,128)(2,1)}), bf16[40,128,256]{2,0,1:T(8,128)(2,1)S(1)}, u32[]{:S(2)}, u32[]{:S(2)}) async-start(bf16[40,128,256]{2,0,1:T(8,128)(2,1)} %copy.32), calls=%async_computation.2 | async-start | bytes 5242880 | tf_op jit(solution)/shard_map/all_to_all | solution.py:61
  197.6 0.0 all-gather.2.cloned.1.call-start
  197.7 58.6 %all-to-all-done.1 = bf16[40,128,256]{2,0,1:T(8,128)(2,1)S(1)} async-done(((bf16[40,128,256]{2,0,1:T(8,128)(2,1)}), bf16[40,128,256]{2,0,1:T(8,128)(2,1)S(1)}, u32[]{:S(2)}, u32[]{:S(2)}) %all-to-all-start.1) | async-done | bytes 2621472 | tf_op jit(solution)/shard_map/all_to_all | solution.py:61
  256.3 2.1 copy.34
  258.3 2.6 gather_fusion.1
  260.9 0.0 copy-start.3
  260.9 0.0 copy-start.4
  261.0 1.3 broadcast_select_fusion.2
  262.2 0.0 all-gather.2.cloned.1.call-update
  262.3 0.8 convert_multiply_fusion
  263.1 0.7 multiply_subtract_fusion
  263.7 38.4 %all-gather.2.cloned.1.call-done = bf16[160,16,1024]{2,1,0:T(8,128)(2,1)} async-done(((bf16[160,16,256]{2,1,0:T(8,128)(2,1)}), bf16[160,16,1024]{2,1,0:T(8,128)(2,1)}) %all-gather.2.cloned.1.call-update) | async-done | bytes 5242896 | tf_op jit(solution)/shard_map/all_gather | solution.py:63
  302.1 6.0 %copy.39 = bf16[160,16,1024]{2,1,0:T(8,128)(2,1)} copy(bf16[160,16,1024]{2,1,0:T(8,128)(2,1)} %all-gather.2.cloned.1.call-done) | data formatting | bytes 10485760
  308.1 0.0 copy-done.1
  (15 shorter events, 0.1 us)
Async XLA Ops:
  7.2 130.8 %copy-start = (f32[64,1024]{1,0:T(8,128)S(1)}, f32[64,1024]{1,0:T(8,128)}, u32[]{:S(2)}) copy-start(f32[64,1024]{1,0:T(8,128)} %param.12) | copy-start | bytes 786436
  7.2 57.5 %reduce-scatter.2.cloned.1.call-start = ((), (), s32[]{:S(2)}) async-start(), calls=%async_computation.3 | async-start | bytes 6553600 | tf_op jit(solution)/shard_map/reduce_scatter | solution.py:28
  7.2 0.7 copy-start.6
  68.9 5.7 %copy-start.5 = (bf16[1,13,1024]{2,1,0:T(8,128)(2,1)S(1)}, bf16[1,13,1024]{2,1,0:T(8,128)(2,1)}, u32[]{:S(2)}) copy-start(bf16[1,13,1024]{2,1,0:T(8,128)(2,1)} %param.13) | copy-start | bytes 79876
  68.9 65.1 %all-to-all-start = ((bf16[8,40,16,256]{3,2,1,0:T(8,128)(2,1)}), bf16[8,40,16,256]{3,2,1,0:T(8,128)(2,1)S(1)}, u32[]{:S(2)}, u32[]{:S(2)}) async-start(bf16[8,40,16,256]{3,2,1,0:T(8,128)(2,1)} %broadcast_select_fusion.1), calls=%async_computation.1 | async-start | bytes 5242880 | tf_op jit(solution)/shard_map/all_to_all | solution.py:30
  74.5 103.3 %all-reduce.2.cloned.1.call-start = ((), (), s32[]{:S(2)}) async-start(), calls=%async_computation.4 | async-start | bytes 1363968 | tf_op jit(solution)/shard_map/psum | solution.py:50
  134.0 4.0 %slice-start = ((s8[5242880]{0:T(1024)(128)(4,1)}), s8[4194304]{0:T(1024)(128)(4,1)S(1)}, s32[]{:S(2)}) async-start(s8[5242880]{0:T(1024)(128)(4,1)} %bitcast.57), calls=%async_computation.6 | async-start | bytes 8388608
  134.8 3.2 %slice-start.1 = ((s8[5242880]{0:T(1024)(128)(4,1)}), s8[1048576]{0:T(1024)(128)(4,1)S(1)}, s32[]{:S(2)}) async-start(s8[5242880]{0:T(1024)(128)(4,1)} %bitcast.57), calls=%async_computation.7 | async-start | bytes 2097152
  135.6 2.4 copy-start.2
  192.1 64.2 %all-to-all-start.1 = ((bf16[40,128,256]{2,0,1:T(8,128)(2,1)}), bf16[40,128,256]{2,0,1:T(8,128)(2,1)S(1)}, u32[]{:S(2)}, u32[]{:S(2)}) async-start(bf16[40,128,256]{2,0,1:T(8,128)(2,1)} %copy.32), calls=%async_computation.2 | async-start | bytes 5242880 | tf_op jit(solution)/shard_map/all_to_all | solution.py:61
  197.6 104.5 %all-gather.2.cloned.1.call-start = ((), (), s32[]{:S(2)}) async-start(), calls=%async_computation.5 | async-start | bytes 6553600 | tf_op jit(solution)/shard_map/all_gather | solution.py:63
  260.9 2.1 copy-start.3
  260.9 2.1 copy-start.4
  302.1 6.0 %copy-start.1 = (f32[64,1024]{1,0:T(8,128)S(1)}, f32[64,1024]{1,0:T(8,128)}, u32[]{:S(2)}) copy-start(f32[64,1024]{1,0:T(8,128)} %param.12) | copy-start | bytes 786436
Sparse Core Ops, SparseCore 0:
  10.6 54.0 reduce-scatter.1
  145.8 32.0 all-reduce.1
  262.4 39.6 all-gather.1

commit v2 on v1

v2 whole, which is shorter than its diff:
```python
import jax
import jax.numpy as jnp
from jax import lax
from jax.sharding import PartitionSpec as P

EMB_FIRST = 96
CHUNKS = 2


outer_rate = 0.7
outer_momentum = 0.9


def body(group_weights, owner, start_weights, momentum, basis, vec_groups, vec_start, vec_momentum):
    dev_count = lax.axis_size("dev")
    rep_count = lax.axis_size("rep")
    unit_count = owner.shape[0]
    slot_count = start_weights.shape[1]
    quarter = start_weights.shape[3]
    width = quarter // CHUNKS
    unit_ids = jnp.arange(unit_count, dtype=jnp.int32)
    same_owner = owner[:, None] == owner[None, :]
    earlier = unit_ids[None, :] < unit_ids[:, None]
    slot_of = jnp.sum((same_owner & earlier).astype(jnp.int32), axis=1)
    target = owner * slot_count + slot_of
    positions = jnp.arange(dev_count * slot_count, dtype=jnp.int32)
    placed = target[:, None] == positions[None, :]
    source_unit = jnp.sum(jnp.where(placed, unit_ids[:, None], 0), axis=0)
    own_rows = group_weights[0]
    rows = own_rows.shape[1]
    split_rows = own_rows.reshape(unit_count, rows, rep_count, CHUNKS, width)
    start_rows = start_weights[0]
    momentum_rows = momentum[0]
    my_slots = lax.axis_index("dev") * slot_count + jnp.arange(slot_count, dtype=jnp.int32)
    own_placed = target[:, None] == my_slots[None, :]
    is_owned = jnp.any(own_placed, axis=0)
    is_embedding = jnp.any(own_placed & (unit_ids >= EMB_FIRST)[:, None], axis=0)
    first_column = lax.axis_index("rep") * quarter
    basis_part = lax.dynamic_slice_in_dim(basis, first_column, quarter, 1)

    changes = []
    coeff_terms = None
    for c in range(CHUNKS):
        chunk = split_rows[:, :, :, c, :].reshape(unit_count, rows, rep_count * width)
        summed = lax.psum_scatter(chunk, "rep", scatter_dimension=2, tiled=True)
        picked = jnp.take(summed, source_unit, axis=0, mode="clip")
        arrived = lax.all_to_all(
            picked.reshape(dev_count, slot_count, rows, width),
            "dev",
            split_axis=0,
            concat_axis=2,
            tiled=True,
        )
        group_mean = arrived[0].astype(jnp.float32) / rep_count
        change = start_rows[:, :, c * width:(c + 1) * width] - group_mean
        changes.append(change)
        term = jnp.einsum(
            "sbq,kq->sbk", change, basis_part[:, c * width:(c + 1) * width], precision=lax.Precision.HIGHEST
        )
        coeff_terms = term if coeff_terms is None else coeff_terms + term

    vec_terms = vec_groups[0].astype(jnp.float32)
    coeff_flat = coeff_terms.reshape(-1)
    joined = lax.psum(jnp.concatenate([coeff_flat, vec_terms.reshape(-1)]), "rep")
    coeffs = joined[: coeff_flat.shape[0]].reshape(coeff_terms.shape)
    vec_summed = joined[coeff_flat.shape[0]:].reshape(vec_terms.shape)

    owned_mask = is_owned[:, None, None]
    new_starts, new_momenta, returned_parts = [], [], []
    for c in range(CHUNKS):
        cols = slice(c * width, (c + 1) * width)
        projected = jnp.einsum("sbk,kq->sbq", coeffs, basis_part[:, cols], precision=lax.Precision.HIGHEST)
        outer_grad = jnp.where(is_embedding[:, None, None], projected, changes[c])
        fresh_momentum = outer_momentum * momentum_rows[:, :, cols] + outer_grad
        fresh_start = start_rows[:, :, cols] - outer_rate * (outer_grad + outer_momentum * fresh_momentum)
        new_momenta.append(jnp.where(owned_mask, fresh_momentum, momentum_rows[:, :, cols]))
        new_starts.append(jnp.where(owned_mask, fresh_start, start_rows[:, :, cols]))
        rounded = fresh_start.astype(jnp.bfloat16)
        pieces = lax.all_to_all(rounded, "dev", split_axis=1, concat_axis=0, tiled=True)
        picked = jnp.take(pieces, target, axis=0, mode="clip")
        returned_parts.append(lax.all_gather(picked[:, :, None, :], "rep", axis=2, tiled=True))
    returned = jnp.stack(returned_parts, axis=3).reshape(unit_count, rows, rep_count * quarter)
    new_start = jnp.concatenate(new_starts, axis=2)
    new_momentum = jnp.concatenate(new_momenta, axis=2)
    vec_change = vec_start - vec_summed / rep_count
    vec_new_momentum = outer_momentum * vec_momentum + vec_change
    vec_new = vec_start - outer_rate * (vec_change + outer_momentum * vec_new_momentum)
    return (new_start[None], new_momentum[None], returned, vec_new, vec_new_momentum)


def solution(mesh):
    return jax.shard_map(
        body,
        mesh=mesh,
        in_specs=(
            P("rep", None, "dev", None),
            P(),
            P("dev", None, None, "rep"),
            P("dev", None, None, "rep"),
            P(),
            P("rep", None, None),
            P(),
            P(),
        ),
        out_specs=(
            P("dev", None, None, "rep"),
            P("dev", None, None, "rep"),
            P(None, "dev", None),
            P(),
            P(),
        ),
        check_vma=False,
    )
```

time: 315 us -> 495 us (1.57); the launches traced: 315 us -> 488 us
  local copies, waits for them, and re-layouts: 22.5 us -> 271 us
  waiting for transfers between devices: 245 us -> 106 us
  blocking collectives: 0 us -> 35.2 us
  other arithmetic: 6.64 us -> 20.2 us
  matrix products: 15 us -> 24.5 us
  starting transfers between devices: 11.3 us -> 17.2 us
    unnamed x19 -> x36, local copies, waits for them, and re-layouts: 8.42 us -> 169 us
    reduce_scatter x1 -> x0, waiting for transfers between devices: 56.3 us -> none  [body(): summed = lax.psum_scatter(own_rows, 'rep', scatter_dimension=2, tiled=True)]
    another operation x1 -> x4, local copies, waits for them, and re-layouts: 0.04 us -> 41.6 us  [the longest x3 32.3 us: body(): jnp.stack(returned_parts, axis=3)]
    all_gather x1 -> x2, waiting for transfers between devices: 38.4 us -> 1.21 us  [body(): lax.all_gather(picked[:, :, None, :], 'rep', axis=2, tiled=True)]
    all_to_all x0 -> x1, blocking collectives: none -> 35.2 us  [body(): lax.all_to_all(rounded, 'dev', split_axis=1, concat_axis=0, tiled=True)]
    all_to_all x1 -> x2, waiting for transfers between devices: 59.4 us -> 24.3 us  [body(): lax.all_to_all(picked.reshape(dev_count, slot_count, rows, width), 'dev',...]
    all_to_all x1, waiting for transfers between devices: 58.6 us -> 31.5 us  [body(): lax.all_to_all(rounded, 'dev', split_axis=1, concat_axis=0, tiled=True)]
    slice x1 -> x3, local copies, waits for them, and re-layouts: 1.13 us -> 19.9 us  [the longest x1 18.6 us: body(): split_rows[:, :, :, c, :].reshape(unit_count, rows, rep_count * width)]
  transfers between devices with their start and end apart: 5 -> 8, of which waited for: 5 -> 6; matrix products, arithmetic and copies ran while one was open for 1% -> 27% of each run, Pallas kernels for 0% -> 0%
where the time goes in v2:
time: 495 us; the launch traced here: 488 us
  local copies, waits for them, and re-layouts  271 us (55%)
  waiting for transfers between devices  106 us (21%)
  blocking collectives  35.2 us (7%)
  matrix products  24.5 us (5%)
  other arithmetic  20.2 us (4%)
  starting transfers between devices  17.2 us (3%)
  between operations  14.3 us (3%)
    unnamed x36, local copies, waits for them, and re-layouts  169 us
    all_to_all x1, blocking collectives, body(): lax.all_to_all(rounded, 'dev', split_axis=1, concat_axis=0, tiled=True)  35.2 us
    psum x1, waiting for transfers between devices, body(): lax.psum(jnp.concatenate([coeff_flat, vec_terms.reshape(-1)]), 'rep')  32.9 us
    another operation x3, local copies, waits for them, and re-layouts, body(): jnp.stack(returned_parts, axis=3)  32.3 us
    all_to_all x1, waiting for transfers between devices, body(): lax.all_to_all(rounded, 'dev', split_axis=1, concat_axis=0, tiled=True)  31.5 us
    all_to_all x2, waiting for transfers between devices, body(): lax.all_to_all(picked.reshape(dev_count, slot_count, rows, width), 'dev',...  24.3 us
    slice x1, local copies, waits for them, and re-layouts, body(): split_rows[:, :, :, c, :].reshape(unit_count, rows, rep_count * width)  18.6 us
    unnamed x7, waiting for transfers between devices  15.7 us
  transfers between devices with their start and end apart: 8, of which 6 were waited for; matrix products, arithmetic and copies ran while one was open for 27% of the time, Pallas kernels for 0%

profile of v2, /device:TPU:0, one launch (start us, length us, event | category | flops | bytes accessed | tf_op | source)
XLA Modules:
  0.0 487.9 jit_solution(6789020381084791406)
XLA Ops:
  7.2 9.4 %reshape_squeeze.9 = bf16[160,16,4,2,128]{4,3,2,1,0:T(2,128)(2,1)} reshape(bf16[1,160,16,1024]{3,2,1,0:T(8,128)(2,1)} %param.8) | data formatting | bytes 10485760 | tf_op jit(solution)/shard_map/reshape;squeeze | solution.py:31
  16.6 18.6 %fusion.11 = (bf16[160,16,4,1,128]{4,3,2,1,0:T(2,128)(2,1)}, bf16[160,16,4,1,128]{4,3,2,1,0:T(2,128)(2,1)}) fusion(bf16[160,16,4,2,128]{4,3,2,1,0:T(2,128)(2,1)} %reshape_squeeze.9), kind=kLoop, calls=%fused_computation.48 | loop fusion | bytes 10485760 | tf_op jit(solution)/shard_map/slice | solution.py:44
  35.2 25.5 %copy.112 = bf16[160,16,4,1,128]{1,0,4,2,3:T(8,128)(2,1)} copy(bf16[160,16,4,1,128]{4,3,2,1,0:T(2,128)(2,1)} %get-tuple-element.43) | data formatting | bytes 5242880
  60.7 35.4 %reshape.115 = bf16[512,2560]{1,0:T(8,128)(2,1)} reshape(bf16[512,160,16]{2,1,0:T(8,128)(2,1)} %bitcast.48) | data formatting | bytes 5242880
  96.2 25.7 %copy.113 = bf16[160,16,4,1,128]{1,0,4,2,3:T(8,128)(2,1)} copy(bf16[160,16,4,1,128]{4,3,2,1,0:T(2,128)(2,1)} %get-tuple-element.42) | data formatting | bytes 5242880
  121.9 35.4 %reshape.117 = bf16[512,2560]{1,0:T(8,128)(2,1)} reshape(bf16[512,160,16]{2,1,0:T(8,128)(2,1)} %bitcast.49) | data formatting | bytes 5242880
  158.3 6.5 %reshape.116 = bf16[128,160,16]{2,1,0:T(8,128)(2,1)} reshape(bf16[128,2560]{1,0:T(8,128)(2,1)} %reduce-scatter.7.cloned.1.call-done) | data formatting | bytes 1310720
  164.8 5.1 %copy.109 = bf16[160,16,128]{2,1,0:T(8,128)(2,1)S(1)} copy(bf16[160,16,128]{1,0,2:T(8,128)(2,1)} %bitcast.56) | data formatting | bytes 1310720
  169.9 2.5 gather_fusion
  172.4 6.9 %all-to-all-start = ((bf16[8,40,16,128]{3,2,1,0:T(8,128)(2,1)}), bf16[8,40,16,128]{3,2,1,0:T(8,128)(2,1)S(1)}, u32[]{:S(2)}, u32[]{:S(2)}) async-start(bf16[8,40,16,128]{3,2,1,0:T(8,128)(2,1)} %bitcast.1), calls=%async_computation | async-start | bytes 2621440 | tf_op jit(solution)/shard_map/all_to_all | solution.py:47
  179.3 15.6 %reduce-scatter.9.cloned.1.call-done = bf16[128,2560]{1,0:T(8,128)(2,1)} async-done(((bf16[512,2560]{1,0:T(8,128)(2,1)}), bf16[128,2560]{1,0:T(8,128)(2,1)}) %reduce-scatter.9.cloned.1.call-update) | async-done | bytes 655376
  194.9 6.5 %reshape.118 = bf16[128,160,16]{2,1,0:T(8,128)(2,1)} reshape(bf16[128,2560]{1,0:T(8,128)(2,1)} %reduce-scatter.9.cloned.1.call-done) | data formatting | bytes 1310720
  201.4 4.6 copy.111
  206.0 2.5 gather_fusion.1
  208.4 2.2 all-to-all-done
  210.7 4.3 all-to-all-start.1
  215.3 5.9 %copy.80 = f32[1,40,128,256]{2,3,1,0:T(8,128)} copy(f32[1,40,128,256]{3,2,1,0:T(8,128)} %param.10) | data formatting | bytes 10485760 | tf_op args[2]
  221.8 2.1 copy.83
  223.9 22.1 %all-to-all-done.1 = bf16[8,40,16,128]{3,2,1,0:T(8,128)(2,1)} async-done(((bf16[8,40,16,128]{3,2,1,0:T(8,128)(2,1)}), bf16[8,40,16,128]{3,2,1,0:T(8,128)(2,1)}, u32[]{:S(2)}, u32[]{:S(2)}) %all-to-all-start.1) | async-done | bytes 1310752 | tf_op jit(solution)/shard_map/all_to_all | solution.py:47
  246.0 1.6 multiply_bitcast_fusion
  247.5 1.9 copy.86
  249.4 2.1 copy.87
  251.6 5.1 %fusion.2 = f32[40,128,64]{1,2,0:T(8,128)S(1)} fusion(f32[40,128,128]{1,2,0:T(8,128)} %copy.83, f32[40,128,256]{1,2,0:T(8,128)} %bitcast.50, f32[64,1024]{1,0:T(8,128)S(1)} %copy-done, s32[]{:T(128)S(6)} %select_n.27), kind=kOutput, calls=%fused_computation.23 | convolution fusion | flops 503971840 | bytes 6586372 | tf_op jit(solution)/shard_map/sbq,kq->sbk/dot_general | solution.py:57
  256.7 4.5 convolution_add_fusion
  261.3 1.9 copy.89
  263.2 1.5 reshape.69
  264.7 2.5 pad_maximum_fusion.1
  267.2 5.9 %copy.91 = f32[1,40,128,256]{2,3,1,0:T(8,128)} copy(f32[1,40,128,256]{3,2,1,0:T(8,128)} %param.11) | data formatting | bytes 10485760 | tf_op args[3]
  273.3 32.9 %all-reduce.2.cloned.1.call-done = f32[340992]{0:T(1024)} async-done(((f32[340992]{0:T(1024)}), f32[340992]{0:T(1024)}) %all-reduce.2.cloned.1.call-update) | async-done | bytes 1363984 | tf_op jit(solution)/shard_map/psum | solution.py:64
  307.5 1.9 reshape.70
  309.4 6.4 %convolution_select_fusion.1 = f32[40,128,128]{1,2,0:T(8,128)S(1)} fusion(f32[40,128,64]{2,1,0:T(8,128)} %reshape.70, pred[40]{0:T(512)(128)(4,1)S(1)} %get-tuple-element.30, f32[40,128,128]{1,2,0:T(8,128)} %copy.83, f32[40,128,256]{1,2,0:T(8,128)} %bitcast.52, f32[64,1024]{1,0:T(8,128)S(1)} %copy-done, s32[]{:T(128)S(6)} %select_n.27), kind=kOutput, calls=%fused_computation.20 | convolution fusion | flops 504627200 | bytes 9208324 | tf_op jit(solution)/shard_map/sbk,kq->sbq/dot_general | solution.py:72
  315.8 8.4 %fusion.10 = (bf16[40,128,128]{1,2,0:T(8,128)(2,1)}, f32[40,128,128]{1,2,0:T(8,128)}, f32[40,128,128]{1,2,0:T(8,128)}, bf16[40,128,128]{1,2,0:T(8,128)(2,1)S(1)}...) fusion(f32[40,128,256]{1,2,0:T(8,128)} %bitcast.58, f32[40,128,256]{1,2,0:T(8,128)S(1)} %bitcast.55, ...), kind=kOutput, calls=%fused_computation.47 | convolution fusion | flops 516423680 | bytes 31491076 | tf_op jit(solution)/shard_map/sbk,kq->sbq/dot_general | solution.py:72
  324.2 2.7 copy.96
  326.9 5.5 %all-to-all-start.3 = ((bf16[40,128,128]{2,0,1:T(8,128)(2,1)}), bf16[40,128,128]{2,0,1:T(8,128)(2,1)}, u32[]{:S(2)}, u32[]{:S(2)}) async-start(bf16[40,128,128]{2,0,1:T(8,128)(2,1)} %copy.96), calls=%async_computation.3 | async-start | bytes 2621440 | tf_op jit(solution)/shard_map/all_to_all | solution.py:79
  332.5 31.5 %all-to-all-done.3 = bf16[40,128,128]{2,0,1:T(8,128)(2,1)} async-done(((bf16[40,128,128]{2,0,1:T(8,128)(2,1)}), bf16[40,128,128]{2,0,1:T(8,128)(2,1)}, u32[]{:S(2)}, u32[]{:S(2)}) %all-to-all-start.3) | async-done | bytes 1310752 | tf_op jit(solution)/shard_map/all_to_all | solution.py:79
  364.0 2.6 copy.98
  366.6 2.9 gather_fusion.3
  369.6 1.9 copy.93
  371.4 35.2 %all_to_all.54 = bf16[40,128,128]{2,0,1:T(8,128)(2,1)S(1)} all-to-all(bf16[40,128,128]{2,0,1:T(8,128)(2,1)} %copy.93), channel_id=1, replica_groups=mesh['rep'=4,'dev'=8] {'dev'}, dimensions={1} | all-to-all | bytes 2621440 | tf_op jit(solution)/shard_map/all_to_all | solution.py:79
  407.8 2.9 gather_fusion.2
  410.8 6.7 %maximum_bitcast_fusion = (f32[1,40,128,256]{2,3,1,0:T(8,128)}, f32[1,40,128,256]{2,3,1,0:T(8,128)}) fusion(f32[40,128,128]{1,2,0:T(8,128)S(1)} %copy-done.4, f32[40,128,128]{1,2,0:T(8,128)} %get-tuple-element.38, f32[40,128,128]{1,2,0:T(8,128)} %get-tuple-element.41, f32[40,128,128]{1,2,0:T(8,128)} %get-tuple-element.40), kind=kLoop, calls=%fused_computation.4 | loop fusion | flops 2621440 | bytes 20971520 | tf_op jit(solution)/shard_map/broadcast_in_dim | solution.py:88
  417.5 5.9 %copy.100 = f32[1,40,128,256]{3,2,1,0:T(8,128)} copy(f32[1,40,128,256]{2,3,1,0:T(8,128)} %get-tuple-element.44) | data formatting | bytes 10485760
  423.4 6.1 %copy.101 = f32[1,40,128,256]{3,2,1,0:T(8,128)} copy(f32[1,40,128,256]{2,3,1,0:T(8,128)} %get-tuple-element.45) | data formatting | bytes 10485760
  430.3 3.5 stack.10
  435.0 13.4 %stack.9 = bf16[160,16,4,1,128]{4,2,1,0,3:T(4,128)(2,1)} reshape(bf16[160,16,512]{2,1,0:T(8,128)(2,1)} %all-gather.5.cloned.1.call-done) | data formatting | bytes 5242880 | tf_op jit(solution)/shard_map/stack | solution.py:82
  448.4 8.0 %pad_maximum_fusion = bf16[160,16,4,2,128]{4,2,1,0,3:T(4,128)(2,1)} fusion(bf16[160,16,4,1,128]{4,2,1,0,3:T(4,128)(2,1)S(1)} %stack.10, bf16[160,16,4,1,128]{4,2,1,0,3:T(4,128)(2,1)} %stack.9), kind=kLoop, calls=%fused_computation.6 | loop fusion | flops 2621440 | bytes 10485760 | tf_op jit(solution)/shard_map/stack | solution.py:82
  456.4 15.4 %copy.99 = bf16[160,16,4,2,128]{4,3,2,1,0:T(2,128)(2,1)} copy(bf16[160,16,4,2,128]{4,2,1,0,3:T(4,128)(2,1)} %pad_maximum_fusion) | data formatting | bytes 10485760 | tf_op jit(solution)/shard_map/stack | solution.py:82
  471.8 9.3 %reshape.71 = bf16[160,16,1024]{2,1,0:T(8,128)(2,1)} reshape(bf16[160,16,4,2,128]{4,3,2,1,0:T(2,128)(2,1)} %copy.99) | data formatting | bytes 10485760 | tf_op jit(solution)/shard_map/reshape | solution.py:82
  (55 shorter events, 6.9 us)
Async XLA Ops:
  7.2 244.4 %copy-start = (f32[64,1024]{1,0:T(8,128)S(1)}, f32[64,1024]{1,0:T(8,128)}, u32[]{:S(2)}) copy-start(f32[64,1024]{1,0:T(8,128)} %param.12) | copy-start | bytes 786436
  7.2 151.1 %reduce-scatter.7.cloned.1.call-start = ((), (), s32[]{:S(2)}) async-start(), calls=%async_computation.9 | async-start | bytes 3276800
  96.2 98.8 %reduce-scatter.9.cloned.1.call-start = ((), (), s32[]{:S(2)}) async-start(), calls=%async_computation.10 | async-start | bytes 3276800
  157.3 0.7 copy-start.9
  172.4 38.3 %all-to-all-start = ((bf16[8,40,16,128]{3,2,1,0:T(8,128)(2,1)}), bf16[8,40,16,128]{3,2,1,0:T(8,128)(2,1)S(1)}, u32[]{:S(2)}, u32[]{:S(2)}) async-start(bf16[8,40,16,128]{3,2,1,0:T(8,128)(2,1)} %bitcast.1), calls=%async_computation | async-start | bytes 2621440 | tf_op jit(solution)/shard_map/all_to_all | solution.py:47
  210.7 35.3 %all-to-all-start.1 = ((bf16[8,40,16,128]{3,2,1,0:T(8,128)(2,1)}), bf16[8,40,16,128]{3,2,1,0:T(8,128)(2,1)}, u32[]{:S(2)}, u32[]{:S(2)}) async-start(bf16[8,40,16,128]{3,2,1,0:T(8,128)(2,1)} %bitcast.6), calls=%async_computation.1 | async-start | bytes 2621440 | tf_op jit(solution)/shard_map/all_to_all | solution.py:47
  214.9 91.2 %all-reduce.2.cloned.1.call-start = ((), (), s32[]{:S(2)}) async-start(), calls=%async_computation.6 | async-start | bytes 2727936 | tf_op jit(solution)/shard_map/psum | solution.py:64
  215.2 5.9 %copy-start.8 = (bf16[1,13,1024]{2,1,0:T(8,128)(2,1)S(1)}, bf16[1,13,1024]{2,1,0:T(8,128)(2,1)}, u32[]{:S(2)}) copy-start(bf16[1,13,1024]{2,1,0:T(8,128)(2,1)} %param.13) | copy-start | bytes 79876
  251.6 5.2 %copy-start.1 = (f32[40,128,128]{1,2,0:T(8,128)}, f32[40,128,128]{1,2,0:T(8,128)S(1)}, u32[]{:S(2)}) copy-start(f32[40,128,128]{1,2,0:T(8,128)S(1)} %copy.87) | copy-start | bytes 7864324
  306.1 1.3 slice-start.2
  307.5 8.3 %slice-start = ((s8[5242880]{0:T(1024)(128)(4,1)}), s8[1048576]{0:T(1024)(128)(4,1)S(1)}, s32[]{:S(2)}) async-start(s8[5242880]{0:T(1024)(128)(4,1)} %bitcast.53), calls=%async_computation.11 | async-start | bytes 2097152
  309.4 6.4 %slice-start.1 = ((s8[5242880]{0:T(1024)(128)(4,1)}), s8[4194304]{0:T(1024)(128)(4,1)S(1)}, s32[]{:S(2)}) async-start(s8[5242880]{0:T(1024)(128)(4,1)} %bitcast.53), calls=%async_computation.12 | async-start | bytes 8388608
  309.4 6.4 %copy-start.2 = (f32[40,128,128]{1,2,0:T(8,128)S(1)}, f32[40,128,128]{1,2,0:T(8,128)}, u32[]{:S(2)}) copy-start(f32[40,128,128]{1,2,0:T(8,128)} %copy-done.1) | copy-start | bytes 7864324
  309.4 6.4 %copy-start.3 = (f32[40,128,64]{2,1,0:T(8,128)S(1)}, f32[40,128,64]{2,1,0:T(8,128)}, u32[]{:S(2)}) copy-start(f32[40,128,64]{2,1,0:T(8,128)} %reshape.70) | copy-start | bytes 3932164
  326.9 37.1 %all-to-all-start.3 = ((bf16[40,128,128]{2,0,1:T(8,128)(2,1)}), bf16[40,128,128]{2,0,1:T(8,128)(2,1)}, u32[]{:S(2)}, u32[]{:S(2)}) async-start(bf16[40,128,128]{2,0,1:T(8,128)(2,1)} %copy.96), calls=%async_computation.3 | async-start | bytes 2621440 | tf_op jit(solution)/shard_map/all_to_all | solution.py:79
  332.4 97.8 %all-gather.7.cloned.1.call-start = ((), (), s32[]{:S(2)}) async-start(), calls=%async_computation.8 | async-start | bytes 3276800 | tf_op jit(solution)/shard_map/all_gather | solution.py:81
  369.5 65.5 %all-gather.5.cloned.1.call-start = ((), (), s32[]{:S(2)}) async-start(), calls=%async_computation.7 | async-start | bytes 3276800 | tf_op jit(solution)/shard_map/all_gather | solution.py:81
  406.6 4.2 copy-start.4
  423.4 6.1 %copy-start.5 = (f32[340992]{0:T(1024)S(1)}, f32[340992]{0:T(1024)}, u32[]{:S(2)}) copy-start(f32[340992]{0:T(1024)} %all-reduce.2.cloned.1.call-done) | copy-start | bytes 4091908
  423.4 6.1 %copy-start.6 = (f32[13,1024]{1,0:T(8,128)S(1)}, f32[13,1024]{1,0:T(8,128)}, u32[]{:S(2)}) copy-start(f32[13,1024]{1,0:T(8,128)} %param.14) | copy-start | bytes 159748
  423.4 6.1 %copy-start.7 = (f32[13,1024]{1,0:T(8,128)S(1)}, f32[13,1024]{1,0:T(8,128)}, u32[]{:S(2)}) copy-start(f32[13,1024]{1,0:T(8,128)} %param.15) | copy-start | bytes 159748
Sparse Core Ops, SparseCore 0:
  96.3 37.3 reduce-scatter.6
  157.4 37.4 reduce-scatter.8
  267.3 38.7 all-reduce.1
  369.6 24.0 all-gather.6
  410.9 24.0 all-gather.4

commit v3 on v1

--- a/solution.py
+++ b/solution.py
@@ -8,6 +8,19 @@
 
 outer_rate = 0.7
 outer_momentum = 0.9
+
+
+def rep_sum(x):
+    rep_count = lax.axis_size("rep")
+    total = x.astype(jnp.bfloat16)
+    step = 1
+    while step < rep_count:
+        other = lax.ppermute(total, "rep", [(i, i ^ step) for i in range(rep_count)])
+        total = total.astype(jnp.float32) + other.astype(jnp.float32)
+        step *= 2
+        if step < rep_count:
+            total = total.astype(jnp.bfloat16)
+    return total
 
 
 def body(group_weights, owner, start_weights, momentum, basis, vec_groups, vec_start, vec_momentum):
@@ -26,7 +39,7 @@
     source_unit = jnp.sum(jnp.where(placed, unit_ids[:, None], 0), axis=0)
     own_rows = group_weights[0]
     summed = lax.psum_scatter(own_rows, "rep", scatter_dimension=2, tiled=True)
-    picked = jnp.take(summed, source_unit, axis=0)
+    picked = jnp.take(summed, source_unit, axis=0, mode="clip")
     arrived = lax.all_to_all(
         picked.reshape(dev_count, slot_count, summed.shape[1], summed.shape[2]),
         "dev",
@@ -47,9 +60,9 @@
     coeff_terms = jnp.einsum("sbq,kq->sbk", change, basis_part, precision=lax.Precision.HIGHEST)
     vec_terms = vec_groups[0]
     coeff_flat = coeff_terms.astype(jnp.bfloat16).reshape(-1)
-    joined = lax.psum(jnp.concatenate([coeff_flat, vec_terms.reshape(-1)]), "rep")
-    coeffs = joined[: coeff_flat.shape[0]].reshape(coeff_terms.shape).astype(jnp.float32)
-    vec_summed = joined[coeff_flat.shape[0]:].reshape(vec_terms.shape).astype(jnp.float32)
+    joined = rep_sum(jnp.concatenate([coeff_flat, vec_terms.reshape(-1)]))
+    coeffs = joined[: coeff_flat.shape[0]].reshape(coeff_terms.shape)
+    vec_summed = joined[coeff_flat.shape[0]:].reshape(vec_terms.shape)
     projected = jnp.einsum("sbk,kq->sbq", coeffs, basis_part, precision=lax.Precision.HIGHEST)
     outer_grad = jnp.where(is_embedding[:, None, None], projected, change)
     fresh_momentum = outer_momentum * momentum_rows + outer_grad
@@ -59,7 +72,7 @@
     new_start = jnp.where(owned_mask, fresh_start, start_rows)
     rounded = fresh_start.astype(jnp.bfloat16)
     pieces = lax.all_to_all(rounded, "dev", split_axis=1, concat_axis=0, tiled=True)
-    picked = jnp.take(pieces, target, axis=0)
+    picked = jnp.take(pieces, target, axis=0, mode="clip")
     returned = lax.all_gather(picked, "rep", axis=2, tiled=True)
     vec_change = vec_start - vec_summed / rep_count
     vec_new_momentum = outer_momentum * vec_momentum + vec_change

time: 315 us -> 304 us (0.965)
  waiting for transfers between devices: 245 us -> 232 us
  local copies, waits for them, and re-layouts: 22.5 us -> 27.5 us
  other arithmetic: 6.64 us -> 3.02 us
    psum x1 -> x0, waiting for transfers between devices: 32 us -> none  [body(): lax.psum(jnp.concatenate([coeff_flat, vec_terms.reshape(-1)]), 'rep')]
    ppermute x0 -> x2, waiting for transfers between devices: none -> 18.7 us  [rep_sum(): lax.ppermute(total, 'rep', [(i, i ^ step) for i in range(rep_count)])]
    unnamed x19 -> x22, local copies, waits for them, and re-layouts: 8.42 us -> 9.58 us
  transfers between devices with their start and end apart: 5 -> 6, of which waited for: 5 -> 6; matrix products, arithmetic and copies ran while one was open for 1% -> 1% of each run, Pallas kernels for 0% -> 0%
where the time goes in v3:
time: 304 us
  waiting for transfers between devices  232 us (76%)
  local copies, waits for them, and re-layouts  27.5 us (9%)
  matrix products  16.7 us (5%)
  between operations  14.2 us (5%)
  starting transfers between devices  10.1 us (3%)
    all_to_all x1, waiting for transfers between devices, body(): lax.all_to_all(picked.reshape(dev_count, slot_count, summed.shape[1], sum...  59.4 us
    all_to_all x1, waiting for transfers between devices, body(): lax.all_to_all(rounded, 'dev', split_axis=1, concat_axis=0, tiled=True)  59.1 us
    reduce_scatter x1, waiting for transfers between devices, body(): summed = lax.psum_scatter(own_rows, 'rep', scatter_dimension=2, tiled=True)  56.4 us
    all_gather x1, waiting for transfers between devices, body(): returned = lax.all_gather(picked, 'rep', axis=2, tiled=True)  37.9 us
    ppermute x2, waiting for transfers between devices, rep_sum(): lax.ppermute(total, 'rep', [(i, i ^ step) for i in range(rep_count)])  18.7 us
    dot_general x1, matrix products, body(): jnp.einsum('sbk,kq->sbq', coeffs, basis_part, precision=lax.Precision.HIG...  11.4 us
    unnamed x22, local copies, waits for them, and re-layouts  9.58 us
  transfers between devices with their start and end apart: 6, of which 6 were waited for; matrix products, arithmetic and copies ran while one was open for 1% of the time, Pallas kernels for 0%

profile of v3, /device:TPU:0, one launch (start us, length us, event | category | flops | bytes accessed | tf_op | source)
XLA Modules:
  0.0 303.6 jit_solution(663076342900306698)
XLA Ops:
  7.2 0.0 copy-start
  7.2 0.0 reduce-scatter.2.cloned.1.call-start
  7.2 0.0 copy-start.7
  7.2 0.7 reduce-scatter.2.cloned.1.call-update
  7.9 0.0 copy-done.7
  7.9 0.2 convert_reduce_fusion
  8.1 0.1 select_reduce_fusion
  8.3 56.4 %reduce-scatter.2.cloned.1.call-done = bf16[160,16,256]{2,1,0:T(8,128)(2,1)} async-done(((bf16[160,16,1024]{2,1,0:T(8,128)(2,1)}), bf16[160,16,256]{2,1,0:T(8,128)(2,1)}) %reduce-scatter.2.cloned.1.call-update) | async-done | bytes 1310736 | tf_op jit(solution)/shard_map/reduce_scatter | solution.py:41
  64.7 4.0 %gather_fusion = bf16[320,16,256]{2,1,0:T(8,128)(2,1)} fusion(bf16[160,16,256]{2,1,0:T(8,128)(2,1)} %reduce-scatter.2.cloned.1.call-done, s32[1024]{0:T(1024)S(1)} %pad_clamp_fusion.1), kind=kCustom, calls=%fused_computation | custom fusion | bytes 5244160 | tf_op jit(solution)/shard_map/jit(_take)/gather | solution.py:42
  68.7 5.6 %all-to-all-start = ((bf16[8,40,16,256]{3,2,1,0:T(8,128)(2,1)}), bf16[8,40,16,256]{3,2,1,0:T(8,128)(2,1)S(1)}, u32[]{:S(2)}, u32[]{:S(2)}) async-start(bf16[8,40,16,256]{3,2,1,0:T(8,128)(2,1)} %bitcast.2), calls=%async_computation.1 | async-start | bytes 5242880 | tf_op jit(solution)/shard_map/all_to_all | solution.py:43
  74.3 0.0 copy-done.6
  74.4 59.4 %all-to-all-done = bf16[8,40,16,256]{3,2,1,0:T(8,128)(2,1)S(1)} async-done(((bf16[8,40,16,256]{3,2,1,0:T(8,128)(2,1)}), bf16[8,40,16,256]{3,2,1,0:T(8,128)(2,1)S(1)}, u32[]{:S(2)}, u32[]{:S(2)}) %all-to-all-start) | async-done | bytes 2621472 | tf_op jit(solution)/shard_map/all_to_all | solution.py:43
  133.8 0.7 multiply_bitcast_fusion
  134.5 0.0 slice-start.1
  134.6 0.8 copy.28
  135.4 0.0 copy-start.2
  135.4 2.3 copy-done.2
  137.8 0.0 copy-done
  137.8 0.0 slice-done
  137.8 0.0 slice-done.1
  137.8 5.4 %fusion.4 = bf16[40,128,64]{1,2,0:T(8,128)(2,1)S(1)} fusion(f32[40,128,256]{2,1,0:T(8,128)S(1)} %bitcast.55, f32[1,40,128,256]{3,2,1,0:T(8,128)S(1)} %bitcast.58, f32[64,1024]{1,0:T(8,128)S(1)} %copy-done, s32[]{:T(128)S(6)} %select_n.18), kind=kOutput, calls=%fused_computation.15 | convolution fusion | flops 1008271360 | bytes 11206660 | tf_op jit(solution)/shard_map/sbq,kq->sbk/dot_general | solution.py:60
  143.1 0.7 copy.29
  143.9 0.6 reshape.51
  144.6 0.1 collective-permute-start
  144.7 2.1 collective-permute-done
  146.8 0.2 add_convert_fusion
  147.0 0.6 collective-permute-start.1
  147.6 0.2 fusion.11
  147.8 16.6 %collective-permute-done.1 = bf16[340992]{0:T(1024)(128)(2,1)S(1)} collective-permute-done((bf16[340992]{0:T(1024)(128)(2,1)S(1)}, bf16[340992]{0:T(1024)(128)(2,1)S(1)}, u32[]{:S(2)}, u32[]{:S(2)}) %collective-permute-start.1) | collective-permute-done | bytes 682016 | tf_op jit(solution)/shard_map/ppermute | solution.py:18
  164.4 0.1 convert_add_fusion
  164.5 0.0 copy-start.3
  164.5 1.1 copy-done.3
  165.7 1.1 slice.20
  166.8 1.6 reshape.52
  168.4 11.4 %fusion.5 = (bf16[40,128,256]{2,1,0:T(8,128)(2,1)S(1)}, f32[1,40,128,256]{3,2,1,0:T(8,128)}, f32[1,40,128,256]{3,2,1,0:T(8,128)}) fusion(f32[1,40,128,256]{3,2,1,0:T(8,128)} %param.11, f32[1,40,128,256]{3,2,1,0:T(8,128)} %param.10, pred[40]{0:T(512)(128)(4,1)S(1)} %get-tuple-element.6, f32[40,128,256]{2,1,0:T(8,128)} %bitcast.56, ...), kind=kOutput, calls=%fused_computation.16 | convolution fusion | flops 1021050880 | bytes 31523844 | tf_op jit(solution)/shard_map/sbk,kq->sbq/dot_general | solution.py:66
  179.8 3.0 copy.31
  182.8 3.6 %all-to-all-start.1 = ((bf16[40,128,256]{2,0,1:T(8,128)(2,1)}), bf16[40,128,256]{2,0,1:T(8,128)(2,1)S(1)}, u32[]{:S(2)}, u32[]{:S(2)}) async-start(bf16[40,128,256]{2,0,1:T(8,128)(2,1)} %copy.31), calls=%async_computation.2 | async-start | bytes 5242880 | tf_op jit(solution)/shard_map/all_to_all | solution.py:74
  186.4 0.0 all-gather.3.cloned.1.call-start
  186.5 59.1 %all-to-all-done.1 = bf16[40,128,256]{2,0,1:T(8,128)(2,1)S(1)} async-done(((bf16[40,128,256]{2,0,1:T(8,128)(2,1)}), bf16[40,128,256]{2,0,1:T(8,128)(2,1)S(1)}, u32[]{:S(2)}, u32[]{:S(2)}) %all-to-all-start.1) | async-done | bytes 2621472 | tf_op jit(solution)/shard_map/all_to_all | solution.py:74
  245.6 2.1 copy.33
  247.6 3.8 %gather_fusion.1 = bf16[160,16,256]{2,1,0:T(8,128)(2,1)} fusion(bf16[320,16,256]{2,1,0:T(8,128)(2,1)} %bitcast.60, s32[1024]{0:T(1024)S(1)} %pad_clamp_fusion), kind=kCustom, calls=%fused_computation.1 | custom fusion | bytes 2622080 | tf_op jit(solution)/shard_map/jit(_take)/gather | solution.py:75
  251.4 0.0 all-gather.3.cloned.1.call-update
  251.4 0.8 slice_multiply_fusion
  252.2 0.0 copy-done.4
  252.3 0.7 multiply_subtract_fusion
  252.9 37.9 %all-gather.3.cloned.1.call-done = bf16[160,16,1024]{2,1,0:T(8,128)(2,1)} async-done(((bf16[160,16,256]{2,1,0:T(8,128)(2,1)}), bf16[160,16,1024]{2,1,0:T(8,128)(2,1)}) %all-gather.3.cloned.1.call-update) | async-done | bytes 5242896 | tf_op jit(solution)/shard_map/all_gather | solution.py:76
  290.8 6.0 %copy.38 = bf16[160,16,1024]{2,1,0:T(8,128)(2,1)} copy(bf16[160,16,1024]{2,1,0:T(8,128)(2,1)} %all-gather.3.cloned.1.call-done) | data formatting | bytes 10485760
  296.8 0.0 copy-done.1
  (16 shorter events, 0.1 us)
Async XLA Ops:
  7.2 130.6 %copy-start = (f32[64,1024]{1,0:T(8,128)S(1)}, f32[64,1024]{1,0:T(8,128)}, u32[]{:S(2)}) copy-start(f32[64,1024]{1,0:T(8,128)} %param.12) | copy-start | bytes 786436
  7.2 57.5 %reduce-scatter.2.cloned.1.call-start = ((), (), s32[]{:S(2)}) async-start(), calls=%async_computation.3 | async-start | bytes 6553600 | tf_op jit(solution)/shard_map/reduce_scatter | solution.py:41
  7.2 0.7 copy-start.7
  68.7 5.7 %copy-start.6 = (bf16[1,13,1024]{2,1,0:T(8,128)(2,1)S(1)}, bf16[1,13,1024]{2,1,0:T(8,128)(2,1)}, u32[]{:S(2)}) copy-start(bf16[1,13,1024]{2,1,0:T(8,128)(2,1)} %param.13) | copy-start | bytes 79876
  68.7 65.1 %all-to-all-start = ((bf16[8,40,16,256]{3,2,1,0:T(8,128)(2,1)}), bf16[8,40,16,256]{3,2,1,0:T(8,128)(2,1)S(1)}, u32[]{:S(2)}, u32[]{:S(2)}) async-start(bf16[8,40,16,256]{3,2,1,0:T(8,128)(2,1)} %bitcast.2), calls=%async_computation.1 | async-start | bytes 5242880 | tf_op jit(solution)/shard_map/all_to_all | solution.py:43
  133.8 4.0 %slice-start = ((s8[5242880]{0:T(1024)(128)(4,1)}), s8[4194304]{0:T(1024)(128)(4,1)S(1)}, s32[]{:S(2)}) async-start(s8[5242880]{0:T(1024)(128)(4,1)} %bitcast.57), calls=%async_computation.5 | async-start | bytes 8388608
  134.5 3.2 %slice-start.1 = ((s8[5242880]{0:T(1024)(128)(4,1)}), s8[1048576]{0:T(1024)(128)(4,1)S(1)}, s32[]{:S(2)}) async-start(s8[5242880]{0:T(1024)(128)(4,1)} %bitcast.57), calls=%async_computation.6 | async-start | bytes 2097152
  135.4 2.4 copy-start.2
  144.6 2.2 collective-permute-start
  147.0 17.4 %collective-permute-start.1 = (bf16[340992]{0:T(1024)(128)(2,1)S(1)}, bf16[340992]{0:T(1024)(128)(2,1)S(1)}, u32[]{:S(2)}, u32[]{:S(2)}) collective-permute-start(bf16[340992]{0:T(1024)(128)(2,1)S(1)} %add_convert_fusion), channel_id=1, source_target_pairs={{0,16},{8,24},{16,0},{24,8},{1,17},{9,25},{17,1},{25,9},{2,18},{10... | collective-permute-start | bytes 2045960 | tf_op jit(solution)/shard_map/ppermute | solution.py:18
  164.5 1.1 copy-start.3
  182.8 62.8 %all-to-all-start.1 = ((bf16[40,128,256]{2,0,1:T(8,128)(2,1)}), bf16[40,128,256]{2,0,1:T(8,128)(2,1)S(1)}, u32[]{:S(2)}, u32[]{:S(2)}) async-start(bf16[40,128,256]{2,0,1:T(8,128)(2,1)} %copy.31), calls=%async_computation.2 | async-start | bytes 5242880 | tf_op jit(solution)/shard_map/all_to_all | solution.py:74
  186.4 104.4 %all-gather.3.cloned.1.call-start = ((), (), s32[]{:S(2)}) async-start(), calls=%async_computation.4 | async-start | bytes 6553600 | tf_op jit(solution)/shard_map/all_gather | solution.py:76
  247.6 4.6 %copy-start.4 = (f32[13,1024]{1,0:T(8,128)S(1)}, f32[13,1024]{1,0:T(8,128)}, u32[]{:S(2)}) copy-start(f32[13,1024]{1,0:T(8,128)} %param.14) | copy-start | bytes 159748
  247.6 4.6 %copy-start.5 = (f32[13,1024]{1,0:T(8,128)S(1)}, f32[13,1024]{1,0:T(8,128)}, u32[]{:S(2)}) copy-start(f32[13,1024]{1,0:T(8,128)} %param.15) | copy-start | bytes 159748
  290.8 6.0 %copy-start.1 = (f32[64,1024]{1,0:T(8,128)S(1)}, f32[64,1024]{1,0:T(8,128)}, u32[]{:S(2)}) copy-start(f32[64,1024]{1,0:T(8,128)} %param.12) | copy-start | bytes 786436
Sparse Core Ops, SparseCore 0:
  10.6 54.0 reduce-scatter.1
  251.5 39.2 all-gather.2

commit v4 on v3

--- a/solution.py
+++ b/solution.py
@@ -2,6 +2,7 @@
 import jax.numpy as jnp
 from jax import lax
 from jax.sharding import PartitionSpec as P
+from jax.experimental import pallas as pl
 
 EMB_FIRST = 96
 
@@ -23,6 +24,44 @@
     return total
 
 
+def _split_kernel(x_ref, a_ref, b_ref):
+    w = a_ref.shape[-1]
+    a_ref[0] = x_ref[:, :, :w]
+    b_ref[0] = x_ref[:, :, w:]
+
+
+def split_halves(x, width):
+    units, rows, full = x.shape
+    quarters = full // (2 * width)
+    spec = pl.BlockSpec((1, units, rows, width), lambda q: (q, 0, 0, 0))
+    return pl.pallas_call(
+        _split_kernel,
+        grid=(quarters,),
+        in_specs=[pl.BlockSpec((units, rows, 2 * width), lambda q: (0, 0, q))],
+        out_specs=[spec, spec],
+        out_shape=[jax.ShapeDtypeStruct((quarters, units, rows, width), x.dtype)] * 2,
+    )(x)
+
+
+def _join_kernel(a_ref, b_ref, o_ref):
+    w = a_ref.shape[-1]
+    o_ref[:, :, :w] = a_ref[...]
+    o_ref[:, :, w:] = b_ref[...]
+
+
+def join_halves(a, b, width):
+    units, rows, part = a.shape
+    quarters = part // width
+    spec = pl.BlockSpec((units, rows, width), lambda q: (0, 0, q))
+    return pl.pallas_call(
+        _join_kernel,
+        grid=(quarters,),
+        in_specs=[spec, spec],
+        out_specs=pl.BlockSpec((units, rows, 2 * width), lambda q: (0, 0, q)),
+        out_shape=jax.ShapeDtypeStruct((units, rows, 2 * part), a.dtype),
+    )(a, b)
+
+
 def body(group_weights, owner, start_weights, momentum, basis, vec_groups, vec_start, vec_momentum):
     dev_count = lax.axis_size("dev")
     rep_count = lax.axis_size("rep")
@@ -38,15 +77,20 @@
     placed = target[:, None] == positions[None, :]
     source_unit = jnp.sum(jnp.where(placed, unit_ids[:, None], 0), axis=0)
     own_rows = group_weights[0]
-    summed = lax.psum_scatter(own_rows, "rep", scatter_dimension=2, tiled=True)
-    picked = jnp.take(summed, source_unit, axis=0, mode="clip")
-    arrived = lax.all_to_all(
-        picked.reshape(dev_count, slot_count, summed.shape[1], summed.shape[2]),
-        "dev",
-        split_axis=0,
-        concat_axis=2,
-        tiled=True,
-    )
+    width = quarter // 2
+    halves = split_halves(own_rows, width)
+    arrived_parts = []
+    for half in halves:
+        summed = lax.psum_scatter(half, "rep", scatter_dimension=0, tiled=True)[0]
+        picked = jnp.take(summed, source_unit, axis=0, mode="clip")
+        arrived_parts.append(lax.all_to_all(
+            picked.reshape(dev_count, slot_count, summed.shape[1], summed.shape[2]),
+            "dev",
+            split_axis=0,
+            concat_axis=2,
+            tiled=True,
+        ))
+    arrived = jnp.concatenate(arrived_parts, axis=3)
     group_mean = arrived[0].astype(jnp.float32) / rep_count
     start_rows = start_weights[0]
     momentum_rows = momentum[0]
@@ -71,9 +115,12 @@
     new_momentum = jnp.where(owned_mask, fresh_momentum, momentum_rows)
     new_start = jnp.where(owned_mask, fresh_start, start_rows)
     rounded = fresh_start.astype(jnp.bfloat16)
-    pieces = lax.all_to_all(rounded, "dev", split_axis=1, concat_axis=0, tiled=True)
-    picked = jnp.take(pieces, target, axis=0, mode="clip")
-    returned = lax.all_gather(picked, "rep", axis=2, tiled=True)
+    gathered = []
+    for c in range(2):
+        pieces = lax.all_to_all(rounded[:, :, c * width:(c + 1) * width], "dev", split_axis=1, concat_axis=0, tiled=True)
+        picked = jnp.take(pieces, target, axis=0, mode="clip")
+        gathered.append(lax.all_gather(picked, "rep", axis=2, tiled=True))
+    returned = join_halves(gathered[0], gathered[1], width)
     vec_change = vec_start - vec_summed / rep_count
     vec_new_momentum = outer_momentum * vec_momentum + vec_change
     vec_new = vec_start - outer_rate * (vec_change + outer_momentum * vec_new_momentum)

time: 304 us -> 297 us (0.977)
  waiting for transfers between devices: 232 us -> 170 us
  blocking collectives: 0 us -> 34.9 us
  Pallas kernels: 0 us -> 11.2 us
  starting transfers between devices: 10.1 us -> 15.4 us
    all_to_all x0 -> x1, blocking collectives: none -> 34.9 us  [body(): lax.all_to_all(rounded[:, :, c * width:(c + 1) * width], 'dev', split_axi...]
    all_to_all x1 -> x2, waiting for transfers between devices: 59.4 us -> 30.5 us  [body(): lax.all_to_all(picked.reshape(dev_count, slot_count, summed.shape[1], sum...]
    all_to_all x1, waiting for transfers between devices: 59.1 us -> 30.9 us  [body(): lax.all_to_all(rounded[:, :, c * width:(c + 1) * width], 'dev', split_axi...]
    all_gather x1 -> x2, waiting for transfers between devices: 37.9 us -> 22.6 us  [body(): gathered.append(lax.all_gather(picked, 'rep', axis=2, tiled=True))]
    pallas_call x0 -> x2, Pallas kernels: none -> 11.2 us  [the longest x1 5.61 us: split_halves(): pl.pallas_call(_split_kernel, grid=(quarters,), in_specs=[pl.BlockSpec((u...]
    reduce_scatter x1 -> x2, waiting for transfers between devices: 56.4 us -> 65.8 us  [body(): summed = lax.psum_scatter(half, 'rep', scatter_dimension=0, tiled=True)[0]]
    unnamed x22 -> x15, local copies, waits for them, and re-layouts: 9.58 us -> 1.21 us
    all_to_all x1 -> x2, starting transfers between devices: 5.65 us -> 11 us  [body(): lax.all_to_all(picked.reshape(dev_count, slot_count, summed.shape[1], sum...]
  transfers between devices with their start and end apart: 6 -> 9, of which waited for: 6 -> 7; matrix products, arithmetic and copies ran while one was open for 1% -> 4% of each run, Pallas kernels for 0% -> 0%
where the time goes in v4:
time: 297 us; the launch traced here: 296 us
  waiting for transfers between devices  170 us (57%)
  blocking collectives  34.9 us (12%)
  local copies, waits for them, and re-layouts  27.2 us (9%)
  matrix products  19.3 us (6%)
  starting transfers between devices  15.4 us (5%)
  between operations  13.9 us (5%)
  Pallas kernels  11.2 us (4%)
  other arithmetic  4.44 us (1%)
    reduce_scatter x2, waiting for transfers between devices, body(): summed = lax.psum_scatter(half, 'rep', scatter_dimension=0, tiled=True)[0]  65.8 us
    all_to_all x1, blocking collectives, body(): lax.all_to_all(rounded[:, :, c * width:(c + 1) * width], 'dev', split_axi...  34.9 us
    all_to_all x1, waiting for transfers between devices, body(): lax.all_to_all(rounded[:, :, c * width:(c + 1) * width], 'dev', split_axi...  30.9 us
    all_to_all x2, waiting for transfers between devices, body(): lax.all_to_all(picked.reshape(dev_count, slot_count, summed.shape[1], sum...  30.5 us
    all_gather x2, waiting for transfers between devices, body(): gathered.append(lax.all_gather(picked, 'rep', axis=2, tiled=True))  22.6 us
    ppermute x2, waiting for transfers between devices, rep_sum(): lax.ppermute(total, 'rep', [(i, i ^ step) for i in range(rep_count)])  19.1 us
    dot_general x1, matrix products, body(): jnp.einsum('sbk,kq->sbq', coeffs, basis_part, precision=lax.Precision.HIG...  11.2 us
    all_to_all x2, starting transfers between devices, body(): lax.all_to_all(picked.reshape(dev_count, slot_count, summed.shape[1], sum...  11 us
  transfers between devices with their start and end apart: 9, of which 7 were waited for; matrix products, arithmetic and copies ran while one was open for 4% of the time, Pallas kernels for 0%

profile of v4, /device:TPU:0, one launch (start us, length us, event | category | flops | bytes accessed | tf_op | source)
XLA Modules:
  0.0 296.0 jit_solution(14545333060513201423)
XLA Ops:
  7.2 0.0 reduce-scatter.5.cloned.1.call-start
  7.2 5.6 %shard_map.119 = (bf16[4,160,16,128]{3,2,1,0:T(8,128)(2,1)}, bf16[4,160,16,128]{3,2,1,0:T(8,128)(2,1)}) custom-call(bf16[160,16,1024]{2,1,0:T(8,128)(2,1)} %bitcast.86), custom_call_target="tpu_custom_call" | custom-call | tf_op jit(solution)/shard_map/pallas_call | solution.py:37
  12.8 0.0 reduce-scatter.5.cloned.1.call-update
  12.9 0.0 reduce-scatter.3.cloned.1.call-start
  12.9 0.7 reduce-scatter.3.cloned.1.call-update
  13.6 0.2 convert_reduce_fusion
  13.8 0.1 select_reduce_fusion
  14.0 36.4 %reduce-scatter.5.cloned.1.call-done = bf16[1,160,16,128]{3,2,1,0:T(8,128)(2,1)} async-done(((bf16[4,160,16,128]{3,2,1,0:T(8,128)(2,1)}), bf16[1,160,16,128]{3,2,1,0:T(8,128)(2,1)}) %reduce-scatter.5.cloned.1.call-update) | async-done | bytes 655376 | tf_op jit(solution)/shard_map/reduce_scatter | solution.py:84
  50.4 3.0 %gather_fusion.1 = bf16[320,16,128]{2,1,0:T(8,128)(2,1)} fusion(bf16[160,16,128]{2,1,0:T(8,128)(2,1)} %bitcast.92, s32[1024]{0:T(1024)S(1)} %pad_clamp_fusion.1), kind=kCustom, calls=%fused_computation.1 | custom fusion | bytes 2622720 | tf_op jit(solution)/shard_map/jit(_take)/gather | solution.py:85
  53.4 5.5 %all-to-all-start.1 = ((bf16[8,40,16,128]{3,2,1,0:T(8,128)(2,1)}), bf16[8,40,16,128]{3,2,1,0:T(8,128)(2,1)S(1)}, u32[]{:S(2)}, u32[]{:S(2)}) async-start(bf16[8,40,16,128]{3,2,1,0:T(8,128)(2,1)} %bitcast.8), calls=%async_computation.3 | async-start | bytes 2621440 | tf_op jit(solution)/shard_map/all_to_all | solution.py:86
  58.9 29.4 %reduce-scatter.3.cloned.1.call-done = bf16[1,160,16,128]{3,2,1,0:T(8,128)(2,1)} async-done(((bf16[4,160,16,128]{3,2,1,0:T(8,128)(2,1)}), bf16[1,160,16,128]{3,2,1,0:T(8,128)(2,1)}) %reduce-scatter.3.cloned.1.call-update) | async-done | bytes 655376 | tf_op jit(solution)/shard_map/reduce_scatter | solution.py:84
  88.3 3.0 %gather_fusion = bf16[320,16,128]{2,1,0:T(8,128)(2,1)} fusion(bf16[160,16,128]{2,1,0:T(8,128)(2,1)} %bitcast.93, s32[1024]{0:T(1024)S(1)} %pad_clamp_fusion.1), kind=kCustom, calls=%fused_computation | custom fusion | bytes 2622720 | tf_op jit(solution)/shard_map/jit(_take)/gather | solution.py:85
  91.4 5.5 %all-to-all-start = ((bf16[8,40,16,128]{3,2,1,0:T(8,128)(2,1)}), bf16[8,40,16,128]{3,2,1,0:T(8,128)(2,1)}, u32[]{:S(2)}, u32[]{:S(2)}) async-start(bf16[8,40,16,128]{3,2,1,0:T(8,128)(2,1)} %bitcast.3), calls=%async_computation.1 | async-start | bytes 2621440 | tf_op jit(solution)/shard_map/all_to_all | solution.py:86
  96.9 0.6 reshape_squeeze.3
  97.6 0.4 copy.38
  97.9 30.5 %all-to-all-done = bf16[8,40,16,128]{3,2,1,0:T(8,128)(2,1)} async-done(((bf16[8,40,16,128]{3,2,1,0:T(8,128)(2,1)}), bf16[8,40,16,128]{3,2,1,0:T(8,128)(2,1)}, u32[]{:S(2)}, u32[]{:S(2)}) %all-to-all-start) | async-done | bytes 1310752 | tf_op jit(solution)/shard_map/all_to_all | solution.py:86
  128.4 1.7 copy.37
  130.1 8.1 %fusion.6 = bf16[40,128,64]{1,2,0:T(8,128)(2,1)S(1)} fusion(f32[1,40,128,256]{3,2,1,0:T(8,128)} %param.10, bf16[1,40,128,128]{3,2,1,0:T(8,128)(2,1)S(1)} %bitcast.82, bf16[1,40,128,128]{3,2,1,0:T(8,128)(2,1)S(1)} %bitcast.84, f32[64,1024]{1,0:T(8,128)S(1)} %copy-done, s32[]{:T(128)S(6)} %select_n.18), kind=kOutput, calls=%fused_computation.18 | convolution fusion | flops 1014824960 | bytes 8585220 | tf_op jit(solution)/shard_map/sbq,kq->sbk/dot_general | solution.py:104
  138.2 1.4 copy.39
  139.6 1.9 reshape.51
  141.6 0.8 constant_dynamic-update-slice_fusion
  142.3 2.1 collective-permute-done
  144.4 1.0 add_convert_fusion
  145.4 0.5 collective-permute-start.1
  146.0 0.2 fusion.13
  146.2 16.9 %collective-permute-done.1 = bf16[340992]{0:T(1024)(128)(2,1)} collective-permute-done((bf16[340992]{0:T(1024)(128)(2,1)}, bf16[340992]{0:T(1024)(128)(2,1)}, u32[]{:S(2)}, u32[]{:S(2)}) %collective-permute-start.1) | collective-permute-done | bytes 682016 | tf_op jit(solution)/shard_map/ppermute | solution.py:19
  163.1 1.4 convert_add_fusion
  164.6 1.1 copy-done.2
  165.7 1.1 slice.32
  166.8 2.8 reshape.52
  169.7 11.2 %fusion.1 = (f32[1,40,128,256]{3,2,1,0:T(8,128)}, f32[1,40,128,256]{3,2,1,0:T(8,128)}, bf16[40,128,256]{2,1,0:T(8,128)(2,1)S(1)}) fusion(f32[1,40,128,256]{3,2,1,0:T(8,128)} %param.11, f32[1,40,128,256]{3,2,1,0:T(8,128)} %param.10, pred[40]{0:T(512)(128)(4,1)S(1)} %get-tuple-element.9, pred[40]{0:T(512)(128)(4,1)S(1)} %get-tuple-element.10, ...), kind=kOutput, calls=%fused_computation.7 | convolution fusion | flops 1027604480 | bytes 27591684 | tf_op jit(solution)/shard_map/sbk,kq->sbq/dot_general | solution.py:110
  180.9 0.5 fusion.19
  181.4 1.9 copy.44
  183.3 3.6 %all-to-all-start.3 = ((bf16[40,128,128]{2,0,1:T(8,128)(2,1)}), bf16[40,128,128]{2,0,1:T(8,128)(2,1)S(1)}, u32[]{:S(2)}, u32[]{:S(2)}) async-start(bf16[40,128,128]{2,0,1:T(8,128)(2,1)} %copy.44), calls=%async_computation.5 | async-start | bytes 2621440 | tf_op jit(solution)/shard_map/all_to_all | solution.py:120
  186.9 0.0 all-gather.7.cloned.1.call-start
  187.0 30.9 %all-to-all-done.3 = bf16[40,128,128]{2,0,1:T(8,128)(2,1)S(1)} async-done(((bf16[40,128,128]{2,0,1:T(8,128)(2,1)}), bf16[40,128,128]{2,0,1:T(8,128)(2,1)S(1)}, u32[]{:S(2)}, u32[]{:S(2)}) %all-to-all-start.3) | async-done | bytes 1310752 | tf_op jit(solution)/shard_map/all_to_all | solution.py:120
  217.9 1.3 copy.46
  219.2 2.9 gather_fusion.3
  222.1 0.0 all-gather.7.cloned.1.call-update
  222.1 0.0 all-gather.5.cloned.1.call-start
  222.1 0.8 copy.41
  223.0 34.9 %all_to_all.72 = bf16[40,128,128]{2,0,1:T(8,128)(2,1)S(1)} all-to-all(bf16[40,128,128]{2,0,1:T(8,128)(2,1)S(1)} %copy.41), channel_id=1, replica_groups=mesh['rep'=4,'dev'=8] {'dev'}, dimensions={1} | all-to-all | bytes 2621440 | tf_op jit(solution)/shard_map/all_to_all | solution.py:120
  257.9 0.2 copy.43
  258.1 1.6 gather_fusion.2
  259.7 0.8 slice_multiply_fusion
  260.5 0.7 multiply_subtract_fusion
  261.2 22.6 %all-gather.5.cloned.1.call-done.a_ref = bf16[160,16,512]{2,1,0:T(8,128)(2,1)} async-done(((bf16[160,16,128]{2,1,0:T(8,128)(2,1)}), bf16[160,16,512]{2,1,0:T(8,128)(2,1)}) %all-gather.5.cloned.1.call-update) | async-done | bytes 2621456 | tf_op jit(solution)/shard_map/all_gather | solution.py:122
  283.9 5.6 %shard_map.120 = bf16[160,16,1024]{2,1,0:T(8,128)(2,1)} custom-call(bf16[160,16,512]{2,1,0:T(8,128)(2,1)} %all-gather.5.cloned.1.call-done.a_ref, bf16[160,16,512]{2,1,0:T(8,128)(2,1)} %all-gather.7.cloned.1.call-done.b_ref), custom_call_target="tpu_custom_call" | custom-call | tf_op jit(solution)/shard_map/pallas_call | solution.py:56
  (24 shorter events, 0.1 us)
Async XLA Ops:
  7.2 122.9 %copy-start = (f32[64,1024]{1,0:T(8,128)S(1)}, f32[64,1024]{1,0:T(8,128)}, u32[]{:S(2)}) copy-start(f32[64,1024]{1,0:T(8,128)} %param.12) | copy-start | bytes 786436
  7.2 43.2 %reduce-scatter.5.cloned.1.call-start = ((), (), s32[]{:S(2)}) async-start(), calls=%async_computation.7 | async-start | bytes 3276800 | tf_op jit(solution)/shard_map/reduce_scatter | solution.py:84
  12.8 0.8 copy-start.6
  12.9 75.5 %reduce-scatter.3.cloned.1.call-start = ((), (), s32[]{:S(2)}) async-start(), calls=%async_computation.6 | async-start | bytes 3276800 | tf_op jit(solution)/shard_map/reduce_scatter | solution.py:84
  53.4 38.0 %all-to-all-start.1 = ((bf16[8,40,16,128]{3,2,1,0:T(8,128)(2,1)}), bf16[8,40,16,128]{3,2,1,0:T(8,128)(2,1)S(1)}, u32[]{:S(2)}, u32[]{:S(2)}) async-start(bf16[8,40,16,128]{3,2,1,0:T(8,128)(2,1)} %bitcast.8), calls=%async_computation.3 | async-start | bytes 2621440 | tf_op jit(solution)/shard_map/all_to_all | solution.py:86
  88.3 8.6 %copy-start.5 = (bf16[1,13,1024]{2,1,0:T(8,128)(2,1)S(1)}, bf16[1,13,1024]{2,1,0:T(8,128)(2,1)}, u32[]{:S(2)}) copy-start(bf16[1,13,1024]{2,1,0:T(8,128)(2,1)} %param.13) | copy-start | bytes 79876
  91.4 37.0 %all-to-all-start = ((bf16[8,40,16,128]{3,2,1,0:T(8,128)(2,1)}), bf16[8,40,16,128]{3,2,1,0:T(8,128)(2,1)}, u32[]{:S(2)}, u32[]{:S(2)}) async-start(bf16[8,40,16,128]{3,2,1,0:T(8,128)(2,1)} %bitcast.3), calls=%async_computation.1 | async-start | bytes 2621440 | tf_op jit(solution)/shard_map/all_to_all | solution.py:86
  142.3 2.1 collective-permute-start
  145.4 17.7 %collective-permute-start.1 = (bf16[340992]{0:T(1024)(128)(2,1)}, bf16[340992]{0:T(1024)(128)(2,1)}, u32[]{:S(2)}, u32[]{:S(2)}) collective-permute-start(bf16[340992]{0:T(1024)(128)(2,1)} %add_convert_fusion), channel_id=1, source_target_pairs={{0,16},{8,24},{16,0},{24,8},{1,17},{9,25},{17,1},{25,9},{2,18},{10... | collective-permute-start | bytes 2045960 | tf_op jit(solution)/shard_map/ppermute | solution.py:19
  164.5 1.1 copy-start.2
  183.3 34.6 %all-to-all-start.3 = ((bf16[40,128,128]{2,0,1:T(8,128)(2,1)}), bf16[40,128,128]{2,0,1:T(8,128)(2,1)S(1)}, u32[]{:S(2)}, u32[]{:S(2)}) async-start(bf16[40,128,128]{2,0,1:T(8,128)(2,1)} %copy.44), calls=%async_computation.5 | async-start | bytes 2621440 | tf_op jit(solution)/shard_map/all_to_all | solution.py:120
  186.9 74.3 %all-gather.7.cloned.1.call-start = ((), (), s32[]{:S(2)}) async-start(), calls=%async_computation.9 | async-start | bytes 3276800 | tf_op jit(solution)/shard_map/all_gather | solution.py:122
  222.1 61.8 %all-gather.5.cloned.1.call-start = ((), (), s32[]{:S(2)}) async-start(), calls=%async_computation.8 | async-start | bytes 3276800 | tf_op jit(solution)/shard_map/all_gather | solution.py:122
  257.9 2.6 copy-start.3
  257.9 2.6 copy-start.4
  283.9 5.6 %copy-start.1 = (f32[64,1024]{1,0:T(8,128)S(1)}, f32[64,1024]{1,0:T(8,128)}, u32[]{:S(2)}) copy-start(f32[64,1024]{1,0:T(8,128)} %param.12) | copy-start | bytes 786436
Sparse Core Ops, SparseCore 0:
  13.0 37.3 reduce-scatter.4
  53.6 34.6 reduce-scatter.2
  222.2 23.9 all-gather.6
  259.8 23.9 all-gather.4

commit v5 on v4

--- a/solution.py
+++ b/solution.py
@@ -24,42 +24,45 @@
     return total
 
 
-def _split_kernel(x_ref, a_ref, b_ref):
-    w = a_ref.shape[-1]
-    a_ref[0] = x_ref[:, :, :w]
-    b_ref[0] = x_ref[:, :, w:]
+def _copy_kernel(x_ref, o_ref):
+    o_ref[...] = x_ref[...].reshape(o_ref.shape)
 
 
-def split_halves(x, width):
+def take_half(x, width, half):
     units, rows, full = x.shape
     quarters = full // (2 * width)
-    spec = pl.BlockSpec((1, units, rows, width), lambda q: (q, 0, 0, 0))
     return pl.pallas_call(
-        _split_kernel,
+        _copy_kernel,
         grid=(quarters,),
-        in_specs=[pl.BlockSpec((units, rows, 2 * width), lambda q: (0, 0, q))],
-        out_specs=[spec, spec],
-        out_shape=[jax.ShapeDtypeStruct((quarters, units, rows, width), x.dtype)] * 2,
+        in_specs=[pl.BlockSpec((units, rows, width), lambda q: (0, 0, 2 * q + half))],
+        out_specs=pl.BlockSpec((1, units, rows, width), lambda q: (q, 0, 0, 0)),
+        out_shape=jax.ShapeDtypeStruct((quarters, units, rows, width), x.dtype),
     )(x)
 
 
-def _join_kernel(a_ref, b_ref, o_ref):
-    w = a_ref.shape[-1]
-    o_ref[:, :, :w] = a_ref[...]
-    o_ref[:, :, w:] = b_ref[...]
+def _place_kernel(a_ref, base_ref, o_ref):
+    del base_ref
+    o_ref[...] = a_ref[...]
 
 
-def join_halves(a, b, width):
+def place_half(a, width, half, base=None):
     units, rows, part = a.shape
     quarters = part // width
-    spec = pl.BlockSpec((units, rows, width), lambda q: (0, 0, q))
+    in_spec = pl.BlockSpec((units, rows, width), lambda q: (0, 0, q))
+    out_spec = pl.BlockSpec((units, rows, width), lambda q: (0, 0, 2 * q + half))
+    out_shape = jax.ShapeDtypeStruct((units, rows, 2 * part), a.dtype)
+    if base is None:
+        return pl.pallas_call(
+            _copy_kernel, grid=(quarters,), in_specs=[in_spec], out_specs=out_spec, out_shape=out_shape
+        )(a)
     return pl.pallas_call(
-        _join_kernel,
+        _place_kernel,
         grid=(quarters,),
-        in_specs=[spec, spec],
-        out_specs=pl.BlockSpec((units, rows, 2 * width), lambda q: (0, 0, q)),
-        out_shape=jax.ShapeDtypeStruct((units, rows, 2 * part), a.dtype),
-    )(a, b)
+        in_specs=[in_spec, pl.BlockSpec(memory_space=pl.ANY)],
+        out_specs=out_spec,
+        out_shape=out_shape,
+        input_output_aliases={1: 0},
+    )(a, base)
 
 
 def body(group_weights, owner, start_weights, momentum, basis, vec_groups, vec_start, vec_momentum):
@@ -78,9 +81,9 @@
     source_unit = jnp.sum(jnp.where(placed, unit_ids[:, None], 0), axis=0)
     own_rows = group_weights[0]
     width = quarter // 2
-    halves = split_halves(own_rows, width)
     arrived_parts = []
-    for half in halves:
+    for c in range(2):
+        half = take_half(own_rows, width, c)
         summed = lax.psum_scatter(half, "rep", scatter_dimension=0, tiled=True)[0]
         picked = jnp.take(summed, source_unit, axis=0, mode="clip")
         arrived_parts.append(lax.all_to_all(
@@ -101,13 +104,13 @@
     change = start_rows - group_mean
     first_column = lax.axis_index("rep") * quarter
     basis_part = lax.dynamic_slice_in_dim(basis, first_column, quarter, 1)
-    coeff_terms = jnp.einsum("sbq,kq->sbk", change, basis_part, precision=lax.Precision.HIGHEST)
+    coeff_terms = jnp.einsum("sbq,kq->sbk", change, basis_part, precision=lax.Precision.HIGH)
     vec_terms = vec_groups[0]
     coeff_flat = coeff_terms.astype(jnp.bfloat16).reshape(-1)
     joined = rep_sum(jnp.concatenate([coeff_flat, vec_terms.reshape(-1)]))
     coeffs = joined[: coeff_flat.shape[0]].reshape(coeff_terms.shape)
     vec_summed = joined[coeff_flat.shape[0]:].reshape(vec_terms.shape)
-    projected = jnp.einsum("sbk,kq->sbq", coeffs, basis_part, precision=lax.Precision.HIGHEST)
+    projected = jnp.einsum("sbk,kq->sbq", coeffs, basis_part, precision=lax.Precision.HIGH)
     outer_grad = jnp.where(is_embedding[:, None, None], projected, change)
     fresh_momentum = outer_momentum * momentum_rows + outer_grad
     fresh_start = start_rows - outer_rate * (outer_grad + outer_momentum * fresh_momentum)
@@ -115,12 +118,12 @@
     new_momentum = jnp.where(owned_mask, fresh_momentum, momentum_rows)
     new_start = jnp.where(owned_mask, fresh_start, start_rows)
     rounded = fresh_start.astype(jnp.bfloat16)
-    gathered = []
+    returned = None
     for c in range(2):
         pieces = lax.all_to_all(rounded[:, :, c * width:(c + 1) * width], "dev", split_axis=1, concat_axis=0, tiled=True)
         picked = jnp.take(pieces, target, axis=0, mode="clip")
-        gathered.append(lax.all_gather(picked, "rep", axis=2, tiled=True))
-    returned = join_halves(gathered[0], gathered[1], width)
+        gathered = lax.all_gather(picked, "rep", axis=2, tiled=True)
+        returned = place_half(gathered, width, c, returned)
     vec_change = vec_start - vec_summed / rep_count
     vec_new_momentum = outer_momentum * vec_momentum + vec_change
     vec_new = vec_start - outer_rate * (vec_change + outer_momentum * vec_new_momentum)

time: 297 us -> 290 us (0.976)
  waiting for transfers between devices: 170 us -> 161 us
  Pallas kernels: 11.2 us -> 16.1 us
  matrix products: 19.3 us -> 15.4 us
    pallas_call x2 -> x4, Pallas kernels: 11.2 us -> 16.1 us  [the longest x2 8.02 us: take_half(): pl.pallas_call(_copy_kernel, grid=(quarters,), in_specs=[pl.BlockSpec((un...]
    all_gather x2, waiting for transfers between devices: 22.6 us -> 18.6 us  [body(): gathered = lax.all_gather(picked, 'rep', axis=2, tiled=True)]
    reduce_scatter x2, waiting for transfers between devices: 65.8 us -> 61.9 us  [body(): summed = lax.psum_scatter(half, 'rep', scatter_dimension=0, tiled=True)[0]]
    dot_general x2, matrix products: 19.3 us -> 15.4 us  [the longest x1 10.1 us: body(): jnp.einsum('sbk,kq->sbq', coeffs, basis_part, precision=lax.Precision.HIGH)]
  transfers between devices with their start and end apart: 9 -> 9, of which waited for: 7 -> 7; matrix products, arithmetic and copies ran while one was open for 4% -> 4% of each run, Pallas kernels for 0% -> 3%
where the time goes in v5:
time: 290 us; the launch traced here: 289 us
  waiting for transfers between devices  161 us (56%)
  blocking collectives  34.9 us (12%)
  local copies, waits for them, and re-layouts  27.8 us (10%)
  Pallas kernels  16.1 us (6%)
  starting transfers between devices  15.4 us (5%)
  matrix products  15.4 us (5%)
  between operations  13.9 us (5%)
  other arithmetic  4.43 us (2%)
    reduce_scatter x2, waiting for transfers between devices, body(): summed = lax.psum_scatter(half, 'rep', scatter_dimension=0, tiled=True)[0]  61.9 us
    all_to_all x1, blocking collectives, body(): lax.all_to_all(rounded[:, :, c * width:(c + 1) * width], 'dev', split_axi...  34.9 us
    all_to_all x1, waiting for transfers between devices, body(): lax.all_to_all(rounded[:, :, c * width:(c + 1) * width], 'dev', split_axi...  30.9 us
    all_to_all x2, waiting for transfers between devices, body(): lax.all_to_all(picked.reshape(dev_count, slot_count, summed.shape[1], sum...  30.5 us
    ppermute x2, waiting for transfers between devices, rep_sum(): lax.ppermute(total, 'rep', [(i, i ^ step) for i in range(rep_count)])  19.1 us
    all_gather x2, waiting for transfers between devices, body(): gathered = lax.all_gather(picked, 'rep', axis=2, tiled=True)  18.6 us
    all_to_all x2, starting transfers between devices, body(): lax.all_to_all(picked.reshape(dev_count, slot_count, summed.shape[1], sum...  11 us
    dot_general x1, matrix products, body(): jnp.einsum('sbk,kq->sbq', coeffs, basis_part, precision=lax.Precision.HIGH)  10.1 us
  transfers between devices with their start and end apart: 9, of which 7 were waited for; matrix products, arithmetic and copies ran while one was open for 4% of the time, Pallas kernels for 3%

profile of v5, /device:TPU:0, one launch (start us, length us, event | category | flops | bytes accessed | tf_op | source)
XLA Modules:
  0.0 288.9 jit_solution(103873673527208270)
XLA Ops:
  7.2 0.0 reduce-scatter.5.cloned.1.call-start
  7.2 4.0 %shard_map.120 = bf16[4,160,16,128]{3,2,1,0:T(8,128)(2,1)} custom-call(bf16[160,16,1024]{2,1,0:T(8,128)(2,1)} %bitcast.82), custom_call_target="tpu_custom_call" | custom-call | tf_op jit(solution)/shard_map/pallas_call | solution.py:34
  11.3 0.0 reduce-scatter.3.cloned.1.call-start
  11.3 4.0 %shard_map.119 = bf16[4,160,16,128]{3,2,1,0:T(8,128)(2,1)} custom-call(bf16[160,16,1024]{2,1,0:T(8,128)(2,1)} %bitcast.83), custom_call_target="tpu_custom_call" | custom-call | tf_op jit(solution)/shard_map/pallas_call | solution.py:34
  15.3 0.7 copy-done.6
  16.0 0.2 convert_reduce_fusion
  16.2 0.1 select_reduce_fusion
  16.3 32.4 %reduce-scatter.5.cloned.1.call-done = bf16[1,160,16,128]{3,2,1,0:T(8,128)(2,1)} async-done(((bf16[4,160,16,128]{3,2,1,0:T(8,128)(2,1)}), bf16[1,160,16,128]{3,2,1,0:T(8,128)(2,1)}) %reduce-scatter.5.cloned.1.call-update) | async-done | bytes 655376 | tf_op jit(solution)/shard_map/reduce_scatter | solution.py:87
  48.8 3.0 %gather_fusion.1 = bf16[320,16,128]{2,1,0:T(8,128)(2,1)} fusion(bf16[160,16,128]{2,1,0:T(8,128)(2,1)} %bitcast.93, s32[1024]{0:T(1024)S(1)} %pad_clamp_fusion.1), kind=kCustom, calls=%fused_computation.1 | custom fusion | bytes 2622720 | tf_op jit(solution)/shard_map/jit(_take)/gather | solution.py:88
  51.8 5.5 %all-to-all-start.1 = ((bf16[8,40,16,128]{3,2,1,0:T(8,128)(2,1)}), bf16[8,40,16,128]{3,2,1,0:T(8,128)(2,1)S(1)}, u32[]{:S(2)}, u32[]{:S(2)}) async-start(bf16[8,40,16,128]{3,2,1,0:T(8,128)(2,1)} %bitcast.8), calls=%async_computation.3 | async-start | bytes 2621440 | tf_op jit(solution)/shard_map/all_to_all | solution.py:89
  57.3 29.4 %reduce-scatter.3.cloned.1.call-done = bf16[1,160,16,128]{3,2,1,0:T(8,128)(2,1)} async-done(((bf16[4,160,16,128]{3,2,1,0:T(8,128)(2,1)}), bf16[1,160,16,128]{3,2,1,0:T(8,128)(2,1)}) %reduce-scatter.3.cloned.1.call-update) | async-done | bytes 655376 | tf_op jit(solution)/shard_map/reduce_scatter | solution.py:87
  86.8 3.0 %gather_fusion = bf16[320,16,128]{2,1,0:T(8,128)(2,1)} fusion(bf16[160,16,128]{2,1,0:T(8,128)(2,1)} %bitcast.94, s32[1024]{0:T(1024)S(1)} %pad_clamp_fusion.1), kind=kCustom, calls=%fused_computation | custom fusion | bytes 2622720 | tf_op jit(solution)/shard_map/jit(_take)/gather | solution.py:88
  89.8 5.5 %all-to-all-start = ((bf16[8,40,16,128]{3,2,1,0:T(8,128)(2,1)}), bf16[8,40,16,128]{3,2,1,0:T(8,128)(2,1)}, u32[]{:S(2)}, u32[]{:S(2)}) async-start(bf16[8,40,16,128]{3,2,1,0:T(8,128)(2,1)} %bitcast.3), calls=%async_computation.1 | async-start | bytes 2621440 | tf_op jit(solution)/shard_map/all_to_all | solution.py:89
  95.3 0.6 reshape_squeeze.3
  96.0 0.4 copy.39
  96.3 30.5 %all-to-all-done = bf16[8,40,16,128]{3,2,1,0:T(8,128)(2,1)} async-done(((bf16[8,40,16,128]{3,2,1,0:T(8,128)(2,1)}), bf16[8,40,16,128]{3,2,1,0:T(8,128)(2,1)}, u32[]{:S(2)}, u32[]{:S(2)}) %all-to-all-start) | async-done | bytes 1310752 | tf_op jit(solution)/shard_map/all_to_all | solution.py:89
  126.8 1.7 copy.38
  128.5 5.3 %fusion.6 = bf16[40,128,64]{1,2,0:T(8,128)(2,1)S(1)} fusion(f32[1,40,128,256]{3,2,1,0:T(8,128)} %param.10, bf16[1,40,128,128]{3,2,1,0:T(8,128)(2,1)S(1)} %bitcast.84, bf16[1,40,128,128]{3,2,1,0:T(8,128)(2,1)S(1)} %bitcast.86, f32[64,1024]{1,0:T(8,128)S(1)} %copy-done, s32[]{:T(128)S(6)} %select_n.18), kind=kOutput, calls=%fused_computation.18 | convolution fusion | flops 511508480 | bytes 8585220 | tf_op jit(solution)/shard_map/sbq,kq->sbk/dot_general | solution.py:107
  133.8 1.4 copy.40
  135.2 1.9 reshape.51
  137.1 0.8 constant_dynamic-update-slice_fusion
  137.9 2.1 collective-permute-done
  140.0 1.0 add_convert_fusion
  141.0 0.5 collective-permute-start.1
  141.6 0.2 fusion.13
  141.8 16.9 %collective-permute-done.1 = bf16[340992]{0:T(1024)(128)(2,1)} collective-permute-done((bf16[340992]{0:T(1024)(128)(2,1)}, bf16[340992]{0:T(1024)(128)(2,1)}, u32[]{:S(2)}, u32[]{:S(2)}) %collective-permute-start.1) | collective-permute-done | bytes 682016 | tf_op jit(solution)/shard_map/ppermute | solution.py:19
  158.7 1.4 convert_add_fusion
  160.1 1.1 copy-done.2
  161.2 1.1 slice.32
  162.4 2.8 reshape.52
  165.2 10.1 %fusion.1 = (f32[1,40,128,256]{3,2,1,0:T(8,128)}, f32[1,40,128,256]{3,2,1,0:T(8,128)}, bf16[40,128,256]{2,1,0:T(8,128)(2,1)S(1)}) fusion(f32[1,40,128,256]{3,2,1,0:T(8,128)} %param.11, f32[1,40,128,256]{3,2,1,0:T(8,128)} %param.10, pred[40]{0:T(512)(128)(4,1)S(1)} %get-tuple-element.5, pred[40]{0:T(512)(128)(4,1)S(1)} %get-tuple-element.6, ...), kind=kOutput, calls=%fused_computation.7 | convolution fusion | flops 524288000 | bytes 27591684 | tf_op jit(solution)/shard_map/sbk,kq->sbq/dot_general | solution.py:113
  175.4 0.5 fusion.19
  175.9 1.9 copy.45
  177.8 3.6 %all-to-all-start.3 = ((bf16[40,128,128]{2,0,1:T(8,128)(2,1)}), bf16[40,128,128]{2,0,1:T(8,128)(2,1)S(1)}, u32[]{:S(2)}, u32[]{:S(2)}) async-start(bf16[40,128,128]{2,0,1:T(8,128)(2,1)} %copy.45), calls=%async_computation.5 | async-start | bytes 2621440 | tf_op jit(solution)/shard_map/all_to_all | solution.py:123
  181.4 0.0 all-gather.7.cloned.1.call-start
  181.5 30.9 %all-to-all-done.3 = bf16[40,128,128]{2,0,1:T(8,128)(2,1)S(1)} async-done(((bf16[40,128,128]{2,0,1:T(8,128)(2,1)}), bf16[40,128,128]{2,0,1:T(8,128)(2,1)S(1)}, u32[]{:S(2)}, u32[]{:S(2)}) %all-to-all-start.3) | async-done | bytes 1310752 | tf_op jit(solution)/shard_map/all_to_all | solution.py:123
  212.4 1.3 copy.47
  213.7 2.9 gather_fusion.3
  216.6 0.0 all-gather.5.cloned.1.call-start
  216.6 0.8 copy.42
  217.5 34.9 %all_to_all.72 = bf16[40,128,128]{2,0,1:T(8,128)(2,1)S(1)} all-to-all(bf16[40,128,128]{2,0,1:T(8,128)(2,1)S(1)} %copy.42), channel_id=1, replica_groups=mesh['rep'=4,'dev'=8] {'dev'}, dimensions={1} | all-to-all | bytes 2621440 | tf_op jit(solution)/shard_map/all_to_all | solution.py:123
  252.4 0.2 copy.44
  252.6 1.6 gather_fusion.2
  254.2 0.8 slice_multiply_fusion
  255.0 0.7 multiply_subtract_fusion
  255.7 4.0 %shard_map.121.base_ref = bf16[160,16,1024]{2,1,0:T(8,128)(2,1)} custom-call(bf16[160,16,512]{2,1,0:T(8,128)(2,1)} %all-gather.7.cloned.1.call-done.x_ref), custom_call_target="tpu_custom_call" | custom-call | tf_op jit(solution)/shard_map/pallas_call | solution.py:55
  259.7 18.6 %all-gather.5.cloned.1.call-done.a_ref = bf16[160,16,512]{2,1,0:T(8,128)(2,1)} async-done(((bf16[160,16,128]{2,1,0:T(8,128)(2,1)}), bf16[160,16,512]{2,1,0:T(8,128)(2,1)}) %all-gather.5.cloned.1.call-update) | async-done | bytes 2621456 | tf_op jit(solution)/shard_map/all_gather | solution.py:125
  278.4 4.0 %shard_map.122 = bf16[160,16,1024]{2,1,0:T(8,128)(2,1)} custom-call(bf16[160,16,512]{2,1,0:T(8,128)(2,1)} %all-gather.5.cloned.1.call-done.a_ref, bf16[160,16,1024]{2,1,0:T(8,128)(2,1)} %shard_map.121.base_ref), custom_call_target="tpu_custom_call", output_to_operand_aliasing={{}: (1, {})} | custom-call | tf_op jit(solution)/shard_map/pallas_call | solution.py:58
  (26 shorter events, 0.2 us)
Async XLA Ops:
  7.2 121.3 %copy-start = (f32[64,1024]{1,0:T(8,128)S(1)}, f32[64,1024]{1,0:T(8,128)}, u32[]{:S(2)}) copy-start(f32[64,1024]{1,0:T(8,128)} %param.12) | copy-start | bytes 786436
  7.2 41.6 %reduce-scatter.5.cloned.1.call-start = ((), (), s32[]{:S(2)}) async-start(), calls=%async_computation.7 | async-start | bytes 3276800 | tf_op jit(solution)/shard_map/reduce_scatter | solution.py:87
  11.3 75.5 %reduce-scatter.3.cloned.1.call-start = ((), (), s32[]{:S(2)}) async-start(), calls=%async_computation.6 | async-start | bytes 3276800 | tf_op jit(solution)/shard_map/reduce_scatter | solution.py:87
  15.3 0.7 copy-start.6
  51.8 38.0 %all-to-all-start.1 = ((bf16[8,40,16,128]{3,2,1,0:T(8,128)(2,1)}), bf16[8,40,16,128]{3,2,1,0:T(8,128)(2,1)S(1)}, u32[]{:S(2)}, u32[]{:S(2)}) async-start(bf16[8,40,16,128]{3,2,1,0:T(8,128)(2,1)} %bitcast.8), calls=%async_computation.3 | async-start | bytes 2621440 | tf_op jit(solution)/shard_map/all_to_all | solution.py:89
  86.8 8.6 %copy-start.5 = (bf16[1,13,1024]{2,1,0:T(8,128)(2,1)S(1)}, bf16[1,13,1024]{2,1,0:T(8,128)(2,1)}, u32[]{:S(2)}) copy-start(bf16[1,13,1024]{2,1,0:T(8,128)(2,1)} %param.13) | copy-start | bytes 79876
  89.8 37.0 %all-to-all-start = ((bf16[8,40,16,128]{3,2,1,0:T(8,128)(2,1)}), bf16[8,40,16,128]{3,2,1,0:T(8,128)(2,1)}, u32[]{:S(2)}, u32[]{:S(2)}) async-start(bf16[8,40,16,128]{3,2,1,0:T(8,128)(2,1)} %bitcast.3), calls=%async_computation.1 | async-start | bytes 2621440 | tf_op jit(solution)/shard_map/all_to_all | solution.py:89
  137.9 2.1 collective-permute-start
  141.0 17.7 %collective-permute-start.1 = (bf16[340992]{0:T(1024)(128)(2,1)}, bf16[340992]{0:T(1024)(128)(2,1)}, u32[]{:S(2)}, u32[]{:S(2)}) collective-permute-start(bf16[340992]{0:T(1024)(128)(2,1)} %add_convert_fusion), channel_id=1, source_target_pairs={{0,16},{8,24},{16,0},{24,8},{1,17},{9,25},{17,1},{25,9},{2,18},{10... | collective-permute-start | bytes 2045960 | tf_op jit(solution)/shard_map/ppermute | solution.py:19
  160.1 1.1 copy-start.2
  177.8 34.6 %all-to-all-start.3 = ((bf16[40,128,128]{2,0,1:T(8,128)(2,1)}), bf16[40,128,128]{2,0,1:T(8,128)(2,1)S(1)}, u32[]{:S(2)}, u32[]{:S(2)}) async-start(bf16[40,128,128]{2,0,1:T(8,128)(2,1)} %copy.45), calls=%async_computation.5 | async-start | bytes 2621440 | tf_op jit(solution)/shard_map/all_to_all | solution.py:123
  181.4 74.3 %all-gather.7.cloned.1.call-start = ((), (), s32[]{:S(2)}) async-start(), calls=%async_computation.9 | async-start | bytes 3276800 | tf_op jit(solution)/shard_map/all_gather | solution.py:125
  216.6 61.8 %all-gather.5.cloned.1.call-start = ((), (), s32[]{:S(2)}) async-start(), calls=%async_computation.8 | async-start | bytes 3276800 | tf_op jit(solution)/shard_map/all_gather | solution.py:125
  252.4 2.6 copy-start.3
  252.4 2.7 copy-start.4
  278.3 4.0 %copy-start.1 = (f32[64,1024]{1,0:T(8,128)S(1)}, f32[64,1024]{1,0:T(8,128)}, u32[]{:S(2)}) copy-start(f32[64,1024]{1,0:T(8,128)} %param.12) | copy-start | bytes 786436
Sparse Core Ops, SparseCore 0:
  11.4 37.3 reduce-scatter.4
  52.0 34.6 reduce-scatter.2
  216.7 23.9 all-gather.6
  254.3 23.9 all-gather.4

commit v6 on v5

--- a/solution.py
+++ b/solution.py
@@ -81,49 +81,65 @@
     source_unit = jnp.sum(jnp.where(placed, unit_ids[:, None], 0), axis=0)
     own_rows = group_weights[0]
     width = quarter // 2
-    arrived_parts = []
-    for c in range(2):
-        half = take_half(own_rows, width, c)
-        summed = lax.psum_scatter(half, "rep", scatter_dimension=0, tiled=True)[0]
-        picked = jnp.take(summed, source_unit, axis=0, mode="clip")
-        arrived_parts.append(lax.all_to_all(
-            picked.reshape(dev_count, slot_count, summed.shape[1], summed.shape[2]),
-            "dev",
-            split_axis=0,
-            concat_axis=2,
-            tiled=True,
-        ))
-    arrived = jnp.concatenate(arrived_parts, axis=3)
-    group_mean = arrived[0].astype(jnp.float32) / rep_count
     start_rows = start_weights[0]
     momentum_rows = momentum[0]
     my_slots = lax.axis_index("dev") * slot_count + jnp.arange(slot_count, dtype=jnp.int32)
     own_placed = target[:, None] == my_slots[None, :]
     is_owned = jnp.any(own_placed, axis=0)
     is_embedding = jnp.any(own_placed & (unit_ids >= EMB_FIRST)[:, None], axis=0)
-    change = start_rows - group_mean
     first_column = lax.axis_index("rep") * quarter
     basis_part = lax.dynamic_slice_in_dim(basis, first_column, quarter, 1)
-    coeff_terms = jnp.einsum("sbq,kq->sbk", change, basis_part, precision=lax.Precision.HIGH)
+    halves = [slice(c * width, (c + 1) * width) for c in range(2)]
+    changes = []
+    coeff_terms = None
+    for c in range(2):
+        half = take_half(own_rows, width, c)
+        summed = lax.psum_scatter(half, "rep", scatter_dimension=0, tiled=True)[0]
+        picked = jnp.take(summed, source_unit, axis=0, mode="clip")
+        arrived = lax.all_to_all(
+            picked.reshape(dev_count, slot_count, summed.shape[1], summed.shape[2]),
+            "dev",
+            split_axis=0,
+            concat_axis=2,
+            tiled=True,
+        )
+        change = start_rows[:, :, halves[c]] - arrived[0].astype(jnp.float32) / rep_count
+        changes.append(change)
+        term = jnp.einsum("sbq,kq->skb", change, basis_part[:, halves[c]], precision=lax.Precision.HIGH)
+        coeff_terms = term if coeff_terms is None else coeff_terms + term
+    rank = coeff_terms.shape[1]
+    rows_all = coeff_terms.shape[2]
     vec_terms = vec_groups[0]
-    coeff_flat = coeff_terms.astype(jnp.bfloat16).reshape(-1)
-    joined = rep_sum(jnp.concatenate([coeff_flat, vec_terms.reshape(-1)]))
-    coeffs = joined[: coeff_flat.shape[0]].reshape(coeff_terms.shape)
-    vec_summed = joined[coeff_flat.shape[0]:].reshape(vec_terms.shape)
-    projected = jnp.einsum("sbk,kq->sbq", coeffs, basis_part, precision=lax.Precision.HIGH)
-    outer_grad = jnp.where(is_embedding[:, None, None], projected, change)
-    fresh_momentum = outer_momentum * momentum_rows + outer_grad
-    fresh_start = start_rows - outer_rate * (outer_grad + outer_momentum * fresh_momentum)
+    vec_rows = vec_terms.shape[0]
+    vec_padded = jnp.pad(vec_terms, ((0, (-vec_rows) % 16), (0, 0)))
+    coeff_block = coeff_terms.astype(jnp.bfloat16).reshape(slot_count * rank, rows_all)
+    vec_block = vec_padded.reshape(-1, rows_all)
+    joined = rep_sum(jnp.concatenate([coeff_block, vec_block], axis=0))
+    coeffs = joined[: slot_count * rank].reshape(slot_count, rank, rows_all)
+    vec_summed = joined[slot_count * rank:].reshape(vec_padded.shape)[:vec_rows]
     owned_mask = is_owned[:, None, None]
-    new_momentum = jnp.where(owned_mask, fresh_momentum, momentum_rows)
-    new_start = jnp.where(owned_mask, fresh_start, start_rows)
-    rounded = fresh_start.astype(jnp.bfloat16)
+    emb_mask = is_embedding[:, None, None]
+
+    def fresh(c):
+        projected = jnp.einsum("skb,kq->sbq", coeffs, basis_part[:, halves[c]], precision=lax.Precision.HIGH)
+        outer_grad = jnp.where(emb_mask, projected, changes[c])
+        fresh_momentum = outer_momentum * momentum_rows[:, :, halves[c]] + outer_grad
+        fresh_start = start_rows[:, :, halves[c]] - outer_rate * (outer_grad + outer_momentum * fresh_momentum)
+        return fresh_start, fresh_momentum
+
     returned = None
+    new_starts, new_momenta = [], []
     for c in range(2):
-        pieces = lax.all_to_all(rounded[:, :, c * width:(c + 1) * width], "dev", split_axis=1, concat_axis=0, tiled=True)
+        fresh_start, fresh_momentum = fresh(c)
+        new_momenta.append(jnp.where(owned_mask, fresh_momentum, momentum_rows[:, :, halves[c]]))
+        new_starts.append(jnp.where(owned_mask, fresh_start, start_rows[:, :, halves[c]]))
+        rounded = fresh_start.astype(jnp.bfloat16)
+        pieces = lax.all_to_all(rounded, "dev", split_axis=1, concat_axis=0, tiled=True)
         picked = jnp.take(pieces, target, axis=0, mode="clip")
         gathered = lax.all_gather(picked, "rep", axis=2, tiled=True)
         returned = place_half(gathered, width, c, returned)
+    new_start = jnp.concatenate(new_starts, axis=2)
+    new_momentum = jnp.concatenate(new_momenta, axis=2)
     vec_change = vec_start - vec_summed / rep_count
     vec_new_momentum = outer_momentum * vec_momentum + vec_change
     vec_new = vec_start - outer_rate * (vec_change + outer_momentum * vec_new_momentum)

time: 290 us -> 294 us (1.014)
  waiting for transfers between devices: 161 us -> 128 us
  local copies, waits for them, and re-layouts: 27.8 us -> 52 us
  other arithmetic: 4.43 us -> 16.4 us
    unnamed x15 -> x28, local copies, waits for them, and re-layouts: 1.84 us -> 25.3 us
    all_gather x2, waiting for transfers between devices: 18.6 us -> 0.01 us  [body(): gathered = lax.all_gather(picked, 'rep', axis=2, tiled=True)]
    all_to_all x2, waiting for transfers between devices: 30.5 us -> 21.6 us  [body(): lax.all_to_all(picked.reshape(dev_count, slot_count, summed.shape[1], sum...]
    broadcast_in_dim x0 -> x1, other arithmetic: none -> 6.73 us  [body(): new_start[None]]
    ppermute x2, waiting for transfers between devices: 19.1 us -> 13.3 us  [rep_sum(): lax.ppermute(total, 'rep', [(i, i ^ step) for i in range(rep_count)])]
    div x0 -> x2, local copies, waits for them, and re-layouts: none -> 5.35 us  [body(): arrived[0].astype(jnp.float32) / rep_count]
    div x0 -> x2, other arithmetic: none -> 4.97 us  [body(): arrived[0].astype(jnp.float32) / rep_count]
    reshape x2 -> x1, local copies, waits for them, and re-layouts: 4.74 us -> 0.02 us  [body(): vec_block = vec_padded.reshape(-1, rows_all)]
  transfers between devices with their start and end apart: 9 -> 9, of which waited for: 7 -> 6; matrix products, arithmetic and copies ran while one was open for 4% -> 17% of each run, Pallas kernels for 3% -> 3%
where the time goes in v6:
time: 294 us; the launch traced here: 293 us
  waiting for transfers between devices  128 us (44%)
  local copies, waits for them, and re-layouts  52 us (18%)
  blocking collectives  35.1 us (12%)
  other arithmetic  16.4 us (6%)
  starting transfers between devices  16.1 us (5%)
  Pallas kernels  16 us (5%)
  matrix products  15.3 us (5%)
  between operations  14 us (5%)
    reduce_scatter x2, waiting for transfers between devices, body(): summed = lax.psum_scatter(half, 'rep', scatter_dimension=0, tiled=True)[0]  61.9 us
    all_to_all x1, blocking collectives, body(): lax.all_to_all(rounded, 'dev', split_axis=1, concat_axis=0, tiled=True)  35.1 us
    all_to_all x1, waiting for transfers between devices, body(): lax.all_to_all(rounded, 'dev', split_axis=1, concat_axis=0, tiled=True)  31.1 us
    unnamed x28, local copies, waits for them, and re-layouts  25.3 us
    all_to_all x2, waiting for transfers between devices, body(): lax.all_to_all(picked.reshape(dev_count, slot_count, summed.shape[1], sum...  21.6 us
    ppermute x2, waiting for transfers between devices, rep_sum(): lax.ppermute(total, 'rep', [(i, i ^ step) for i in range(rep_count)])  13.3 us
    all_to_all x2, starting transfers between devices, body(): lax.all_to_all(picked.reshape(dev_count, slot_count, summed.shape[1], sum...  11 us
    dot_general x2, matrix products, fresh(): jnp.einsum('skb,kq->sbq', coeffs, basis_part[:, halves[c]], precision=lax...  9.68 us
  transfers between devices with their start and end apart: 9, of which 6 were waited for; matrix products, arithmetic and copies ran while one was open for 17% of the time, Pallas kernels for 3%

profile of v6, /device:TPU:0, one launch (start us, length us, event | category | flops | bytes accessed | tf_op | source)
XLA Modules:
  0.0 292.8 jit_solution(9707729717719638978)
XLA Ops:
  7.2 4.0 %shard_map.119 = bf16[4,160,16,128]{3,2,1,0:T(8,128)(2,1)} custom-call(bf16[160,16,1024]{2,1,0:T(8,128)(2,1)} %bitcast.52), custom_call_target="tpu_custom_call" | custom-call | tf_op jit(solution)/shard_map/pallas_call | solution.py:34
  11.3 0.0 reduce-scatter.5.cloned.1.call-start
  11.3 4.0 %shard_map.120 = bf16[4,160,16,128]{3,2,1,0:T(8,128)(2,1)} custom-call(bf16[160,16,1024]{2,1,0:T(8,128)(2,1)} %bitcast.53), custom_call_target="tpu_custom_call" | custom-call | tf_op jit(solution)/shard_map/pallas_call | solution.py:34
  15.4 0.7 copy-done.9
  16.0 0.2 convert_reduce_fusion
  16.2 0.1 select_reduce_fusion
  16.3 32.4 %reduce-scatter.3.cloned.1.call-done = bf16[1,160,16,128]{3,2,1,0:T(8,128)(2,1)} async-done(((bf16[4,160,16,128]{3,2,1,0:T(8,128)(2,1)}), bf16[1,160,16,128]{3,2,1,0:T(8,128)(2,1)}) %reduce-scatter.3.cloned.1.call-update) | async-done | bytes 655376 | tf_op jit(solution)/shard_map/reduce_scatter | solution.py:97
  48.8 3.0 %gather_fusion = bf16[320,16,128]{2,1,0:T(8,128)(2,1)} fusion(bf16[160,16,128]{2,1,0:T(8,128)(2,1)} %bitcast.64, s32[1024]{0:T(1024)S(1)} %pad_clamp_fusion.1), kind=kCustom, calls=%fused_computation | custom fusion | bytes 2622720 | tf_op jit(solution)/shard_map/jit(_take)/gather | solution.py:98
  51.8 5.5 %all-to-all-start = ((bf16[8,40,16,128]{3,2,1,0:T(8,128)(2,1)}), bf16[8,40,16,128]{3,2,1,0:T(8,128)(2,1)S(1)}, u32[]{:S(2)}, u32[]{:S(2)}) async-start(bf16[8,40,16,128]{3,2,1,0:T(8,128)(2,1)} %bitcast.4), calls=%async_computation.1 | async-start | bytes 2621440 | tf_op jit(solution)/shard_map/all_to_all | solution.py:99
  57.3 29.4 %reduce-scatter.5.cloned.1.call-done = bf16[1,160,16,128]{3,2,1,0:T(8,128)(2,1)} async-done(((bf16[4,160,16,128]{3,2,1,0:T(8,128)(2,1)}), bf16[1,160,16,128]{3,2,1,0:T(8,128)(2,1)}) %reduce-scatter.5.cloned.1.call-update) | async-done | bytes 655376 | tf_op jit(solution)/shard_map/reduce_scatter | solution.py:97
  86.8 3.0 %gather_fusion.1 = bf16[320,16,128]{2,1,0:T(8,128)(2,1)} fusion(bf16[160,16,128]{2,1,0:T(8,128)(2,1)} %bitcast.65, s32[1024]{0:T(1024)S(1)} %pad_clamp_fusion.1), kind=kCustom, calls=%fused_computation.1 | custom fusion | bytes 2622720 | tf_op jit(solution)/shard_map/jit(_take)/gather | solution.py:98
  89.8 5.5 %all-to-all-start.1 = ((bf16[8,40,16,128]{3,2,1,0:T(8,128)(2,1)}), bf16[8,40,16,128]{3,2,1,0:T(8,128)(2,1)}, u32[]{:S(2)}, u32[]{:S(2)}) async-start(bf16[8,40,16,128]{3,2,1,0:T(8,128)(2,1)} %bitcast.10), calls=%async_computation.3 | async-start | bytes 2621440 | tf_op jit(solution)/shard_map/all_to_all | solution.py:99
  95.3 5.9 %copy.52 = f32[1,40,128,256]{2,3,1,0:T(8,128)} copy(f32[1,40,128,256]{3,2,1,0:T(8,128)} %param.10) | data formatting | bytes 10485760 | tf_op args[2]
  101.2 1.8 convert_multiply_fusion.1
  103.1 2.1 copy.54
  105.2 21.6 %all-to-all-done.1 = bf16[8,40,16,128]{3,2,1,0:T(8,128)(2,1)} async-done(((bf16[8,40,16,128]{3,2,1,0:T(8,128)(2,1)}), bf16[8,40,16,128]{3,2,1,0:T(8,128)(2,1)}, u32[]{:S(2)}, u32[]{:S(2)}) %all-to-all-start.1) | async-done | bytes 1310752 | tf_op jit(solution)/shard_map/all_to_all | solution.py:99
  126.8 3.1 %convert_multiply_fusion = f32[8,40,16,128]{3,2,0,1:T(8,128)} fusion(bf16[8,40,16,128]{3,2,1,0:T(8,128)(2,1)} %all-to-all-done.1), kind=kLoop, calls=%fused_computation.12 | loop fusion | flops 1310720 | bytes 3932160 | tf_op jit(solution)/shard_map/div | solution.py:106
  129.9 3.2 %copy.57 = f32[40,128,128]{1,2,0:T(8,128)} copy(f32[40,128,128]{2,1,0:T(8,128)} %bitcast.58) | data formatting | bytes 5242880 | tf_op jit(solution)/shard_map/div | solution.py:106
  133.2 2.8 fusion.3
  136.0 2.8 fusion.2
  138.8 0.1 collective-permute-start
  138.9 2.1 collective-permute-done
  141.0 1.1 add_convert_fusion
  142.1 0.5 collective-permute-start.1
  142.6 5.9 %copy.59 = f32[1,40,128,256]{2,3,1,0:T(8,128)} copy(f32[1,40,128,256]{3,2,1,0:T(8,128)} %param.11) | data formatting | bytes 10485760 | tf_op args[3]
  148.5 0.2 fusion.5
  148.7 11.2 %collective-permute-done.1 = bf16[2688,128]{1,0:T(8,128)(2,1)} collective-permute-done((bf16[2688,128]{1,0:T(8,128)(2,1)}, bf16[2688,128]{1,0:T(8,128)(2,1)}, u32[]{:S(2)}, u32[]{:S(2)}) %collective-permute-start.1) | collective-permute-done | bytes 688160 | tf_op jit(solution)/shard_map/ppermute | solution.py:19
  159.9 1.6 convert_add_fusion
  161.5 0.1 slice.53
  161.6 1.0 copy-done.5
  162.6 4.0 %convolution_select_fusion.1 = f32[40,128,128]{1,2,0:T(8,128)S(1)} fusion(f32[40,64,128]{2,1,0:T(8,128)S(1)} %bitcast.54, pred[40]{0:T(512)(128)(4,1)S(1)} %get-tuple-element.25, f32[40,128,128]{1,2,0:T(8,128)S(1)} %copy.54, f32[40,128,256]{1,2,0:T(8,128)} %bitcast.48, f32[64,1024]{1,0:T(8,128)S(1)} %copy-done, s32[]{:T(128)S(6)} %select_n.26), kind=kOutput, calls=%fused_computation.19 | convolution fusion | flops 252968960 | bytes 9208324 | tf_op jit(solution)/shard_map/skb,kq->sbq/dot_general | solution.py:124
  166.6 5.7 %fusion.11 = (bf16[40,128,128]{1,2,0:T(8,128)(2,1)}, f32[40,128,128]{1,2,0:T(8,128)S(1)}, f32[40,128,128]{1,2,0:T(8,128)}, bf16[40,128,128]{1,2,0:T(8,128)(2,1)}...) fusion(f32[40,128,256]{1,2,0:T(8,128)S(1)} %bitcast.56, f32[40,128,256]{1,2,0:T(8,128)S(1)} %bitcast.51, ...), kind=kOutput, calls=%fused_computation.49 | convolution fusion | flops 264765440 | bytes 30180356 | tf_op jit(solution)/shard_map/skb,kq->sbq/dot_general | solution.py:124
  172.3 2.7 copy.63
  175.0 4.3 %all-to-all-start.3 = ((bf16[40,128,128]{2,0,1:T(8,128)(2,1)}), bf16[40,128,128]{2,0,1:T(8,128)(2,1)}, u32[]{:S(2)}, u32[]{:S(2)}) async-start(bf16[40,128,128]{2,0,1:T(8,128)(2,1)} %copy.63), calls=%async_computation.5 | async-start | bytes 2621440 | tf_op jit(solution)/shard_map/all_to_all | solution.py:137
  179.4 31.1 %all-to-all-done.3 = bf16[40,128,128]{2,0,1:T(8,128)(2,1)} async-done(((bf16[40,128,128]{2,0,1:T(8,128)(2,1)}), bf16[40,128,128]{2,0,1:T(8,128)(2,1)}, u32[]{:S(2)}, u32[]{:S(2)}) %all-to-all-start.3) | async-done | bytes 1310752 | tf_op jit(solution)/shard_map/all_to_all | solution.py:137
  210.4 2.6 copy.65
  213.0 2.9 gather_fusion.3
  216.0 2.7 copy.60
  218.7 35.1 %all_to_all.54 = bf16[40,128,128]{2,0,1:T(8,128)(2,1)S(1)} all-to-all(bf16[40,128,128]{2,0,1:T(8,128)(2,1)} %copy.60), channel_id=1, replica_groups=mesh['rep'=4,'dev'=8] {'dev'}, dimensions={1} | all-to-all | bytes 2621440 | tf_op jit(solution)/shard_map/all_to_all | solution.py:137
  253.9 1.3 copy.62
  255.1 2.9 gather_fusion.2
  258.1 6.7 %maximum_bitcast_fusion = (f32[1,40,128,256]{2,3,1,0:T(8,128)}, f32[1,40,128,256]{2,3,1,0:T(8,128)}) fusion(f32[40,128,128]{1,2,0:T(8,128)S(1)} %get-tuple-element.32, f32[40,128,128]{1,2,0:T(8,128)} %get-tuple-element.33, f32[40,128,128]{1,2,0:T(8,128)} %get-tuple-element.36, f32[40,128,128]{1,2,0:T(8,128)} %get-tuple-element.35), kind=kLoop, calls=%fused_computation.4 | loop fusion | flops 2621440 | bytes 20971520 | tf_op jit(solution)/shard_map/broadcast_in_dim | solution.py:146
  264.8 5.9 %copy.66 = f32[1,40,128,256]{3,2,1,0:T(8,128)} copy(f32[1,40,128,256]{2,3,1,0:T(8,128)} %get-tuple-element.37) | data formatting | bytes 10485760
  270.7 6.0 %copy.67 = f32[1,40,128,256]{3,2,1,0:T(8,128)} copy(f32[1,40,128,256]{2,3,1,0:T(8,128)} %get-tuple-element.38) | data formatting | bytes 10485760
  276.7 0.8 slice_multiply_fusion
  277.6 0.7 multiply_subtract_fusion.2
  278.2 4.0 %shard_map.121.base_ref = bf16[160,16,1024]{2,1,0:T(8,128)(2,1)} custom-call(bf16[160,16,512]{2,1,0:T(8,128)(2,1)} %all-gather.7.cloned.1.call-done.x_ref), custom_call_target="tpu_custom_call" | custom-call | tf_op jit(solution)/shard_map/pallas_call | solution.py:55
  282.2 4.0 %shard_map.122 = bf16[160,16,1024]{2,1,0:T(8,128)(2,1)} custom-call(bf16[160,16,512]{2,1,0:T(8,128)(2,1)} %all-gather.5.cloned.1.call-done.a_ref, bf16[160,16,1024]{2,1,0:T(8,128)(2,1)} %shard_map.121.base_ref), custom_call_target="tpu_custom_call", output_to_operand_aliasing={{}: (1, {})} | custom-call | tf_op jit(solution)/shard_map/pallas_call | solution.py:58
  (42 shorter events, 0.4 us)
Async XLA Ops:
  7.2 126.0 %copy-start = (f32[64,1024]{1,0:T(8,128)S(1)}, f32[64,1024]{1,0:T(8,128)}, u32[]{:S(2)}) copy-start(f32[64,1024]{1,0:T(8,128)} %param.12) | copy-start | bytes 786436
  7.2 41.6 %reduce-scatter.3.cloned.1.call-start = ((), (), s32[]{:S(2)}) async-start(), calls=%async_computation.6 | async-start | bytes 3276800 | tf_op jit(solution)/shard_map/reduce_scatter | solution.py:97
  11.3 75.5 %reduce-scatter.5.cloned.1.call-start = ((), (), s32[]{:S(2)}) async-start(), calls=%async_computation.7 | async-start | bytes 3276800 | tf_op jit(solution)/shard_map/reduce_scatter | solution.py:97
  15.3 0.7 copy-start.9
  51.8 38.0 %all-to-all-start = ((bf16[8,40,16,128]{3,2,1,0:T(8,128)(2,1)}), bf16[8,40,16,128]{3,2,1,0:T(8,128)(2,1)S(1)}, u32[]{:S(2)}, u32[]{:S(2)}) async-start(bf16[8,40,16,128]{3,2,1,0:T(8,128)(2,1)} %bitcast.4), calls=%async_computation.1 | async-start | bytes 2621440 | tf_op jit(solution)/shard_map/all_to_all | solution.py:99
  89.8 37.0 %all-to-all-start.1 = ((bf16[8,40,16,128]{3,2,1,0:T(8,128)(2,1)}), bf16[8,40,16,128]{3,2,1,0:T(8,128)(2,1)}, u32[]{:S(2)}, u32[]{:S(2)}) async-start(bf16[8,40,16,128]{3,2,1,0:T(8,128)(2,1)} %bitcast.10), calls=%async_computation.3 | async-start | bytes 2621440 | tf_op jit(solution)/shard_map/all_to_all | solution.py:99
  95.3 5.9 %copy-start.8 = (bf16[1,13,1024]{2,1,0:T(8,128)(2,1)S(1)}, bf16[1,13,1024]{2,1,0:T(8,128)(2,1)}, u32[]{:S(2)}) copy-start(bf16[1,13,1024]{2,1,0:T(8,128)(2,1)} %param.13) | copy-start | bytes 79876
  133.2 2.8 copy-start.2
  138.8 2.2 collective-permute-start
  142.1 17.8 %collective-permute-start.1 = (bf16[2688,128]{1,0:T(8,128)(2,1)}, bf16[2688,128]{1,0:T(8,128)(2,1)}, u32[]{:S(2)}, u32[]{:S(2)}) collective-permute-start(bf16[2688,128]{1,0:T(8,128)(2,1)} %add_convert_fusion), channel_id=1, source_target_pairs={{0,16},{8,24},{16,0},{24,8},{1,17},{9,25},{17,1},{25,9},{2,18},{10... | collective-permute-start | bytes 2064392 | tf_op jit(solution)/shard_map/ppermute | solution.py:19
  159.9 6.7 %copy-start.4 = (f32[1,40,128,256]{2,3,1,0:T(8,128)S(1)}, f32[1,40,128,256]{2,3,1,0:T(8,128)}, u32[]{:S(2)}) copy-start(f32[1,40,128,256]{2,3,1,0:T(8,128)} %copy.59) | copy-start | bytes 15728644
  161.5 1.1 copy-start.5
  161.5 5.1 %slice-start = ((s8[5242880]{0:T(1024)(128)(4,1)}), s8[4194304]{0:T(1024)(128)(4,1)S(1)}, s32[]{:S(2)}) async-start(s8[5242880]{0:T(1024)(128)(4,1)} %bitcast.49), calls=%async_computation.10 | async-start | bytes 8388608
  162.6 4.0 %slice-start.1 = ((s8[5242880]{0:T(1024)(128)(4,1)}), s8[1048576]{0:T(1024)(128)(4,1)S(1)}, s32[]{:S(2)}) async-start(s8[5242880]{0:T(1024)(128)(4,1)} %bitcast.49), calls=%async_computation.11 | async-start | bytes 2097152
  162.6 4.0 %copy-start.3 = (f32[40,128,128]{1,2,0:T(8,128)S(1)}, f32[40,128,128]{1,2,0:T(8,128)}, u32[]{:S(2)}) copy-start(f32[40,128,128]{1,2,0:T(8,128)} %copy.57) | copy-start | bytes 7864324
  175.0 35.4 %all-to-all-start.3 = ((bf16[40,128,128]{2,0,1:T(8,128)(2,1)}), bf16[40,128,128]{2,0,1:T(8,128)(2,1)}, u32[]{:S(2)}, u32[]{:S(2)}) async-start(bf16[40,128,128]{2,0,1:T(8,128)(2,1)} %copy.63), calls=%async_computation.5 | async-start | bytes 2621440 | tf_op jit(solution)/shard_map/all_to_all | solution.py:137
  179.3 98.9 %all-gather.7.cloned.1.call-start = ((), (), s32[]{:S(2)}) async-start(), calls=%async_computation.9 | async-start | bytes 3276800 | tf_op jit(solution)/shard_map/all_gather | solution.py:139
  216.0 66.3 %all-gather.5.cloned.1.call-start = ((), (), s32[]{:S(2)}) async-start(), calls=%async_computation.8 | async-start | bytes 3276800 | tf_op jit(solution)/shard_map/all_gather | solution.py:139
  270.7 6.8 %copy-start.6 = (f32[13,1024]{1,0:T(8,128)S(1)}, f32[13,1024]{1,0:T(8,128)}, u32[]{:S(2)}) copy-start(f32[13,1024]{1,0:T(8,128)} %param.14) | copy-start | bytes 159748
  270.7 6.8 %copy-start.7 = (f32[13,1024]{1,0:T(8,128)S(1)}, f32[13,1024]{1,0:T(8,128)}, u32[]{:S(2)}) copy-start(f32[13,1024]{1,0:T(8,128)} %param.15) | copy-start | bytes 159748
  282.2 4.0 %copy-start.1 = (f32[64,1024]{1,0:T(8,128)S(1)}, f32[64,1024]{1,0:T(8,128)}, u32[]{:S(2)}) copy-start(f32[64,1024]{1,0:T(8,128)} %param.12) | copy-start | bytes 786436
Sparse Core Ops, SparseCore 0:
  11.4 37.3 reduce-scatter.2
  52.0 34.6 reduce-scatter.4
  216.1 23.9 all-gather.6
  258.2 23.9 all-gather.4

commit v7 on v6

--- a/solution.py
+++ b/solution.py
@@ -120,26 +120,28 @@
     owned_mask = is_owned[:, None, None]
     emb_mask = is_embedding[:, None, None]
 
-    def fresh(c):
-        projected = jnp.einsum("skb,kq->sbq", coeffs, basis_part[:, halves[c]], precision=lax.Precision.HIGH)
-        outer_grad = jnp.where(emb_mask, projected, changes[c])
-        fresh_momentum = outer_momentum * momentum_rows[:, :, halves[c]] + outer_grad
-        fresh_start = start_rows[:, :, halves[c]] - outer_rate * (outer_grad + outer_momentum * fresh_momentum)
+    def fresh(start_part, momentum_part, change, basis_cols):
+        projected = jnp.einsum("skb,kq->sbq", coeffs, basis_cols, precision=lax.Precision.HIGH)
+        outer_grad = jnp.where(emb_mask, projected, change)
+        fresh_momentum = outer_momentum * momentum_part + outer_grad
+        fresh_start = start_part - outer_rate * (outer_grad + outer_momentum * fresh_momentum)
         return fresh_start, fresh_momentum
 
     returned = None
-    new_starts, new_momenta = [], []
     for c in range(2):
-        fresh_start, fresh_momentum = fresh(c)
-        new_momenta.append(jnp.where(owned_mask, fresh_momentum, momentum_rows[:, :, halves[c]]))
-        new_starts.append(jnp.where(owned_mask, fresh_start, start_rows[:, :, halves[c]]))
+        fresh_start, _ = fresh(start_rows[:, :, halves[c]], momentum_rows[:, :, halves[c]], changes[c], basis_part[:, halves[c]])
         rounded = fresh_start.astype(jnp.bfloat16)
         pieces = lax.all_to_all(rounded, "dev", split_axis=1, concat_axis=0, tiled=True)
         picked = jnp.take(pieces, target, axis=0, mode="clip")
         gathered = lax.all_gather(picked, "rep", axis=2, tiled=True)
+        if c == 0:
+            late_inputs = lax.optimization_barrier((start_rows, momentum_rows, changes[0], changes[1], gathered))
+            gathered = late_inputs[4]
         returned = place_half(gathered, width, c, returned)
-    new_start = jnp.concatenate(new_starts, axis=2)
-    new_momentum = jnp.concatenate(new_momenta, axis=2)
+    late_start, late_momentum, late_change0, late_change1, _ = late_inputs
+    fresh_start, fresh_momentum = fresh(late_start, late_momentum, jnp.concatenate([late_change0, late_change1], axis=2), basis_part)
+    new_momentum = jnp.where(owned_mask, fresh_momentum, late_momentum)
+    new_start = jnp.where(owned_mask, fresh_start, late_start)
     vec_change = vec_start - vec_summed / rep_count
     vec_new_momentum = outer_momentum * vec_momentum + vec_change
     vec_new = vec_start - outer_rate * (vec_change + outer_momentum * vec_new_momentum)

time: 294 us -> 289 us (0.983)
  local copies, waits for them, and re-layouts: 52 us -> 23.9 us
  waiting for transfers between devices: 128 us -> 146 us
  matrix products: 15.3 us -> 29.1 us
  other arithmetic: 16.4 us -> 8.55 us
    unnamed x28 -> x20, local copies, waits for them, and re-layouts: 25.3 us -> 3.14 us
    dot_general x2 -> x3, matrix products: 9.68 us -> 26.2 us  [fresh(): jnp.einsum('skb,kq->sbq', coeffs, basis_cols, precision=lax.Precision.HIGH)]
    all_to_all x2, waiting for transfers between devices: 21.6 us -> 29.2 us  [body(): lax.all_to_all(picked.reshape(dev_count, slot_count, summed.shape[1], sum...]
    broadcast_in_dim x1 -> x0, other arithmetic: 6.73 us -> none  [body(): new_start[None]]
    ppermute x2, waiting for transfers between devices: 13.3 us -> 19.2 us  [rep_sum(): lax.ppermute(total, 'rep', [(i, i ^ step) for i in range(rep_count)])]
    div x2, other arithmetic: 4.97 us -> 0.48 us  [body(): arrived[0].astype(jnp.float32) / rep_count]
    all_gather x2, waiting for transfers between devices: 0.01 us -> 4.29 us  [body(): gathered = lax.all_gather(picked, 'rep', axis=2, tiled=True)]
    sub x0 -> x1, other arithmetic: none -> 3.56 us  [body(): start_rows[:, :, halves[c]] - arrived[0].astype(jnp.float32) / rep_count]
  transfers between devices with their start and end apart: 9 -> 9, of which waited for: 6 -> 7; matrix products, arithmetic and copies ran while one was open for 17% -> 12% of each run, Pallas kernels for 3% -> 3%
where the time goes in v7:
time: 289 us
  waiting for transfers between devices  146 us (51%)
  blocking collectives  34.9 us (12%)
  matrix products  29.1 us (10%)
  local copies, waits for them, and re-layouts  23.9 us (8%)
  starting transfers between devices  16.3 us (6%)
  Pallas kernels  16 us (6%)
  between operations  14 us (5%)
  other arithmetic  8.55 us (3%)
    reduce_scatter x2, waiting for transfers between devices, body(): summed = lax.psum_scatter(half, 'rep', scatter_dimension=0, tiled=True)[0]  61.9 us
    all_to_all x1, blocking collectives, body(): lax.all_to_all(rounded, 'dev', split_axis=1, concat_axis=0, tiled=True)  34.9 us
    all_to_all x1, waiting for transfers between devices, body(): lax.all_to_all(rounded, 'dev', split_axis=1, concat_axis=0, tiled=True)  31.1 us
    all_to_all x2, waiting for transfers between devices, body(): lax.all_to_all(picked.reshape(dev_count, slot_count, summed.shape[1], sum...  29.2 us
    dot_general x3, matrix products, fresh(): jnp.einsum('skb,kq->sbq', coeffs, basis_cols, precision=lax.Precision.HIGH)  26.2 us
    ppermute x2, waiting for transfers between devices, rep_sum(): lax.ppermute(total, 'rep', [(i, i ^ step) for i in range(rep_count)])  19.2 us
    all_to_all x2, starting transfers between devices, body(): lax.all_to_all(picked.reshape(dev_count, slot_count, summed.shape[1], sum...  11 us
    pallas_call x2, Pallas kernels, take_half(): pl.pallas_call(_copy_kernel, grid=(quarters,), in_specs=[pl.BlockSpec((un...  8.02 us
  transfers between devices with their start and end apart: 9, of which 7 were waited for; matrix products, arithmetic and copies ran while one was open for 12% of the time, Pallas kernels for 3%

profile of v7, /device:TPU:0, one launch (start us, length us, event | category | flops | bytes accessed | tf_op | source)
XLA Modules:
  0.0 288.6 jit_solution(10192743095926603577)
XLA Ops:
  7.2 4.0 %shard_map.120 = bf16[4,160,16,128]{3,2,1,0:T(8,128)(2,1)} custom-call(bf16[160,16,1024]{2,1,0:T(8,128)(2,1)} %bitcast.59), custom_call_target="tpu_custom_call" | custom-call | tf_op jit(solution)/shard_map/pallas_call | solution.py:34
  11.3 0.0 reduce-scatter.3.cloned.1.call-start
  11.3 4.0 %shard_map.119 = bf16[4,160,16,128]{3,2,1,0:T(8,128)(2,1)} custom-call(bf16[160,16,1024]{2,1,0:T(8,128)(2,1)} %bitcast.60), custom_call_target="tpu_custom_call" | custom-call | tf_op jit(solution)/shard_map/pallas_call | solution.py:34
  15.3 0.7 copy-done.9
  16.0 0.2 convert_reduce_fusion
  16.2 0.1 select_reduce_fusion
  16.3 32.4 %reduce-scatter.5.cloned.1.call-done = bf16[1,160,16,128]{3,2,1,0:T(8,128)(2,1)} async-done(((bf16[4,160,16,128]{3,2,1,0:T(8,128)(2,1)}), bf16[1,160,16,128]{3,2,1,0:T(8,128)(2,1)}) %reduce-scatter.5.cloned.1.call-update) | async-done | bytes 655376 | tf_op jit(solution)/shard_map/reduce_scatter | solution.py:97
  48.8 3.0 %gather_fusion.1 = bf16[320,16,128]{2,1,0:T(8,128)(2,1)} fusion(bf16[160,16,128]{2,1,0:T(8,128)(2,1)} %bitcast.71, s32[1024]{0:T(1024)S(1)} %pad_clamp_fusion.1), kind=kCustom, calls=%fused_computation.1 | custom fusion | bytes 2622720 | tf_op jit(solution)/shard_map/jit(_take)/gather | solution.py:98
  51.8 5.5 %all-to-all-start.1 = ((bf16[8,40,16,128]{3,2,1,0:T(8,128)(2,1)}), bf16[8,40,16,128]{3,2,1,0:T(8,128)(2,1)S(1)}, u32[]{:S(2)}, u32[]{:S(2)}) async-start(bf16[8,40,16,128]{3,2,1,0:T(8,128)(2,1)} %bitcast.9), calls=%async_computation.3 | async-start | bytes 2621440 | tf_op jit(solution)/shard_map/all_to_all | solution.py:99
  57.3 29.4 %reduce-scatter.3.cloned.1.call-done = bf16[1,160,16,128]{3,2,1,0:T(8,128)(2,1)} async-done(((bf16[4,160,16,128]{3,2,1,0:T(8,128)(2,1)}), bf16[1,160,16,128]{3,2,1,0:T(8,128)(2,1)}) %reduce-scatter.3.cloned.1.call-update) | async-done | bytes 655376 | tf_op jit(solution)/shard_map/reduce_scatter | solution.py:97
  86.8 3.0 %gather_fusion = bf16[320,16,128]{2,1,0:T(8,128)(2,1)} fusion(bf16[160,16,128]{2,1,0:T(8,128)(2,1)} %bitcast.72, s32[1024]{0:T(1024)S(1)} %pad_clamp_fusion.1), kind=kCustom, calls=%fused_computation | custom fusion | bytes 2622720 | tf_op jit(solution)/shard_map/jit(_take)/gather | solution.py:98
  89.8 5.5 %all-to-all-start = ((bf16[8,40,16,128]{3,2,1,0:T(8,128)(2,1)}), bf16[8,40,16,128]{3,2,1,0:T(8,128)(2,1)S(1)}, u32[]{:S(2)}, u32[]{:S(2)}) async-start(bf16[8,40,16,128]{3,2,1,0:T(8,128)(2,1)} %bitcast.4), calls=%async_computation.1 | async-start | bytes 2621440 | tf_op jit(solution)/shard_map/all_to_all | solution.py:99
  95.4 0.2 multiply_bitcast_fusion
  95.6 1.9 copy.33
  97.5 29.2 %all-to-all-done = bf16[8,40,16,128]{3,2,1,0:T(8,128)(2,1)S(1)} async-done(((bf16[8,40,16,128]{3,2,1,0:T(8,128)(2,1)}), bf16[8,40,16,128]{3,2,1,0:T(8,128)(2,1)S(1)}, u32[]{:S(2)}, u32[]{:S(2)}) %all-to-all-start) | async-done | bytes 1310752 | tf_op jit(solution)/shard_map/all_to_all | solution.py:99
  126.7 0.2 multiply_bitcast_fusion.1
  127.0 0.3 copy.32
  127.3 1.4 copy-done.4
  128.7 3.6 %slice_subtract_fusion = (f32[40,128,128]{2,1,0:T(8,128)S(1)}, f32[40,128,128]{2,1,0:T(8,128)S(1)}) fusion(f32[40,128,128]{2,1,0:T(8,128)S(1)} %bitcast.64, f32[40,128,256]{2,1,0:T(8,128)} %bitcast.52, f32[40,128,128]{2,1,0:T(8,128)S(1)} %bitcast.65), kind=kLoop, calls=%fused_computation.25 | loop fusion | flops 1310720 | bytes 15728640 | tf_op jit(solution)/shard_map/sub | solution.py:106
  132.3 1.5 fusion.18
  133.8 1.5 fusion.13
  135.3 0.1 collective-permute-start
  135.4 2.1 collective-permute-done
  137.5 1.0 add_convert_fusion
  138.6 0.5 collective-permute-start.1
  139.1 0.2 compare_reduce_fusion
  139.3 17.0 %collective-permute-done.1 = bf16[2688,128]{1,0:T(8,128)(2,1)} collective-permute-done((bf16[2688,128]{1,0:T(8,128)(2,1)}, bf16[2688,128]{1,0:T(8,128)(2,1)}, u32[]{:S(2)}, u32[]{:S(2)}) %collective-permute-start.1) | collective-permute-done | bytes 688160 | tf_op jit(solution)/shard_map/ppermute | solution.py:19
  156.3 1.4 convert_add_fusion
  157.8 1.1 copy-done.5
  158.9 0.1 slice.49
  159.0 6.0 %fusion.12 = bf16[40,128,128]{2,1,0:T(8,128)(2,1)S(1)} fusion(f32[40,128,256]{2,1,0:T(8,128)} %bitcast.61, f32[40,128,128]{2,1,0:T(8,128)S(1)} %copy-done.2, f32[40,128,256]{2,1,0:T(8,128)} %bitcast.53, f32[40,64,128]{2,1,0:T(8,128)S(1)} %bitcast.56, pred[40]{0:T(512)(128)(4,1)S(1)} %get-tuple-element.16, f32[64,1024]{1,0:T(8,128)S(1)} %copy-done, ...), kind=kOutput, calls=%fused_computation.22 | convolution fusion | flops 256901120 | bytes 10519044 | tf_op jit(solution)/shard_map/skb,kq->sbq/dot_general | solution.py:124
  165.0 1.9 copy.34
  166.9 4.3 %all-to-all-start.2 = ((bf16[40,128,128]{2,0,1:T(8,128)(2,1)}), bf16[40,128,128]{2,0,1:T(8,128)(2,1)}, u32[]{:S(2)}, u32[]{:S(2)}) async-start(bf16[40,128,128]{2,0,1:T(8,128)(2,1)} %copy.34), calls=%async_computation.4 | async-start | bytes 2621440 | tf_op jit(solution)/shard_map/all_to_all | solution.py:134
  171.2 31.1 %all-to-all-done.2 = bf16[40,128,128]{2,0,1:T(8,128)(2,1)} async-done(((bf16[40,128,128]{2,0,1:T(8,128)(2,1)}), bf16[40,128,128]{2,0,1:T(8,128)(2,1)}, u32[]{:S(2)}, u32[]{:S(2)}) %all-to-all-start.2) | async-done | bytes 1310752 | tf_op jit(solution)/shard_map/all_to_all | solution.py:134
  202.3 2.6 copy.36
  204.9 2.9 gather_fusion.2
  207.8 0.2 all-gather.7.cloned.1.call-start
  208.0 5.8 %fusion.6 = bf16[40,128,128]{2,1,0:T(8,128)(2,1)S(1)} fusion(f32[40,128,256]{2,1,0:T(8,128)} %bitcast.62, f32[40,128,128]{2,1,0:T(8,128)S(1)} %get-tuple-element.12, f32[40,128,256]{2,1,0:T(8,128)} %bitcast.54, f32[40,64,128]{2,1,0:T(8,128)} %bitcast.57, pred[40]{0:T(512)(128)(4,1)S(1)} %get-tuple-element.16, f32[64,1024]{1,0:T(8,128)S(1)} %copy-done, ...), kind=kOutput, calls=%fused_computation.15 | convolution fusion | flops 256901120 | bytes 10519044 | tf_op jit(solution)/shard_map/skb,kq->sbq/dot_general | solution.py:124
  213.9 0.8 copy.37
  214.7 34.9 %all_to_all.54 = bf16[40,128,128]{2,0,1:T(8,128)(2,1)S(1)} all-to-all(bf16[40,128,128]{2,0,1:T(8,128)(2,1)S(1)} %copy.37), channel_id=1, replica_groups=mesh['rep'=4,'dev'=8] {'dev'}, dimensions={1} | all-to-all | bytes 2621440 | tf_op jit(solution)/shard_map/all_to_all | solution.py:134
  249.7 1.3 copy.39
  251.0 2.9 %gather_fusion.3 = bf16[160,16,128]{2,1,0:T(8,128)(2,1)} fusion(bf16[320,16,128]{2,1,0:T(8,128)(2,1)} %bitcast.69, s32[1024]{0:T(1024)S(1)} %pad_clamp_fusion), kind=kCustom, calls=%fused_computation.3 | custom fusion | bytes 1311360 | tf_op jit(solution)/shard_map/jit(_take)/gather | solution.py:135
  253.9 0.8 slice_multiply_fusion.2
  254.7 0.7 multiply_subtract_fusion
  255.4 4.0 %shard_map.121.base_ref = bf16[160,16,1024]{2,1,0:T(8,128)(2,1)} custom-call(bf16[160,16,512]{2,1,0:T(8,128)(2,1)} %all-gather.5.cloned.1.call-done.x_ref), custom_call_target="tpu_custom_call" | custom-call | tf_op jit(solution)/shard_map/pallas_call | solution.py:55
  259.4 14.3 %select_bitcast_fusion = (f32[1,40,128,256]{3,2,1,0:T(8,128)}, f32[1,40,128,256]{3,2,1,0:T(8,128)}) fusion(f32[40,128,256]{2,1,0:T(8,128)} %bitcast.63, pred[40]{0:T(512)(128)(4,1)S(1)} %get-tuple-element.15, f32[40,128,256]{2,1,0:T(8,128)} %bitcast.55, f32[40,128,128]{2,1,0:T(8,128)S(1)} %get-tuple-element.12, f32[40,128,128]{2,1,0:T(8,128)} %copy-done.1, ...), kind=kOutput, calls=%fused_computation.7 | convolution fusion | flops 516423680 | bytes 27591684 | tf_op jit(solution)/shard_map/skb,kq->sbq/dot_general | solution.py:124
  273.8 4.3 %all-gather.7.cloned.1.call-done.a_ref = bf16[160,16,512]{2,1,0:T(8,128)(2,1)} async-done(((bf16[160,16,128]{2,1,0:T(8,128)(2,1)}), bf16[160,16,512]{2,1,0:T(8,128)(2,1)}) %all-gather.7.cloned.1.call-update) | async-done | bytes 2621456 | tf_op jit(solution)/shard_map/all_gather | solution.py:136
  278.0 4.0 %shard_map.122 = bf16[160,16,1024]{2,1,0:T(8,128)(2,1)} custom-call(bf16[160,16,512]{2,1,0:T(8,128)(2,1)} %all-gather.7.cloned.1.call-done.a_ref, bf16[160,16,1024]{2,1,0:T(8,128)(2,1)} %shard_map.121.base_ref), custom_call_target="tpu_custom_call", output_to_operand_aliasing={{}: (1, {})} | custom-call | tf_op jit(solution)/shard_map/pallas_call | solution.py:58
  (34 shorter events, 0.3 us)
Async XLA Ops:
  7.2 125.1 %copy-start = (f32[64,1024]{1,0:T(8,128)S(1)}, f32[64,1024]{1,0:T(8,128)}, u32[]{:S(2)}) copy-start(f32[64,1024]{1,0:T(8,128)} %param.12) | copy-start | bytes 786436
  7.2 41.6 %reduce-scatter.5.cloned.1.call-start = ((), (), s32[]{:S(2)}) async-start(), calls=%async_computation.7 | async-start | bytes 3276800 | tf_op jit(solution)/shard_map/reduce_scatter | solution.py:97
  11.3 75.5 %reduce-scatter.3.cloned.1.call-start = ((), (), s32[]{:S(2)}) async-start(), calls=%async_computation.6 | async-start | bytes 3276800 | tf_op jit(solution)/shard_map/reduce_scatter | solution.py:97
  15.3 0.7 copy-start.9
  51.8 38.0 %all-to-all-start.1 = ((bf16[8,40,16,128]{3,2,1,0:T(8,128)(2,1)}), bf16[8,40,16,128]{3,2,1,0:T(8,128)(2,1)S(1)}, u32[]{:S(2)}, u32[]{:S(2)}) async-start(bf16[8,40,16,128]{3,2,1,0:T(8,128)(2,1)} %bitcast.9), calls=%async_computation.3 | async-start | bytes 2621440 | tf_op jit(solution)/shard_map/all_to_all | solution.py:99
  86.8 8.6 %copy-start.8 = (bf16[1,13,1024]{2,1,0:T(8,128)(2,1)S(1)}, bf16[1,13,1024]{2,1,0:T(8,128)(2,1)}, u32[]{:S(2)}) copy-start(bf16[1,13,1024]{2,1,0:T(8,128)(2,1)} %param.13) | copy-start | bytes 79876
  89.8 36.9 %all-to-all-start = ((bf16[8,40,16,128]{3,2,1,0:T(8,128)(2,1)}), bf16[8,40,16,128]{3,2,1,0:T(8,128)(2,1)S(1)}, u32[]{:S(2)}, u32[]{:S(2)}) async-start(bf16[8,40,16,128]{3,2,1,0:T(8,128)(2,1)} %bitcast.4), calls=%async_computation.1 | async-start | bytes 2621440 | tf_op jit(solution)/shard_map/all_to_all | solution.py:99
  127.0 1.7 copy-start.4
  132.3 3.0 %copy-start.1 = (f32[40,128,128]{2,1,0:T(8,128)}, f32[40,128,128]{2,1,0:T(8,128)S(1)}, u32[]{:S(2)}) copy-start(f32[40,128,128]{2,1,0:T(8,128)S(1)} %get-tuple-element.11) | copy-start | bytes 7864324
  135.3 2.2 collective-permute-start
  138.6 17.8 %collective-permute-start.1 = (bf16[2688,128]{1,0:T(8,128)(2,1)}, bf16[2688,128]{1,0:T(8,128)(2,1)}, u32[]{:S(2)}, u32[]{:S(2)}) collective-permute-start(bf16[2688,128]{1,0:T(8,128)(2,1)} %add_convert_fusion), channel_id=1, source_target_pairs={{0,16},{8,24},{16,0},{24,8},{1,17},{9,25},{17,1},{25,9},{2,18},{10... | collective-permute-start | bytes 2064392 | tf_op jit(solution)/shard_map/ppermute | solution.py:19
  139.3 19.7 %copy-start.2 = (f32[40,128,128]{2,1,0:T(8,128)S(1)}, f32[40,128,128]{2,1,0:T(8,128)}, u32[]{:S(2)}) copy-start(f32[40,128,128]{2,1,0:T(8,128)} %copy-done.1) | copy-start | bytes 7864324
  157.8 1.1 copy-start.5
  159.0 6.0 %copy-start.3 = (f32[2560,128]{1,0:T(8,128)}, f32[2560,128]{1,0:T(8,128)S(1)}, u32[]{:S(2)}) copy-start(f32[2560,128]{1,0:T(8,128)S(1)} %slice.49) | copy-start | bytes 3932164
  166.9 35.4 %all-to-all-start.2 = ((bf16[40,128,128]{2,0,1:T(8,128)(2,1)}), bf16[40,128,128]{2,0,1:T(8,128)(2,1)}, u32[]{:S(2)}, u32[]{:S(2)}) async-start(bf16[40,128,128]{2,0,1:T(8,128)(2,1)} %copy.34), calls=%async_computation.4 | async-start | bytes 2621440 | tf_op jit(solution)/shard_map/all_to_all | solution.py:134
  171.2 84.2 %all-gather.5.cloned.1.call-start = ((), (), s32[]{:S(2)}) async-start(), calls=%async_computation.8 | async-start | bytes 3276800 | tf_op jit(solution)/shard_map/all_gather | solution.py:136
  207.8 70.2 %all-gather.7.cloned.1.call-start = ((), (), s32[]{:S(2)}) async-start(), calls=%async_computation.9 | async-start | bytes 3276800 | tf_op jit(solution)/shard_map/all_gather | solution.py:136
  249.7 5.0 %copy-start.6 = (f32[13,1024]{1,0:T(8,128)S(1)}, f32[13,1024]{1,0:T(8,128)}, u32[]{:S(2)}) copy-start(f32[13,1024]{1,0:T(8,128)} %param.14) | copy-start | bytes 159748
  249.7 5.0 %copy-start.7 = (f32[13,1024]{1,0:T(8,128)S(1)}, f32[13,1024]{1,0:T(8,128)}, u32[]{:S(2)}) copy-start(f32[13,1024]{1,0:T(8,128)} %param.15) | copy-start | bytes 159748
Sparse Core Ops, SparseCore 0:
  11.4 37.3 reduce-scatter.4
  52.0 34.6 reduce-scatter.2
  207.9 23.9 all-gather.4
  254.0 23.9 all-gather.6

commit v8 on v7

--- a/solution.py
+++ b/solution.py
@@ -128,9 +128,10 @@
         return fresh_start, fresh_momentum
 
     returned = None
+    all_changes = jnp.concatenate(changes, axis=2)
+    rounded_all = fresh(start_rows, momentum_rows, all_changes, basis_part)[0].astype(jnp.bfloat16)
     for c in range(2):
-        fresh_start, _ = fresh(start_rows[:, :, halves[c]], momentum_rows[:, :, halves[c]], changes[c], basis_part[:, halves[c]])
-        rounded = fresh_start.astype(jnp.bfloat16)
+        rounded = rounded_all[:, :, halves[c]]
         pieces = lax.all_to_all(rounded, "dev", split_axis=1, concat_axis=0, tiled=True)
         picked = jnp.take(pieces, target, axis=0, mode="clip")
         gathered = lax.all_gather(picked, "rep", axis=2, tiled=True)

time: 289 us -> 288 us (level)
  matrix products: 29.1 us -> 10.9 us
  other arithmetic: 8.55 us -> 19.5 us
  local copies, waits for them, and re-layouts: 23.9 us -> 26.9 us
  waiting for transfers between devices: 146 us -> 149 us
    dot_general x3 -> x1, matrix products: 26.2 us -> 7.94 us  [fresh(): jnp.einsum('skb,kq->sbq', coeffs, basis_cols, precision=lax.Precision.HIGH)]
    broadcast_in_dim x0 -> x1, other arithmetic: none -> 11 us  [body(): new_momentum[None]]
    slice x0 -> x3, local copies, waits for them, and re-layouts: none -> 5.62 us  [body(): rounded = rounded_all[:, :, halves[c]]]
    all_gather x2, waiting for transfers between devices: 4.29 us -> 7.64 us  [body(): gathered = lax.all_gather(picked, 'rep', axis=2, tiled=True)]
  transfers between devices with their start and end apart: 9 -> 9, of which waited for: 7 -> 7; matrix products, arithmetic and copies ran while one was open for 12% -> 10% of each run, Pallas kernels for 3% -> 3%
where the time goes in v8:
time: 288 us; the launch traced here: 287 us
  waiting for transfers between devices  149 us (52%)
  blocking collectives  34.9 us (12%)
  local copies, waits for them, and re-layouts  26.9 us (9%)
  other arithmetic  19.5 us (7%)
  starting transfers between devices  16.1 us (6%)
  Pallas kernels  16.1 us (6%)
  between operations  14 us (5%)
  matrix products  10.9 us (4%)
    reduce_scatter x2, waiting for transfers between devices, body(): summed = lax.psum_scatter(half, 'rep', scatter_dimension=0, tiled=True)[0]  61.9 us
    all_to_all x1, blocking collectives, body(): lax.all_to_all(rounded, 'dev', split_axis=1, concat_axis=0, tiled=True)  34.9 us
    all_to_all x1, waiting for transfers between devices, body(): lax.all_to_all(rounded, 'dev', split_axis=1, concat_axis=0, tiled=True)  31.1 us
    all_to_all x2, waiting for transfers between devices, body(): lax.all_to_all(picked.reshape(dev_count, slot_count, summed.shape[1], sum...  29.2 us
    ppermute x2, waiting for transfers between devices, rep_sum(): lax.ppermute(total, 'rep', [(i, i ^ step) for i in range(rep_count)])  19.2 us
    all_to_all x2, starting transfers between devices, body(): lax.all_to_all(picked.reshape(dev_count, slot_count, summed.shape[1], sum...  11 us
    broadcast_in_dim x1, other arithmetic, body(): new_momentum[None]  11 us
    pallas_call x2, Pallas kernels, take_half(): pl.pallas_call(_copy_kernel, grid=(quarters,), in_specs=[pl.BlockSpec((un...  8.02 us
  transfers between devices with their start and end apart: 9, of which 7 were waited for; matrix products, arithmetic and copies ran while one was open for 10% of the time, Pallas kernels for 3%

profile of v8, /device:TPU:0, one launch (start us, length us, event | category | flops | bytes accessed | tf_op | source)
XLA Modules:
  0.0 287.4 jit_solution(9103572725846473318)
XLA Ops:
  7.2 4.0 %shard_map.120 = bf16[4,160,16,128]{3,2,1,0:T(8,128)(2,1)} custom-call(bf16[160,16,1024]{2,1,0:T(8,128)(2,1)} %bitcast.52), custom_call_target="tpu_custom_call" | custom-call | tf_op jit(solution)/shard_map/pallas_call | solution.py:34
  11.3 0.0 reduce-scatter.3.cloned.1.call-start
  11.3 4.0 %shard_map.119 = bf16[4,160,16,128]{3,2,1,0:T(8,128)(2,1)} custom-call(bf16[160,16,1024]{2,1,0:T(8,128)(2,1)} %bitcast.53), custom_call_target="tpu_custom_call" | custom-call | tf_op jit(solution)/shard_map/pallas_call | solution.py:34
  15.3 0.7 copy-done.9
  16.0 0.2 convert_reduce_fusion
  16.2 0.1 select_reduce_fusion
  16.3 32.4 %reduce-scatter.5.cloned.1.call-done = bf16[1,160,16,128]{3,2,1,0:T(8,128)(2,1)} async-done(((bf16[4,160,16,128]{3,2,1,0:T(8,128)(2,1)}), bf16[1,160,16,128]{3,2,1,0:T(8,128)(2,1)}) %reduce-scatter.5.cloned.1.call-update) | async-done | bytes 655376 | tf_op jit(solution)/shard_map/reduce_scatter | solution.py:97
  48.8 3.0 %gather_fusion.1 = bf16[320,16,128]{2,1,0:T(8,128)(2,1)} fusion(bf16[160,16,128]{2,1,0:T(8,128)(2,1)} %bitcast.63, s32[1024]{0:T(1024)S(1)} %pad_clamp_fusion.1), kind=kCustom, calls=%fused_computation.1 | custom fusion | bytes 2622720 | tf_op jit(solution)/shard_map/jit(_take)/gather | solution.py:98
  51.8 5.5 %all-to-all-start.1 = ((bf16[8,40,16,128]{3,2,1,0:T(8,128)(2,1)}), bf16[8,40,16,128]{3,2,1,0:T(8,128)(2,1)S(1)}, u32[]{:S(2)}, u32[]{:S(2)}) async-start(bf16[8,40,16,128]{3,2,1,0:T(8,128)(2,1)} %bitcast.9), calls=%async_computation.3 | async-start | bytes 2621440 | tf_op jit(solution)/shard_map/all_to_all | solution.py:99
  57.3 29.4 %reduce-scatter.3.cloned.1.call-done = bf16[1,160,16,128]{3,2,1,0:T(8,128)(2,1)} async-done(((bf16[4,160,16,128]{3,2,1,0:T(8,128)(2,1)}), bf16[1,160,16,128]{3,2,1,0:T(8,128)(2,1)}) %reduce-scatter.3.cloned.1.call-update) | async-done | bytes 655376 | tf_op jit(solution)/shard_map/reduce_scatter | solution.py:97
  86.8 3.0 %gather_fusion = bf16[320,16,128]{2,1,0:T(8,128)(2,1)} fusion(bf16[160,16,128]{2,1,0:T(8,128)(2,1)} %bitcast.64, s32[1024]{0:T(1024)S(1)} %pad_clamp_fusion.1), kind=kCustom, calls=%fused_computation | custom fusion | bytes 2622720 | tf_op jit(solution)/shard_map/jit(_take)/gather | solution.py:98
  89.8 5.5 %all-to-all-start = ((bf16[8,40,16,128]{3,2,1,0:T(8,128)(2,1)}), bf16[8,40,16,128]{3,2,1,0:T(8,128)(2,1)S(1)}, u32[]{:S(2)}, u32[]{:S(2)}) async-start(bf16[8,40,16,128]{3,2,1,0:T(8,128)(2,1)} %bitcast.4), calls=%async_computation.1 | async-start | bytes 2621440 | tf_op jit(solution)/shard_map/all_to_all | solution.py:99
  95.4 0.2 multiply_bitcast_fusion
  95.6 1.9 copy.33
  97.5 29.2 %all-to-all-done = bf16[8,40,16,128]{3,2,1,0:T(8,128)(2,1)S(1)} async-done(((bf16[8,40,16,128]{3,2,1,0:T(8,128)(2,1)}), bf16[8,40,16,128]{3,2,1,0:T(8,128)(2,1)S(1)}, u32[]{:S(2)}, u32[]{:S(2)}) %all-to-all-start) | async-done | bytes 1310752 | tf_op jit(solution)/shard_map/all_to_all | solution.py:99
  126.7 0.2 multiply_bitcast_fusion.1
  127.0 0.3 copy.32
  127.3 1.4 copy-done.4
  128.7 3.6 %slice_subtract_fusion = (f32[40,128,128]{2,1,0:T(8,128)S(1)}, f32[40,128,128]{2,1,0:T(8,128)S(1)}) fusion(f32[40,128,128]{2,1,0:T(8,128)S(1)} %bitcast.55, f32[40,128,256]{2,1,0:T(8,128)} %bitcast.50, f32[40,128,128]{2,1,0:T(8,128)S(1)} %bitcast.56), kind=kLoop, calls=%fused_computation.11 | loop fusion | flops 1310720 | bytes 15728640 | tf_op jit(solution)/shard_map/sub | solution.py:106
  132.3 1.5 fusion.7
  133.8 1.5 fusion.1
  135.3 0.1 collective-permute-start
  135.4 2.1 collective-permute-done
  137.5 1.0 add_convert_fusion
  138.6 0.5 collective-permute-start.1
  139.1 0.2 compare_reduce_fusion
  139.3 17.0 %collective-permute-done.1 = bf16[2688,128]{1,0:T(8,128)(2,1)} collective-permute-done((bf16[2688,128]{1,0:T(8,128)(2,1)}, bf16[2688,128]{1,0:T(8,128)(2,1)}, u32[]{:S(2)}, u32[]{:S(2)}) %collective-permute-start.1) | collective-permute-done | bytes 688160 | tf_op jit(solution)/shard_map/ppermute | solution.py:19
  156.3 1.4 convert_add_fusion
  157.8 0.1 slice.45
  157.9 1.0 copy-done.5
  158.9 7.9 %subtract_convert_fusion = (bf16[40,128,256]{2,1,0:T(8,128)(2,1)S(1)}, f32[40,128,256]{2,1,0:T(8,128)}) fusion(f32[40,128,128]{2,1,0:T(8,128)S(1)} %get-tuple-element.12, f32[40,128,128]{2,1,0:T(8,128)S(1)} %copy-done.3, pred[40]{0:T(512)(128)(4,1)S(1)} %get-tuple-element.16, f32[1,40,128,256]{3,2,1,0:T(8,128)} %param.11, f32[1,40,128,256]{3,2,1,0:T(8,128)} %param.10, ...), kind=kOutput, calls=%fused_computation.10 | convolution fusion | flops 515112960 | bytes 24969732 | tf_op jit(solution)/shard_map/skb,kq->sbq/dot_general | solution.py:124
  166.8 1.5 fusion.11
  168.4 1.9 copy.34
  170.3 4.3 %all-to-all-start.2 = ((bf16[40,128,128]{2,0,1:T(8,128)(2,1)}), bf16[40,128,128]{2,0,1:T(8,128)(2,1)}, u32[]{:S(2)}, u32[]{:S(2)}) async-start(bf16[40,128,128]{2,0,1:T(8,128)(2,1)} %copy.34), calls=%async_computation.4 | async-start | bytes 2621440 | tf_op jit(solution)/shard_map/all_to_all | solution.py:135
  174.5 0.0 all-gather.5.cloned.1.call-start
  174.6 31.1 %all-to-all-done.2 = bf16[40,128,128]{2,0,1:T(8,128)(2,1)} async-done(((bf16[40,128,128]{2,0,1:T(8,128)(2,1)}), bf16[40,128,128]{2,0,1:T(8,128)(2,1)}, u32[]{:S(2)}, u32[]{:S(2)}) %all-to-all-start.2) | async-done | bytes 1310752 | tf_op jit(solution)/shard_map/all_to_all | solution.py:135
  205.7 2.6 copy.36
  208.3 3.0 %gather_fusion.2 = bf16[160,16,128]{2,1,0:T(8,128)(2,1)} fusion(bf16[320,16,128]{2,1,0:T(8,128)(2,1)} %bitcast.62, s32[1024]{0:T(1024)S(1)} %pad_clamp_fusion), kind=kCustom, calls=%fused_computation.2 | custom fusion | bytes 1311360 | tf_op jit(solution)/shard_map/jit(_take)/gather | solution.py:136
  211.3 2.2 copy.37
  213.5 34.9 %all_to_all.54 = bf16[40,128,128]{2,0,1:T(8,128)(2,1)S(1)} all-to-all(bf16[40,128,128]{2,0,1:T(8,128)(2,1)S(1)} %copy.37), channel_id=1, replica_groups=mesh['rep'=4,'dev'=8] {'dev'}, dimensions={1} | all-to-all | bytes 2621440 | tf_op jit(solution)/shard_map/all_to_all | solution.py:135
  248.4 1.3 copy.39
  249.7 3.0 %gather_fusion.3 = bf16[160,16,128]{2,1,0:T(8,128)(2,1)} fusion(bf16[320,16,128]{2,1,0:T(8,128)(2,1)} %bitcast.61, s32[1024]{0:T(1024)S(1)} %pad_clamp_fusion), kind=kCustom, calls=%fused_computation.3 | custom fusion | bytes 1311360 | tf_op jit(solution)/shard_map/jit(_take)/gather | solution.py:136
  252.7 0.8 slice_multiply_fusion
  253.6 0.7 multiply_subtract_fusion
  254.2 4.0 %shard_map.121.base_ref = bf16[160,16,1024]{2,1,0:T(8,128)(2,1)} custom-call(bf16[160,16,512]{2,1,0:T(8,128)(2,1)} %all-gather.5.cloned.1.call-done.x_ref), custom_call_target="tpu_custom_call" | custom-call | tf_op jit(solution)/shard_map/pallas_call | solution.py:55
  258.3 11.0 %select_bitcast_fusion = (f32[1,40,128,256]{3,2,1,0:T(8,128)}, f32[1,40,128,256]{3,2,1,0:T(8,128)}) fusion(f32[40,128,256]{2,1,0:T(8,128)} %bitcast.54, pred[40]{0:T(512)(128)(4,1)S(1)} %get-tuple-element.15, f32[40,128,256]{2,1,0:T(8,128)} %get-tuple-element.26, f32[40,128,128]{2,1,0:T(8,128)S(1)} %get-tuple-element.12, f32[40,128,128]{2,1,0:T(8,128)} %copy-done.2, ...), kind=kLoop, calls=%fused_computation.8 | loop fusion | flops 13107200 | bytes 31457360 | tf_op jit(solution)/shard_map/broadcast_in_dim | solution.py:149
  269.2 7.6 %all-gather.7.cloned.1.call-done.a_ref = bf16[160,16,512]{2,1,0:T(8,128)(2,1)} async-done(((bf16[160,16,128]{2,1,0:T(8,128)(2,1)}), bf16[160,16,512]{2,1,0:T(8,128)(2,1)}) %all-gather.7.cloned.1.call-update) | async-done | bytes 2621456 | tf_op jit(solution)/shard_map/all_gather | solution.py:137
  276.9 4.0 %shard_map.122 = bf16[160,16,1024]{2,1,0:T(8,128)(2,1)} custom-call(bf16[160,16,512]{2,1,0:T(8,128)(2,1)} %all-gather.7.cloned.1.call-done.a_ref, bf16[160,16,1024]{2,1,0:T(8,128)(2,1)} %shard_map.121.base_ref), custom_call_target="tpu_custom_call", output_to_operand_aliasing={{}: (1, {})} | custom-call | tf_op jit(solution)/shard_map/pallas_call | solution.py:58
  (34 shorter events, 0.3 us)
Async XLA Ops:
  7.2 125.1 %copy-start = (f32[64,1024]{1,0:T(8,128)S(1)}, f32[64,1024]{1,0:T(8,128)}, u32[]{:S(2)}) copy-start(f32[64,1024]{1,0:T(8,128)} %param.12) | copy-start | bytes 786436
  7.2 41.6 %reduce-scatter.5.cloned.1.call-start = ((), (), s32[]{:S(2)}) async-start(), calls=%async_computation.7 | async-start | bytes 3276800 | tf_op jit(solution)/shard_map/reduce_scatter | solution.py:97
  11.3 75.5 %reduce-scatter.3.cloned.1.call-start = ((), (), s32[]{:S(2)}) async-start(), calls=%async_computation.6 | async-start | bytes 3276800 | tf_op jit(solution)/shard_map/reduce_scatter | solution.py:97
  15.3 0.7 copy-start.9
  51.8 38.0 %all-to-all-start.1 = ((bf16[8,40,16,128]{3,2,1,0:T(8,128)(2,1)}), bf16[8,40,16,128]{3,2,1,0:T(8,128)(2,1)S(1)}, u32[]{:S(2)}, u32[]{:S(2)}) async-start(bf16[8,40,16,128]{3,2,1,0:T(8,128)(2,1)} %bitcast.9), calls=%async_computation.3 | async-start | bytes 2621440 | tf_op jit(solution)/shard_map/all_to_all | solution.py:99
  86.8 8.6 %copy-start.8 = (bf16[1,13,1024]{2,1,0:T(8,128)(2,1)S(1)}, bf16[1,13,1024]{2,1,0:T(8,128)(2,1)}, u32[]{:S(2)}) copy-start(bf16[1,13,1024]{2,1,0:T(8,128)(2,1)} %param.13) | copy-start | bytes 79876
  89.8 36.9 %all-to-all-start = ((bf16[8,40,16,128]{3,2,1,0:T(8,128)(2,1)}), bf16[8,40,16,128]{3,2,1,0:T(8,128)(2,1)S(1)}, u32[]{:S(2)}, u32[]{:S(2)}) async-start(bf16[8,40,16,128]{3,2,1,0:T(8,128)(2,1)} %bitcast.4), calls=%async_computation.1 | async-start | bytes 2621440 | tf_op jit(solution)/shard_map/all_to_all | solution.py:99
  127.0 1.7 copy-start.4
  132.3 3.0 %copy-start.2 = (f32[40,128,128]{2,1,0:T(8,128)}, f32[40,128,128]{2,1,0:T(8,128)S(1)}, u32[]{:S(2)}) copy-start(f32[40,128,128]{2,1,0:T(8,128)S(1)} %get-tuple-element.11) | copy-start | bytes 7864324
  135.3 2.2 collective-permute-start
  138.6 17.8 %collective-permute-start.1 = (bf16[2688,128]{1,0:T(8,128)(2,1)}, bf16[2688,128]{1,0:T(8,128)(2,1)}, u32[]{:S(2)}, u32[]{:S(2)}) collective-permute-start(bf16[2688,128]{1,0:T(8,128)(2,1)} %add_convert_fusion), channel_id=1, source_target_pairs={{0,16},{8,24},{16,0},{24,8},{1,17},{9,25},{17,1},{25,9},{2,18},{10... | collective-permute-start | bytes 2064392 | tf_op jit(solution)/shard_map/ppermute | solution.py:19
  139.3 19.6 %copy-start.3 = (f32[40,128,128]{2,1,0:T(8,128)S(1)}, f32[40,128,128]{2,1,0:T(8,128)}, u32[]{:S(2)}) copy-start(f32[40,128,128]{2,1,0:T(8,128)} %copy-done.2) | copy-start | bytes 7864324
  157.8 1.1 copy-start.5
  170.3 35.4 %all-to-all-start.2 = ((bf16[40,128,128]{2,0,1:T(8,128)(2,1)}), bf16[40,128,128]{2,0,1:T(8,128)(2,1)}, u32[]{:S(2)}, u32[]{:S(2)}) async-start(bf16[40,128,128]{2,0,1:T(8,128)(2,1)} %copy.34), calls=%async_computation.4 | async-start | bytes 2621440 | tf_op jit(solution)/shard_map/all_to_all | solution.py:135
  174.5 79.7 %all-gather.5.cloned.1.call-start = ((), (), s32[]{:S(2)}) async-start(), calls=%async_computation.8 | async-start | bytes 3276800 | tf_op jit(solution)/shard_map/all_gather | solution.py:137
  211.3 65.6 %all-gather.7.cloned.1.call-start = ((), (), s32[]{:S(2)}) async-start(), calls=%async_computation.9 | async-start | bytes 3276800 | tf_op jit(solution)/shard_map/all_gather | solution.py:137
  248.4 5.1 %copy-start.6 = (f32[13,1024]{1,0:T(8,128)S(1)}, f32[13,1024]{1,0:T(8,128)}, u32[]{:S(2)}) copy-start(f32[13,1024]{1,0:T(8,128)} %param.14) | copy-start | bytes 159748
  248.4 5.1 %copy-start.7 = (f32[13,1024]{1,0:T(8,128)S(1)}, f32[13,1024]{1,0:T(8,128)}, u32[]{:S(2)}) copy-start(f32[13,1024]{1,0:T(8,128)} %param.15) | copy-start | bytes 159748
  276.9 4.0 %copy-start.1 = (f32[64,1024]{1,0:T(8,128)S(1)}, f32[64,1024]{1,0:T(8,128)}, u32[]{:S(2)}) copy-start(f32[64,1024]{1,0:T(8,128)} %param.12) | copy-start | bytes 786436
Sparse Core Ops, SparseCore 0:
  11.4 37.3 reduce-scatter.4
  52.0 34.6 reduce-scatter.2
  211.4 23.9 all-gather.4
  252.8 23.9 all-gather.6

commit v9 on v8

--- a/solution.py
+++ b/solution.py
@@ -13,15 +13,28 @@
 
 def rep_sum(x):
     rep_count = lax.axis_size("rep")
-    total = x.astype(jnp.bfloat16)
-    step = 1
-    while step < rep_count:
-        other = lax.ppermute(total, "rep", [(i, i ^ step) for i in range(rep_count)])
-        total = total.astype(jnp.float32) + other.astype(jnp.float32)
-        step *= 2
-        if step < rep_count:
-            total = total.astype(jnp.bfloat16)
-    return total
+    if rep_count != 4:
+        total = x.astype(jnp.bfloat16)
+        step = 1
+        while step < rep_count:
+            other = lax.ppermute(total, "rep", [(i, i ^ step) for i in range(rep_count)])
+            total = total.astype(jnp.float32) + other.astype(jnp.float32)
+            step *= 2
+            if step < rep_count:
+                total = total.astype(jnp.bfloat16)
+        return total
+    core = lax.axis_index("rep") % 2
+    mine = x.astype(jnp.bfloat16)
+    other = lax.ppermute(mine, "rep", [(i, i ^ 1) for i in range(4)])
+    pair = (mine.astype(jnp.float32) + other.astype(jnp.float32)).astype(jnp.bfloat16)
+    pair = pair.reshape((2, x.shape[0] // 2) + x.shape[1:])
+    part = lax.dynamic_index_in_dim(pair, core, 0, keepdims=False)
+    across = lax.ppermute(part, "rep", [(i, i ^ 2) for i in range(4)])
+    done = part.astype(jnp.float32) + across.astype(jnp.float32)
+    rest = lax.ppermute(done, "rep", [(i, i ^ 1) for i in range(4)])
+    first = jnp.where(core == 0, done, rest)
+    second = jnp.where(core == 0, rest, done)
+    return jnp.concatenate([first, second], axis=0)
 
 
 def _copy_kernel(x_ref, o_ref):
@@ -90,6 +103,7 @@
     first_column = lax.axis_index("rep") * quarter
     basis_part = lax.dynamic_slice_in_dim(basis, first_column, quarter, 1)
     halves = [slice(c * width, (c + 1) * width) for c in range(2)]
+    held = start_rows - (outer_rate * outer_momentum * outer_momentum) * momentum_rows
     changes = []
     coeff_terms = None
     for c in range(2):
@@ -129,7 +143,9 @@
 
     returned = None
     all_changes = jnp.concatenate(changes, axis=2)
-    rounded_all = fresh(start_rows, momentum_rows, all_changes, basis_part)[0].astype(jnp.bfloat16)
+    projected_all = jnp.einsum("skb,kq->sbq", coeffs, basis_part, precision=lax.Precision.HIGH)
+    grad_all = jnp.where(emb_mask, projected_all, all_changes)
+    rounded_all = (held - (outer_rate * (1.0 + outer_momentum)) * grad_all).astype(jnp.bfloat16)
     for c in range(2):
         rounded = rounded_all[:, :, halves[c]]
         pieces = lax.all_to_all(rounded, "dev", split_axis=1, concat_axis=0, tiled=True)

time: 288 us -> 287 us (level)
  waiting for transfers between devices: 149 us -> 143 us
  other arithmetic: 19.5 us -> 24.1 us
    ppermute x2 -> x3, waiting for transfers between devices: 19.2 us -> 14.3 us  [the longest x1 9.56 us: rep_sum(): across = lax.ppermute(part, 'rep', [(i, i ^ 2) for i in range(4)])]
  transfers between devices with their start and end apart: 9 -> 10, of which waited for: 7 -> 8; matrix products, arithmetic and copies ran while one was open for 10% -> 10% of each run, Pallas kernels for 3% -> 3%
where the time goes in v9:
time: 287 us; the launch traced here: 286 us
  waiting for transfers between devices  143 us (50%)
  blocking collectives  35 us (12%)
  local copies, waits for them, and re-layouts  27.2 us (9%)
  other arithmetic  24.1 us (8%)
  starting transfers between devices  16.1 us (6%)
  Pallas kernels  16.1 us (6%)
  between operations  14 us (5%)
  matrix products  10.5 us (4%)
    reduce_scatter x2, waiting for transfers between devices, body(): summed = lax.psum_scatter(half, 'rep', scatter_dimension=0, tiled=True)[0]  61.9 us
    all_to_all x1, blocking collectives, body(): lax.all_to_all(rounded, 'dev', split_axis=1, concat_axis=0, tiled=True)  35 us
    all_to_all x1, waiting for transfers between devices, body(): lax.all_to_all(rounded, 'dev', split_axis=1, concat_axis=0, tiled=True)  31.9 us
    all_to_all x2, waiting for transfers between devices, body(): lax.all_to_all(picked.reshape(dev_count, slot_count, summed.shape[1], sum...  27.4 us
    all_to_all x2, starting transfers between devices, body(): lax.all_to_all(picked.reshape(dev_count, slot_count, summed.shape[1], sum...  11 us
    broadcast_in_dim x1, other arithmetic, body(): new_momentum[None]  11 us
    ppermute x1, waiting for transfers between devices, rep_sum(): across = lax.ppermute(part, 'rep', [(i, i ^ 2) for i in range(4)])  9.56 us
    pallas_call x2, Pallas kernels, take_half(): pl.pallas_call(_copy_kernel, grid=(quarters,), in_specs=[pl.BlockSpec((un...  8.02 us
  transfers between devices with their start and end apart: 10, of which 8 were waited for; matrix products, arithmetic and copies ran while one was open for 10% of the time, Pallas kernels for 3%

profile of v9, /device:TPU:0, one launch (start us, length us, event | category | flops | bytes accessed | tf_op | source)
XLA Modules:
  0.0 286.2 jit_solution(9449694388575509265)
XLA Ops:
  7.2 4.0 %shard_map.120 = bf16[4,160,16,128]{3,2,1,0:T(8,128)(2,1)} custom-call(bf16[160,16,1024]{2,1,0:T(8,128)(2,1)} %bitcast.59), custom_call_target="tpu_custom_call" | custom-call | tf_op jit(solution)/shard_map/pallas_call | solution.py:47
  11.3 4.0 %shard_map.119 = bf16[4,160,16,128]{3,2,1,0:T(8,128)(2,1)} custom-call(bf16[160,16,1024]{2,1,0:T(8,128)(2,1)} %bitcast.60), custom_call_target="tpu_custom_call" | custom-call | tf_op jit(solution)/shard_map/pallas_call | solution.py:47
  15.3 0.7 copy-done.12
  16.0 0.2 convert_reduce_fusion
  16.2 0.1 select_reduce_fusion
  16.3 32.4 %reduce-scatter.5.cloned.1.call-done = bf16[1,160,16,128]{3,2,1,0:T(8,128)(2,1)} async-done(((bf16[4,160,16,128]{3,2,1,0:T(8,128)(2,1)}), bf16[1,160,16,128]{3,2,1,0:T(8,128)(2,1)}) %reduce-scatter.5.cloned.1.call-update) | async-done | bytes 655376 | tf_op jit(solution)/shard_map/reduce_scatter | solution.py:111
  48.8 3.0 %gather_fusion.1 = bf16[320,16,128]{2,1,0:T(8,128)(2,1)} fusion(bf16[160,16,128]{2,1,0:T(8,128)(2,1)} %bitcast.73, s32[1024]{0:T(1024)S(1)} %pad_clamp_fusion.1), kind=kCustom, calls=%fused_computation.1 | custom fusion | bytes 2622720 | tf_op jit(solution)/shard_map/jit(_take)/gather | solution.py:112
  51.8 5.5 %all-to-all-start.1 = ((bf16[8,40,16,128]{3,2,1,0:T(8,128)(2,1)}), bf16[8,40,16,128]{3,2,1,0:T(8,128)(2,1)S(1)}, u32[]{:S(2)}, u32[]{:S(2)}) async-start(bf16[8,40,16,128]{3,2,1,0:T(8,128)(2,1)} %bitcast.9), calls=%async_computation.3 | async-start | bytes 2621440 | tf_op jit(solution)/shard_map/all_to_all | solution.py:113
  57.3 29.4 %reduce-scatter.3.cloned.1.call-done = bf16[1,160,16,128]{3,2,1,0:T(8,128)(2,1)} async-done(((bf16[4,160,16,128]{3,2,1,0:T(8,128)(2,1)}), bf16[1,160,16,128]{3,2,1,0:T(8,128)(2,1)}) %reduce-scatter.3.cloned.1.call-update) | async-done | bytes 655376 | tf_op jit(solution)/shard_map/reduce_scatter | solution.py:111
  86.8 3.0 %gather_fusion = bf16[320,16,128]{2,1,0:T(8,128)(2,1)} fusion(bf16[160,16,128]{2,1,0:T(8,128)(2,1)} %bitcast.74, s32[1024]{0:T(1024)S(1)} %pad_clamp_fusion.1), kind=kCustom, calls=%fused_computation | custom fusion | bytes 2622720 | tf_op jit(solution)/shard_map/jit(_take)/gather | solution.py:112
  89.8 5.5 %all-to-all-start = ((bf16[8,40,16,128]{3,2,1,0:T(8,128)(2,1)}), bf16[8,40,16,128]{3,2,1,0:T(8,128)(2,1)}, u32[]{:S(2)}, u32[]{:S(2)}) async-start(bf16[8,40,16,128]{3,2,1,0:T(8,128)(2,1)} %bitcast.4), calls=%async_computation.1 | async-start | bytes 2621440 | tf_op jit(solution)/shard_map/all_to_all | solution.py:113
  95.3 0.6 reshape.62
  96.0 1.6 multiply_bitcast_fusion
  97.5 1.9 copy.33
  99.4 27.4 %all-to-all-done = bf16[8,40,16,128]{3,2,1,0:T(8,128)(2,1)} async-done(((bf16[8,40,16,128]{3,2,1,0:T(8,128)(2,1)}), bf16[8,40,16,128]{3,2,1,0:T(8,128)(2,1)}, u32[]{:S(2)}, u32[]{:S(2)}) %all-to-all-start) | async-done | bytes 1310752 | tf_op jit(solution)/shard_map/all_to_all | solution.py:113
  126.8 1.6 multiply_bitcast_fusion.1
  128.4 0.3 copy.32
  128.7 1.4 copy-done.4
  130.1 3.6 %slice_subtract_fusion = (f32[40,128,128]{2,1,0:T(8,128)S(1)}, f32[40,128,128]{2,1,0:T(8,128)S(1)}) fusion(f32[40,128,128]{2,1,0:T(8,128)S(1)} %bitcast.62, f32[40,128,256]{2,1,0:T(8,128)} %bitcast.57, f32[40,128,128]{2,1,0:T(8,128)S(1)} %bitcast.63), kind=kLoop, calls=%fused_computation.13 | loop fusion | flops 1310720 | bytes 15728640 | tf_op jit(solution)/shard_map/sub | solution.py:120
  133.7 1.5 fusion.10
  135.2 1.5 fusion.4
  136.7 0.9 pad_maximum_fusion.1
  137.6 2.5 collective-permute-done
  140.1 1.3 add_convert_fusion
  141.4 0.6 collective-permute-start.1
  142.0 9.6 %collective-permute-done.1 = bf16[1344,128]{1,0:T(8,128)(2,1)S(1)} collective-permute-done((bf16[1344,128]{1,0:T(8,128)(2,1)S(1)}, bf16[1344,128]{1,0:T(8,128)(2,1)S(1)}, u32[]{:S(2)}, u32[]{:S(2)}) %collective-permute-start.1) | collective-permute-done | bytes 344096 | tf_op jit(solution)/shard_map/ppermute | solution.py:32
  151.6 0.9 convert_add_fusion
  152.5 0.2 compare_reduce_fusion
  152.7 2.3 collective-permute-done.2
  155.0 1.3 broadcast_select_fusion.1
  156.4 0.8 copy-done.7
  157.2 7.6 %fusion.3 = (bf16[40,128,256]{2,1,0:T(8,128)(2,1)S(1)}, f32[40,128,256]{2,1,0:T(8,128)}) fusion(f32[40,128,128]{2,1,0:T(8,128)S(1)} %get-tuple-element.12, f32[40,128,128]{2,1,0:T(8,128)S(1)} %copy-done.3, pred[40]{0:T(512)(128)(4,1)S(1)} %get-tuple-element.16, f32[1,40,128,256]{3,2,1,0:T(8,128)} %param.11, f32[1,40,128,256]{3,2,1,0:T(8,128)} %param.10, ...), kind=kOutput, calls=%fused_computation.9 | convolution fusion | flops 512491520 | bytes 24969732 | tf_op jit(solution)/shard_map/skb,kq->sbq/dot_general | solution.py:146
  164.8 1.5 fusion.14
  166.4 1.9 copy.34
  168.3 4.3 %all-to-all-start.2 = ((bf16[40,128,128]{2,0,1:T(8,128)(2,1)}), bf16[40,128,128]{2,0,1:T(8,128)(2,1)}, u32[]{:S(2)}, u32[]{:S(2)}) async-start(bf16[40,128,128]{2,0,1:T(8,128)(2,1)} %copy.34), calls=%async_computation.4 | async-start | bytes 2621440 | tf_op jit(solution)/shard_map/all_to_all | solution.py:151
  172.6 31.9 %all-to-all-done.2 = bf16[40,128,128]{2,0,1:T(8,128)(2,1)} async-done(((bf16[40,128,128]{2,0,1:T(8,128)(2,1)}), bf16[40,128,128]{2,0,1:T(8,128)(2,1)}, u32[]{:S(2)}, u32[]{:S(2)}) %all-to-all-start.2) | async-done | bytes 1310752 | tf_op jit(solution)/shard_map/all_to_all | solution.py:151
  204.5 2.6 copy.36
  207.1 2.9 %gather_fusion.2 = bf16[160,16,128]{2,1,0:T(8,128)(2,1)} fusion(bf16[320,16,128]{2,1,0:T(8,128)(2,1)} %bitcast.72, s32[1024]{0:T(1024)S(1)} %pad_clamp_fusion), kind=kCustom, calls=%fused_computation.2 | custom fusion | bytes 1311360 | tf_op jit(solution)/shard_map/jit(_take)/gather | solution.py:152
  210.1 2.2 copy.37
  212.2 35.0 %all_to_all.54 = bf16[40,128,128]{2,0,1:T(8,128)(2,1)S(1)} all-to-all(bf16[40,128,128]{2,0,1:T(8,128)(2,1)S(1)} %copy.37), channel_id=1, replica_groups=mesh['rep'=4,'dev'=8] {'dev'}, dimensions={1} | all-to-all | bytes 2621440 | tf_op jit(solution)/shard_map/all_to_all | solution.py:151
  247.2 1.3 copy.39
  248.5 3.0 %gather_fusion.3 = bf16[160,16,128]{2,1,0:T(8,128)(2,1)} fusion(bf16[320,16,128]{2,1,0:T(8,128)(2,1)} %bitcast.71, s32[1024]{0:T(1024)S(1)} %pad_clamp_fusion), kind=kCustom, calls=%fused_computation.3 | custom fusion | bytes 1311360 | tf_op jit(solution)/shard_map/jit(_take)/gather | solution.py:152
  251.4 0.8 slice_multiply_fusion
  252.3 0.7 multiply_subtract_fusion
  253.0 4.0 %shard_map.121.base_ref = bf16[160,16,1024]{2,1,0:T(8,128)(2,1)} custom-call(bf16[160,16,512]{2,1,0:T(8,128)(2,1)} %all-gather.5.cloned.1.call-done.x_ref), custom_call_target="tpu_custom_call" | custom-call | tf_op jit(solution)/shard_map/pallas_call | solution.py:68
  257.0 11.0 %select_bitcast_fusion = (f32[1,40,128,256]{3,2,1,0:T(8,128)}, f32[1,40,128,256]{3,2,1,0:T(8,128)}) fusion(f32[40,128,256]{2,1,0:T(8,128)} %bitcast.61, pred[40]{0:T(512)(128)(4,1)S(1)} %get-tuple-element.15, f32[40,128,256]{2,1,0:T(8,128)} %get-tuple-element.28, f32[40,128,128]{2,1,0:T(8,128)S(1)} %get-tuple-element.12, f32[40,128,128]{2,1,0:T(8,128)} %copy-done.2, ...), kind=kLoop, calls=%fused_computation.11 | loop fusion | flops 13107200 | bytes 31457360 | tf_op jit(solution)/shard_map/broadcast_in_dim | solution.py:165
  267.9 7.6 %all-gather.7.cloned.1.call-done.a_ref = bf16[160,16,512]{2,1,0:T(8,128)(2,1)} async-done(((bf16[160,16,128]{2,1,0:T(8,128)(2,1)}), bf16[160,16,512]{2,1,0:T(8,128)(2,1)}) %all-gather.7.cloned.1.call-update) | async-done | bytes 2621456 | tf_op jit(solution)/shard_map/all_gather | solution.py:153
  275.6 4.0 %shard_map.122 = bf16[160,16,1024]{2,1,0:T(8,128)(2,1)} custom-call(bf16[160,16,512]{2,1,0:T(8,128)(2,1)} %all-gather.7.cloned.1.call-done.a_ref, bf16[160,16,1024]{2,1,0:T(8,128)(2,1)} %shard_map.121.base_ref), custom_call_target="tpu_custom_call", output_to_operand_aliasing={{}: (1, {})} | custom-call | tf_op jit(solution)/shard_map/pallas_call | solution.py:71
  (44 shorter events, 0.5 us)
Async XLA Ops:
  7.2 126.5 %copy-start = (f32[64,1024]{1,0:T(8,128)S(1)}, f32[64,1024]{1,0:T(8,128)}, u32[]{:S(2)}) copy-start(f32[64,1024]{1,0:T(8,128)} %param.12) | copy-start | bytes 786436
  7.2 41.6 %reduce-scatter.5.cloned.1.call-start = ((), (), s32[]{:S(2)}) async-start(), calls=%async_computation.7 | async-start | bytes 3276800 | tf_op jit(solution)/shard_map/reduce_scatter | solution.py:111
  11.3 75.5 %reduce-scatter.3.cloned.1.call-start = ((), (), s32[]{:S(2)}) async-start(), calls=%async_computation.6 | async-start | bytes 3276800 | tf_op jit(solution)/shard_map/reduce_scatter | solution.py:111
  15.3 0.7 copy-start.12
  51.8 38.0 %all-to-all-start.1 = ((bf16[8,40,16,128]{3,2,1,0:T(8,128)(2,1)}), bf16[8,40,16,128]{3,2,1,0:T(8,128)(2,1)S(1)}, u32[]{:S(2)}, u32[]{:S(2)}) async-start(bf16[8,40,16,128]{3,2,1,0:T(8,128)(2,1)} %bitcast.9), calls=%async_computation.3 | async-start | bytes 2621440 | tf_op jit(solution)/shard_map/all_to_all | solution.py:113
  86.8 8.6 %copy-start.11 = (bf16[1,13,1024]{2,1,0:T(8,128)(2,1)S(1)}, bf16[1,13,1024]{2,1,0:T(8,128)(2,1)}, u32[]{:S(2)}) copy-start(bf16[1,13,1024]{2,1,0:T(8,128)(2,1)} %param.13) | copy-start | bytes 79876
  89.8 6.2 %copy-start.5 = (bf16[8,40,16,128]{3,2,1,0:T(8,128)(2,1)}, bf16[8,40,16,128]{3,2,1,0:T(8,128)(2,1)S(1)}, u32[]{:S(2)}) copy-start(bf16[8,40,16,128]{3,2,1,0:T(8,128)(2,1)S(1)} %all-to-all-done.1) | copy-start | bytes 3932164
  89.8 37.0 %all-to-all-start = ((bf16[8,40,16,128]{3,2,1,0:T(8,128)(2,1)}), bf16[8,40,16,128]{3,2,1,0:T(8,128)(2,1)}, u32[]{:S(2)}, u32[]{:S(2)}) async-start(bf16[8,40,16,128]{3,2,1,0:T(8,128)(2,1)} %bitcast.4), calls=%async_computation.1 | async-start | bytes 2621440 | tf_op jit(solution)/shard_map/all_to_all | solution.py:113
  128.4 1.7 copy-start.4
  133.7 3.0 %copy-start.2 = (f32[40,128,128]{2,1,0:T(8,128)}, f32[40,128,128]{2,1,0:T(8,128)S(1)}, u32[]{:S(2)}) copy-start(f32[40,128,128]{2,1,0:T(8,128)S(1)} %get-tuple-element.11) | copy-start | bytes 7864324
  135.2 1.5 copy-start.8
  137.6 2.5 collective-permute-start
  141.4 10.2 %copy-start.6 = (bf16[2688,128]{1,0:T(8,128)(2,1)}, bf16[2688,128]{1,0:T(8,128)(2,1)S(1)}, u32[]{:S(2)}) copy-start(bf16[2688,128]{1,0:T(8,128)(2,1)S(1)} %add_convert_fusion) | copy-start | bytes 2064388
  141.4 10.2 %collective-permute-start.1 = (bf16[1344,128]{1,0:T(8,128)(2,1)S(1)}, bf16[1344,128]{1,0:T(8,128)(2,1)S(1)}, u32[]{:S(2)}, u32[]{:S(2)}) collective-permute-start(bf16[1344,128]{1,0:T(8,128)(2,1)S(1)} %dynamic-slice_bitcast_fusion), channel_id=1, source_target_pairs={{0,16},{8,24},{16,0},{24,8},{1,17},{9,25},{17,1},{25,9},{2,18},{10... | collective-permute-start | bytes 1032200 | tf_op jit(solution)/shard_map/ppermute | solution.py:32
  152.5 2.5 collective-permute-start.2
  152.7 4.5 %copy-start.3 = (f32[40,128,128]{2,1,0:T(8,128)S(1)}, f32[40,128,128]{2,1,0:T(8,128)}, u32[]{:S(2)}) copy-start(f32[40,128,128]{2,1,0:T(8,128)} %copy-done.2) | copy-start | bytes 7864324
  156.3 0.9 copy-start.7
  168.3 36.2 %all-to-all-start.2 = ((bf16[40,128,128]{2,0,1:T(8,128)(2,1)}), bf16[40,128,128]{2,0,1:T(8,128)(2,1)}, u32[]{:S(2)}, u32[]{:S(2)}) async-start(bf16[40,128,128]{2,0,1:T(8,128)(2,1)} %copy.34), calls=%async_computation.4 | async-start | bytes 2621440 | tf_op jit(solution)/shard_map/all_to_all | solution.py:151
  172.5 80.4 %all-gather.5.cloned.1.call-start = ((), (), s32[]{:S(2)}) async-start(), calls=%async_computation.8 | async-start | bytes 3276800 | tf_op jit(solution)/shard_map/all_gather | solution.py:153
  210.0 65.6 %all-gather.7.cloned.1.call-start = ((), (), s32[]{:S(2)}) async-start(), calls=%async_computation.9 | async-start | bytes 3276800 | tf_op jit(solution)/shard_map/all_gather | solution.py:153
  247.2 5.1 %copy-start.9 = (f32[13,1024]{1,0:T(8,128)S(1)}, f32[13,1024]{1,0:T(8,128)}, u32[]{:S(2)}) copy-start(f32[13,1024]{1,0:T(8,128)} %param.14) | copy-start | bytes 159748
  247.2 5.1 %copy-start.10 = (f32[13,1024]{1,0:T(8,128)S(1)}, f32[13,1024]{1,0:T(8,128)}, u32[]{:S(2)}) copy-start(f32[13,1024]{1,0:T(8,128)} %param.15) | copy-start | bytes 159748
  275.6 4.0 %copy-start.1 = (f32[64,1024]{1,0:T(8,128)S(1)}, f32[64,1024]{1,0:T(8,128)}, u32[]{:S(2)}) copy-start(f32[64,1024]{1,0:T(8,128)} %param.12) | copy-start | bytes 786436
Sparse Core Ops, SparseCore 0:
  11.4 37.3 reduce-scatter.4
  52.0 34.6 reduce-scatter.2
  210.1 23.9 all-gather.4
  251.6 23.9 all-gather.6

commit v10 on v9

--- a/solution.py
+++ b/solution.py
@@ -146,9 +146,11 @@
     projected_all = jnp.einsum("skb,kq->sbq", coeffs, basis_part, precision=lax.Precision.HIGH)
     grad_all = jnp.where(emb_mask, projected_all, all_changes)
     rounded_all = (held - (outer_rate * (1.0 + outer_momentum)) * grad_all).astype(jnp.bfloat16)
+    slots, rows_all, _ = rounded_all.shape
+    outgoing_all = rounded_all.reshape(slots, dev_count, rows_all // dev_count, 2, width).transpose(3, 1, 0, 2, 4)
     for c in range(2):
-        rounded = rounded_all[:, :, halves[c]]
-        pieces = lax.all_to_all(rounded, "dev", split_axis=1, concat_axis=0, tiled=True)
+        pieces = lax.all_to_all(outgoing_all[c], "dev", split_axis=0, concat_axis=0, tiled=True)
+        pieces = pieces.reshape(dev_count * slots, rows_all // dev_count, width)
         picked = jnp.take(pieces, target, axis=0, mode="clip")
         gathered = lax.all_gather(picked, "rep", axis=2, tiled=True)
         if c == 0:

time: 287 us -> 288 us (level)
    reshape x0 -> x2, local copies, waits for them, and re-layouts: none -> 7.13 us  [body(): rounded_all.reshape(slots, dev_count, rows_all // dev_count, 2, width)]
    slice x3 -> x0, local copies, waits for them, and re-layouts: 5.61 us -> none  [body(): rounded = rounded_all[:, :, halves[c]]]
    all_to_all x2 -> x0, local copies, waits for them, and re-layouts: 3.85 us -> none  [body(): lax.all_to_all(rounded, 'dev', split_axis=1, concat_axis=0, tiled=True)]
  transfers between devices with their start and end apart: 10 -> 10, of which waited for: 8 -> 8; matrix products, arithmetic and copies ran while one was open for 10% -> 9% of each run, Pallas kernels for 3% -> 3%
where the time goes in v10:
time: 288 us; the launch traced here: 287 us
  waiting for transfers between devices  143 us (50%)
  blocking collectives  35.5 us (12%)
  local copies, waits for them, and re-layouts  26.9 us (9%)
  other arithmetic  24.1 us (8%)
  starting transfers between devices  16.1 us (6%)
  Pallas kernels  16.1 us (6%)
  between operations  14 us (5%)
  matrix products  11 us (4%)
    reduce_scatter x2, waiting for transfers between devices, body(): summed = lax.psum_scatter(half, 'rep', scatter_dimension=0, tiled=True)[0]  61.9 us
    all_to_all x1, blocking collectives, body(): lax.all_to_all(outgoing_all[c], 'dev', split_axis=0, concat_axis=0, tiled...  35.5 us
    all_to_all x1, waiting for transfers between devices, body(): lax.all_to_all(outgoing_all[c], 'dev', split_axis=0, concat_axis=0, tiled...  31.9 us
    all_to_all x2, waiting for transfers between devices, body(): lax.all_to_all(picked.reshape(dev_count, slot_count, summed.shape[1], sum...  27.4 us
    all_to_all x2, starting transfers between devices, body(): lax.all_to_all(picked.reshape(dev_count, slot_count, summed.shape[1], sum...  11 us
    broadcast_in_dim x1, other arithmetic, body(): new_momentum[None]  10.9 us
    ppermute x1, waiting for transfers between devices, rep_sum(): across = lax.ppermute(part, 'rep', [(i, i ^ 2) for i in range(4)])  9.56 us
    dot_general x1, matrix products, body(): jnp.einsum('skb,kq->sbq', coeffs, basis_part, precision=lax.Precision.HIGH)  8.06 us
  transfers between devices with their start and end apart: 10, of which 8 were waited for; matrix products, arithmetic and copies ran while one was open for 9% of the time, Pallas kernels for 3%

profile of v10, /device:TPU:0, one launch (start us, length us, event | category | flops | bytes accessed | tf_op | source)
XLA Modules:
  0.0 286.7 jit_solution(16743045964013162475)
XLA Ops:
  7.2 4.0 %shard_map.120 = bf16[4,160,16,128]{3,2,1,0:T(8,128)(2,1)} custom-call(bf16[160,16,1024]{2,1,0:T(8,128)(2,1)} %bitcast.60), custom_call_target="tpu_custom_call" | custom-call | tf_op jit(solution)/shard_map/pallas_call | solution.py:47
  11.3 4.0 %shard_map.119 = bf16[4,160,16,128]{3,2,1,0:T(8,128)(2,1)} custom-call(bf16[160,16,1024]{2,1,0:T(8,128)(2,1)} %bitcast.61), custom_call_target="tpu_custom_call" | custom-call | tf_op jit(solution)/shard_map/pallas_call | solution.py:47
  15.3 0.7 copy-done.12
  16.0 0.2 convert_reduce_fusion
  16.2 0.1 select_reduce_fusion
  16.3 32.4 %reduce-scatter.5.cloned.1.call-done = bf16[1,160,16,128]{3,2,1,0:T(8,128)(2,1)} async-done(((bf16[4,160,16,128]{3,2,1,0:T(8,128)(2,1)}), bf16[1,160,16,128]{3,2,1,0:T(8,128)(2,1)}) %reduce-scatter.5.cloned.1.call-update) | async-done | bytes 655376 | tf_op jit(solution)/shard_map/reduce_scatter | solution.py:111
  48.8 3.0 %gather_fusion.1 = bf16[320,16,128]{2,1,0:T(8,128)(2,1)} fusion(bf16[160,16,128]{2,1,0:T(8,128)(2,1)} %bitcast.73, s32[1024]{0:T(1024)S(1)} %pad_clamp_fusion.1), kind=kCustom, calls=%fused_computation.1 | custom fusion | bytes 2622720 | tf_op jit(solution)/shard_map/jit(_take)/gather | solution.py:112
  51.8 5.5 %all-to-all-start.1 = ((bf16[8,40,16,128]{3,2,1,0:T(8,128)(2,1)}), bf16[8,40,16,128]{3,2,1,0:T(8,128)(2,1)S(1)}, u32[]{:S(2)}, u32[]{:S(2)}) async-start(bf16[8,40,16,128]{3,2,1,0:T(8,128)(2,1)} %bitcast.9), calls=%async_computation.3 | async-start | bytes 2621440 | tf_op jit(solution)/shard_map/all_to_all | solution.py:113
  57.3 29.4 %reduce-scatter.3.cloned.1.call-done = bf16[1,160,16,128]{3,2,1,0:T(8,128)(2,1)} async-done(((bf16[4,160,16,128]{3,2,1,0:T(8,128)(2,1)}), bf16[1,160,16,128]{3,2,1,0:T(8,128)(2,1)}) %reduce-scatter.3.cloned.1.call-update) | async-done | bytes 655376 | tf_op jit(solution)/shard_map/reduce_scatter | solution.py:111
  86.8 3.0 %gather_fusion = bf16[320,16,128]{2,1,0:T(8,128)(2,1)} fusion(bf16[160,16,128]{2,1,0:T(8,128)(2,1)} %bitcast.74, s32[1024]{0:T(1024)S(1)} %pad_clamp_fusion.1), kind=kCustom, calls=%fused_computation | custom fusion | bytes 2622720 | tf_op jit(solution)/shard_map/jit(_take)/gather | solution.py:112
  89.8 5.5 %all-to-all-start = ((bf16[8,40,16,128]{3,2,1,0:T(8,128)(2,1)}), bf16[8,40,16,128]{3,2,1,0:T(8,128)(2,1)}, u32[]{:S(2)}, u32[]{:S(2)}) async-start(bf16[8,40,16,128]{3,2,1,0:T(8,128)(2,1)} %bitcast.4), calls=%async_computation.1 | async-start | bytes 2621440 | tf_op jit(solution)/shard_map/all_to_all | solution.py:113
  95.3 0.6 reshape.71
  96.0 1.6 multiply_bitcast_fusion
  97.5 1.9 copy.20
  99.4 27.4 %all-to-all-done = bf16[8,40,16,128]{3,2,1,0:T(8,128)(2,1)} async-done(((bf16[8,40,16,128]{3,2,1,0:T(8,128)(2,1)}), bf16[8,40,16,128]{3,2,1,0:T(8,128)(2,1)}, u32[]{:S(2)}, u32[]{:S(2)}) %all-to-all-start) | async-done | bytes 1310752 | tf_op jit(solution)/shard_map/all_to_all | solution.py:113
  126.8 1.6 multiply_bitcast_fusion.1
  128.4 0.3 copy.19
  128.7 1.4 copy-done.4
  130.1 3.6 %slice_subtract_fusion = (f32[40,128,128]{2,1,0:T(8,128)S(1)}, f32[40,128,128]{2,1,0:T(8,128)S(1)}) fusion(f32[40,128,128]{2,1,0:T(8,128)S(1)} %bitcast.64, f32[40,128,256]{2,1,0:T(8,128)} %bitcast.58, f32[40,128,128]{2,1,0:T(8,128)S(1)} %bitcast.65), kind=kLoop, calls=%fused_computation.13 | loop fusion | flops 1310720 | bytes 15728640 | tf_op jit(solution)/shard_map/sub | solution.py:120
  133.7 1.5 fusion.10
  135.2 1.5 fusion.4
  136.7 0.9 pad_maximum_fusion.1
  137.6 2.5 collective-permute-done
  140.1 1.3 add_convert_fusion
  141.4 0.6 collective-permute-start.1
  142.0 9.6 %collective-permute-done.1 = bf16[1344,128]{1,0:T(8,128)(2,1)S(1)} collective-permute-done((bf16[1344,128]{1,0:T(8,128)(2,1)S(1)}, bf16[1344,128]{1,0:T(8,128)(2,1)S(1)}, u32[]{:S(2)}, u32[]{:S(2)}) %collective-permute-start.1) | collective-permute-done | bytes 344096 | tf_op jit(solution)/shard_map/ppermute | solution.py:32
  151.6 0.9 convert_add_fusion
  152.5 0.2 compare_reduce_fusion
  152.7 2.3 collective-permute-done.2
  155.0 1.3 broadcast_select_fusion.1
  156.3 0.9 copy-done.7
  157.2 0.1 pad_maximum_fusion
  157.3 8.1 %fusion.3 = (bf16[40,128,256]{2,1,0:T(8,128)(2,1)}, f32[40,128,256]{2,1,0:T(8,128)}) fusion(f32[40,128,128]{2,1,0:T(8,128)S(1)} %get-tuple-element.12, f32[40,128,128]{2,1,0:T(8,128)S(1)} %copy-done.3, pred[40]{0:T(512)(128)(4,1)S(1)} %get-tuple-element.16, f32[1,40,128,256]{3,2,1,0:T(8,128)} %param.11, f32[1,40,128,256]{3,2,1,0:T(8,128)} %param.10, ...), kind=kOutput, calls=%fused_computation.9 | convolution fusion | flops 512491520 | bytes 24969732 | tf_op jit(solution)/shard_map/skb,kq->sbq/dot_general | solution.py:146
  165.4 4.9 %reshape.74 = bf16[40,8,16,2,128]{4,3,2,1,0:T(2,128)(2,1)} reshape(bf16[40,128,256]{2,1,0:T(8,128)(2,1)} %get-tuple-element.27) | data formatting | bytes 5242880 | tf_op jit(solution)/shard_map/reshape | solution.py:150
  170.3 2.2 copy.23
  172.5 1.9 slice_bitcast_fusion
  174.5 4.3 %all-to-all-start.2 = ((bf16[8,40,16,128]{3,2,1,0:T(8,128)(2,1)}), bf16[8,40,16,128]{3,2,1,0:T(8,128)(2,1)}, u32[]{:S(2)}, u32[]{:S(2)}) async-start(bf16[8,40,16,128]{3,2,1,0:T(8,128)(2,1)} %get-tuple-element.24), calls=%async_computation.4 | async-start | bytes 2621440 | tf_op jit(solution)/shard_map/all_to_all | solution.py:152
  178.8 0.0 all-gather.5.cloned.1.call-start
  178.8 31.9 %all-to-all-done.2 = bf16[8,40,16,128]{3,2,1,0:T(8,128)(2,1)} async-done(((bf16[8,40,16,128]{3,2,1,0:T(8,128)(2,1)}), bf16[8,40,16,128]{3,2,1,0:T(8,128)(2,1)}, u32[]{:S(2)}, u32[]{:S(2)}) %all-to-all-start.2) | async-done | bytes 1310752 | tf_op jit(solution)/shard_map/all_to_all | solution.py:152
  210.7 2.9 %gather_fusion.2 = bf16[160,16,128]{2,1,0:T(8,128)(2,1)} fusion(bf16[320,16,128]{2,1,0:T(8,128)(2,1)} %bitcast.24, s32[1024]{0:T(1024)S(1)} %pad_clamp_fusion), kind=kCustom, calls=%fused_computation.2 | custom fusion | bytes 1311360 | tf_op jit(solution)/shard_map/jit(_take)/gather | solution.py:154
  213.7 35.5 %all_to_all.28 = bf16[8,40,16,128]{3,2,1,0:T(8,128)(2,1)} all-to-all(bf16[8,40,16,128]{3,2,1,0:T(8,128)(2,1)} %get-tuple-element.23), channel_id=1, replica_groups=mesh['rep'=4,'dev'=8] {'dev'}, dimensions={0} | all-to-all | bytes 2621440 | tf_op jit(solution)/shard_map/all_to_all | solution.py:152
  249.1 3.0 %gather_fusion.3 = bf16[160,16,128]{2,1,0:T(8,128)(2,1)} fusion(bf16[320,16,128]{2,1,0:T(8,128)(2,1)} %bitcast.72, s32[1024]{0:T(1024)S(1)} %pad_clamp_fusion), kind=kCustom, calls=%fused_computation.3 | custom fusion | bytes 1311360 | tf_op jit(solution)/shard_map/jit(_take)/gather | solution.py:154
  252.1 0.8 slice_multiply_fusion
  253.0 0.7 multiply_subtract_fusion
  253.6 4.0 %shard_map.121.base_ref = bf16[160,16,1024]{2,1,0:T(8,128)(2,1)} custom-call(bf16[160,16,512]{2,1,0:T(8,128)(2,1)} %all-gather.5.cloned.1.call-done.x_ref), custom_call_target="tpu_custom_call" | custom-call | tf_op jit(solution)/shard_map/pallas_call | solution.py:68
  257.7 10.9 %select_bitcast_fusion = (f32[1,40,128,256]{3,2,1,0:T(8,128)}, f32[1,40,128,256]{3,2,1,0:T(8,128)}) fusion(f32[40,128,256]{2,1,0:T(8,128)} %bitcast.62, pred[40]{0:T(512)(128)(4,1)S(1)} %get-tuple-element.15, f32[40,128,256]{2,1,0:T(8,128)} %get-tuple-element.28, f32[40,128,128]{2,1,0:T(8,128)S(1)} %get-tuple-element.12, f32[40,128,128]{2,1,0:T(8,128)} %copy-done.2, ...), kind=kLoop, calls=%fused_computation.11 | loop fusion | flops 13107200 | bytes 31457360 | tf_op jit(solution)/shard_map/broadcast_in_dim | solution.py:167
  268.6 7.6 %all-gather.7.cloned.1.call-done.a_ref = bf16[160,16,512]{2,1,0:T(8,128)(2,1)} async-done(((bf16[160,16,128]{2,1,0:T(8,128)(2,1)}), bf16[160,16,512]{2,1,0:T(8,128)(2,1)}) %all-gather.7.cloned.1.call-update) | async-done | bytes 2621456 | tf_op jit(solution)/shard_map/all_gather | solution.py:155
  276.2 4.0 %shard_map.122 = bf16[160,16,1024]{2,1,0:T(8,128)(2,1)} custom-call(bf16[160,16,512]{2,1,0:T(8,128)(2,1)} %all-gather.7.cloned.1.call-done.a_ref, bf16[160,16,1024]{2,1,0:T(8,128)(2,1)} %shard_map.121.base_ref), custom_call_target="tpu_custom_call", output_to_operand_aliasing={{}: (1, {})} | custom-call | tf_op jit(solution)/shard_map/pallas_call | solution.py:71
  (42 shorter events, 0.3 us)
Async XLA Ops:
  7.2 126.5 %copy-start = (f32[64,1024]{1,0:T(8,128)S(1)}, f32[64,1024]{1,0:T(8,128)}, u32[]{:S(2)}) copy-start(f32[64,1024]{1,0:T(8,128)} %param.12) | copy-start | bytes 786436
  7.2 41.6 %reduce-scatter.5.cloned.1.call-start = ((), (), s32[]{:S(2)}) async-start(), calls=%async_computation.7 | async-start | bytes 3276800 | tf_op jit(solution)/shard_map/reduce_scatter | solution.py:111
  11.3 75.5 %reduce-scatter.3.cloned.1.call-start = ((), (), s32[]{:S(2)}) async-start(), calls=%async_computation.6 | async-start | bytes 3276800 | tf_op jit(solution)/shard_map/reduce_scatter | solution.py:111
  15.3 0.7 copy-start.12
  51.8 38.0 %all-to-all-start.1 = ((bf16[8,40,16,128]{3,2,1,0:T(8,128)(2,1)}), bf16[8,40,16,128]{3,2,1,0:T(8,128)(2,1)S(1)}, u32[]{:S(2)}, u32[]{:S(2)}) async-start(bf16[8,40,16,128]{3,2,1,0:T(8,128)(2,1)} %bitcast.9), calls=%async_computation.3 | async-start | bytes 2621440 | tf_op jit(solution)/shard_map/all_to_all | solution.py:113
  86.8 8.6 %copy-start.11 = (bf16[1,13,1024]{2,1,0:T(8,128)(2,1)S(1)}, bf16[1,13,1024]{2,1,0:T(8,128)(2,1)}, u32[]{:S(2)}) copy-start(bf16[1,13,1024]{2,1,0:T(8,128)(2,1)} %param.13) | copy-start | bytes 79876
  89.8 6.2 %copy-start.5 = (bf16[8,40,16,128]{3,2,1,0:T(8,128)(2,1)}, bf16[8,40,16,128]{3,2,1,0:T(8,128)(2,1)S(1)}, u32[]{:S(2)}) copy-start(bf16[8,40,16,128]{3,2,1,0:T(8,128)(2,1)S(1)} %all-to-all-done.1) | copy-start | bytes 3932164
  89.8 37.0 %all-to-all-start = ((bf16[8,40,16,128]{3,2,1,0:T(8,128)(2,1)}), bf16[8,40,16,128]{3,2,1,0:T(8,128)(2,1)}, u32[]{:S(2)}, u32[]{:S(2)}) async-start(bf16[8,40,16,128]{3,2,1,0:T(8,128)(2,1)} %bitcast.4), calls=%async_computation.1 | async-start | bytes 2621440 | tf_op jit(solution)/shard_map/all_to_all | solution.py:113
  128.4 1.7 copy-start.4
  133.7 3.0 %copy-start.2 = (f32[40,128,128]{2,1,0:T(8,128)}, f32[40,128,128]{2,1,0:T(8,128)S(1)}, u32[]{:S(2)}) copy-start(f32[40,128,128]{2,1,0:T(8,128)S(1)} %get-tuple-element.11) | copy-start | bytes 7864324
  135.2 1.5 copy-start.8
  137.6 2.5 collective-permute-start
  141.4 10.2 %copy-start.6 = (bf16[2688,128]{1,0:T(8,128)(2,1)}, bf16[2688,128]{1,0:T(8,128)(2,1)S(1)}, u32[]{:S(2)}) copy-start(bf16[2688,128]{1,0:T(8,128)(2,1)S(1)} %add_convert_fusion) | copy-start | bytes 2064388
  141.4 10.2 %collective-permute-start.1 = (bf16[1344,128]{1,0:T(8,128)(2,1)S(1)}, bf16[1344,128]{1,0:T(8,128)(2,1)S(1)}, u32[]{:S(2)}, u32[]{:S(2)}) collective-permute-start(bf16[1344,128]{1,0:T(8,128)(2,1)S(1)} %dynamic-slice_bitcast_fusion), channel_id=1, source_target_pairs={{0,16},{8,24},{16,0},{24,8},{1,17},{9,25},{17,1},{25,9},{2,18},{10... | collective-permute-start | bytes 1032200 | tf_op jit(solution)/shard_map/ppermute | solution.py:32
  152.5 2.5 collective-permute-start.2
  152.7 4.6 %copy-start.3 = (f32[40,128,128]{2,1,0:T(8,128)S(1)}, f32[40,128,128]{2,1,0:T(8,128)}, u32[]{:S(2)}) copy-start(f32[40,128,128]{2,1,0:T(8,128)} %copy-done.2) | copy-start | bytes 7864324
  156.3 0.9 copy-start.7
  174.5 36.2 %all-to-all-start.2 = ((bf16[8,40,16,128]{3,2,1,0:T(8,128)(2,1)}), bf16[8,40,16,128]{3,2,1,0:T(8,128)(2,1)}, u32[]{:S(2)}, u32[]{:S(2)}) async-start(bf16[8,40,16,128]{3,2,1,0:T(8,128)(2,1)} %get-tuple-element.24), calls=%async_computation.4 | async-start | bytes 2621440 | tf_op jit(solution)/shard_map/all_to_all | solution.py:152
  178.8 74.9 %all-gather.5.cloned.1.call-start = ((), (), s32[]{:S(2)}) async-start(), calls=%async_computation.8 | async-start | bytes 3276800 | tf_op jit(solution)/shard_map/all_gather | solution.py:155
  213.6 39.3 %copy-start.9 = (f32[13,1024]{1,0:T(8,128)S(1)}, f32[13,1024]{1,0:T(8,128)}, u32[]{:S(2)}) copy-start(f32[13,1024]{1,0:T(8,128)} %param.14) | copy-start | bytes 159748
  213.6 39.4 %copy-start.10 = (f32[13,1024]{1,0:T(8,128)S(1)}, f32[13,1024]{1,0:T(8,128)}, u32[]{:S(2)}) copy-start(f32[13,1024]{1,0:T(8,128)} %param.15) | copy-start | bytes 159748
  213.6 62.5 %all-gather.7.cloned.1.call-start = ((), (), s32[]{:S(2)}) async-start(), calls=%async_computation.9 | async-start | bytes 3276800 | tf_op jit(solution)/shard_map/all_gather | solution.py:155
  276.2 4.0 %copy-start.1 = (f32[64,1024]{1,0:T(8,128)S(1)}, f32[64,1024]{1,0:T(8,128)}, u32[]{:S(2)}) copy-start(f32[64,1024]{1,0:T(8,128)} %param.12) | copy-start | bytes 786436
Sparse Core Ops, SparseCore 0:
  11.4 37.3 reduce-scatter.4
  52.0 34.6 reduce-scatter.2
  213.8 23.9 all-gather.4
  252.2 23.8 all-gather.6

commit v11 on v9

--- a/solution.py
+++ b/solution.py
@@ -152,10 +152,11 @@
         picked = jnp.take(pieces, target, axis=0, mode="clip")
         gathered = lax.all_gather(picked, "rep", axis=2, tiled=True)
         if c == 0:
-            late_inputs = lax.optimization_barrier((start_rows, momentum_rows, changes[0], changes[1], gathered))
-            gathered = late_inputs[4]
+            late_inputs = lax.optimization_barrier((start_rows, momentum_rows, changes[0], changes[1], coeffs, gathered))
+            gathered = late_inputs[5]
         returned = place_half(gathered, width, c, returned)
-    late_start, late_momentum, late_change0, late_change1, _ = late_inputs
+    late_start, late_momentum, late_change0, late_change1, late_coeffs, _ = late_inputs
+    coeffs = late_coeffs
     fresh_start, fresh_momentum = fresh(late_start, late_momentum, jnp.concatenate([late_change0, late_change1], axis=2), basis_part)
     new_momentum = jnp.where(owned_mask, fresh_momentum, late_momentum)
     new_start = jnp.where(owned_mask, fresh_start, late_start)

time: 287 us -> 286 us (level)
  matrix products: 10.5 us -> 23.4 us
  other arithmetic: 24.1 us -> 13.2 us
  waiting for transfers between devices: 143 us -> 140 us
    dot_general x0 -> x1, matrix products: none -> 14.3 us  [fresh(): jnp.einsum('skb,kq->sbq', coeffs, basis_cols, precision=lax.Precision.HIGH)]
    broadcast_in_dim x1 -> x0, other arithmetic: 11 us -> none  [body(): new_momentum[None]]
    all_gather x2, waiting for transfers between devices: 7.65 us -> 4.29 us  [body(): gathered = lax.all_gather(picked, 'rep', axis=2, tiled=True)]
  transfers between devices with their start and end apart: 10 -> 10, of which waited for: 8 -> 8; matrix products, arithmetic and copies ran while one was open for 10% -> 12% of each run, Pallas kernels for 3% -> 3%
where the time goes in v11:
time: 286 us; the launch traced here: 285 us
  waiting for transfers between devices  140 us (49%)
  blocking collectives  35 us (12%)
  local copies, waits for them, and re-layouts  27.1 us (9%)
  matrix products  23.4 us (8%)
  starting transfers between devices  16.1 us (6%)
  Pallas kernels  16 us (6%)
  between operations  14 us (5%)
  other arithmetic  13.2 us (5%)
    reduce_scatter x2, waiting for transfers between devices, body(): summed = lax.psum_scatter(half, 'rep', scatter_dimension=0, tiled=True)[0]  61.9 us
    all_to_all x1, blocking collectives, body(): lax.all_to_all(rounded, 'dev', split_axis=1, concat_axis=0, tiled=True)  35 us
    all_to_all x1, waiting for transfers between devices, body(): lax.all_to_all(rounded, 'dev', split_axis=1, concat_axis=0, tiled=True)  31.9 us
    all_to_all x2, waiting for transfers between devices, body(): lax.all_to_all(picked.reshape(dev_count, slot_count, summed.shape[1], sum...  27.4 us
    dot_general x1, matrix products, fresh(): jnp.einsum('skb,kq->sbq', coeffs, basis_cols, precision=lax.Precision.HIGH)  14.3 us
    all_to_all x2, starting transfers between devices, body(): lax.all_to_all(picked.reshape(dev_count, slot_count, summed.shape[1], sum...  11 us
    ppermute x1, waiting for transfers between devices, rep_sum(): across = lax.ppermute(part, 'rep', [(i, i ^ 2) for i in range(4)])  9.56 us
    pallas_call x2, Pallas kernels, take_half(): pl.pallas_call(_copy_kernel, grid=(quarters,), in_specs=[pl.BlockSpec((un...  8.02 us
  transfers between devices with their start and end apart: 10, of which 8 were waited for; matrix products, arithmetic and copies ran while one was open for 12% of the time, Pallas kernels for 3%

profile of v11, /device:TPU:0, one launch (start us, length us, event | category | flops | bytes accessed | tf_op | source)
XLA Modules:
  0.0 284.6 jit_solution(15032606040046565343)
XLA Ops:
  7.2 4.0 %shard_map.120 = bf16[4,160,16,128]{3,2,1,0:T(8,128)(2,1)} custom-call(bf16[160,16,1024]{2,1,0:T(8,128)(2,1)} %bitcast.62), custom_call_target="tpu_custom_call" | custom-call | tf_op jit(solution)/shard_map/pallas_call | solution.py:47
  11.3 4.0 %shard_map.119 = bf16[4,160,16,128]{3,2,1,0:T(8,128)(2,1)} custom-call(bf16[160,16,1024]{2,1,0:T(8,128)(2,1)} %bitcast.63), custom_call_target="tpu_custom_call" | custom-call | tf_op jit(solution)/shard_map/pallas_call | solution.py:47
  15.3 0.7 copy-done.12
  16.0 0.2 convert_reduce_fusion
  16.2 0.1 select_reduce_fusion
  16.3 32.4 %reduce-scatter.5.cloned.1.call-done = bf16[1,160,16,128]{3,2,1,0:T(8,128)(2,1)} async-done(((bf16[4,160,16,128]{3,2,1,0:T(8,128)(2,1)}), bf16[1,160,16,128]{3,2,1,0:T(8,128)(2,1)}) %reduce-scatter.5.cloned.1.call-update) | async-done | bytes 655376 | tf_op jit(solution)/shard_map/reduce_scatter | solution.py:111
  48.8 3.0 %gather_fusion.1 = bf16[320,16,128]{2,1,0:T(8,128)(2,1)} fusion(bf16[160,16,128]{2,1,0:T(8,128)(2,1)} %bitcast.77, s32[1024]{0:T(1024)S(1)} %pad_clamp_fusion.1), kind=kCustom, calls=%fused_computation.1 | custom fusion | bytes 2622720 | tf_op jit(solution)/shard_map/jit(_take)/gather | solution.py:112
  51.8 5.5 %all-to-all-start.1 = ((bf16[8,40,16,128]{3,2,1,0:T(8,128)(2,1)}), bf16[8,40,16,128]{3,2,1,0:T(8,128)(2,1)S(1)}, u32[]{:S(2)}, u32[]{:S(2)}) async-start(bf16[8,40,16,128]{3,2,1,0:T(8,128)(2,1)} %bitcast.9), calls=%async_computation.3 | async-start | bytes 2621440 | tf_op jit(solution)/shard_map/all_to_all | solution.py:113
  57.3 29.4 %reduce-scatter.3.cloned.1.call-done = bf16[1,160,16,128]{3,2,1,0:T(8,128)(2,1)} async-done(((bf16[4,160,16,128]{3,2,1,0:T(8,128)(2,1)}), bf16[1,160,16,128]{3,2,1,0:T(8,128)(2,1)}) %reduce-scatter.3.cloned.1.call-update) | async-done | bytes 655376 | tf_op jit(solution)/shard_map/reduce_scatter | solution.py:111
  86.8 3.0 %gather_fusion = bf16[320,16,128]{2,1,0:T(8,128)(2,1)} fusion(bf16[160,16,128]{2,1,0:T(8,128)(2,1)} %bitcast.78, s32[1024]{0:T(1024)S(1)} %pad_clamp_fusion.1), kind=kCustom, calls=%fused_computation | custom fusion | bytes 2622720 | tf_op jit(solution)/shard_map/jit(_take)/gather | solution.py:112
  89.8 5.5 %all-to-all-start = ((bf16[8,40,16,128]{3,2,1,0:T(8,128)(2,1)}), bf16[8,40,16,128]{3,2,1,0:T(8,128)(2,1)}, u32[]{:S(2)}, u32[]{:S(2)}) async-start(bf16[8,40,16,128]{3,2,1,0:T(8,128)(2,1)} %bitcast.4), calls=%async_computation.1 | async-start | bytes 2621440 | tf_op jit(solution)/shard_map/all_to_all | solution.py:113
  95.3 0.6 reshape.62
  96.0 1.6 multiply_bitcast_fusion
  97.5 1.9 copy.33
  99.4 27.4 %all-to-all-done = bf16[8,40,16,128]{3,2,1,0:T(8,128)(2,1)} async-done(((bf16[8,40,16,128]{3,2,1,0:T(8,128)(2,1)}), bf16[8,40,16,128]{3,2,1,0:T(8,128)(2,1)}, u32[]{:S(2)}, u32[]{:S(2)}) %all-to-all-start) | async-done | bytes 1310752 | tf_op jit(solution)/shard_map/all_to_all | solution.py:113
  126.8 1.6 multiply_bitcast_fusion.1
  128.4 0.3 copy.32
  128.7 1.4 copy-done.4
  130.1 3.6 %slice_subtract_fusion = (f32[40,128,128]{2,1,0:T(8,128)S(1)}, f32[40,128,128]{2,1,0:T(8,128)S(1)}) fusion(f32[40,128,128]{2,1,0:T(8,128)S(1)} %bitcast.67, f32[40,128,256]{2,1,0:T(8,128)} %bitcast.60, f32[40,128,128]{2,1,0:T(8,128)S(1)} %bitcast.68), kind=kLoop, calls=%fused_computation.13 | loop fusion | flops 1310720 | bytes 15728640 | tf_op jit(solution)/shard_map/sub | solution.py:120
  133.7 1.5 fusion.11
  135.2 1.5 fusion.4
  136.7 0.9 pad_maximum_fusion.1
  137.6 2.5 collective-permute-done
  140.1 1.3 add_convert_fusion
  141.4 0.6 collective-permute-start.1
  142.0 9.6 %collective-permute-done.1 = bf16[1344,128]{1,0:T(8,128)(2,1)S(1)} collective-permute-done((bf16[1344,128]{1,0:T(8,128)(2,1)S(1)}, bf16[1344,128]{1,0:T(8,128)(2,1)S(1)}, u32[]{:S(2)}, u32[]{:S(2)}) %collective-permute-start.1) | collective-permute-done | bytes 344096 | tf_op jit(solution)/shard_map/ppermute | solution.py:32
  151.6 0.9 convert_add_fusion
  152.5 0.2 compare_reduce_fusion
  152.7 2.3 collective-permute-done.2
  155.0 1.3 broadcast_select_fusion.1
  156.4 0.7 copy-done.7
  157.2 6.1 %fusion.3 = bf16[40,128,256]{2,1,0:T(8,128)(2,1)S(1)} fusion(f32[40,128,128]{2,1,0:T(8,128)S(1)} %get-tuple-element.14, f32[40,128,128]{2,1,0:T(8,128)S(1)} %copy-done.2, pred[40]{0:T(512)(128)(4,1)S(1)} %get-tuple-element.18, f32[40,64,128]{2,1,0:T(8,128)S(1)} %bitcast.65, f32[64,1024]{1,0:T(8,128)S(1)} %copy-done, s32[]{:T(128)S(6)} %select_n.46, ...), kind=kOutput, calls=%fused_computation.9 | convolution fusion | flops 512491520 | bytes 19726852 | tf_op jit(solution)/shard_map/skb,kq->sbq/dot_general | solution.py:146
  163.3 1.5 fusion.16
  164.9 1.9 copy.34
  166.8 4.3 %all-to-all-start.2 = ((bf16[40,128,128]{2,0,1:T(8,128)(2,1)}), bf16[40,128,128]{2,0,1:T(8,128)(2,1)}, u32[]{:S(2)}, u32[]{:S(2)}) async-start(bf16[40,128,128]{2,0,1:T(8,128)(2,1)} %copy.34), calls=%async_computation.4 | async-start | bytes 2621440 | tf_op jit(solution)/shard_map/all_to_all | solution.py:151
  171.1 31.9 %all-to-all-done.2 = bf16[40,128,128]{2,0,1:T(8,128)(2,1)} async-done(((bf16[40,128,128]{2,0,1:T(8,128)(2,1)}), bf16[40,128,128]{2,0,1:T(8,128)(2,1)}, u32[]{:S(2)}, u32[]{:S(2)}) %all-to-all-start.2) | async-done | bytes 1310752 | tf_op jit(solution)/shard_map/all_to_all | solution.py:151
  203.0 2.6 copy.36
  205.6 2.9 %gather_fusion.2 = bf16[160,16,128]{2,1,0:T(8,128)(2,1)} fusion(bf16[320,16,128]{2,1,0:T(8,128)(2,1)} %bitcast.76, s32[1024]{0:T(1024)S(1)} %pad_clamp_fusion), kind=kCustom, calls=%fused_computation.2 | custom fusion | bytes 1311360 | tf_op jit(solution)/shard_map/jit(_take)/gather | solution.py:152
  208.6 2.2 copy.37
  210.8 35.0 %all_to_all.54 = bf16[40,128,128]{2,0,1:T(8,128)(2,1)S(1)} all-to-all(bf16[40,128,128]{2,0,1:T(8,128)(2,1)S(1)} %copy.37), channel_id=1, replica_groups=mesh['rep'=4,'dev'=8] {'dev'}, dimensions={1} | all-to-all | bytes 2621440 | tf_op jit(solution)/shard_map/all_to_all | solution.py:151
  245.7 1.3 copy.39
  247.0 2.9 %gather_fusion.3 = bf16[160,16,128]{2,1,0:T(8,128)(2,1)} fusion(bf16[320,16,128]{2,1,0:T(8,128)(2,1)} %bitcast.75, s32[1024]{0:T(1024)S(1)} %pad_clamp_fusion), kind=kCustom, calls=%fused_computation.3 | custom fusion | bytes 1311360 | tf_op jit(solution)/shard_map/jit(_take)/gather | solution.py:152
  249.9 0.8 slice_multiply_fusion
  250.8 0.7 multiply_subtract_fusion
  251.4 4.0 %shard_map.121.base_ref = bf16[160,16,1024]{2,1,0:T(8,128)(2,1)} custom-call(bf16[160,16,512]{2,1,0:T(8,128)(2,1)} %all-gather.5.cloned.1.call-done.x_ref), custom_call_target="tpu_custom_call" | custom-call | tf_op jit(solution)/shard_map/pallas_call | solution.py:68
  255.5 14.3 %select_bitcast_fusion = (f32[1,40,128,256]{3,2,1,0:T(8,128)}, f32[1,40,128,256]{3,2,1,0:T(8,128)}) fusion(f32[40,128,256]{2,1,0:T(8,128)} %bitcast.64, pred[40]{0:T(512)(128)(4,1)S(1)} %get-tuple-element.17, f32[40,128,256]{2,1,0:T(8,128)} %bitcast.61, f32[40,128,128]{2,1,0:T(8,128)S(1)} %get-tuple-element.14, f32[40,128,128]{2,1,0:T(8,128)} %copy-done.1, ...), kind=kOutput, calls=%fused_computation.11 | convolution fusion | flops 516423680 | bytes 27591684 | tf_op jit(solution)/shard_map/skb,kq->sbq/dot_general | solution.py:138
  269.8 4.3 %all-gather.7.cloned.1.call-done.a_ref = bf16[160,16,512]{2,1,0:T(8,128)(2,1)} async-done(((bf16[160,16,128]{2,1,0:T(8,128)(2,1)}), bf16[160,16,512]{2,1,0:T(8,128)(2,1)}) %all-gather.7.cloned.1.call-update) | async-done | bytes 2621456 | tf_op jit(solution)/shard_map/all_gather | solution.py:153
  274.1 4.0 %shard_map.122 = bf16[160,16,1024]{2,1,0:T(8,128)(2,1)} custom-call(bf16[160,16,512]{2,1,0:T(8,128)(2,1)} %all-gather.7.cloned.1.call-done.a_ref, bf16[160,16,1024]{2,1,0:T(8,128)(2,1)} %shard_map.121.base_ref), custom_call_target="tpu_custom_call", output_to_operand_aliasing={{}: (1, {})} | custom-call | tf_op jit(solution)/shard_map/pallas_call | solution.py:71
  (44 shorter events, 0.5 us)
Async XLA Ops:
  7.2 126.5 %copy-start = (f32[64,1024]{1,0:T(8,128)S(1)}, f32[64,1024]{1,0:T(8,128)}, u32[]{:S(2)}) copy-start(f32[64,1024]{1,0:T(8,128)} %param.12) | copy-start | bytes 786436
  7.2 41.6 %reduce-scatter.5.cloned.1.call-start = ((), (), s32[]{:S(2)}) async-start(), calls=%async_computation.7 | async-start | bytes 3276800 | tf_op jit(solution)/shard_map/reduce_scatter | solution.py:111
  11.3 75.5 %reduce-scatter.3.cloned.1.call-start = ((), (), s32[]{:S(2)}) async-start(), calls=%async_computation.6 | async-start | bytes 3276800 | tf_op jit(solution)/shard_map/reduce_scatter | solution.py:111
  15.3 0.7 copy-start.12
  51.8 38.0 %all-to-all-start.1 = ((bf16[8,40,16,128]{3,2,1,0:T(8,128)(2,1)}), bf16[8,40,16,128]{3,2,1,0:T(8,128)(2,1)S(1)}, u32[]{:S(2)}, u32[]{:S(2)}) async-start(bf16[8,40,16,128]{3,2,1,0:T(8,128)(2,1)} %bitcast.9), calls=%async_computation.3 | async-start | bytes 2621440 | tf_op jit(solution)/shard_map/all_to_all | solution.py:113
  86.7 8.6 %copy-start.11 = (bf16[1,13,1024]{2,1,0:T(8,128)(2,1)S(1)}, bf16[1,13,1024]{2,1,0:T(8,128)(2,1)}, u32[]{:S(2)}) copy-start(bf16[1,13,1024]{2,1,0:T(8,128)(2,1)} %param.13) | copy-start | bytes 79876
  89.8 6.2 %copy-start.5 = (bf16[8,40,16,128]{3,2,1,0:T(8,128)(2,1)}, bf16[8,40,16,128]{3,2,1,0:T(8,128)(2,1)S(1)}, u32[]{:S(2)}) copy-start(bf16[8,40,16,128]{3,2,1,0:T(8,128)(2,1)S(1)} %all-to-all-done.1) | copy-start | bytes 3932164
  89.8 37.0 %all-to-all-start = ((bf16[8,40,16,128]{3,2,1,0:T(8,128)(2,1)}), bf16[8,40,16,128]{3,2,1,0:T(8,128)(2,1)}, u32[]{:S(2)}, u32[]{:S(2)}) async-start(bf16[8,40,16,128]{3,2,1,0:T(8,128)(2,1)} %bitcast.4), calls=%async_computation.1 | async-start | bytes 2621440 | tf_op jit(solution)/shard_map/all_to_all | solution.py:113
  128.4 1.7 copy-start.4
  133.7 3.0 %copy-start.1 = (f32[40,128,128]{2,1,0:T(8,128)}, f32[40,128,128]{2,1,0:T(8,128)S(1)}, u32[]{:S(2)}) copy-start(f32[40,128,128]{2,1,0:T(8,128)S(1)} %get-tuple-element.13) | copy-start | bytes 7864324
  135.2 1.5 copy-start.8
  137.6 2.5 collective-permute-start
  141.4 10.2 %copy-start.6 = (bf16[2688,128]{1,0:T(8,128)(2,1)}, bf16[2688,128]{1,0:T(8,128)(2,1)S(1)}, u32[]{:S(2)}) copy-start(bf16[2688,128]{1,0:T(8,128)(2,1)S(1)} %add_convert_fusion) | copy-start | bytes 2064388
  141.4 10.2 %collective-permute-start.1 = (bf16[1344,128]{1,0:T(8,128)(2,1)S(1)}, bf16[1344,128]{1,0:T(8,128)(2,1)S(1)}, u32[]{:S(2)}, u32[]{:S(2)}) collective-permute-start(bf16[1344,128]{1,0:T(8,128)(2,1)S(1)} %dynamic-slice_bitcast_fusion), channel_id=1, source_target_pairs={{0,16},{8,24},{16,0},{24,8},{1,17},{9,25},{17,1},{25,9},{2,18},{10... | collective-permute-start | bytes 1032200 | tf_op jit(solution)/shard_map/ppermute | solution.py:32
  152.5 2.5 collective-permute-start.2
  152.7 4.4 %copy-start.2 = (f32[40,128,128]{2,1,0:T(8,128)S(1)}, f32[40,128,128]{2,1,0:T(8,128)}, u32[]{:S(2)}) copy-start(f32[40,128,128]{2,1,0:T(8,128)} %copy-done.1) | copy-start | bytes 7864324
  156.3 0.8 copy-start.7
  156.4 6.9 %copy-start.3 = (f32[2560,128]{1,0:T(8,128)}, f32[2560,128]{1,0:T(8,128)S(1)}, u32[]{:S(2)}) copy-start(f32[2560,128]{1,0:T(8,128)S(1)} %pad_maximum_fusion) | copy-start | bytes 3932164
  166.8 36.3 %all-to-all-start.2 = ((bf16[40,128,128]{2,0,1:T(8,128)(2,1)}), bf16[40,128,128]{2,0,1:T(8,128)(2,1)}, u32[]{:S(2)}, u32[]{:S(2)}) async-start(bf16[40,128,128]{2,0,1:T(8,128)(2,1)} %copy.34), calls=%async_computation.4 | async-start | bytes 2621440 | tf_op jit(solution)/shard_map/all_to_all | solution.py:151
  171.1 80.4 %all-gather.5.cloned.1.call-start = ((), (), s32[]{:S(2)}) async-start(), calls=%async_computation.8 | async-start | bytes 3276800 | tf_op jit(solution)/shard_map/all_gather | solution.py:153
  208.6 65.5 %all-gather.7.cloned.1.call-start = ((), (), s32[]{:S(2)}) async-start(), calls=%async_computation.9 | async-start | bytes 3276800 | tf_op jit(solution)/shard_map/all_gather | solution.py:153
  245.7 5.0 %copy-start.9 = (f32[13,1024]{1,0:T(8,128)S(1)}, f32[13,1024]{1,0:T(8,128)}, u32[]{:S(2)}) copy-start(f32[13,1024]{1,0:T(8,128)} %param.14) | copy-start | bytes 159748
  245.7 5.0 %copy-start.10 = (f32[13,1024]{1,0:T(8,128)S(1)}, f32[13,1024]{1,0:T(8,128)}, u32[]{:S(2)}) copy-start(f32[13,1024]{1,0:T(8,128)} %param.15) | copy-start | bytes 159748
Sparse Core Ops, SparseCore 0:
  11.4 37.3 reduce-scatter.4
  52.0 34.6 reduce-scatter.2
  208.7 23.9 all-gather.4
  250.0 23.9 all-gather.6

commit v12 on v11

--- a/solution.py
+++ b/solution.py
@@ -148,8 +148,19 @@
     rounded_all = (held - (outer_rate * (1.0 + outer_momentum)) * grad_all).astype(jnp.bfloat16)
     for c in range(2):
         rounded = rounded_all[:, :, halves[c]]
-        pieces = lax.all_to_all(rounded, "dev", split_axis=1, concat_axis=0, tiled=True)
-        picked = jnp.take(pieces, target, axis=0, mode="clip")
+        if c == 1 and dev_count <= 8:
+            me = lax.axis_index("dev")
+            part_rows = rounded.shape[1] // dev_count
+            blocks = [lax.dynamic_slice_in_dim(rounded, me * part_rows, part_rows, 1)]
+            for k in range(1, dev_count):
+                out_rows = lax.dynamic_slice_in_dim(rounded, ((me + k) % dev_count) * part_rows, part_rows, 1)
+                blocks.append(lax.ppermute(out_rows, "dev", [(i, (i + k) % dev_count) for i in range(dev_count)]))
+            pieces = jnp.concatenate(blocks, axis=0)
+            shifted = ((me - owner) % dev_count) * slot_count + slot_of
+            picked = jnp.take(pieces, shifted, axis=0, mode="clip")
+        else:
+            pieces = lax.all_to_all(rounded, "dev", split_axis=1, concat_axis=0, tiled=True)
+            picked = jnp.take(pieces, target, axis=0, mode="clip")
         gathered = lax.all_gather(picked, "rep", axis=2, tiled=True)
         if c == 0:
             late_inputs = lax.optimization_barrier((start_rows, momentum_rows, changes[0], changes[1], coeffs, gathered))

time: 286 us -> 282 us (0.986)
  blocking collectives: 35 us -> 0 us
  waiting for transfers between devices: 140 us -> 157 us
  starting transfers between devices: 16.1 us -> 27 us
  local copies, waits for them, and re-layouts: 27.1 us -> 30.7 us
    all_to_all x1 -> x0, blocking collectives: 35 us -> none  [body(): lax.all_to_all(rounded, 'dev', split_axis=1, concat_axis=0, tiled=True)]
    ppermute x0 -> x7, starting transfers between devices: none -> 10.9 us  [body(): lax.ppermute(out_rows, 'dev', [(i, (i + k) % dev_count) for i in range(de...]
    ppermute x0 -> x7, waiting for transfers between devices: none -> 10 us  [body(): lax.ppermute(out_rows, 'dev', [(i, (i + k) % dev_count) for i in range(de...]
    all_gather x2, waiting for transfers between devices: 4.29 us -> 11.8 us  [body(): gathered = lax.all_gather(picked, 'rep', axis=2, tiled=True)]
    unnamed x26 -> x32, local copies, waits for them, and re-layouts: 2.82 us -> 6.88 us
    gather x0 -> x1, local copies, waits for them, and re-layouts: none -> 2.89 us  [body(): picked = jnp.take(pieces, shifted, axis=0, mode='clip')]
    gather x2 -> x1, local copies, waits for them, and re-layouts: 5.81 us -> 2.93 us  [body(): picked = jnp.take(pieces, target, axis=0, mode='clip')]
  transfers between devices with their start and end apart: 10 -> 17, of which waited for: 8 -> 10; matrix products, arithmetic and copies ran while one was open for 12% -> 13% of each run, Pallas kernels for 3% -> 3%
where the time goes in v12:
time: 282 us; the launch traced here: 281 us
  waiting for transfers between devices  157 us (56%)
  local copies, waits for them, and re-layouts  30.7 us (11%)
  starting transfers between devices  27 us (10%)
  matrix products  23 us (8%)
  Pallas kernels  16 us (6%)
  between operations  14.1 us (5%)
  other arithmetic  13.2 us (5%)
    reduce_scatter x2, waiting for transfers between devices, body(): summed = lax.psum_scatter(half, 'rep', scatter_dimension=0, tiled=True)[0]  61.9 us
    all_to_all x1, waiting for transfers between devices, body(): lax.all_to_all(rounded, 'dev', split_axis=1, concat_axis=0, tiled=True)  31.9 us
    all_to_all x2, waiting for transfers between devices, body(): lax.all_to_all(picked.reshape(dev_count, slot_count, summed.shape[1], sum...  27.4 us
    dot_general x1, matrix products, fresh(): jnp.einsum('skb,kq->sbq', coeffs, basis_cols, precision=lax.Precision.HIGH)  13.9 us
    all_gather x2, waiting for transfers between devices, body(): gathered = lax.all_gather(picked, 'rep', axis=2, tiled=True)  11.8 us
    all_to_all x2, starting transfers between devices, body(): lax.all_to_all(picked.reshape(dev_count, slot_count, summed.shape[1], sum...  11 us
    ppermute x7, starting transfers between devices, body(): lax.ppermute(out_rows, 'dev', [(i, (i + k) % dev_count) for i in range(de...  10.9 us
    ppermute x7, waiting for transfers between devices, body(): lax.ppermute(out_rows, 'dev', [(i, (i + k) % dev_count) for i in range(de...  10 us
  transfers between devices with their start and end apart: 17, of which 10 were waited for; matrix products, arithmetic and copies ran while one was open for 13% of the time, Pallas kernels for 3%

profile of v12, /device:TPU:0, one launch (start us, length us, event | category | flops | bytes accessed | tf_op | source)
XLA Modules:
  0.0 281.4 jit_solution(4366519752320170533)
XLA Ops:
  7.2 4.0 %shard_map.120 = bf16[4,160,16,128]{3,2,1,0:T(8,128)(2,1)} custom-call(bf16[160,16,1024]{2,1,0:T(8,128)(2,1)} %bitcast.58), custom_call_target="tpu_custom_call" | custom-call | tf_op jit(solution)/shard_map/pallas_call | solution.py:47
  11.3 4.0 %shard_map.119 = bf16[4,160,16,128]{3,2,1,0:T(8,128)(2,1)} custom-call(bf16[160,16,1024]{2,1,0:T(8,128)(2,1)} %bitcast.59), custom_call_target="tpu_custom_call" | custom-call | tf_op jit(solution)/shard_map/pallas_call | solution.py:47
  16.3 32.4 %reduce-scatter.5.cloned.1.call-done = bf16[1,160,16,128]{3,2,1,0:T(8,128)(2,1)} async-done(((bf16[4,160,16,128]{3,2,1,0:T(8,128)(2,1)}), bf16[1,160,16,128]{3,2,1,0:T(8,128)(2,1)}) %reduce-scatter.5.cloned.1.call-update) | async-done | bytes 655376 | tf_op jit(solution)/shard_map/reduce_scatter | solution.py:111
  48.8 3.0 %gather_fusion.1 = bf16[320,16,128]{2,1,0:T(8,128)(2,1)} fusion(bf16[160,16,128]{2,1,0:T(8,128)(2,1)} %bitcast.71, s32[1024]{0:T(1024)S(1)} %pad_clamp_fusion.2), kind=kCustom, calls=%fused_computation.1 | custom fusion | bytes 2622720 | tf_op jit(solution)/shard_map/jit(_take)/gather | solution.py:112
  51.8 5.5 %all-to-all-start.1 = ((bf16[8,40,16,128]{3,2,1,0:T(8,128)(2,1)}), bf16[8,40,16,128]{3,2,1,0:T(8,128)(2,1)S(1)}, u32[]{:S(2)}, u32[]{:S(2)}) async-start(bf16[8,40,16,128]{3,2,1,0:T(8,128)(2,1)} %bitcast.9), calls=%async_computation.3 | async-start | bytes 2621440 | tf_op jit(solution)/shard_map/all_to_all | solution.py:113
  57.3 29.4 %reduce-scatter.3.cloned.1.call-done = bf16[1,160,16,128]{3,2,1,0:T(8,128)(2,1)} async-done(((bf16[4,160,16,128]{3,2,1,0:T(8,128)(2,1)}), bf16[1,160,16,128]{3,2,1,0:T(8,128)(2,1)}) %reduce-scatter.3.cloned.1.call-update) | async-done | bytes 655376 | tf_op jit(solution)/shard_map/reduce_scatter | solution.py:111
  86.8 3.0 %gather_fusion = bf16[320,16,128]{2,1,0:T(8,128)(2,1)} fusion(bf16[160,16,128]{2,1,0:T(8,128)(2,1)} %bitcast.72, s32[1024]{0:T(1024)S(1)} %pad_clamp_fusion.2), kind=kCustom, calls=%fused_computation | custom fusion | bytes 2622720 | tf_op jit(solution)/shard_map/jit(_take)/gather | solution.py:112
  89.8 5.5 %all-to-all-start = ((bf16[8,40,16,128]{3,2,1,0:T(8,128)(2,1)}), bf16[8,40,16,128]{3,2,1,0:T(8,128)(2,1)}, u32[]{:S(2)}, u32[]{:S(2)}) async-start(bf16[8,40,16,128]{3,2,1,0:T(8,128)(2,1)} %bitcast.4), calls=%async_computation.1 | async-start | bytes 2621440 | tf_op jit(solution)/shard_map/all_to_all | solution.py:113
  96.0 1.6 multiply_bitcast_fusion
  97.5 1.9 copy.28
  99.4 27.4 %all-to-all-done = bf16[8,40,16,128]{3,2,1,0:T(8,128)(2,1)} async-done(((bf16[8,40,16,128]{3,2,1,0:T(8,128)(2,1)}), bf16[8,40,16,128]{3,2,1,0:T(8,128)(2,1)}, u32[]{:S(2)}, u32[]{:S(2)}) %all-to-all-start) | async-done | bytes 1310752 | tf_op jit(solution)/shard_map/all_to_all | solution.py:113
  126.8 1.6 multiply_bitcast_fusion.1
  128.7 1.4 copy-done.4
  130.1 3.6 %slice_subtract_fusion = (f32[40,128,128]{2,1,0:T(8,128)S(1)}, f32[40,128,128]{2,1,0:T(8,128)S(1)}) fusion(f32[40,128,128]{2,1,0:T(8,128)S(1)} %bitcast.63, f32[40,128,256]{2,1,0:T(8,128)} %bitcast.56, f32[40,128,128]{2,1,0:T(8,128)S(1)} %bitcast.64), kind=kLoop, calls=%fused_computation.13 | loop fusion | flops 1310720 | bytes 15728640 | tf_op jit(solution)/shard_map/sub | solution.py:120
  133.7 1.5 fusion.11
  135.2 1.5 fusion.4
  136.7 0.9 pad_maximum_fusion.1
  137.6 2.5 collective-permute-done
  140.1 1.3 add_convert_fusion
  142.0 9.6 %collective-permute-done.1 = bf16[1344,128]{1,0:T(8,128)(2,1)S(1)} collective-permute-done((bf16[1344,128]{1,0:T(8,128)(2,1)S(1)}, bf16[1344,128]{1,0:T(8,128)(2,1)S(1)}, u32[]{:S(2)}, u32[]{:S(2)}) %collective-permute-start.1) | collective-permute-done | bytes 344096 | tf_op jit(solution)/shard_map/ppermute | solution.py:32
  151.6 0.9 convert_add_fusion
  152.7 2.3 collective-permute-done.2
  155.0 1.3 broadcast_select_fusion.1
  156.4 0.7 copy-done.7
  157.2 6.1 %fusion.3 = bf16[40,128,256]{2,1,0:T(8,128)(2,1)S(1)} fusion(f32[40,128,128]{2,1,0:T(8,128)S(1)} %get-tuple-element.14, f32[40,128,128]{2,1,0:T(8,128)S(1)} %copy-done.2, pred[40]{0:T(512)(128)(4,1)S(1)} %get-tuple-element.18, f32[40,64,128]{2,1,0:T(8,128)S(1)} %bitcast.61, f32[64,1024]{1,0:T(8,128)S(1)} %copy-done, s32[]{:T(128)S(6)} %select_n.104, ...), kind=kOutput, calls=%fused_computation.9 | convolution fusion | flops 512491520 | bytes 19726852 | tf_op jit(solution)/shard_map/skb,kq->sbq/dot_general | solution.py:146
  163.3 1.5 fusion.19
  164.9 1.9 copy.29
  166.8 4.3 %all-to-all-start.2 = ((bf16[40,128,128]{2,0,1:T(8,128)(2,1)}), bf16[40,128,128]{2,0,1:T(8,128)(2,1)}, u32[]{:S(2)}, u32[]{:S(2)}) async-start(bf16[40,128,128]{2,0,1:T(8,128)(2,1)} %copy.29), calls=%async_computation.4 | async-start | bytes 2621440 | tf_op jit(solution)/shard_map/all_to_all | solution.py:162
  171.1 31.9 %all-to-all-done.2 = bf16[40,128,128]{2,0,1:T(8,128)(2,1)} async-done(((bf16[40,128,128]{2,0,1:T(8,128)(2,1)}), bf16[40,128,128]{2,0,1:T(8,128)(2,1)}, u32[]{:S(2)}, u32[]{:S(2)}) %all-to-all-start.2) | async-done | bytes 1310752 | tf_op jit(solution)/shard_map/all_to_all | solution.py:162
  203.0 2.6 copy.31
  205.6 2.9 %gather_fusion.2 = bf16[160,16,128]{2,1,0:T(8,128)(2,1)} fusion(bf16[320,16,128]{2,1,0:T(8,128)(2,1)} %bitcast.70, s32[1024]{0:T(1024)S(1)} %pad_clamp_fusion.1), kind=kCustom, calls=%fused_computation.2 | custom fusion | bytes 1311360 | tf_op jit(solution)/shard_map/jit(_take)/gather | solution.py:163
  208.7 2.3 constant_dynamic-slice_fusion
  211.0 1.5 collective-permute-start.3
  212.5 2.9 %collective-permute-start.5 = (bf16[40,16,128]{2,1,0:T(8,128)(2,1)S(1)}, bf16[40,16,128]{2,1,0:T(8,128)(2,1)S(1)}, u32[]{:S(2)}, u32[]{:S(2)}) collective-permute-start(bf16[40,16,128]{2,1,0:T(8,128)(2,1)S(1)} %get-tuple-element.33), channel_id=1, source_target_pairs={{0,3},{1,4},{2,5},{3,6},{4,7},{5,0},{6,1},{7,2},{8,11},{9,12},{10,... | collective-permute-start | bytes 491528 | tf_op jit(solution)/shard_map/ppermute | solution.py:157
  215.3 1.0 collective-permute-start.6
  216.4 1.9 collective-permute-start.7
  218.3 2.7 collective-permute-done.3
  221.1 0.9 collective-permute-start.8
  222.7 2.7 collective-permute-start.9
  226.0 7.3 %collective-permute-done.5 = bf16[40,16,128]{2,1,0:T(8,128)(2,1)S(1)} collective-permute-done((bf16[40,16,128]{2,1,0:T(8,128)(2,1)S(1)}, bf16[40,16,128]{2,1,0:T(8,128)(2,1)S(1)}, u32[]{:S(2)}, u32[]{:S(2)}) %collective-permute-start.5) | collective-permute-done | bytes 163872 | tf_op jit(solution)/shard_map/ppermute | solution.py:157
  234.0 0.7 constant_dynamic-update-slice_fusion.3
  234.7 0.7 constant_dynamic-update-slice_fusion.2
  236.7 2.9 %gather_fusion.3 = bf16[160,16,128]{2,1,0:T(8,128)(2,1)} fusion(bf16[320,16,128]{2,1,0:T(8,128)(2,1)} %constant_dynamic-update-slice_fusion, s32[1024]{0:T(1024)S(1)} %pad_clamp_fusion), kind=kCustom, calls=%fused_computation.3 | custom fusion | bytes 1311360 | tf_op jit(solution)/shard_map/jit(_take)/gather | solution.py:160
  239.6 0.8 slice_multiply_fusion
  241.2 4.0 %shard_map.121.base_ref = bf16[160,16,1024]{2,1,0:T(8,128)(2,1)} custom-call(bf16[160,16,512]{2,1,0:T(8,128)(2,1)} %all-gather.5.cloned.1.call-done.x_ref), custom_call_target="tpu_custom_call" | custom-call | tf_op jit(solution)/shard_map/pallas_call | solution.py:68
  245.1 13.9 %select_bitcast_fusion = (f32[1,40,128,256]{3,2,1,0:T(8,128)}, f32[1,40,128,256]{3,2,1,0:T(8,128)}) fusion(f32[40,128,256]{2,1,0:T(8,128)} %bitcast.60, pred[40]{0:T(512)(128)(4,1)S(1)} %get-tuple-element.17, f32[40,128,256]{2,1,0:T(8,128)} %bitcast.57, f32[40,128,128]{2,1,0:T(8,128)S(1)} %get-tuple-element.14, f32[40,128,128]{2,1,0:T(8,128)} %copy-done.1, ...), kind=kOutput, calls=%fused_computation.11 | convolution fusion | flops 516423680 | bytes 27591684 | tf_op jit(solution)/shard_map/skb,kq->sbq/dot_general | solution.py:138
  259.0 11.8 %all-gather.7.cloned.1.call-done.a_ref = bf16[160,16,512]{2,1,0:T(8,128)(2,1)} async-done(((bf16[160,16,128]{2,1,0:T(8,128)(2,1)}), bf16[160,16,512]{2,1,0:T(8,128)(2,1)}) %all-gather.7.cloned.1.call-update) | async-done | bytes 2621456 | tf_op jit(solution)/shard_map/all_gather | solution.py:164
  270.8 4.0 %shard_map.122 = bf16[160,16,1024]{2,1,0:T(8,128)(2,1)} custom-call(bf16[160,16,512]{2,1,0:T(8,128)(2,1)} %all-gather.7.cloned.1.call-done.a_ref, bf16[160,16,1024]{2,1,0:T(8,128)(2,1)} %shard_map.121.base_ref), custom_call_target="tpu_custom_call", output_to_operand_aliasing={{}: (1, {})} | custom-call | tf_op jit(solution)/shard_map/pallas_call | solution.py:71
  (64 shorter events, 7.3 us)
Async XLA Ops:
  7.2 126.5 %copy-start = (f32[64,1024]{1,0:T(8,128)S(1)}, f32[64,1024]{1,0:T(8,128)}, u32[]{:S(2)}) copy-start(f32[64,1024]{1,0:T(8,128)} %param.12) | copy-start | bytes 786436
  7.2 41.6 %reduce-scatter.5.cloned.1.call-start = ((), (), s32[]{:S(2)}) async-start(), calls=%async_computation.6 | async-start | bytes 3276800 | tf_op jit(solution)/shard_map/reduce_scatter | solution.py:111
  11.3 75.5 %reduce-scatter.3.cloned.1.call-start = ((), (), s32[]{:S(2)}) async-start(), calls=%async_computation.5 | async-start | bytes 3276800 | tf_op jit(solution)/shard_map/reduce_scatter | solution.py:111
  15.3 0.7 copy-start.12
  51.8 38.0 %all-to-all-start.1 = ((bf16[8,40,16,128]{3,2,1,0:T(8,128)(2,1)}), bf16[8,40,16,128]{3,2,1,0:T(8,128)(2,1)S(1)}, u32[]{:S(2)}, u32[]{:S(2)}) async-start(bf16[8,40,16,128]{3,2,1,0:T(8,128)(2,1)} %bitcast.9), calls=%async_computation.3 | async-start | bytes 2621440 | tf_op jit(solution)/shard_map/all_to_all | solution.py:113
  86.7 8.6 %copy-start.11 = (bf16[1,13,1024]{2,1,0:T(8,128)(2,1)S(1)}, bf16[1,13,1024]{2,1,0:T(8,128)(2,1)}, u32[]{:S(2)}) copy-start(bf16[1,13,1024]{2,1,0:T(8,128)(2,1)} %param.13) | copy-start | bytes 79876
  89.8 6.2 %copy-start.5 = (bf16[8,40,16,128]{3,2,1,0:T(8,128)(2,1)}, bf16[8,40,16,128]{3,2,1,0:T(8,128)(2,1)S(1)}, u32[]{:S(2)}) copy-start(bf16[8,40,16,128]{3,2,1,0:T(8,128)(2,1)S(1)} %all-to-all-done.1) | copy-start | bytes 3932164
  89.8 37.0 %all-to-all-start = ((bf16[8,40,16,128]{3,2,1,0:T(8,128)(2,1)}), bf16[8,40,16,128]{3,2,1,0:T(8,128)(2,1)}, u32[]{:S(2)}, u32[]{:S(2)}) async-start(bf16[8,40,16,128]{3,2,1,0:T(8,128)(2,1)} %bitcast.4), calls=%async_computation.1 | async-start | bytes 2621440 | tf_op jit(solution)/shard_map/all_to_all | solution.py:113
  128.4 1.7 copy-start.4
  133.7 3.0 %copy-start.1 = (f32[40,128,128]{2,1,0:T(8,128)}, f32[40,128,128]{2,1,0:T(8,128)S(1)}, u32[]{:S(2)}) copy-start(f32[40,128,128]{2,1,0:T(8,128)S(1)} %get-tuple-element.13) | copy-start | bytes 7864324
  135.2 1.5 copy-start.8
  137.6 2.5 collective-permute-start
  141.4 10.2 %copy-start.6 = (bf16[2688,128]{1,0:T(8,128)(2,1)}, bf16[2688,128]{1,0:T(8,128)(2,1)S(1)}, u32[]{:S(2)}) copy-start(bf16[2688,128]{1,0:T(8,128)(2,1)S(1)} %add_convert_fusion) | copy-start | bytes 2064388
  141.4 10.2 %collective-permute-start.1 = (bf16[1344,128]{1,0:T(8,128)(2,1)S(1)}, bf16[1344,128]{1,0:T(8,128)(2,1)S(1)}, u32[]{:S(2)}, u32[]{:S(2)}) collective-permute-start(bf16[1344,128]{1,0:T(8,128)(2,1)S(1)} %dynamic-slice_bitcast_fusion), channel_id=1, source_target_pairs={{0,16},{8,24},{16,0},{24,8},{1,17},{9,25},{17,1},{25,9},{2,18},{10... | collective-permute-start | bytes 1032200 | tf_op jit(solution)/shard_map/ppermute | solution.py:32
  152.5 2.5 collective-permute-start.2
  152.7 4.4 %copy-start.2 = (f32[40,128,128]{2,1,0:T(8,128)S(1)}, f32[40,128,128]{2,1,0:T(8,128)}, u32[]{:S(2)}) copy-start(f32[40,128,128]{2,1,0:T(8,128)} %copy-done.1) | copy-start | bytes 7864324
  156.3 0.8 copy-start.7
  156.4 6.9 %copy-start.3 = (f32[2560,128]{1,0:T(8,128)}, f32[2560,128]{1,0:T(8,128)S(1)}, u32[]{:S(2)}) copy-start(f32[2560,128]{1,0:T(8,128)S(1)} %pad_maximum_fusion) | copy-start | bytes 3932164
  166.8 36.2 %all-to-all-start.2 = ((bf16[40,128,128]{2,0,1:T(8,128)(2,1)}), bf16[40,128,128]{2,0,1:T(8,128)(2,1)}, u32[]{:S(2)}, u32[]{:S(2)}) async-start(bf16[40,128,128]{2,0,1:T(8,128)(2,1)} %copy.29), calls=%async_computation.4 | async-start | bytes 2621440 | tf_op jit(solution)/shard_map/all_to_all | solution.py:162
  171.0 70.1 %all-gather.5.cloned.1.call-start = ((), (), s32[]{:S(2)}) async-start(), calls=%async_computation.7 | async-start | bytes 3276800 | tf_op jit(solution)/shard_map/all_gather | solution.py:164
  208.5 62.3 %all-gather.7.cloned.1.call-start = ((), (), s32[]{:S(2)}) async-start(), calls=%async_computation.8 | async-start | bytes 3276800 | tf_op jit(solution)/shard_map/all_gather | solution.py:164
  211.0 29.5 %copy-start.9 = (f32[13,1024]{1,0:T(8,128)S(1)}, f32[13,1024]{1,0:T(8,128)}, u32[]{:S(2)}) copy-start(f32[13,1024]{1,0:T(8,128)} %param.14) | copy-start | bytes 159748
  211.0 29.5 %copy-start.10 = (f32[13,1024]{1,0:T(8,128)S(1)}, f32[13,1024]{1,0:T(8,128)}, u32[]{:S(2)}) copy-start(f32[13,1024]{1,0:T(8,128)} %param.15) | copy-start | bytes 159748
  211.0 10.0 %collective-permute-start.3 = (bf16[40,16,128]{2,1,0:T(8,128)(2,1)S(1)}, bf16[40,16,128]{2,1,0:T(8,128)(2,1)S(1)}, u32[]{:S(2)}, u32[]{:S(2)}) collective-permute-start(bf16[40,16,128]{2,1,0:T(8,128)(2,1)S(1)} %get-tuple-element.35), channel_id=1, source_target_pairs={{0,1},{1,2},{2,3},{3,4},{4,5},{5,6},{6,7},{7,0},{8,9},{9,10},{10,1... | collective-permute-start | bytes 491528 | tf_op jit(solution)/shard_map/ppermute | solution.py:157
  212.5 10.2 %collective-permute-start.4 = (bf16[40,16,128]{2,1,0:T(8,128)(2,1)S(1)}, bf16[40,16,128]{2,1,0:T(8,128)(2,1)S(1)}, u32[]{:S(2)}, u32[]{:S(2)}) collective-permute-start(bf16[40,16,128]{2,1,0:T(8,128)(2,1)S(1)} %get-tuple-element.34), channel_id=1, source_target_pairs={{0,2},{1,3},{2,4},{3,5},{4,6},{5,7},{6,0},{7,1},{8,10},{9,11},{10,... | collective-permute-start | bytes 491528 | tf_op jit(solution)/shard_map/ppermute | solution.py:157
  212.5 20.8 %collective-permute-start.5 = (bf16[40,16,128]{2,1,0:T(8,128)(2,1)S(1)}, bf16[40,16,128]{2,1,0:T(8,128)(2,1)S(1)}, u32[]{:S(2)}, u32[]{:S(2)}) collective-permute-start(bf16[40,16,128]{2,1,0:T(8,128)(2,1)S(1)} %get-tuple-element.33), channel_id=1, source_target_pairs={{0,3},{1,4},{2,5},{3,6},{4,7},{5,0},{6,1},{7,2},{8,11},{9,12},{10,... | collective-permute-start | bytes 491528 | tf_op jit(solution)/shard_map/ppermute | solution.py:157
  215.3 18.7 %collective-permute-start.6 = (bf16[40,16,128]{2,1,0:T(8,128)(2,1)S(1)}, bf16[40,16,128]{2,1,0:T(8,128)(2,1)S(1)}, u32[]{:S(2)}, u32[]{:S(2)}) collective-permute-start(bf16[40,16,128]{2,1,0:T(8,128)(2,1)S(1)} %get-tuple-element.32), channel_id=1, source_target_pairs={{0,4},{1,5},{2,6},{3,7},{4,0},{5,1},{6,2},{7,3},{8,12},{9,13},{10,... | collective-permute-start | bytes 491528 | tf_op jit(solution)/shard_map/ppermute | solution.py:157
  216.4 18.3 %collective-permute-start.7 = (bf16[40,16,128]{2,1,0:T(8,128)(2,1)S(1)}, bf16[40,16,128]{2,1,0:T(8,128)(2,1)S(1)}, u32[]{:S(2)}, u32[]{:S(2)}) collective-permute-start(bf16[40,16,128]{2,1,0:T(8,128)(2,1)S(1)} %get-tuple-element.31), channel_id=1, source_target_pairs={{0,5},{1,6},{2,7},{3,0},{4,1},{5,2},{6,3},{7,4},{8,13},{9,14},{10,... | collective-permute-start | bytes 491528 | tf_op jit(solution)/shard_map/ppermute | solution.py:157
  221.1 14.3 %collective-permute-start.8 = (bf16[40,16,128]{2,1,0:T(8,128)(2,1)S(1)}, bf16[40,16,128]{2,1,0:T(8,128)(2,1)S(1)}, u32[]{:S(2)}, u32[]{:S(2)}) collective-permute-start(bf16[40,16,128]{2,1,0:T(8,128)(2,1)S(1)} %get-tuple-element.30), channel_id=1, source_target_pairs={{0,6},{1,7},{2,0},{3,1},{4,2},{5,3},{6,4},{7,5},{8,14},{9,15},{10,... | collective-permute-start | bytes 491528 | tf_op jit(solution)/shard_map/ppermute | solution.py:157
  222.7 13.4 %collective-permute-start.9 = (bf16[40,16,128]{2,1,0:T(8,128)(2,1)S(1)}, bf16[40,16,128]{2,1,0:T(8,128)(2,1)S(1)}, u32[]{:S(2)}, u32[]{:S(2)}) collective-permute-start(bf16[40,16,128]{2,1,0:T(8,128)(2,1)S(1)} %get-tuple-element.29), channel_id=1, source_target_pairs={{0,7},{1,0},{2,1},{3,2},{4,3},{5,4},{6,5},{7,6},{8,15},{9,8},{10,9... | collective-permute-start | bytes 491528 | tf_op jit(solution)/shard_map/ppermute | solution.py:157
Sparse Core Ops, SparseCore 0:
  11.4 37.3 reduce-scatter.4
  52.0 34.6 reduce-scatter.2
  208.7 23.9 all-gather.4
  239.8 31.0 all-gather.6

commit v13 on v12

--- a/solution.py
+++ b/solution.py
@@ -148,7 +148,7 @@
     rounded_all = (held - (outer_rate * (1.0 + outer_momentum)) * grad_all).astype(jnp.bfloat16)
     for c in range(2):
         rounded = rounded_all[:, :, halves[c]]
-        if c == 1 and dev_count <= 8:
+        if dev_count <= 8:
             me = lax.axis_index("dev")
             part_rows = rounded.shape[1] // dev_count
             blocks = [lax.dynamic_slice_in_dim(rounded, me * part_rows, part_rows, 1)]

time: 282 us -> 280 us (level)
  waiting for transfers between devices: 157 us -> 139 us
  starting transfers between devices: 27 us -> 40.1 us
  local copies, waits for them, and re-layouts: 30.7 us -> 34.6 us
    all_to_all x1 -> x0, waiting for transfers between devices: 31.9 us -> none  [body(): lax.all_to_all(rounded, 'dev', split_axis=1, concat_axis=0, tiled=True)]
    ppermute x7 -> x14, starting transfers between devices: 10.9 us -> 28.2 us  [body(): lax.ppermute(out_rows, 'dev', [(i, (i + k) % dev_count) for i in range(de...]
    ppermute x7 -> x14, waiting for transfers between devices: 10 us -> 20.3 us  [body(): lax.ppermute(out_rows, 'dev', [(i, (i + k) % dev_count) for i in range(de...]
    unnamed x32 -> x38, local copies, waits for them, and re-layouts: 6.88 us -> 13.6 us
    all_to_all x1 -> x0, starting transfers between devices: 4.27 us -> none  [body(): lax.all_to_all(rounded, 'dev', split_axis=1, concat_axis=0, tiled=True)]
    all_gather x2, waiting for transfers between devices: 11.8 us -> 14.7 us  [body(): gathered = lax.all_gather(picked, 'rep', axis=2, tiled=True)]
    gather x1 -> x0, local copies, waits for them, and re-layouts: 2.93 us -> none  [body(): picked = jnp.take(pieces, target, axis=0, mode='clip')]
    gather x1 -> x2, local copies, waits for them, and re-layouts: 2.89 us -> 5.79 us  [body(): picked = jnp.take(pieces, shifted, axis=0, mode='clip')]
  transfers between devices with their start and end apart: 17 -> 23, of which waited for: 10 -> 12; matrix products, arithmetic and copies ran while one was open for 13% -> 14% of each run, Pallas kernels for 3% -> 3%
where the time goes in v13:
time: 280 us; the launch traced here: 279 us
  waiting for transfers between devices  139 us (50%)
  starting transfers between devices  40.1 us (14%)
  local copies, waits for them, and re-layouts  34.6 us (12%)
  matrix products  23 us (8%)
  Pallas kernels  16 us (6%)
  between operations  14 us (5%)
  other arithmetic  13.2 us (5%)
    reduce_scatter x2, waiting for transfers between devices, body(): summed = lax.psum_scatter(half, 'rep', scatter_dimension=0, tiled=True)[0]  61.9 us
    ppermute x14, starting transfers between devices, body(): lax.ppermute(out_rows, 'dev', [(i, (i + k) % dev_count) for i in range(de...  28.2 us
    all_to_all x2, waiting for transfers between devices, body(): lax.all_to_all(picked.reshape(dev_count, slot_count, summed.shape[1], sum...  27.4 us
    ppermute x14, waiting for transfers between devices, body(): lax.ppermute(out_rows, 'dev', [(i, (i + k) % dev_count) for i in range(de...  20.3 us
    all_gather x2, waiting for transfers between devices, body(): gathered = lax.all_gather(picked, 'rep', axis=2, tiled=True)  14.7 us
    dot_general x1, matrix products, fresh(): jnp.einsum('skb,kq->sbq', coeffs, basis_cols, precision=lax.Precision.HIGH)  13.9 us
    unnamed x38, local copies, waits for them, and re-layouts  13.6 us
    all_to_all x2, starting transfers between devices, body(): lax.all_to_all(picked.reshape(dev_count, slot_count, summed.shape[1], sum...  11 us
  transfers between devices with their start and end apart: 23, of which 12 were waited for; matrix products, arithmetic and copies ran while one was open for 14% of the time, Pallas kernels for 3%

profile of v13, /device:TPU:0, one launch (start us, length us, event | category | flops | bytes accessed | tf_op | source)
XLA Modules:
  0.0 279.5 jit_solution(9264728379418722242)
XLA Ops:
  7.2 4.0 %shard_map.120 = bf16[4,160,16,128]{3,2,1,0:T(8,128)(2,1)} custom-call(bf16[160,16,1024]{2,1,0:T(8,128)(2,1)} %bitcast.54), custom_call_target="tpu_custom_call" | custom-call | tf_op jit(solution)/shard_map/pallas_call | solution.py:47
  11.3 4.0 %shard_map.119 = bf16[4,160,16,128]{3,2,1,0:T(8,128)(2,1)} custom-call(bf16[160,16,1024]{2,1,0:T(8,128)(2,1)} %bitcast.55), custom_call_target="tpu_custom_call" | custom-call | tf_op jit(solution)/shard_map/pallas_call | solution.py:47
  16.3 32.4 %reduce-scatter.5.cloned.1.call-done = bf16[1,160,16,128]{3,2,1,0:T(8,128)(2,1)} async-done(((bf16[4,160,16,128]{3,2,1,0:T(8,128)(2,1)}), bf16[1,160,16,128]{3,2,1,0:T(8,128)(2,1)}) %reduce-scatter.5.cloned.1.call-update) | async-done | bytes 655376 | tf_op jit(solution)/shard_map/reduce_scatter | solution.py:111
  48.8 3.0 %gather_fusion.1 = bf16[320,16,128]{2,1,0:T(8,128)(2,1)} fusion(bf16[160,16,128]{2,1,0:T(8,128)(2,1)} %bitcast.66, s32[1024]{0:T(1024)S(1)} %pad_clamp_fusion.1), kind=kCustom, calls=%fused_computation.1 | custom fusion | bytes 2622720 | tf_op jit(solution)/shard_map/jit(_take)/gather | solution.py:112
  51.8 5.5 %all-to-all-start.1 = ((bf16[8,40,16,128]{3,2,1,0:T(8,128)(2,1)}), bf16[8,40,16,128]{3,2,1,0:T(8,128)(2,1)S(1)}, u32[]{:S(2)}, u32[]{:S(2)}) async-start(bf16[8,40,16,128]{3,2,1,0:T(8,128)(2,1)} %bitcast.9), calls=%async_computation.3 | async-start | bytes 2621440 | tf_op jit(solution)/shard_map/all_to_all | solution.py:113
  57.3 29.4 %reduce-scatter.3.cloned.1.call-done = bf16[1,160,16,128]{3,2,1,0:T(8,128)(2,1)} async-done(((bf16[4,160,16,128]{3,2,1,0:T(8,128)(2,1)}), bf16[1,160,16,128]{3,2,1,0:T(8,128)(2,1)}) %reduce-scatter.3.cloned.1.call-update) | async-done | bytes 655376 | tf_op jit(solution)/shard_map/reduce_scatter | solution.py:111
  86.7 3.0 %gather_fusion = bf16[320,16,128]{2,1,0:T(8,128)(2,1)} fusion(bf16[160,16,128]{2,1,0:T(8,128)(2,1)} %bitcast.67, s32[1024]{0:T(1024)S(1)} %pad_clamp_fusion.1), kind=kCustom, calls=%fused_computation | custom fusion | bytes 2622720 | tf_op jit(solution)/shard_map/jit(_take)/gather | solution.py:112
  89.8 1.1 copy-done.5
  90.8 5.5 %all-to-all-start = ((bf16[8,40,16,128]{3,2,1,0:T(8,128)(2,1)}), bf16[8,40,16,128]{3,2,1,0:T(8,128)(2,1)}, u32[]{:S(2)}, u32[]{:S(2)}) async-start(bf16[8,40,16,128]{3,2,1,0:T(8,128)(2,1)} %bitcast.4), calls=%async_computation.1 | async-start | bytes 2621440 | tf_op jit(solution)/shard_map/all_to_all | solution.py:113
  97.1 1.6 multiply_bitcast_fusion
  98.6 1.9 copy.17
  100.5 27.4 %all-to-all-done = bf16[8,40,16,128]{3,2,1,0:T(8,128)(2,1)} async-done(((bf16[8,40,16,128]{3,2,1,0:T(8,128)(2,1)}), bf16[8,40,16,128]{3,2,1,0:T(8,128)(2,1)}, u32[]{:S(2)}, u32[]{:S(2)}) %all-to-all-start) | async-done | bytes 1310752 | tf_op jit(solution)/shard_map/all_to_all | solution.py:113
  127.9 1.6 multiply_bitcast_fusion.1
  129.8 1.4 copy-done.4
  131.2 3.6 %slice_subtract_fusion = (f32[40,128,128]{2,1,0:T(8,128)S(1)}, f32[40,128,128]{2,1,0:T(8,128)S(1)}) fusion(f32[40,128,128]{2,1,0:T(8,128)S(1)} %bitcast.59, f32[40,128,256]{2,1,0:T(8,128)} %bitcast.52, f32[40,128,128]{2,1,0:T(8,128)S(1)} %bitcast.60), kind=kLoop, calls=%fused_computation.13 | loop fusion | flops 1310720 | bytes 15728640 | tf_op jit(solution)/shard_map/sub | solution.py:120
  134.7 1.5 fusion.11
  136.2 1.5 fusion.4
  138.6 2.5 collective-permute-done
  141.1 1.3 add_convert_fusion
  143.1 9.6 %collective-permute-done.1 = bf16[1344,128]{1,0:T(8,128)(2,1)S(1)} collective-permute-done((bf16[1344,128]{1,0:T(8,128)(2,1)S(1)}, bf16[1344,128]{1,0:T(8,128)(2,1)S(1)}, u32[]{:S(2)}, u32[]{:S(2)}) %collective-permute-start.1) | collective-permute-done | bytes 344096 | tf_op jit(solution)/shard_map/ppermute | solution.py:32
  153.8 2.3 collective-permute-done.2
  156.1 1.3 broadcast_select_fusion.1
  158.2 1.6 copy-done.2
  159.8 6.1 %fusion.3 = bf16[40,128,256]{2,1,0:T(8,128)(2,1)S(1)} fusion(f32[40,128,128]{2,1,0:T(8,128)S(1)} %get-tuple-element.14, f32[40,128,128]{2,1,0:T(8,128)S(1)} %copy-done.2, pred[40]{0:T(512)(128)(4,1)S(1)} %get-tuple-element.18, f32[40,64,128]{2,1,0:T(8,128)S(1)} %bitcast.57, f32[64,1024]{1,0:T(8,128)S(1)} %copy-done, s32[]{:T(128)S(6)} %select_n.128, ...), kind=kOutput, calls=%fused_computation.9 | convolution fusion | flops 512491520 | bytes 19726852 | tf_op jit(solution)/shard_map/skb,kq->sbq/dot_general | solution.py:146
  166.0 1.5 fusion.19
  167.5 1.0 constant_dynamic-slice_fusion.7
  168.5 1.4 collective-permute-start.3
  169.9 2.2 collective-permute-start.5
  172.1 1.7 collective-permute-start.6
  173.8 2.0 collective-permute-start.7
  175.8 2.6 collective-permute-done.3
  179.1 3.4 %collective-permute-start.9 = (bf16[40,16,128]{2,1,0:T(8,128)(2,1)S(1)}, bf16[40,16,128]{2,1,0:T(8,128)(2,1)S(1)}, u32[]{:S(2)}, u32[]{:S(2)}) collective-permute-start(bf16[40,16,128]{2,1,0:T(8,128)(2,1)S(1)} %get-tuple-element.37), channel_id=1, source_target_pairs={{0,7},{1,0},{2,1},{3,2},{4,3},{5,4},{6,5},{7,6},{8,15},{9,8},{10,9... | collective-permute-start | bytes 491528 | tf_op jit(solution)/shard_map/ppermute | solution.py:157
  183.1 8.5 %collective-permute-done.5 = bf16[40,16,128]{2,1,0:T(8,128)(2,1)S(1)} collective-permute-done((bf16[40,16,128]{2,1,0:T(8,128)(2,1)S(1)}, bf16[40,16,128]{2,1,0:T(8,128)(2,1)S(1)}, u32[]{:S(2)}, u32[]{:S(2)}) %collective-permute-start.5) | collective-permute-done | bytes 163872 | tf_op jit(solution)/shard_map/ppermute | solution.py:157
  195.0 2.9 %gather_fusion.2 = bf16[160,16,128]{2,1,0:T(8,128)(2,1)} fusion(bf16[320,16,128]{2,1,0:T(8,128)(2,1)} %constant_dynamic-update-slice_fusion, s32[1024]{0:T(1024)S(1)} %pad_clamp_fusion), kind=kCustom, calls=%fused_computation.2 | custom fusion | bytes 1311360 | tf_op jit(solution)/shard_map/jit(_take)/gather | solution.py:160
  198.0 2.3 constant_dynamic-slice_fusion
  200.3 3.8 %collective-permute-start.10 = (bf16[40,16,128]{2,1,0:T(8,128)(2,1)S(1)}, bf16[40,16,128]{2,1,0:T(8,128)(2,1)S(1)}, u32[]{:S(2)}, u32[]{:S(2)}) collective-permute-start(bf16[40,16,128]{2,1,0:T(8,128)(2,1)S(1)} %get-tuple-element.35), channel_id=1, source_target_pairs={{0,1},{1,2},{2,3},{3,4},{4,5},{5,6},{6,7},{7,0},{8,9},{9,10},{10,1... | collective-permute-start | bytes 491528 | tf_op jit(solution)/shard_map/ppermute | solution.py:157
  204.1 6.1 %collective-permute-start.11 = (bf16[40,16,128]{2,1,0:T(8,128)(2,1)S(1)}, bf16[40,16,128]{2,1,0:T(8,128)(2,1)S(1)}, u32[]{:S(2)}, u32[]{:S(2)}) collective-permute-start(bf16[40,16,128]{2,1,0:T(8,128)(2,1)S(1)} %get-tuple-element.34), channel_id=1, source_target_pairs={{0,2},{1,3},{2,4},{3,5},{4,6},{5,7},{6,0},{7,1},{8,10},{9,11},{10,... | collective-permute-start | bytes 491528 | tf_op jit(solution)/shard_map/ppermute | solution.py:157
  210.3 1.6 collective-permute-start.13
  211.8 2.8 %collective-permute-start.14 = (bf16[40,16,128]{2,1,0:T(8,128)(2,1)S(1)}, bf16[40,16,128]{2,1,0:T(8,128)(2,1)S(1)}, u32[]{:S(2)}, u32[]{:S(2)}) collective-permute-start(bf16[40,16,128]{2,1,0:T(8,128)(2,1)S(1)} %get-tuple-element.31), channel_id=1, source_target_pairs={{0,5},{1,6},{2,7},{3,0},{4,1},{5,2},{6,3},{7,4},{8,13},{9,14},{10,... | collective-permute-start | bytes 491528 | tf_op jit(solution)/shard_map/ppermute | solution.py:157
  214.6 1.8 collective-permute-start.15
  217.1 1.5 collective-permute-start.16
  219.3 7.8 %collective-permute-done.12 = bf16[40,16,128]{2,1,0:T(8,128)(2,1)S(1)} collective-permute-done((bf16[40,16,128]{2,1,0:T(8,128)(2,1)S(1)}, bf16[40,16,128]{2,1,0:T(8,128)(2,1)S(1)}, u32[]{:S(2)}, u32[]{:S(2)}) %collective-permute-start.12) | collective-permute-done | bytes 163872 | tf_op jit(solution)/shard_map/ppermute | solution.py:157
  229.9 1.3 collective-permute-done.16
  231.9 2.9 %gather_fusion.3 = bf16[160,16,128]{2,1,0:T(8,128)(2,1)} fusion(bf16[320,16,128]{2,1,0:T(8,128)(2,1)} %constant_dynamic-update-slice_fusion.7, s32[1024]{0:T(1024)S(1)} %pad_clamp_fusion), kind=kCustom, calls=%fused_computation.3 | custom fusion | bytes 1311360 | tf_op jit(solution)/shard_map/jit(_take)/gather | solution.py:160
  236.3 4.0 %shard_map.121.base_ref = bf16[160,16,1024]{2,1,0:T(8,128)(2,1)} custom-call(bf16[160,16,512]{2,1,0:T(8,128)(2,1)} %all-gather.5.cloned.1.call-done.x_ref), custom_call_target="tpu_custom_call" | custom-call | tf_op jit(solution)/shard_map/pallas_call | solution.py:68
  240.3 13.9 %select_bitcast_fusion = (f32[1,40,128,256]{3,2,1,0:T(8,128)}, f32[1,40,128,256]{3,2,1,0:T(8,128)}) fusion(f32[40,128,256]{2,1,0:T(8,128)} %bitcast.56, pred[40]{0:T(512)(128)(4,1)S(1)} %get-tuple-element.17, f32[40,128,256]{2,1,0:T(8,128)} %bitcast.53, f32[40,128,128]{2,1,0:T(8,128)S(1)} %get-tuple-element.14, f32[40,128,128]{2,1,0:T(8,128)} %copy-done.1, ...), kind=kOutput, calls=%fused_computation.11 | convolution fusion | flops 516423680 | bytes 27591684 | tf_op jit(solution)/shard_map/skb,kq->sbq/dot_general | solution.py:138
  254.2 14.7 %all-gather.7.cloned.1.call-done.a_ref = bf16[160,16,512]{2,1,0:T(8,128)(2,1)} async-done(((bf16[160,16,128]{2,1,0:T(8,128)(2,1)}), bf16[160,16,512]{2,1,0:T(8,128)(2,1)}) %all-gather.7.cloned.1.call-update) | async-done | bytes 2621456 | tf_op jit(solution)/shard_map/all_gather | solution.py:164
  269.0 4.0 %shard_map.122 = bf16[160,16,1024]{2,1,0:T(8,128)(2,1)} custom-call(bf16[160,16,512]{2,1,0:T(8,128)(2,1)} %all-gather.7.cloned.1.call-done.a_ref, bf16[160,16,1024]{2,1,0:T(8,128)(2,1)} %shard_map.121.base_ref), custom_call_target="tpu_custom_call", output_to_operand_aliasing={{}: (1, {})} | custom-call | tf_op jit(solution)/shard_map/pallas_call | solution.py:71
  (81 shorter events, 16.8 us)
Async XLA Ops:
  7.2 127.6 %copy-start = (f32[64,1024]{1,0:T(8,128)S(1)}, f32[64,1024]{1,0:T(8,128)}, u32[]{:S(2)}) copy-start(f32[64,1024]{1,0:T(8,128)} %param.12) | copy-start | bytes 786436
  7.2 41.6 %reduce-scatter.5.cloned.1.call-start = ((), (), s32[]{:S(2)}) async-start(), calls=%async_computation.5 | async-start | bytes 3276800 | tf_op jit(solution)/shard_map/reduce_scatter | solution.py:111
  11.3 75.5 %reduce-scatter.3.cloned.1.call-start = ((), (), s32[]{:S(2)}) async-start(), calls=%async_computation.4 | async-start | bytes 3276800 | tf_op jit(solution)/shard_map/reduce_scatter | solution.py:111
  15.3 0.7 copy-start.12
  51.8 38.0 %all-to-all-start.1 = ((bf16[8,40,16,128]{3,2,1,0:T(8,128)(2,1)}), bf16[8,40,16,128]{3,2,1,0:T(8,128)(2,1)S(1)}, u32[]{:S(2)}, u32[]{:S(2)}) async-start(bf16[8,40,16,128]{3,2,1,0:T(8,128)(2,1)} %bitcast.9), calls=%async_computation.3 | async-start | bytes 2621440 | tf_op jit(solution)/shard_map/all_to_all | solution.py:113
  89.8 1.1 copy-start.5
  89.8 6.6 %copy-start.11 = (bf16[1,13,1024]{2,1,0:T(8,128)(2,1)S(1)}, bf16[1,13,1024]{2,1,0:T(8,128)(2,1)}, u32[]{:S(2)}) copy-start(bf16[1,13,1024]{2,1,0:T(8,128)(2,1)} %param.13) | copy-start | bytes 79876
  90.8 37.0 %all-to-all-start = ((bf16[8,40,16,128]{3,2,1,0:T(8,128)(2,1)}), bf16[8,40,16,128]{3,2,1,0:T(8,128)(2,1)}, u32[]{:S(2)}, u32[]{:S(2)}) async-start(bf16[8,40,16,128]{3,2,1,0:T(8,128)(2,1)} %bitcast.4), calls=%async_computation.1 | async-start | bytes 2621440 | tf_op jit(solution)/shard_map/all_to_all | solution.py:113
  96.4 140.0 %all-gather.5.cloned.1.call-start = ((), (), s32[]{:S(2)}) async-start(), calls=%async_computation.6 | async-start | bytes 3276800 | tf_op jit(solution)/shard_map/all_gather | solution.py:164
  129.4 1.7 copy-start.4
  134.7 1.5 copy-start.1
  136.2 1.5 copy-start.8
  138.6 2.5 collective-permute-start
  142.4 10.2 %copy-start.6 = (bf16[2688,128]{1,0:T(8,128)(2,1)}, bf16[2688,128]{1,0:T(8,128)(2,1)S(1)}, u32[]{:S(2)}) copy-start(bf16[2688,128]{1,0:T(8,128)(2,1)S(1)} %add_convert_fusion) | copy-start | bytes 2064388
  142.5 10.2 %collective-permute-start.1 = (bf16[1344,128]{1,0:T(8,128)(2,1)S(1)}, bf16[1344,128]{1,0:T(8,128)(2,1)S(1)}, u32[]{:S(2)}, u32[]{:S(2)}) collective-permute-start(bf16[1344,128]{1,0:T(8,128)(2,1)S(1)} %dynamic-slice_bitcast_fusion), channel_id=1, source_target_pairs={{0,16},{8,24},{16,0},{24,8},{1,17},{9,25},{17,1},{25,9},{2,18},{10... | collective-permute-start | bytes 1032200 | tf_op jit(solution)/shard_map/ppermute | solution.py:32
  153.6 2.5 collective-permute-start.2
  157.4 0.8 copy-start.7
  157.4 2.4 copy-start.2
  158.2 7.7 %copy-start.3 = (f32[2560,128]{1,0:T(8,128)}, f32[2560,128]{1,0:T(8,128)S(1)}, u32[]{:S(2)}) copy-start(f32[2560,128]{1,0:T(8,128)S(1)} %pad_maximum_fusion) | copy-start | bytes 3932164
  168.5 9.9 %collective-permute-start.3 = (bf16[40,16,128]{2,1,0:T(8,128)(2,1)S(1)}, bf16[40,16,128]{2,1,0:T(8,128)(2,1)S(1)}, u32[]{:S(2)}, u32[]{:S(2)}) collective-permute-start(bf16[40,16,128]{2,1,0:T(8,128)(2,1)S(1)} %get-tuple-element.43), channel_id=1, source_target_pairs={{0,1},{1,2},{2,3},{3,4},{4,5},{5,6},{6,7},{7,0},{8,9},{9,10},{10,1... | collective-permute-start | bytes 491528 | tf_op jit(solution)/shard_map/ppermute | solution.py:157
  169.9 9.2 %collective-permute-start.4 = (bf16[40,16,128]{2,1,0:T(8,128)(2,1)S(1)}, bf16[40,16,128]{2,1,0:T(8,128)(2,1)S(1)}, u32[]{:S(2)}, u32[]{:S(2)}) collective-permute-start(bf16[40,16,128]{2,1,0:T(8,128)(2,1)S(1)} %get-tuple-element.42), channel_id=1, source_target_pairs={{0,2},{1,3},{2,4},{3,5},{4,6},{5,7},{6,0},{7,1},{8,10},{9,11},{10,... | collective-permute-start | bytes 491528 | tf_op jit(solution)/shard_map/ppermute | solution.py:157
  169.9 21.7 %collective-permute-start.5 = (bf16[40,16,128]{2,1,0:T(8,128)(2,1)S(1)}, bf16[40,16,128]{2,1,0:T(8,128)(2,1)S(1)}, u32[]{:S(2)}, u32[]{:S(2)}) collective-permute-start(bf16[40,16,128]{2,1,0:T(8,128)(2,1)S(1)} %get-tuple-element.41), channel_id=1, source_target_pairs={{0,3},{1,4},{2,5},{3,6},{4,7},{5,0},{6,1},{7,2},{8,11},{9,12},{10,... | collective-permute-start | bytes 491528 | tf_op jit(solution)/shard_map/ppermute | solution.py:157
  172.1 20.1 %collective-permute-start.6 = (bf16[40,16,128]{2,1,0:T(8,128)(2,1)S(1)}, bf16[40,16,128]{2,1,0:T(8,128)(2,1)S(1)}, u32[]{:S(2)}, u32[]{:S(2)}) collective-permute-start(bf16[40,16,128]{2,1,0:T(8,128)(2,1)S(1)} %get-tuple-element.40), channel_id=1, source_target_pairs={{0,4},{1,5},{2,6},{3,7},{4,0},{5,1},{6,2},{7,3},{8,12},{9,13},{10,... | collective-permute-start | bytes 491528 | tf_op jit(solution)/shard_map/ppermute | solution.py:157
  173.8 19.1 %collective-permute-start.7 = (bf16[40,16,128]{2,1,0:T(8,128)(2,1)S(1)}, bf16[40,16,128]{2,1,0:T(8,128)(2,1)S(1)}, u32[]{:S(2)}, u32[]{:S(2)}) collective-permute-start(bf16[40,16,128]{2,1,0:T(8,128)(2,1)S(1)} %get-tuple-element.39), channel_id=1, source_target_pairs={{0,5},{1,6},{2,7},{3,0},{4,1},{5,2},{6,3},{7,4},{8,13},{9,14},{10,... | collective-permute-start | bytes 491528 | tf_op jit(solution)/shard_map/ppermute | solution.py:157
  178.4 15.2 %collective-permute-start.8 = (bf16[40,16,128]{2,1,0:T(8,128)(2,1)S(1)}, bf16[40,16,128]{2,1,0:T(8,128)(2,1)S(1)}, u32[]{:S(2)}, u32[]{:S(2)}) collective-permute-start(bf16[40,16,128]{2,1,0:T(8,128)(2,1)S(1)} %get-tuple-element.38), channel_id=1, source_target_pairs={{0,6},{1,7},{2,0},{3,1},{4,2},{5,3},{6,4},{7,5},{8,14},{9,15},{10,... | collective-permute-start | bytes 491528 | tf_op jit(solution)/shard_map/ppermute | solution.py:157
  179.1 15.2 %collective-permute-start.9 = (bf16[40,16,128]{2,1,0:T(8,128)(2,1)S(1)}, bf16[40,16,128]{2,1,0:T(8,128)(2,1)S(1)}, u32[]{:S(2)}, u32[]{:S(2)}) collective-permute-start(bf16[40,16,128]{2,1,0:T(8,128)(2,1)S(1)} %get-tuple-element.37), channel_id=1, source_target_pairs={{0,7},{1,0},{2,1},{3,2},{4,3},{5,4},{6,5},{7,6},{8,15},{9,8},{10,9... | collective-permute-start | bytes 491528 | tf_op jit(solution)/shard_map/ppermute | solution.py:157
  197.9 71.0 %all-gather.7.cloned.1.call-start = ((), (), s32[]{:S(2)}) async-start(), calls=%async_computation.7 | async-start | bytes 3276800 | tf_op jit(solution)/shard_map/all_gather | solution.py:164
  200.3 14.3 %collective-permute-start.10 = (bf16[40,16,128]{2,1,0:T(8,128)(2,1)S(1)}, bf16[40,16,128]{2,1,0:T(8,128)(2,1)S(1)}, u32[]{:S(2)}, u32[]{:S(2)}) collective-permute-start(bf16[40,16,128]{2,1,0:T(8,128)(2,1)S(1)} %get-tuple-element.35), channel_id=1, source_target_pairs={{0,1},{1,2},{2,3},{3,4},{4,5},{5,6},{6,7},{7,0},{8,9},{9,10},{10,1... | collective-permute-start | bytes 491528 | tf_op jit(solution)/shard_map/ppermute | solution.py:157
  204.1 13.0 %collective-permute-start.11 = (bf16[40,16,128]{2,1,0:T(8,128)(2,1)S(1)}, bf16[40,16,128]{2,1,0:T(8,128)(2,1)S(1)}, u32[]{:S(2)}, u32[]{:S(2)}) collective-permute-start(bf16[40,16,128]{2,1,0:T(8,128)(2,1)S(1)} %get-tuple-element.34), channel_id=1, source_target_pairs={{0,2},{1,3},{2,4},{3,5},{4,6},{5,7},{6,0},{7,1},{8,10},{9,11},{10,... | collective-permute-start | bytes 491528 | tf_op jit(solution)/shard_map/ppermute | solution.py:157
  210.3 16.9 %collective-permute-start.12 = (bf16[40,16,128]{2,1,0:T(8,128)(2,1)S(1)}, bf16[40,16,128]{2,1,0:T(8,128)(2,1)S(1)}, u32[]{:S(2)}, u32[]{:S(2)}) collective-permute-start(bf16[40,16,128]{2,1,0:T(8,128)(2,1)S(1)} %get-tuple-element.33), channel_id=1, source_target_pairs={{0,3},{1,4},{2,5},{3,6},{4,7},{5,0},{6,1},{7,2},{8,11},{9,12},{10,... | collective-permute-start | bytes 491528 | tf_op jit(solution)/shard_map/ppermute | solution.py:157
  210.3 17.6 %collective-permute-start.13 = (bf16[40,16,128]{2,1,0:T(8,128)(2,1)S(1)}, bf16[40,16,128]{2,1,0:T(8,128)(2,1)S(1)}, u32[]{:S(2)}, u32[]{:S(2)}) collective-permute-start(bf16[40,16,128]{2,1,0:T(8,128)(2,1)S(1)} %get-tuple-element.32), channel_id=1, source_target_pairs={{0,4},{1,5},{2,6},{3,7},{4,0},{5,1},{6,2},{7,3},{8,12},{9,13},{10,... | collective-permute-start | bytes 491528 | tf_op jit(solution)/shard_map/ppermute | solution.py:157
  211.8 16.7 %collective-permute-start.14 = (bf16[40,16,128]{2,1,0:T(8,128)(2,1)S(1)}, bf16[40,16,128]{2,1,0:T(8,128)(2,1)S(1)}, u32[]{:S(2)}, u32[]{:S(2)}) collective-permute-start(bf16[40,16,128]{2,1,0:T(8,128)(2,1)S(1)} %get-tuple-element.31), channel_id=1, source_target_pairs={{0,5},{1,6},{2,7},{3,0},{4,1},{5,2},{6,3},{7,4},{8,13},{9,14},{10,... | collective-permute-start | bytes 491528 | tf_op jit(solution)/shard_map/ppermute | solution.py:157
  214.6 14.6 %collective-permute-start.15 = (bf16[40,16,128]{2,1,0:T(8,128)(2,1)S(1)}, bf16[40,16,128]{2,1,0:T(8,128)(2,1)S(1)}, u32[]{:S(2)}, u32[]{:S(2)}) collective-permute-start(bf16[40,16,128]{2,1,0:T(8,128)(2,1)S(1)} %get-tuple-element.30), channel_id=1, source_target_pairs={{0,6},{1,7},{2,0},{3,1},{4,2},{5,3},{6,4},{7,5},{8,14},{9,15},{10,... | collective-permute-start | bytes 491528 | tf_op jit(solution)/shard_map/ppermute | solution.py:157
  217.1 14.1 %collective-permute-start.16 = (bf16[40,16,128]{2,1,0:T(8,128)(2,1)S(1)}, bf16[40,16,128]{2,1,0:T(8,128)(2,1)S(1)}, u32[]{:S(2)}, u32[]{:S(2)}) collective-permute-start(bf16[40,16,128]{2,1,0:T(8,128)(2,1)S(1)} %get-tuple-element.29), channel_id=1, source_target_pairs={{0,7},{1,0},{2,1},{3,2},{4,3},{5,4},{6,5},{7,6},{8,15},{9,8},{10,9... | collective-permute-start | bytes 491528 | tf_op jit(solution)/shard_map/ppermute | solution.py:157
  229.9 5.7 %copy-start.9 = (f32[13,1024]{1,0:T(8,128)S(1)}, f32[13,1024]{1,0:T(8,128)}, u32[]{:S(2)}) copy-start(f32[13,1024]{1,0:T(8,128)} %param.14) | copy-start | bytes 159748
  229.9 5.7 %copy-start.10 = (f32[13,1024]{1,0:T(8,128)S(1)}, f32[13,1024]{1,0:T(8,128)}, u32[]{:S(2)}) copy-start(f32[13,1024]{1,0:T(8,128)} %param.15) | copy-start | bytes 159748
Sparse Core Ops, SparseCore 0:
  11.4 37.3 reduce-scatter.4
  52.0 34.6 reduce-scatter.2
  198.1 31.0 all-gather.4
  234.9 33.9 all-gather.6

commit v14 on v13

--- a/solution.py
+++ b/solution.py
@@ -109,15 +109,27 @@
     for c in range(2):
         half = take_half(own_rows, width, c)
         summed = lax.psum_scatter(half, "rep", scatter_dimension=0, tiled=True)[0]
-        picked = jnp.take(summed, source_unit, axis=0, mode="clip")
-        arrived = lax.all_to_all(
-            picked.reshape(dev_count, slot_count, summed.shape[1], summed.shape[2]),
-            "dev",
-            split_axis=0,
-            concat_axis=2,
-            tiled=True,
-        )
-        change = start_rows[:, :, halves[c]] - arrived[0].astype(jnp.float32) / rep_count
+        if c == 1 and dev_count <= 8:
+            me = lax.axis_index("dev")
+            part_rows = summed.shape[1]
+            arrived = jnp.zeros((slot_count, dev_count * part_rows, width), summed.dtype)
+            for k in range(dev_count):
+                dest = (me + k) % dev_count
+                units = lax.dynamic_slice_in_dim(source_unit, dest * slot_count, slot_count)
+                block = jnp.take(summed, units, axis=0, mode="clip")
+                if k:
+                    block = lax.ppermute(block, "dev", [(i, (i + k) % dev_count) for i in range(dev_count)])
+                arrived = lax.dynamic_update_slice_in_dim(arrived, block, ((me - k) % dev_count) * part_rows, 1)
+        else:
+            picked = jnp.take(summed, source_unit, axis=0, mode="clip")
+            arrived = lax.all_to_all(
+                picked.reshape(dev_count, slot_count, summed.shape[1], summed.shape[2]),
+                "dev",
+                split_axis=0,
+                concat_axis=2,
+                tiled=True,
+            )[0]
+        change = start_rows[:, :, halves[c]] - arrived.astype(jnp.float32) / rep_count
         changes.append(change)
         term = jnp.einsum("sbq,kq->skb", change, basis_part[:, halves[c]], precision=lax.Precision.HIGH)
         coeff_terms = term if coeff_terms is None else coeff_terms + term

time: 280 us -> 279 us (level)
  waiting for transfers between devices: 139 us -> 115 us
  local copies, waits for them, and re-layouts: 34.6 us -> 46.6 us
  starting transfers between devices: 40.1 us -> 51.8 us
    all_to_all x2 -> x1, waiting for transfers between devices: 27.4 us -> 0.01 us  [body(): lax.all_to_all(picked.reshape(dev_count, slot_count, summed.shape[1], sum...]
    gather x0 -> x8, local copies, waits for them, and re-layouts: none -> 13.4 us  [body(): block = jnp.take(summed, units, axis=0, mode='clip')]
    ppermute x0 -> x7, starting transfers between devices: none -> 12.1 us  [body(): lax.ppermute(block, 'dev', [(i, (i + k) % dev_count) for i in range(dev_c...]
    ppermute x0 -> x7, waiting for transfers between devices: none -> 5.79 us  [body(): lax.ppermute(block, 'dev', [(i, (i + k) % dev_count) for i in range(dev_c...]
    all_to_all x2 -> x1, starting transfers between devices: 11 us -> 5.65 us  [body(): lax.all_to_all(picked.reshape(dev_count, slot_count, summed.shape[1], sum...]
    ppermute x14, starting transfers between devices: 28.2 us -> 33.2 us  [body(): lax.ppermute(out_rows, 'dev', [(i, (i + k) % dev_count) for i in range(de...]
    dynamic_update_slice x0 -> x8, local copies, waits for them, and re-layouts: none -> 4.77 us  [body(): lax.dynamic_update_slice_in_dim(arrived, block, (me - k) % dev_count * pa...]
    gather x2 -> x1, local copies, waits for them, and re-layouts: 6.07 us -> 3.04 us  [body(): picked = jnp.take(summed, source_unit, axis=0, mode='clip')]
  transfers between devices with their start and end apart: 23 -> 29, of which waited for: 12 -> 13; matrix products, arithmetic and copies ran while one was open for 14% -> 19% of each run, Pallas kernels for 3% -> 3%
where the time goes in v14:
time: 279 us; the launch traced here: 278 us
  waiting for transfers between devices  115 us (41%)
  starting transfers between devices  51.8 us (19%)
  local copies, waits for them, and re-layouts  46.6 us (17%)
  matrix products  23 us (8%)
  Pallas kernels  16 us (6%)
  between operations  14.3 us (5%)
  other arithmetic  10.8 us (4%)
    reduce_scatter x2, waiting for transfers between devices, body(): summed = lax.psum_scatter(half, 'rep', scatter_dimension=0, tiled=True)[0]  61.4 us
    ppermute x14, starting transfers between devices, body(): lax.ppermute(out_rows, 'dev', [(i, (i + k) % dev_count) for i in range(de...  33.2 us
    ppermute x14, waiting for transfers between devices, body(): lax.ppermute(out_rows, 'dev', [(i, (i + k) % dev_count) for i in range(de...  19 us
    all_gather x2, waiting for transfers between devices, body(): gathered = lax.all_gather(picked, 'rep', axis=2, tiled=True)  14.5 us
    dot_general x1, matrix products, fresh(): jnp.einsum('skb,kq->sbq', coeffs, basis_cols, precision=lax.Precision.HIGH)  13.9 us
    gather x8, local copies, waits for them, and re-layouts, body(): block = jnp.take(summed, units, axis=0, mode='clip')  13.4 us
    ppermute x7, starting transfers between devices, body(): lax.ppermute(block, 'dev', [(i, (i + k) % dev_count) for i in range(dev_c...  12.1 us
    unnamed x40, local copies, waits for them, and re-layouts  12 us
  transfers between devices with their start and end apart: 29, of which 13 were waited for; matrix products, arithmetic and copies ran while one was open for 19% of the time, Pallas kernels for 3%

profile of v14, /device:TPU:0, one launch (start us, length us, event | category | flops | bytes accessed | tf_op | source)
XLA Modules:
  0.0 277.6 jit_solution(5656009713416016500)
XLA Ops:
  7.2 4.0 %shard_map.119 = bf16[4,160,16,128]{3,2,1,0:T(8,128)(2,1)} custom-call(bf16[160,16,1024]{2,1,0:T(8,128)(2,1)} %bitcast.48), custom_call_target="tpu_custom_call" | custom-call | tf_op jit(solution)/shard_map/pallas_call | solution.py:47
  11.3 4.0 %shard_map.120 = bf16[4,160,16,128]{3,2,1,0:T(8,128)(2,1)} custom-call(bf16[160,16,1024]{2,1,0:T(8,128)(2,1)} %bitcast.49), custom_call_target="tpu_custom_call" | custom-call | tf_op jit(solution)/shard_map/pallas_call | solution.py:47
  16.3 32.4 %reduce-scatter.3.cloned.1.call-done = bf16[1,160,16,128]{3,2,1,0:T(8,128)(2,1)} async-done(((bf16[4,160,16,128]{3,2,1,0:T(8,128)(2,1)}), bf16[1,160,16,128]{3,2,1,0:T(8,128)(2,1)}) %reduce-scatter.3.cloned.1.call-update) | async-done | bytes 655376 | tf_op jit(solution)/shard_map/reduce_scatter | solution.py:111
  48.8 3.0 %gather_fusion = bf16[320,16,128]{2,1,0:T(8,128)(2,1)} fusion(bf16[160,16,128]{2,1,0:T(8,128)(2,1)} %bitcast.67, s32[1024]{0:T(1024)S(1)} %pad_clamp_fusion.9), kind=kCustom, calls=%fused_computation | custom fusion | bytes 2622720 | tf_op jit(solution)/shard_map/jit(_take)/gather | solution.py:124
  51.8 5.6 %all-to-all-start = ((bf16[8,40,16,128]{3,2,1,0:T(8,128)(2,1)}), bf16[8,40,16,128]{3,2,1,0:T(8,128)(2,1)S(1)}, u32[]{:S(2)}, u32[]{:S(2)}) async-start(bf16[8,40,16,128]{3,2,1,0:T(8,128)(2,1)} %bitcast.4), calls=%async_computation.1 | async-start | bytes 2621440 | tf_op jit(solution)/shard_map/all_to_all | solution.py:125
  57.8 28.9 %reduce-scatter.5.cloned.1.call-done = bf16[1,160,16,128]{3,2,1,0:T(8,128)(2,1)} async-done(((bf16[4,160,16,128]{3,2,1,0:T(8,128)(2,1)}), bf16[1,160,16,128]{3,2,1,0:T(8,128)(2,1)}) %reduce-scatter.5.cloned.1.call-update) | async-done | bytes 655376 | tf_op jit(solution)/shard_map/reduce_scatter | solution.py:111
  86.8 2.4 gather_fusion.2
  89.2 1.5 collective-permute-start
  91.3 2.3 gather_fusion.1
  93.6 2.3 gather_fusion.3
  96.0 1.5 collective-permute-start.1
  98.7 2.4 collective-permute-start.2
  102.4 1.4 collective-permute-start.3
  105.1 2.4 collective-permute-start.4
  110.4 1.4 collective-permute-start.5
  112.8 1.5 collective-permute-start.6
  116.4 1.6 collective-permute-done.3
  119.9 3.9 %collective-permute-done.5 = bf16[40,16,128]{2,1,0:T(8,128)(2,1)S(1)} collective-permute-done((bf16[40,16,128]{2,1,0:T(8,128)(2,1)}, bf16[40,16,128]{2,1,0:T(8,128)(2,1)S(1)}, u32[]{:S(2)}, u32[]{:S(2)}) %collective-permute-start.5) | collective-permute-done | bytes 163872 | tf_op jit(solution)/shard_map/ppermute | solution.py:121
  125.3 4.0 %slice_subtract_fusion = (f32[40,128,128]{2,1,0:T(8,128)S(1)}, f32[40,128,128]{2,1,0:T(8,128)S(1)}) fusion(f32[40,128,256]{2,1,0:T(8,128)} %bitcast.46, bf16[40,128,128]{2,1,0:T(8,128)(2,1)} %copy-done.4, f32[40,128,128]{2,1,0:T(8,128)S(1)} %bitcast.53), kind=kLoop, calls=%fused_computation.20 | loop fusion | flops 2621440 | bytes 14417920 | tf_op jit(solution)/shard_map/sub | solution.py:132
  129.3 1.5 fusion.11
  130.8 1.5 fusion.4
  133.3 2.5 collective-permute-done.7
  135.7 1.3 add_convert_fusion
  137.7 9.6 %collective-permute-done.8 = bf16[1344,128]{1,0:T(8,128)(2,1)S(1)} collective-permute-done((bf16[1344,128]{1,0:T(8,128)(2,1)S(1)}, bf16[1344,128]{1,0:T(8,128)(2,1)S(1)}, u32[]{:S(2)}, u32[]{:S(2)}) %collective-permute-start.8) | collective-permute-done | bytes 344096 | tf_op jit(solution)/shard_map/ppermute | solution.py:32
  148.4 2.3 collective-permute-done.9
  150.7 1.3 broadcast_select_fusion.1
  152.8 1.6 copy-done.2
  154.4 6.1 %fusion.3 = bf16[40,128,256]{2,1,0:T(8,128)(2,1)S(1)} fusion(f32[40,128,128]{2,1,0:T(8,128)S(1)} %get-tuple-element.14, f32[40,128,128]{2,1,0:T(8,128)S(1)} %copy-done.2, pred[40]{0:T(512)(128)(4,1)S(1)} %get-tuple-element.18, f32[40,64,128]{2,1,0:T(8,128)S(1)} %bitcast.51, f32[64,1024]{1,0:T(8,128)S(1)} %copy-done, s32[]{:T(128)S(6)} %select_n.255, ...), kind=kOutput, calls=%fused_computation.16 | convolution fusion | flops 512491520 | bytes 19726852 | tf_op jit(solution)/shard_map/skb,kq->sbq/dot_general | solution.py:158
  160.6 1.5 fusion.19
  163.1 3.2 %collective-permute-start.10 = (bf16[40,16,128]{2,1,0:T(8,128)(2,1)S(1)}, bf16[40,16,128]{2,1,0:T(8,128)(2,1)S(1)}, u32[]{:S(2)}, u32[]{:S(2)}) collective-permute-start(bf16[40,16,128]{2,1,0:T(8,128)(2,1)S(1)} %get-tuple-element.43), channel_id=1, source_target_pairs={{0,1},{1,2},{2,3},{3,4},{4,5},{5,6},{6,7},{7,0},{8,9},{9,10},{10,1... | collective-permute-start | bytes 491528 | tf_op jit(solution)/shard_map/ppermute | solution.py:169
  166.3 3.3 %collective-permute-start.11 = (bf16[40,16,128]{2,1,0:T(8,128)(2,1)S(1)}, bf16[40,16,128]{2,1,0:T(8,128)(2,1)S(1)}, u32[]{:S(2)}, u32[]{:S(2)}) collective-permute-start(bf16[40,16,128]{2,1,0:T(8,128)(2,1)S(1)} %get-tuple-element.42), channel_id=1, source_target_pairs={{0,2},{1,3},{2,4},{3,5},{4,6},{5,7},{6,0},{7,1},{8,10},{9,11},{10,... | collective-permute-start | bytes 491528 | tf_op jit(solution)/shard_map/ppermute | solution.py:169
  170.7 1.9 collective-permute-start.13
  172.6 3.4 %collective-permute-start.14 = (bf16[40,16,128]{2,1,0:T(8,128)(2,1)S(1)}, bf16[40,16,128]{2,1,0:T(8,128)(2,1)S(1)}, u32[]{:S(2)}, u32[]{:S(2)}) collective-permute-start(bf16[40,16,128]{2,1,0:T(8,128)(2,1)S(1)} %get-tuple-element.39), channel_id=1, source_target_pairs={{0,5},{1,6},{2,7},{3,0},{4,1},{5,2},{6,3},{7,4},{8,13},{9,14},{10,... | collective-permute-start | bytes 491528 | tf_op jit(solution)/shard_map/ppermute | solution.py:169
  177.3 2.2 collective-permute-start.16
  180.1 9.5 %collective-permute-done.12 = bf16[40,16,128]{2,1,0:T(8,128)(2,1)S(1)} collective-permute-done((bf16[40,16,128]{2,1,0:T(8,128)(2,1)S(1)}, bf16[40,16,128]{2,1,0:T(8,128)(2,1)S(1)}, u32[]{:S(2)}, u32[]{:S(2)}) %collective-permute-start.12) | collective-permute-done | bytes 163872 | tf_op jit(solution)/shard_map/ppermute | solution.py:169
  193.1 2.9 %gather_fusion.9 = bf16[160,16,128]{2,1,0:T(8,128)(2,1)} fusion(bf16[320,16,128]{2,1,0:T(8,128)(2,1)} %constant_dynamic-update-slice_fusion, s32[1024]{0:T(1024)S(1)} %pad_clamp_fusion), kind=kCustom, calls=%fused_computation.9 | custom fusion | bytes 1311360 | tf_op jit(solution)/shard_map/jit(_take)/gather | solution.py:172
  196.1 2.3 constant_dynamic-slice_fusion
  198.4 3.9 %collective-permute-start.17 = (bf16[40,16,128]{2,1,0:T(8,128)(2,1)S(1)}, bf16[40,16,128]{2,1,0:T(8,128)(2,1)S(1)}, u32[]{:S(2)}, u32[]{:S(2)}) collective-permute-start(bf16[40,16,128]{2,1,0:T(8,128)(2,1)S(1)} %get-tuple-element.35), channel_id=1, source_target_pairs={{0,1},{1,2},{2,3},{3,4},{4,5},{5,6},{6,7},{7,0},{8,9},{9,10},{10,1... | collective-permute-start | bytes 491528 | tf_op jit(solution)/shard_map/ppermute | solution.py:169
  202.2 6.1 %collective-permute-start.18 = (bf16[40,16,128]{2,1,0:T(8,128)(2,1)S(1)}, bf16[40,16,128]{2,1,0:T(8,128)(2,1)S(1)}, u32[]{:S(2)}, u32[]{:S(2)}) collective-permute-start(bf16[40,16,128]{2,1,0:T(8,128)(2,1)S(1)} %get-tuple-element.34), channel_id=1, source_target_pairs={{0,2},{1,3},{2,4},{3,5},{4,6},{5,7},{6,0},{7,1},{8,10},{9,11},{10,... | collective-permute-start | bytes 491528 | tf_op jit(solution)/shard_map/ppermute | solution.py:169
  208.4 2.1 collective-permute-start.20
  210.5 3.4 %collective-permute-start.21 = (bf16[40,16,128]{2,1,0:T(8,128)(2,1)S(1)}, bf16[40,16,128]{2,1,0:T(8,128)(2,1)S(1)}, u32[]{:S(2)}, u32[]{:S(2)}) collective-permute-start(bf16[40,16,128]{2,1,0:T(8,128)(2,1)S(1)} %get-tuple-element.31), channel_id=1, source_target_pairs={{0,5},{1,6},{2,7},{3,0},{4,1},{5,2},{6,3},{7,4},{8,13},{9,14},{10,... | collective-permute-start | bytes 491528 | tf_op jit(solution)/shard_map/ppermute | solution.py:169
  215.3 1.9 collective-permute-start.23
  217.9 8.9 %collective-permute-done.19 = bf16[40,16,128]{2,1,0:T(8,128)(2,1)S(1)} collective-permute-done((bf16[40,16,128]{2,1,0:T(8,128)(2,1)S(1)}, bf16[40,16,128]{2,1,0:T(8,128)(2,1)S(1)}, u32[]{:S(2)}, u32[]{:S(2)}) %collective-permute-start.19) | collective-permute-done | bytes 163872 | tf_op jit(solution)/shard_map/ppermute | solution.py:169
  230.2 2.9 %gather_fusion.10 = bf16[160,16,128]{2,1,0:T(8,128)(2,1)} fusion(bf16[320,16,128]{2,1,0:T(8,128)(2,1)} %constant_dynamic-update-slice_fusion.7, s32[1024]{0:T(1024)S(1)} %pad_clamp_fusion), kind=kCustom, calls=%fused_computation.10 | custom fusion | bytes 1311360 | tf_op jit(solution)/shard_map/jit(_take)/gather | solution.py:172
  234.6 4.0 %shard_map.121.base_ref = bf16[160,16,1024]{2,1,0:T(8,128)(2,1)} custom-call(bf16[160,16,512]{2,1,0:T(8,128)(2,1)} %all-gather.5.cloned.1.call-done.x_ref), custom_call_target="tpu_custom_call" | custom-call | tf_op jit(solution)/shard_map/pallas_call | solution.py:68
  238.6 13.9 %select_bitcast_fusion = (f32[1,40,128,256]{3,2,1,0:T(8,128)}, f32[1,40,128,256]{3,2,1,0:T(8,128)}) fusion(f32[40,128,256]{2,1,0:T(8,128)} %bitcast.50, pred[40]{0:T(512)(128)(4,1)S(1)} %get-tuple-element.17, f32[40,128,256]{2,1,0:T(8,128)} %bitcast.47, f32[40,128,128]{2,1,0:T(8,128)S(1)} %get-tuple-element.14, f32[40,128,128]{2,1,0:T(8,128)} %copy-done.1, ...), kind=kOutput, calls=%fused_computation.18 | convolution fusion | flops 516423680 | bytes 27591684 | tf_op jit(solution)/shard_map/skb,kq->sbq/dot_general | solution.py:150
  252.5 14.5 %all-gather.7.cloned.1.call-done.a_ref = bf16[160,16,512]{2,1,0:T(8,128)(2,1)} async-done(((bf16[160,16,128]{2,1,0:T(8,128)(2,1)}), bf16[160,16,512]{2,1,0:T(8,128)(2,1)}) %all-gather.7.cloned.1.call-update) | async-done | bytes 2621456 | tf_op jit(solution)/shard_map/all_gather | solution.py:176
  267.1 4.0 %shard_map.122 = bf16[160,16,1024]{2,1,0:T(8,128)(2,1)} custom-call(bf16[160,16,512]{2,1,0:T(8,128)(2,1)} %all-gather.7.cloned.1.call-done.a_ref, bf16[160,16,1024]{2,1,0:T(8,128)(2,1)} %shard_map.121.base_ref), custom_call_target="tpu_custom_call", output_to_operand_aliasing={{}: (1, {})} | custom-call | tf_op jit(solution)/shard_map/pallas_call | solution.py:71
  (118 shorter events, 33.0 us)
Async XLA Ops:
  7.2 122.1 %copy-start = (f32[64,1024]{1,0:T(8,128)S(1)}, f32[64,1024]{1,0:T(8,128)}, u32[]{:S(2)}) copy-start(f32[64,1024]{1,0:T(8,128)} %param.12) | copy-start | bytes 786436
  7.2 41.6 %reduce-scatter.3.cloned.1.call-start = ((), (), s32[]{:S(2)}) async-start(), calls=%async_computation.3 | async-start | bytes 3276800 | tf_op jit(solution)/shard_map/reduce_scatter | solution.py:111
  11.3 75.5 %reduce-scatter.5.cloned.1.call-start = ((), (), s32[]{:S(2)}) async-start(), calls=%async_computation.4 | async-start | bytes 3276800 | tf_op jit(solution)/shard_map/reduce_scatter | solution.py:111
  15.3 0.7 copy-start.13
  51.8 38.8 %copy-start.12 = (bf16[1,13,1024]{2,1,0:T(8,128)(2,1)S(1)}, bf16[1,13,1024]{2,1,0:T(8,128)(2,1)}, u32[]{:S(2)}) copy-start(bf16[1,13,1024]{2,1,0:T(8,128)(2,1)} %param.13) | copy-start | bytes 79876
  51.8 72.1 %all-to-all-start = ((bf16[8,40,16,128]{3,2,1,0:T(8,128)(2,1)}), bf16[8,40,16,128]{3,2,1,0:T(8,128)(2,1)S(1)}, u32[]{:S(2)}, u32[]{:S(2)}) async-start(bf16[8,40,16,128]{3,2,1,0:T(8,128)(2,1)} %bitcast.4), calls=%async_computation.1 | async-start | bytes 2621440 | tf_op jit(solution)/shard_map/all_to_all | solution.py:125
  57.5 177.2 %all-gather.5.cloned.1.call-start = ((), (), s32[]{:S(2)}) async-start(), calls=%async_computation.5 | async-start | bytes 3276800 | tf_op jit(solution)/shard_map/all_gather | solution.py:176
  86.7 10.7 %copy-start.7 = (bf16[1,160,16,128]{3,2,1,0:T(8,128)(2,1)S(1)}, bf16[1,160,16,128]{3,2,1,0:T(8,128)(2,1)}, u32[]{:S(2)}) copy-start(bf16[1,160,16,128]{3,2,1,0:T(8,128)(2,1)} %reduce-scatter.5.cloned.1.call-done) | copy-start | bytes 1966084
  89.2 21.2 %collective-permute-start = (bf16[40,16,128]{2,1,0:T(8,128)(2,1)}, bf16[40,16,128]{2,1,0:T(8,128)(2,1)}, u32[]{:S(2)}, u32[]{:S(2)}) collective-permute-start(bf16[40,16,128]{2,1,0:T(8,128)(2,1)} %gather_fusion.2), channel_id=1, source_target_pairs={{0,1},{1,2},{2,3},{3,4},{4,5},{5,6},{6,7},{7,0},{8,9},{9,10},{10,1... | collective-permute-start | bytes 491528 | tf_op jit(solution)/shard_map/ppermute | solution.py:121
  96.0 16.8 %collective-permute-start.1 = (bf16[40,16,128]{2,1,0:T(8,128)(2,1)}, bf16[40,16,128]{2,1,0:T(8,128)(2,1)}, u32[]{:S(2)}, u32[]{:S(2)}) collective-permute-start(bf16[40,16,128]{2,1,0:T(8,128)(2,1)} %gather_fusion.3), channel_id=1, source_target_pairs={{0,2},{1,3},{2,4},{3,5},{4,6},{5,7},{6,0},{7,1},{8,10},{9,11},{10,... | collective-permute-start | bytes 491528 | tf_op jit(solution)/shard_map/ppermute | solution.py:121
  98.7 16.7 %collective-permute-start.2 = (bf16[40,16,128]{2,1,0:T(8,128)(2,1)}, bf16[40,16,128]{2,1,0:T(8,128)(2,1)}, u32[]{:S(2)}, u32[]{:S(2)}) collective-permute-start(bf16[40,16,128]{2,1,0:T(8,128)(2,1)} %gather_fusion.4), channel_id=1, source_target_pairs={{0,3},{1,4},{2,5},{3,6},{4,7},{5,0},{6,1},{7,2},{8,11},{9,12},{10,... | collective-permute-start | bytes 491528 | tf_op jit(solution)/shard_map/ppermute | solution.py:121
  102.4 15.6 %collective-permute-start.3 = (bf16[40,16,128]{2,1,0:T(8,128)(2,1)}, bf16[40,16,128]{2,1,0:T(8,128)(2,1)}, u32[]{:S(2)}, u32[]{:S(2)}) collective-permute-start(bf16[40,16,128]{2,1,0:T(8,128)(2,1)} %gather_fusion.5), channel_id=1, source_target_pairs={{0,4},{1,5},{2,6},{3,7},{4,0},{5,1},{6,2},{7,3},{8,12},{9,13},{10,... | collective-permute-start | bytes 491528 | tf_op jit(solution)/shard_map/ppermute | solution.py:121
  105.1 2.7 copy-start.8
  105.1 13.8 %collective-permute-start.4 = (bf16[40,16,128]{2,1,0:T(8,128)(2,1)}, bf16[40,16,128]{2,1,0:T(8,128)(2,1)}, u32[]{:S(2)}, u32[]{:S(2)}) collective-permute-start(bf16[40,16,128]{2,1,0:T(8,128)(2,1)} %gather_fusion.6), channel_id=1, source_target_pairs={{0,5},{1,6},{2,7},{3,0},{4,1},{5,2},{6,3},{7,4},{8,13},{9,14},{10,... | collective-permute-start | bytes 491528 | tf_op jit(solution)/shard_map/ppermute | solution.py:121
  110.4 13.4 %collective-permute-start.5 = (bf16[40,16,128]{2,1,0:T(8,128)(2,1)}, bf16[40,16,128]{2,1,0:T(8,128)(2,1)S(1)}, u32[]{:S(2)}, u32[]{:S(2)}) collective-permute-start(bf16[40,16,128]{2,1,0:T(8,128)(2,1)} %gather_fusion.7), channel_id=1, source_target_pairs={{0,6},{1,7},{2,0},{3,1},{4,2},{5,3},{6,4},{7,5},{8,14},{9,15},{10,... | collective-permute-start | bytes 491528 | tf_op jit(solution)/shard_map/ppermute | solution.py:121
  112.8 11.1 %collective-permute-start.6 = (bf16[40,16,128]{2,1,0:T(8,128)(2,1)}, bf16[40,16,128]{2,1,0:T(8,128)(2,1)S(1)}, u32[]{:S(2)}, u32[]{:S(2)}) collective-permute-start(bf16[40,16,128]{2,1,0:T(8,128)(2,1)} %gather_fusion.8), channel_id=1, source_target_pairs={{0,7},{1,0},{2,1},{3,2},{4,3},{5,4},{6,5},{7,6},{8,15},{9,8},{10,9... | collective-permute-start | bytes 491528 | tf_op jit(solution)/shard_map/ppermute | solution.py:121
  123.9 1.1 copy-start.4
  129.3 1.5 copy-start.1
  130.8 1.5 copy-start.9
  133.3 2.5 collective-permute-start.7
  137.0 10.2 %copy-start.5 = (bf16[2688,128]{1,0:T(8,128)(2,1)}, bf16[2688,128]{1,0:T(8,128)(2,1)S(1)}, u32[]{:S(2)}) copy-start(bf16[2688,128]{1,0:T(8,128)(2,1)S(1)} %add_convert_fusion) | copy-start | bytes 2064388
  137.1 10.2 %collective-permute-start.8 = (bf16[1344,128]{1,0:T(8,128)(2,1)S(1)}, bf16[1344,128]{1,0:T(8,128)(2,1)S(1)}, u32[]{:S(2)}, u32[]{:S(2)}) collective-permute-start(bf16[1344,128]{1,0:T(8,128)(2,1)S(1)} %dynamic-slice_bitcast_fusion), channel_id=1, source_target_pairs={{0,16},{8,24},{16,0},{24,8},{1,17},{9,25},{17,1},{25,9},{2,18},{10... | collective-permute-start | bytes 1032200 | tf_op jit(solution)/shard_map/ppermute | solution.py:32
  148.2 2.5 collective-permute-start.9
  152.0 0.8 copy-start.6
  152.0 2.4 copy-start.2
  152.8 7.7 %copy-start.3 = (f32[2560,128]{1,0:T(8,128)}, f32[2560,128]{1,0:T(8,128)S(1)}, u32[]{:S(2)}) copy-start(f32[2560,128]{1,0:T(8,128)S(1)} %pad_maximum_fusion) | copy-start | bytes 3932164
  163.1 13.1 %collective-permute-start.10 = (bf16[40,16,128]{2,1,0:T(8,128)(2,1)S(1)}, bf16[40,16,128]{2,1,0:T(8,128)(2,1)S(1)}, u32[]{:S(2)}, u32[]{:S(2)}) collective-permute-start(bf16[40,16,128]{2,1,0:T(8,128)(2,1)S(1)} %get-tuple-element.43), channel_id=1, source_target_pairs={{0,1},{1,2},{2,3},{3,4},{4,5},{5,6},{6,7},{7,0},{8,9},{9,10},{10,1... | collective-permute-start | bytes 491528 | tf_op jit(solution)/shard_map/ppermute | solution.py:169
  166.3 11.0 %collective-permute-start.11 = (bf16[40,16,128]{2,1,0:T(8,128)(2,1)S(1)}, bf16[40,16,128]{2,1,0:T(8,128)(2,1)S(1)}, u32[]{:S(2)}, u32[]{:S(2)}) collective-permute-start(bf16[40,16,128]{2,1,0:T(8,128)(2,1)S(1)} %get-tuple-element.42), channel_id=1, source_target_pairs={{0,2},{1,3},{2,4},{3,5},{4,6},{5,7},{6,0},{7,1},{8,10},{9,11},{10,... | collective-permute-start | bytes 491528 | tf_op jit(solution)/shard_map/ppermute | solution.py:169
  169.5 20.1 %collective-permute-start.12 = (bf16[40,16,128]{2,1,0:T(8,128)(2,1)S(1)}, bf16[40,16,128]{2,1,0:T(8,128)(2,1)S(1)}, u32[]{:S(2)}, u32[]{:S(2)}) collective-permute-start(bf16[40,16,128]{2,1,0:T(8,128)(2,1)S(1)} %get-tuple-element.41), channel_id=1, source_target_pairs={{0,3},{1,4},{2,5},{3,6},{4,7},{5,0},{6,1},{7,2},{8,11},{9,12},{10,... | collective-permute-start | bytes 491528 | tf_op jit(solution)/shard_map/ppermute | solution.py:169
  170.7 19.7 %collective-permute-start.13 = (bf16[40,16,128]{2,1,0:T(8,128)(2,1)S(1)}, bf16[40,16,128]{2,1,0:T(8,128)(2,1)S(1)}, u32[]{:S(2)}, u32[]{:S(2)}) collective-permute-start(bf16[40,16,128]{2,1,0:T(8,128)(2,1)S(1)} %get-tuple-element.40), channel_id=1, source_target_pairs={{0,4},{1,5},{2,6},{3,7},{4,0},{5,1},{6,2},{7,3},{8,12},{9,13},{10,... | collective-permute-start | bytes 491528 | tf_op jit(solution)/shard_map/ppermute | solution.py:169
  172.6 18.5 %collective-permute-start.14 = (bf16[40,16,128]{2,1,0:T(8,128)(2,1)S(1)}, bf16[40,16,128]{2,1,0:T(8,128)(2,1)S(1)}, u32[]{:S(2)}, u32[]{:S(2)}) collective-permute-start(bf16[40,16,128]{2,1,0:T(8,128)(2,1)S(1)} %get-tuple-element.39), channel_id=1, source_target_pairs={{0,5},{1,6},{2,7},{3,0},{4,1},{5,2},{6,3},{7,4},{8,13},{9,14},{10,... | collective-permute-start | bytes 491528 | tf_op jit(solution)/shard_map/ppermute | solution.py:169
  176.2 15.5 %collective-permute-start.15 = (bf16[40,16,128]{2,1,0:T(8,128)(2,1)S(1)}, bf16[40,16,128]{2,1,0:T(8,128)(2,1)S(1)}, u32[]{:S(2)}, u32[]{:S(2)}) collective-permute-start(bf16[40,16,128]{2,1,0:T(8,128)(2,1)S(1)} %get-tuple-element.38), channel_id=1, source_target_pairs={{0,6},{1,7},{2,0},{3,1},{4,2},{5,3},{6,4},{7,5},{8,14},{9,15},{10,... | collective-permute-start | bytes 491528 | tf_op jit(solution)/shard_map/ppermute | solution.py:169
  177.3 15.1 %collective-permute-start.16 = (bf16[40,16,128]{2,1,0:T(8,128)(2,1)S(1)}, bf16[40,16,128]{2,1,0:T(8,128)(2,1)S(1)}, u32[]{:S(2)}, u32[]{:S(2)}) collective-permute-start(bf16[40,16,128]{2,1,0:T(8,128)(2,1)S(1)} %get-tuple-element.37), channel_id=1, source_target_pairs={{0,7},{1,0},{2,1},{3,2},{4,3},{5,4},{6,5},{7,6},{8,15},{9,8},{10,9... | collective-permute-start | bytes 491528 | tf_op jit(solution)/shard_map/ppermute | solution.py:169
  196.0 71.0 %all-gather.7.cloned.1.call-start = ((), (), s32[]{:S(2)}) async-start(), calls=%async_computation.6 | async-start | bytes 3276800 | tf_op jit(solution)/shard_map/all_gather | solution.py:176
  198.4 15.9 %collective-permute-start.17 = (bf16[40,16,128]{2,1,0:T(8,128)(2,1)S(1)}, bf16[40,16,128]{2,1,0:T(8,128)(2,1)S(1)}, u32[]{:S(2)}, u32[]{:S(2)}) collective-permute-start(bf16[40,16,128]{2,1,0:T(8,128)(2,1)S(1)} %get-tuple-element.35), channel_id=1, source_target_pairs={{0,1},{1,2},{2,3},{3,4},{4,5},{5,6},{6,7},{7,0},{8,9},{9,10},{10,1... | collective-permute-start | bytes 491528 | tf_op jit(solution)/shard_map/ppermute | solution.py:169
  202.2 13.0 %collective-permute-start.18 = (bf16[40,16,128]{2,1,0:T(8,128)(2,1)S(1)}, bf16[40,16,128]{2,1,0:T(8,128)(2,1)S(1)}, u32[]{:S(2)}, u32[]{:S(2)}) collective-permute-start(bf16[40,16,128]{2,1,0:T(8,128)(2,1)S(1)} %get-tuple-element.34), channel_id=1, source_target_pairs={{0,2},{1,3},{2,4},{3,5},{4,6},{5,7},{6,0},{7,1},{8,10},{9,11},{10,... | collective-permute-start | bytes 491528 | tf_op jit(solution)/shard_map/ppermute | solution.py:169
  208.4 18.4 %collective-permute-start.19 = (bf16[40,16,128]{2,1,0:T(8,128)(2,1)S(1)}, bf16[40,16,128]{2,1,0:T(8,128)(2,1)S(1)}, u32[]{:S(2)}, u32[]{:S(2)}) collective-permute-start(bf16[40,16,128]{2,1,0:T(8,128)(2,1)S(1)} %get-tuple-element.33), channel_id=1, source_target_pairs={{0,3},{1,4},{2,5},{3,6},{4,7},{5,0},{6,1},{7,2},{8,11},{9,12},{10,... | collective-permute-start | bytes 491528 | tf_op jit(solution)/shard_map/ppermute | solution.py:169
  208.4 19.1 %collective-permute-start.20 = (bf16[40,16,128]{2,1,0:T(8,128)(2,1)S(1)}, bf16[40,16,128]{2,1,0:T(8,128)(2,1)S(1)}, u32[]{:S(2)}, u32[]{:S(2)}) collective-permute-start(bf16[40,16,128]{2,1,0:T(8,128)(2,1)S(1)} %get-tuple-element.32), channel_id=1, source_target_pairs={{0,4},{1,5},{2,6},{3,7},{4,0},{5,1},{6,2},{7,3},{8,12},{9,13},{10,... | collective-permute-start | bytes 491528 | tf_op jit(solution)/shard_map/ppermute | solution.py:169
  210.5 17.6 %collective-permute-start.21 = (bf16[40,16,128]{2,1,0:T(8,128)(2,1)S(1)}, bf16[40,16,128]{2,1,0:T(8,128)(2,1)S(1)}, u32[]{:S(2)}, u32[]{:S(2)}) collective-permute-start(bf16[40,16,128]{2,1,0:T(8,128)(2,1)S(1)} %get-tuple-element.31), channel_id=1, source_target_pairs={{0,5},{1,6},{2,7},{3,0},{4,1},{5,2},{6,3},{7,4},{8,13},{9,14},{10,... | collective-permute-start | bytes 491528 | tf_op jit(solution)/shard_map/ppermute | solution.py:169
  214.2 14.6 %collective-permute-start.22 = (bf16[40,16,128]{2,1,0:T(8,128)(2,1)S(1)}, bf16[40,16,128]{2,1,0:T(8,128)(2,1)S(1)}, u32[]{:S(2)}, u32[]{:S(2)}) collective-permute-start(bf16[40,16,128]{2,1,0:T(8,128)(2,1)S(1)} %get-tuple-element.30), channel_id=1, source_target_pairs={{0,6},{1,7},{2,0},{3,1},{4,2},{5,3},{6,4},{7,5},{8,14},{9,15},{10,... | collective-permute-start | bytes 491528 | tf_op jit(solution)/shard_map/ppermute | solution.py:169
  215.3 14.3 %collective-permute-start.23 = (bf16[40,16,128]{2,1,0:T(8,128)(2,1)S(1)}, bf16[40,16,128]{2,1,0:T(8,128)(2,1)S(1)}, u32[]{:S(2)}, u32[]{:S(2)}) collective-permute-start(bf16[40,16,128]{2,1,0:T(8,128)(2,1)S(1)} %get-tuple-element.29), channel_id=1, source_target_pairs={{0,7},{1,0},{2,1},{3,2},{4,3},{5,4},{6,5},{7,6},{8,15},{9,8},{10,9... | collective-permute-start | bytes 491528 | tf_op jit(solution)/shard_map/ppermute | solution.py:169
  229.5 4.4 %copy-start.10 = (f32[13,1024]{1,0:T(8,128)S(1)}, f32[13,1024]{1,0:T(8,128)}, u32[]{:S(2)}) copy-start(f32[13,1024]{1,0:T(8,128)} %param.14) | copy-start | bytes 159748
  229.5 4.4 %copy-start.11 = (f32[13,1024]{1,0:T(8,128)S(1)}, f32[13,1024]{1,0:T(8,128)}, u32[]{:S(2)}) copy-start(f32[13,1024]{1,0:T(8,128)} %param.15) | copy-start | bytes 159748
Sparse Core Ops, SparseCore 0:
  11.4 37.3 reduce-scatter.2
  52.0 34.6 reduce-scatter.4
  196.1 32.1 all-gather.4
  233.2 33.7 all-gather.6

commit v15 on v14

--- a/solution.py
+++ b/solution.py
@@ -113,10 +113,9 @@
             me = lax.axis_index("dev")
             part_rows = summed.shape[1]
             arrived = jnp.zeros((slot_count, dev_count * part_rows, width), summed.dtype)
+            picked = jnp.take(summed, source_unit, axis=0, mode="clip").reshape(dev_count, slot_count, part_rows, width)
             for k in range(dev_count):
-                dest = (me + k) % dev_count
-                units = lax.dynamic_slice_in_dim(source_unit, dest * slot_count, slot_count)
-                block = jnp.take(summed, units, axis=0, mode="clip")
+                block = lax.dynamic_index_in_dim(picked, (me + k) % dev_count, 0, keepdims=False)
                 if k:
                     block = lax.ppermute(block, "dev", [(i, (i + k) % dev_count) for i in range(dev_count)])
                 arrived = lax.dynamic_update_slice_in_dim(arrived, block, ((me - k) % dev_count) * part_rows, 1)

time: 279 us -> 277 us (level)
  local copies, waits for them, and re-layouts: 46.6 us -> 39.3 us
  starting transfers between devices: 51.8 us -> 56 us
    gather x8 -> x1, local copies, waits for them, and re-layouts: 13.4 us -> 2.04 us  [body(): jnp.take(summed, source_unit, axis=0, mode='clip')]
    ppermute x14, starting transfers between devices: 33.2 us -> 37.4 us  [body(): lax.ppermute(out_rows, 'dev', [(i, (i + k) % dev_count) for i in range(de...]
    unnamed x40 -> x32, local copies, waits for them, and re-layouts: 12 us -> 11.2 us
  transfers between devices with their start and end apart: 29 -> 29, of which waited for: 13 -> 13; matrix products, arithmetic and copies ran while one was open for 19% -> 17% of each run, Pallas kernels for 3% -> 3%
where the time goes in v15:
time: 277 us; the launch traced here: 276 us
  waiting for transfers between devices  117 us (42%)
  starting transfers between devices  56 us (20%)
  local copies, waits for them, and re-layouts  39.3 us (14%)
  matrix products  23 us (8%)
  Pallas kernels  16 us (6%)
  between operations  14.1 us (5%)
  other arithmetic  10.7 us (4%)
    reduce_scatter x2, waiting for transfers between devices, body(): summed = lax.psum_scatter(half, 'rep', scatter_dimension=0, tiled=True)[0]  61.7 us
    ppermute x14, starting transfers between devices, body(): lax.ppermute(out_rows, 'dev', [(i, (i + k) % dev_count) for i in range(de...  37.4 us
    ppermute x14, waiting for transfers between devices, body(): lax.ppermute(out_rows, 'dev', [(i, (i + k) % dev_count) for i in range(de...  18.8 us
    all_gather x2, waiting for transfers between devices, body(): gathered = lax.all_gather(picked, 'rep', axis=2, tiled=True)  14.7 us
    dot_general x1, matrix products, fresh(): jnp.einsum('skb,kq->sbq', coeffs, basis_cols, precision=lax.Precision.HIGH)  13.9 us
    ppermute x7, starting transfers between devices, body(): lax.ppermute(block, 'dev', [(i, (i + k) % dev_count) for i in range(dev_c...  12.1 us
    unnamed x32, local copies, waits for them, and re-layouts  11.2 us
    ppermute x1, waiting for transfers between devices, rep_sum(): across = lax.ppermute(part, 'rep', [(i, i ^ 2) for i in range(4)])  9.54 us
  transfers between devices with their start and end apart: 29, of which 13 were waited for; matrix products, arithmetic and copies ran while one was open for 17% of the time, Pallas kernels for 3%

profile of v15, /device:TPU:0, one launch (start us, length us, event | category | flops | bytes accessed | tf_op | source)
XLA Modules:
  0.0 275.9 jit_solution(1026103771856799350)
XLA Ops:
  7.2 4.0 %shard_map.119 = bf16[4,160,16,128]{3,2,1,0:T(8,128)(2,1)} custom-call(bf16[160,16,1024]{2,1,0:T(8,128)(2,1)} %bitcast.65), custom_call_target="tpu_custom_call" | custom-call | tf_op jit(solution)/shard_map/pallas_call | solution.py:47
  11.3 4.0 %shard_map.120 = bf16[4,160,16,128]{3,2,1,0:T(8,128)(2,1)} custom-call(bf16[160,16,1024]{2,1,0:T(8,128)(2,1)} %bitcast.66), custom_call_target="tpu_custom_call" | custom-call | tf_op jit(solution)/shard_map/pallas_call | solution.py:47
  16.3 32.4 %reduce-scatter.3.cloned.1.call-done = bf16[1,160,16,128]{3,2,1,0:T(8,128)(2,1)} async-done(((bf16[4,160,16,128]{3,2,1,0:T(8,128)(2,1)}), bf16[1,160,16,128]{3,2,1,0:T(8,128)(2,1)}) %reduce-scatter.3.cloned.1.call-update) | async-done | bytes 655376 | tf_op jit(solution)/shard_map/reduce_scatter | solution.py:111
  48.8 3.0 %gather_fusion = bf16[320,16,128]{2,1,0:T(8,128)(2,1)} fusion(bf16[160,16,128]{2,1,0:T(8,128)(2,1)} %bitcast.79, s32[1024]{0:T(1024)S(1)} %pad_clamp_fusion.1), kind=kCustom, calls=%fused_computation | custom fusion | bytes 2622720 | tf_op jit(solution)/shard_map/jit(_take)/gather | solution.py:123
  51.8 5.5 %all-to-all-start = ((bf16[8,40,16,128]{3,2,1,0:T(8,128)(2,1)}), bf16[8,40,16,128]{3,2,1,0:T(8,128)(2,1)S(1)}, u32[]{:S(2)}, u32[]{:S(2)}) async-start(bf16[8,40,16,128]{3,2,1,0:T(8,128)(2,1)} %bitcast.4), calls=%async_computation.1 | async-start | bytes 2621440 | tf_op jit(solution)/shard_map/all_to_all | solution.py:124
  57.5 29.3 %reduce-scatter.5.cloned.1.call-done = bf16[1,160,16,128]{3,2,1,0:T(8,128)(2,1)} async-done(((bf16[4,160,16,128]{3,2,1,0:T(8,128)(2,1)}), bf16[1,160,16,128]{3,2,1,0:T(8,128)(2,1)}) %reduce-scatter.5.cloned.1.call-update) | async-done | bytes 655376 | tf_op jit(solution)/shard_map/reduce_scatter | solution.py:111
  86.7 2.0 gather_fusion.1
  89.8 1.5 collective-permute-start
  91.2 1.4 pad.4
  92.6 1.4 reshape.55
  94.0 1.5 collective-permute-start.1
  95.5 2.4 collective-permute-start.2
  97.9 1.4 collective-permute-start.3
  99.3 2.4 collective-permute-start.4
  101.7 1.4 broadcast_in_dim.66
  103.8 1.4 collective-permute-start.5
  105.9 1.4 collective-permute-start.6
  108.0 5.3 %collective-permute-done.2 = bf16[40,16,128]{2,1,0:T(8,128)(2,1)S(1)} collective-permute-done((bf16[40,16,128]{2,1,0:T(8,128)(2,1)}, bf16[40,16,128]{2,1,0:T(8,128)(2,1)S(1)}, u32[]{:S(2)}, u32[]{:S(2)}) %collective-permute-start.2) | collective-permute-done | bytes 163872 | tf_op jit(solution)/shard_map/ppermute | solution.py:120
  114.0 1.9 collective-permute-done.3
  119.3 4.0 %slice_subtract_fusion = (f32[40,128,128]{2,1,0:T(8,128)S(1)}, f32[40,128,128]{2,1,0:T(8,128)S(1)}) fusion(f32[40,128,256]{2,1,0:T(8,128)} %bitcast.63, bf16[40,128,128]{2,1,0:T(8,128)(2,1)} %constant_dynamic-update-slice_fusion.14, f32[40,128,128]{2,1,0:T(8,128)S(1)} %bitcast.70), kind=kLoop, calls=%fused_computation.13 | loop fusion | flops 2621440 | bytes 14417920 | tf_op jit(solution)/shard_map/sub | solution.py:131
  123.3 1.5 fusion.11
  124.8 1.5 fusion.4
  127.3 2.5 collective-permute-done.7
  131.7 9.5 %collective-permute-done.8 = bf16[1344,128]{1,0:T(8,128)(2,1)S(1)} collective-permute-done((bf16[1344,128]{1,0:T(8,128)(2,1)S(1)}, bf16[1344,128]{1,0:T(8,128)(2,1)S(1)}, u32[]{:S(2)}, u32[]{:S(2)}) %collective-permute-start.8) | collective-permute-done | bytes 344096 | tf_op jit(solution)/shard_map/ppermute | solution.py:32
  142.4 2.3 collective-permute-done.9
  146.8 1.6 copy-done.2
  148.4 6.1 %fusion.3 = bf16[40,128,256]{2,1,0:T(8,128)(2,1)S(1)} fusion(f32[40,128,128]{2,1,0:T(8,128)S(1)} %get-tuple-element.14, f32[40,128,128]{2,1,0:T(8,128)S(1)} %copy-done.2, pred[40]{0:T(512)(128)(4,1)S(1)} %get-tuple-element.18, f32[40,64,128]{2,1,0:T(8,128)S(1)} %bitcast.68, f32[64,1024]{1,0:T(8,128)S(1)} %copy-done, s32[]{:T(128)S(6)} %select_n.256, ...), kind=kOutput, calls=%fused_computation.9 | convolution fusion | flops 512491520 | bytes 19726852 | tf_op jit(solution)/shard_map/skb,kq->sbq/dot_general | solution.py:157
  154.6 1.5 fusion.19
  157.1 4.2 %collective-permute-start.10 = (bf16[40,16,128]{2,1,0:T(8,128)(2,1)S(1)}, bf16[40,16,128]{2,1,0:T(8,128)(2,1)S(1)}, u32[]{:S(2)}, u32[]{:S(2)}) collective-permute-start(bf16[40,16,128]{2,1,0:T(8,128)(2,1)S(1)} %get-tuple-element.43), channel_id=1, source_target_pairs={{0,1},{1,2},{2,3},{3,4},{4,5},{5,6},{6,7},{7,0},{8,9},{9,10},{10,1... | collective-permute-start | bytes 491528 | tf_op jit(solution)/shard_map/ppermute | solution.py:168
  161.3 6.1 %collective-permute-start.11 = (bf16[40,16,128]{2,1,0:T(8,128)(2,1)S(1)}, bf16[40,16,128]{2,1,0:T(8,128)(2,1)S(1)}, u32[]{:S(2)}, u32[]{:S(2)}) collective-permute-start(bf16[40,16,128]{2,1,0:T(8,128)(2,1)S(1)} %get-tuple-element.42), channel_id=1, source_target_pairs={{0,2},{1,3},{2,4},{3,5},{4,6},{5,7},{6,0},{7,1},{8,10},{9,11},{10,... | collective-permute-start | bytes 491528 | tf_op jit(solution)/shard_map/ppermute | solution.py:168
  167.4 1.5 collective-permute-start.12
  168.9 1.8 collective-permute-start.13
  170.7 3.4 %collective-permute-start.14 = (bf16[40,16,128]{2,1,0:T(8,128)(2,1)S(1)}, bf16[40,16,128]{2,1,0:T(8,128)(2,1)S(1)}, u32[]{:S(2)}, u32[]{:S(2)}) collective-permute-start(bf16[40,16,128]{2,1,0:T(8,128)(2,1)S(1)} %get-tuple-element.39), channel_id=1, source_target_pairs={{0,5},{1,6},{2,7},{3,0},{4,1},{5,2},{6,3},{7,4},{8,13},{9,14},{10,... | collective-permute-start | bytes 491528 | tf_op jit(solution)/shard_map/ppermute | solution.py:168
  175.5 2.4 collective-permute-start.16
  178.6 9.2 %collective-permute-done.12 = bf16[40,16,128]{2,1,0:T(8,128)(2,1)S(1)} collective-permute-done((bf16[40,16,128]{2,1,0:T(8,128)(2,1)S(1)}, bf16[40,16,128]{2,1,0:T(8,128)(2,1)S(1)}, u32[]{:S(2)}, u32[]{:S(2)}) %collective-permute-start.12) | collective-permute-done | bytes 163872 | tf_op jit(solution)/shard_map/ppermute | solution.py:168
  191.2 2.9 %gather_fusion.2 = bf16[160,16,128]{2,1,0:T(8,128)(2,1)} fusion(bf16[320,16,128]{2,1,0:T(8,128)(2,1)} %constant_dynamic-update-slice_fusion, s32[1024]{0:T(1024)S(1)} %pad_clamp_fusion), kind=kCustom, calls=%fused_computation.2 | custom fusion | bytes 1311360 | tf_op jit(solution)/shard_map/jit(_take)/gather | solution.py:171
  194.4 2.3 constant_dynamic-slice_fusion
  196.7 3.9 %collective-permute-start.17 = (bf16[40,16,128]{2,1,0:T(8,128)(2,1)S(1)}, bf16[40,16,128]{2,1,0:T(8,128)(2,1)S(1)}, u32[]{:S(2)}, u32[]{:S(2)}) collective-permute-start(bf16[40,16,128]{2,1,0:T(8,128)(2,1)S(1)} %get-tuple-element.35), channel_id=1, source_target_pairs={{0,1},{1,2},{2,3},{3,4},{4,5},{5,6},{6,7},{7,0},{8,9},{9,10},{10,1... | collective-permute-start | bytes 491528 | tf_op jit(solution)/shard_map/ppermute | solution.py:168
  200.6 6.1 %collective-permute-start.18 = (bf16[40,16,128]{2,1,0:T(8,128)(2,1)S(1)}, bf16[40,16,128]{2,1,0:T(8,128)(2,1)S(1)}, u32[]{:S(2)}, u32[]{:S(2)}) collective-permute-start(bf16[40,16,128]{2,1,0:T(8,128)(2,1)S(1)} %get-tuple-element.34), channel_id=1, source_target_pairs={{0,2},{1,3},{2,4},{3,5},{4,6},{5,7},{6,0},{7,1},{8,10},{9,11},{10,... | collective-permute-start | bytes 491528 | tf_op jit(solution)/shard_map/ppermute | solution.py:168
  206.7 1.9 collective-permute-start.20
  208.6 3.4 %collective-permute-start.21 = (bf16[40,16,128]{2,1,0:T(8,128)(2,1)S(1)}, bf16[40,16,128]{2,1,0:T(8,128)(2,1)S(1)}, u32[]{:S(2)}, u32[]{:S(2)}) collective-permute-start(bf16[40,16,128]{2,1,0:T(8,128)(2,1)S(1)} %get-tuple-element.31), channel_id=1, source_target_pairs={{0,5},{1,6},{2,7},{3,0},{4,1},{5,2},{6,3},{7,4},{8,13},{9,14},{10,... | collective-permute-start | bytes 491528 | tf_op jit(solution)/shard_map/ppermute | solution.py:168
  213.6 1.7 collective-permute-start.23
  215.9 8.9 %collective-permute-done.19 = bf16[40,16,128]{2,1,0:T(8,128)(2,1)S(1)} collective-permute-done((bf16[40,16,128]{2,1,0:T(8,128)(2,1)S(1)}, bf16[40,16,128]{2,1,0:T(8,128)(2,1)S(1)}, u32[]{:S(2)}, u32[]{:S(2)}) %collective-permute-start.19) | collective-permute-done | bytes 163872 | tf_op jit(solution)/shard_map/ppermute | solution.py:168
  228.4 2.9 %gather_fusion.3 = bf16[160,16,128]{2,1,0:T(8,128)(2,1)} fusion(bf16[320,16,128]{2,1,0:T(8,128)(2,1)} %constant_dynamic-update-slice_fusion.7, s32[1024]{0:T(1024)S(1)} %pad_clamp_fusion), kind=kCustom, calls=%fused_computation.3 | custom fusion | bytes 1311360 | tf_op jit(solution)/shard_map/jit(_take)/gather | solution.py:171
  232.8 4.0 %shard_map.121.base_ref = bf16[160,16,1024]{2,1,0:T(8,128)(2,1)} custom-call(bf16[160,16,512]{2,1,0:T(8,128)(2,1)} %all-gather.5.cloned.1.call-done.x_ref), custom_call_target="tpu_custom_call" | custom-call | tf_op jit(solution)/shard_map/pallas_call | solution.py:68
  236.8 13.9 %select_bitcast_fusion = (f32[1,40,128,256]{3,2,1,0:T(8,128)}, f32[1,40,128,256]{3,2,1,0:T(8,128)}) fusion(f32[40,128,256]{2,1,0:T(8,128)} %bitcast.67, pred[40]{0:T(512)(128)(4,1)S(1)} %get-tuple-element.17, f32[40,128,256]{2,1,0:T(8,128)} %bitcast.64, f32[40,128,128]{2,1,0:T(8,128)S(1)} %get-tuple-element.14, f32[40,128,128]{2,1,0:T(8,128)} %copy-done.1, ...), kind=kOutput, calls=%fused_computation.11 | convolution fusion | flops 516423680 | bytes 27591684 | tf_op jit(solution)/shard_map/skb,kq->sbq/dot_general | solution.py:149
  250.7 14.7 %all-gather.7.cloned.1.call-done.a_ref = bf16[160,16,512]{2,1,0:T(8,128)(2,1)} async-done(((bf16[160,16,128]{2,1,0:T(8,128)(2,1)}), bf16[160,16,512]{2,1,0:T(8,128)(2,1)}) %all-gather.7.cloned.1.call-update) | async-done | bytes 2621456 | tf_op jit(solution)/shard_map/all_gather | solution.py:175
  265.4 4.0 %shard_map.122 = bf16[160,16,1024]{2,1,0:T(8,128)(2,1)} custom-call(bf16[160,16,512]{2,1,0:T(8,128)(2,1)} %all-gather.7.cloned.1.call-done.a_ref, bf16[160,16,1024]{2,1,0:T(8,128)(2,1)} %shard_map.121.base_ref), custom_call_target="tpu_custom_call", output_to_operand_aliasing={{}: (1, {})} | custom-call | tf_op jit(solution)/shard_map/pallas_call | solution.py:71
  (95 shorter events, 28.4 us)
Async XLA Ops:
  7.2 116.2 %copy-start = (f32[64,1024]{1,0:T(8,128)S(1)}, f32[64,1024]{1,0:T(8,128)}, u32[]{:S(2)}) copy-start(f32[64,1024]{1,0:T(8,128)} %param.12) | copy-start | bytes 786436
  7.2 41.6 %reduce-scatter.3.cloned.1.call-start = ((), (), s32[]{:S(2)}) async-start(), calls=%async_computation.3 | async-start | bytes 3276800 | tf_op jit(solution)/shard_map/reduce_scatter | solution.py:111
  11.3 75.5 %reduce-scatter.5.cloned.1.call-start = ((), (), s32[]{:S(2)}) async-start(), calls=%async_computation.4 | async-start | bytes 3276800 | tf_op jit(solution)/shard_map/reduce_scatter | solution.py:111
  15.3 0.7 copy-start.9
  51.8 66.9 %all-to-all-start = ((bf16[8,40,16,128]{3,2,1,0:T(8,128)(2,1)}), bf16[8,40,16,128]{3,2,1,0:T(8,128)(2,1)S(1)}, u32[]{:S(2)}, u32[]{:S(2)}) async-start(bf16[8,40,16,128]{3,2,1,0:T(8,128)(2,1)} %bitcast.4), calls=%async_computation.1 | async-start | bytes 2621440 | tf_op jit(solution)/shard_map/all_to_all | solution.py:124
  57.3 175.5 %all-gather.5.cloned.1.call-start = ((), (), s32[]{:S(2)}) async-start(), calls=%async_computation.5 | async-start | bytes 3276800 | tf_op jit(solution)/shard_map/all_gather | solution.py:175
  89.8 14.0 %collective-permute-start = (bf16[40,16,128]{2,1,0:T(8,128)(2,1)}, bf16[40,16,128]{2,1,0:T(8,128)(2,1)S(1)}, u32[]{:S(2)}, u32[]{:S(2)}) collective-permute-start(bf16[40,16,128]{2,1,0:T(8,128)(2,1)} %get-tuple-element.51), channel_id=1, source_target_pairs={{0,1},{1,2},{2,3},{3,4},{4,5},{5,6},{6,7},{7,0},{8,9},{9,10},{10,1... | collective-permute-start | bytes 491528 | tf_op jit(solution)/shard_map/ppermute | solution.py:120
  94.0 11.9 %collective-permute-start.1 = (bf16[40,16,128]{2,1,0:T(8,128)(2,1)}, bf16[40,16,128]{2,1,0:T(8,128)(2,1)S(1)}, u32[]{:S(2)}, u32[]{:S(2)}) collective-permute-start(bf16[40,16,128]{2,1,0:T(8,128)(2,1)} %get-tuple-element.50), channel_id=1, source_target_pairs={{0,2},{1,3},{2,4},{3,5},{4,6},{5,7},{6,0},{7,1},{8,10},{9,11},{10,... | collective-permute-start | bytes 491528 | tf_op jit(solution)/shard_map/ppermute | solution.py:120
  95.5 17.8 %collective-permute-start.2 = (bf16[40,16,128]{2,1,0:T(8,128)(2,1)}, bf16[40,16,128]{2,1,0:T(8,128)(2,1)S(1)}, u32[]{:S(2)}, u32[]{:S(2)}) collective-permute-start(bf16[40,16,128]{2,1,0:T(8,128)(2,1)} %get-tuple-element.49), channel_id=1, source_target_pairs={{0,3},{1,4},{2,5},{3,6},{4,7},{5,0},{6,1},{7,2},{8,11},{9,12},{10,... | collective-permute-start | bytes 491528 | tf_op jit(solution)/shard_map/ppermute | solution.py:120
  97.9 18.0 %collective-permute-start.3 = (bf16[40,16,128]{2,1,0:T(8,128)(2,1)}, bf16[40,16,128]{2,1,0:T(8,128)(2,1)S(1)}, u32[]{:S(2)}, u32[]{:S(2)}) collective-permute-start(bf16[40,16,128]{2,1,0:T(8,128)(2,1)} %get-tuple-element.48), channel_id=1, source_target_pairs={{0,4},{1,5},{2,6},{3,7},{4,0},{5,1},{6,2},{7,3},{8,12},{9,13},{10,... | collective-permute-start | bytes 491528 | tf_op jit(solution)/shard_map/ppermute | solution.py:120
  99.3 17.3 %collective-permute-start.4 = (bf16[40,16,128]{2,1,0:T(8,128)(2,1)S(1)}, bf16[40,16,128]{2,1,0:T(8,128)(2,1)S(1)}, u32[]{:S(2)}, u32[]{:S(2)}) collective-permute-start(bf16[40,16,128]{2,1,0:T(8,128)(2,1)S(1)} %get-tuple-element.47), channel_id=1, source_target_pairs={{0,5},{1,6},{2,7},{3,0},{4,1},{5,2},{6,3},{7,4},{8,13},{9,14},{10,... | collective-permute-start | bytes 491528 | tf_op jit(solution)/shard_map/ppermute | solution.py:120
  103.8 13.5 %collective-permute-start.5 = (bf16[40,16,128]{2,1,0:T(8,128)(2,1)S(1)}, bf16[40,16,128]{2,1,0:T(8,128)(2,1)S(1)}, u32[]{:S(2)}, u32[]{:S(2)}) collective-permute-start(bf16[40,16,128]{2,1,0:T(8,128)(2,1)S(1)} %get-tuple-element.46), channel_id=1, source_target_pairs={{0,6},{1,7},{2,0},{3,1},{4,2},{5,3},{6,4},{7,5},{8,14},{9,15},{10,... | collective-permute-start | bytes 491528 | tf_op jit(solution)/shard_map/ppermute | solution.py:120
  105.9 12.1 %collective-permute-start.6 = (bf16[40,16,128]{2,1,0:T(8,128)(2,1)S(1)}, bf16[40,16,128]{2,1,0:T(8,128)(2,1)S(1)}, u32[]{:S(2)}, u32[]{:S(2)}) collective-permute-start(bf16[40,16,128]{2,1,0:T(8,128)(2,1)S(1)} %get-tuple-element.45), channel_id=1, source_target_pairs={{0,7},{1,0},{2,1},{3,2},{4,3},{5,4},{6,5},{7,6},{8,15},{9,8},{10,9... | collective-permute-start | bytes 491528 | tf_op jit(solution)/shard_map/ppermute | solution.py:120
  123.3 1.5 copy-start.1
  124.8 1.5 copy-start.6
  127.3 2.5 collective-permute-start.7
  131.0 10.2 %copy-start.4 = (bf16[2688,128]{1,0:T(8,128)(2,1)}, bf16[2688,128]{1,0:T(8,128)(2,1)S(1)}, u32[]{:S(2)}) copy-start(bf16[2688,128]{1,0:T(8,128)(2,1)S(1)} %add_convert_fusion) | copy-start | bytes 2064388
  131.1 10.2 %collective-permute-start.8 = (bf16[1344,128]{1,0:T(8,128)(2,1)S(1)}, bf16[1344,128]{1,0:T(8,128)(2,1)S(1)}, u32[]{:S(2)}, u32[]{:S(2)}) collective-permute-start(bf16[1344,128]{1,0:T(8,128)(2,1)S(1)} %dynamic-slice_bitcast_fusion), channel_id=1, source_target_pairs={{0,16},{8,24},{16,0},{24,8},{1,17},{9,25},{17,1},{25,9},{2,18},{10... | collective-permute-start | bytes 1032200 | tf_op jit(solution)/shard_map/ppermute | solution.py:32
  142.2 2.5 collective-permute-start.9
  146.0 0.8 copy-start.5
  146.0 2.4 copy-start.2
  146.8 7.7 %copy-start.3 = (f32[2560,128]{1,0:T(8,128)}, f32[2560,128]{1,0:T(8,128)S(1)}, u32[]{:S(2)}) copy-start(f32[2560,128]{1,0:T(8,128)S(1)} %pad_maximum_fusion) | copy-start | bytes 3932164
  157.1 17.2 %collective-permute-start.10 = (bf16[40,16,128]{2,1,0:T(8,128)(2,1)S(1)}, bf16[40,16,128]{2,1,0:T(8,128)(2,1)S(1)}, u32[]{:S(2)}, u32[]{:S(2)}) collective-permute-start(bf16[40,16,128]{2,1,0:T(8,128)(2,1)S(1)} %get-tuple-element.43), channel_id=1, source_target_pairs={{0,1},{1,2},{2,3},{3,4},{4,5},{5,6},{6,7},{7,0},{8,9},{9,10},{10,1... | collective-permute-start | bytes 491528 | tf_op jit(solution)/shard_map/ppermute | solution.py:168
  161.3 14.2 %collective-permute-start.11 = (bf16[40,16,128]{2,1,0:T(8,128)(2,1)S(1)}, bf16[40,16,128]{2,1,0:T(8,128)(2,1)S(1)}, u32[]{:S(2)}, u32[]{:S(2)}) collective-permute-start(bf16[40,16,128]{2,1,0:T(8,128)(2,1)S(1)} %get-tuple-element.42), channel_id=1, source_target_pairs={{0,2},{1,3},{2,4},{3,5},{4,6},{5,7},{6,0},{7,1},{8,10},{9,11},{10,... | collective-permute-start | bytes 491528 | tf_op jit(solution)/shard_map/ppermute | solution.py:168
  167.4 20.4 %collective-permute-start.12 = (bf16[40,16,128]{2,1,0:T(8,128)(2,1)S(1)}, bf16[40,16,128]{2,1,0:T(8,128)(2,1)S(1)}, u32[]{:S(2)}, u32[]{:S(2)}) collective-permute-start(bf16[40,16,128]{2,1,0:T(8,128)(2,1)S(1)} %get-tuple-element.41), channel_id=1, source_target_pairs={{0,3},{1,4},{2,5},{3,6},{4,7},{5,0},{6,1},{7,2},{8,11},{9,12},{10,... | collective-permute-start | bytes 491528 | tf_op jit(solution)/shard_map/ppermute | solution.py:168
  168.9 19.6 %collective-permute-start.13 = (bf16[40,16,128]{2,1,0:T(8,128)(2,1)S(1)}, bf16[40,16,128]{2,1,0:T(8,128)(2,1)S(1)}, u32[]{:S(2)}, u32[]{:S(2)}) collective-permute-start(bf16[40,16,128]{2,1,0:T(8,128)(2,1)S(1)} %get-tuple-element.40), channel_id=1, source_target_pairs={{0,4},{1,5},{2,6},{3,7},{4,0},{5,1},{6,2},{7,3},{8,12},{9,13},{10,... | collective-permute-start | bytes 491528 | tf_op jit(solution)/shard_map/ppermute | solution.py:168
  170.7 18.5 %collective-permute-start.14 = (bf16[40,16,128]{2,1,0:T(8,128)(2,1)S(1)}, bf16[40,16,128]{2,1,0:T(8,128)(2,1)S(1)}, u32[]{:S(2)}, u32[]{:S(2)}) collective-permute-start(bf16[40,16,128]{2,1,0:T(8,128)(2,1)S(1)} %get-tuple-element.39), channel_id=1, source_target_pairs={{0,5},{1,6},{2,7},{3,0},{4,1},{5,2},{6,3},{7,4},{8,13},{9,14},{10,... | collective-permute-start | bytes 491528 | tf_op jit(solution)/shard_map/ppermute | solution.py:168
  174.3 15.5 %collective-permute-start.15 = (bf16[40,16,128]{2,1,0:T(8,128)(2,1)S(1)}, bf16[40,16,128]{2,1,0:T(8,128)(2,1)S(1)}, u32[]{:S(2)}, u32[]{:S(2)}) collective-permute-start(bf16[40,16,128]{2,1,0:T(8,128)(2,1)S(1)} %get-tuple-element.38), channel_id=1, source_target_pairs={{0,6},{1,7},{2,0},{3,1},{4,2},{5,3},{6,4},{7,5},{8,14},{9,15},{10,... | collective-permute-start | bytes 491528 | tf_op jit(solution)/shard_map/ppermute | solution.py:168
  175.5 15.0 %collective-permute-start.16 = (bf16[40,16,128]{2,1,0:T(8,128)(2,1)S(1)}, bf16[40,16,128]{2,1,0:T(8,128)(2,1)S(1)}, u32[]{:S(2)}, u32[]{:S(2)}) collective-permute-start(bf16[40,16,128]{2,1,0:T(8,128)(2,1)S(1)} %get-tuple-element.37), channel_id=1, source_target_pairs={{0,7},{1,0},{2,1},{3,2},{4,3},{5,4},{6,5},{7,6},{8,15},{9,8},{10,9... | collective-permute-start | bytes 491528 | tf_op jit(solution)/shard_map/ppermute | solution.py:168
  194.2 71.2 %all-gather.7.cloned.1.call-start = ((), (), s32[]{:S(2)}) async-start(), calls=%async_computation.6 | async-start | bytes 3276800 | tf_op jit(solution)/shard_map/all_gather | solution.py:175
  196.7 15.6 %collective-permute-start.17 = (bf16[40,16,128]{2,1,0:T(8,128)(2,1)S(1)}, bf16[40,16,128]{2,1,0:T(8,128)(2,1)S(1)}, u32[]{:S(2)}, u32[]{:S(2)}) collective-permute-start(bf16[40,16,128]{2,1,0:T(8,128)(2,1)S(1)} %get-tuple-element.35), channel_id=1, source_target_pairs={{0,1},{1,2},{2,3},{3,4},{4,5},{5,6},{6,7},{7,0},{8,9},{9,10},{10,1... | collective-permute-start | bytes 491528 | tf_op jit(solution)/shard_map/ppermute | solution.py:168
  200.6 13.0 %collective-permute-start.18 = (bf16[40,16,128]{2,1,0:T(8,128)(2,1)S(1)}, bf16[40,16,128]{2,1,0:T(8,128)(2,1)S(1)}, u32[]{:S(2)}, u32[]{:S(2)}) collective-permute-start(bf16[40,16,128]{2,1,0:T(8,128)(2,1)S(1)} %get-tuple-element.34), channel_id=1, source_target_pairs={{0,2},{1,3},{2,4},{3,5},{4,6},{5,7},{6,0},{7,1},{8,10},{9,11},{10,... | collective-permute-start | bytes 491528 | tf_op jit(solution)/shard_map/ppermute | solution.py:168
  206.7 18.1 %collective-permute-start.19 = (bf16[40,16,128]{2,1,0:T(8,128)(2,1)S(1)}, bf16[40,16,128]{2,1,0:T(8,128)(2,1)S(1)}, u32[]{:S(2)}, u32[]{:S(2)}) collective-permute-start(bf16[40,16,128]{2,1,0:T(8,128)(2,1)S(1)} %get-tuple-element.33), channel_id=1, source_target_pairs={{0,3},{1,4},{2,5},{3,6},{4,7},{5,0},{6,1},{7,2},{8,11},{9,12},{10,... | collective-permute-start | bytes 491528 | tf_op jit(solution)/shard_map/ppermute | solution.py:168
  206.7 18.8 %collective-permute-start.20 = (bf16[40,16,128]{2,1,0:T(8,128)(2,1)S(1)}, bf16[40,16,128]{2,1,0:T(8,128)(2,1)S(1)}, u32[]{:S(2)}, u32[]{:S(2)}) collective-permute-start(bf16[40,16,128]{2,1,0:T(8,128)(2,1)S(1)} %get-tuple-element.32), channel_id=1, source_target_pairs={{0,4},{1,5},{2,6},{3,7},{4,0},{5,1},{6,2},{7,3},{8,12},{9,13},{10,... | collective-permute-start | bytes 491528 | tf_op jit(solution)/shard_map/ppermute | solution.py:168
  208.6 17.6 %collective-permute-start.21 = (bf16[40,16,128]{2,1,0:T(8,128)(2,1)S(1)}, bf16[40,16,128]{2,1,0:T(8,128)(2,1)S(1)}, u32[]{:S(2)}, u32[]{:S(2)}) collective-permute-start(bf16[40,16,128]{2,1,0:T(8,128)(2,1)S(1)} %get-tuple-element.31), channel_id=1, source_target_pairs={{0,5},{1,6},{2,7},{3,0},{4,1},{5,2},{6,3},{7,4},{8,13},{9,14},{10,... | collective-permute-start | bytes 491528 | tf_op jit(solution)/shard_map/ppermute | solution.py:168
  212.3 14.6 %collective-permute-start.22 = (bf16[40,16,128]{2,1,0:T(8,128)(2,1)S(1)}, bf16[40,16,128]{2,1,0:T(8,128)(2,1)S(1)}, u32[]{:S(2)}, u32[]{:S(2)}) collective-permute-start(bf16[40,16,128]{2,1,0:T(8,128)(2,1)S(1)} %get-tuple-element.30), channel_id=1, source_target_pairs={{0,6},{1,7},{2,0},{3,1},{4,2},{5,3},{6,4},{7,5},{8,14},{9,15},{10,... | collective-permute-start | bytes 491528 | tf_op jit(solution)/shard_map/ppermute | solution.py:168
  213.6 14.1 %collective-permute-start.23 = (bf16[40,16,128]{2,1,0:T(8,128)(2,1)S(1)}, bf16[40,16,128]{2,1,0:T(8,128)(2,1)S(1)}, u32[]{:S(2)}, u32[]{:S(2)}) collective-permute-start(bf16[40,16,128]{2,1,0:T(8,128)(2,1)S(1)} %get-tuple-element.29), channel_id=1, source_target_pairs={{0,7},{1,0},{2,1},{3,2},{4,3},{5,4},{6,5},{7,6},{8,15},{9,8},{10,9... | collective-permute-start | bytes 491528 | tf_op jit(solution)/shard_map/ppermute | solution.py:168
  227.6 4.5 %copy-start.7 = (f32[13,1024]{1,0:T(8,128)S(1)}, f32[13,1024]{1,0:T(8,128)}, u32[]{:S(2)}) copy-start(f32[13,1024]{1,0:T(8,128)} %param.14) | copy-start | bytes 159748
  227.6 4.5 %copy-start.8 = (f32[13,1024]{1,0:T(8,128)S(1)}, f32[13,1024]{1,0:T(8,128)}, u32[]{:S(2)}) copy-start(f32[13,1024]{1,0:T(8,128)} %param.15) | copy-start | bytes 159748
Sparse Core Ops, SparseCore 0:
  11.4 37.3 reduce-scatter.2
  52.0 34.6 reduce-scatter.4
  194.3 31.9 all-gather.4
  231.4 33.9 all-gather.6

commit v16 on v15

--- a/solution.py
+++ b/solution.py
@@ -1,3 +1,5 @@
+import functools
+
 import jax
 import jax.numpy as jnp
 from jax import lax
@@ -41,14 +43,21 @@
     o_ref[...] = x_ref[...].reshape(o_ref.shape)
 
 
+def _half_kernel(half, x_ref, o_ref):
+    w = o_ref.shape[-1]
+    for q in range(o_ref.shape[0]):
+        o_ref[q] = x_ref[:, :, (2 * q + half) * w:(2 * q + half + 1) * w]
+
+
 def take_half(x, width, half):
     units, rows, full = x.shape
     quarters = full // (2 * width)
+    step = units // 4 if units % 32 == 0 else units
     return pl.pallas_call(
-        _copy_kernel,
-        grid=(quarters,),
-        in_specs=[pl.BlockSpec((units, rows, width), lambda q: (0, 0, 2 * q + half))],
-        out_specs=pl.BlockSpec((1, units, rows, width), lambda q: (q, 0, 0, 0)),
+        functools.partial(_half_kernel, half),
+        grid=(units // step,),
+        in_specs=[pl.BlockSpec((step, rows, full), lambda i: (i, 0, 0))],
+        out_specs=pl.BlockSpec((quarters, step, rows, width), lambda i: (0, i, 0, 0)),
         out_shape=jax.ShapeDtypeStruct((quarters, units, rows, width), x.dtype),
     )(x)
 

time: 277 us -> 278 us (level)
  no operation moved by 1% of the time
where the time goes in v16:
time: 278 us; the launch traced here: 277 us
  waiting for transfers between devices  116 us (42%)
  starting transfers between devices  56 us (20%)
  local copies, waits for them, and re-layouts  39.3 us (14%)
  matrix products  23 us (8%)
  Pallas kernels  17.4 us (6%)
  between operations  14.1 us (5%)
  other arithmetic  10.7 us (4%)
    reduce_scatter x2, waiting for transfers between devices, body(): summed = lax.psum_scatter(half, 'rep', scatter_dimension=0, tiled=True)[0]  61.1 us
    ppermute x14, starting transfers between devices, body(): lax.ppermute(out_rows, 'dev', [(i, (i + k) % dev_count) for i in range(de...  37.4 us
    ppermute x14, waiting for transfers between devices, body(): lax.ppermute(out_rows, 'dev', [(i, (i + k) % dev_count) for i in range(de...  18.8 us
    all_gather x2, waiting for transfers between devices, body(): gathered = lax.all_gather(picked, 'rep', axis=2, tiled=True)  14.7 us
    dot_general x1, matrix products, fresh(): jnp.einsum('skb,kq->sbq', coeffs, basis_cols, precision=lax.Precision.HIGH)  13.9 us
    ppermute x7, starting transfers between devices, body(): lax.ppermute(block, 'dev', [(i, (i + k) % dev_count) for i in range(dev_c...  12.1 us
    unnamed x32, local copies, waits for them, and re-layouts  11.2 us
    ppermute x1, waiting for transfers between devices, rep_sum(): across = lax.ppermute(part, 'rep', [(i, i ^ 2) for i in range(4)])  9.53 us
  transfers between devices with their start and end apart: 29, of which 13 were waited for; matrix products, arithmetic and copies ran while one was open for 17% of the time, Pallas kernels for 3%

profile of v16, /device:TPU:0, one launch (start us, length us, event | category | flops | bytes accessed | tf_op | source)
XLA Modules:
  0.0 276.6 jit_solution(8461282631200848947)
XLA Ops:
  7.2 4.7 %shard_map.119 = bf16[4,160,16,128]{3,2,1,0:T(8,128)(2,1)} custom-call(bf16[160,16,1024]{2,1,0:T(8,128)(2,1)} %bitcast.65), custom_call_target="tpu_custom_call" | custom-call | tf_op jit(solution)/shard_map/pallas_call | solution.py:56
  12.0 4.7 %shard_map.120 = bf16[4,160,16,128]{3,2,1,0:T(8,128)(2,1)} custom-call(bf16[160,16,1024]{2,1,0:T(8,128)(2,1)} %bitcast.66), custom_call_target="tpu_custom_call" | custom-call | tf_op jit(solution)/shard_map/pallas_call | solution.py:56
  17.7 31.8 %reduce-scatter.3.cloned.1.call-done = bf16[1,160,16,128]{3,2,1,0:T(8,128)(2,1)} async-done(((bf16[4,160,16,128]{3,2,1,0:T(8,128)(2,1)}), bf16[1,160,16,128]{3,2,1,0:T(8,128)(2,1)}) %reduce-scatter.3.cloned.1.call-update) | async-done | bytes 655376 | tf_op jit(solution)/shard_map/reduce_scatter | solution.py:120
  49.5 3.0 %gather_fusion = bf16[320,16,128]{2,1,0:T(8,128)(2,1)} fusion(bf16[160,16,128]{2,1,0:T(8,128)(2,1)} %bitcast.79, s32[1024]{0:T(1024)S(1)} %pad_clamp_fusion.1), kind=kCustom, calls=%fused_computation | custom fusion | bytes 2622720 | tf_op jit(solution)/shard_map/jit(_take)/gather | solution.py:132
  52.5 5.5 %all-to-all-start = ((bf16[8,40,16,128]{3,2,1,0:T(8,128)(2,1)}), bf16[8,40,16,128]{3,2,1,0:T(8,128)(2,1)S(1)}, u32[]{:S(2)}, u32[]{:S(2)}) async-start(bf16[8,40,16,128]{3,2,1,0:T(8,128)(2,1)} %bitcast.4), calls=%async_computation.1 | async-start | bytes 2621440 | tf_op jit(solution)/shard_map/all_to_all | solution.py:133
  58.2 29.3 %reduce-scatter.5.cloned.1.call-done = bf16[1,160,16,128]{3,2,1,0:T(8,128)(2,1)} async-done(((bf16[4,160,16,128]{3,2,1,0:T(8,128)(2,1)}), bf16[1,160,16,128]{3,2,1,0:T(8,128)(2,1)}) %reduce-scatter.5.cloned.1.call-update) | async-done | bytes 655376 | tf_op jit(solution)/shard_map/reduce_scatter | solution.py:120
  87.5 2.0 gather_fusion.1
  90.5 1.5 collective-permute-start
  91.9 1.4 pad.4
  93.3 1.4 reshape.55
  94.7 1.5 collective-permute-start.1
  96.2 2.4 collective-permute-start.2
  98.6 1.4 collective-permute-start.3
  100.0 2.4 collective-permute-start.4
  102.4 1.4 broadcast_in_dim.66
  104.5 1.4 collective-permute-start.5
  106.6 1.4 collective-permute-start.6
  108.8 5.3 %collective-permute-done.2 = bf16[40,16,128]{2,1,0:T(8,128)(2,1)S(1)} collective-permute-done((bf16[40,16,128]{2,1,0:T(8,128)(2,1)}, bf16[40,16,128]{2,1,0:T(8,128)(2,1)S(1)}, u32[]{:S(2)}, u32[]{:S(2)}) %collective-permute-start.2) | collective-permute-done | bytes 163872 | tf_op jit(solution)/shard_map/ppermute | solution.py:129
  114.7 1.9 collective-permute-done.3
  120.0 4.0 %slice_subtract_fusion = (f32[40,128,128]{2,1,0:T(8,128)S(1)}, f32[40,128,128]{2,1,0:T(8,128)S(1)}) fusion(f32[40,128,256]{2,1,0:T(8,128)} %bitcast.63, bf16[40,128,128]{2,1,0:T(8,128)(2,1)} %constant_dynamic-update-slice_fusion.14, f32[40,128,128]{2,1,0:T(8,128)S(1)} %bitcast.70), kind=kLoop, calls=%fused_computation.13 | loop fusion | flops 2621440 | bytes 14417920 | tf_op jit(solution)/shard_map/sub | solution.py:140
  124.0 1.5 fusion.11
  125.5 1.5 fusion.4
  128.0 2.5 collective-permute-done.7
  132.4 9.5 %collective-permute-done.8 = bf16[1344,128]{1,0:T(8,128)(2,1)S(1)} collective-permute-done((bf16[1344,128]{1,0:T(8,128)(2,1)S(1)}, bf16[1344,128]{1,0:T(8,128)(2,1)S(1)}, u32[]{:S(2)}, u32[]{:S(2)}) %collective-permute-start.8) | collective-permute-done | bytes 344096 | tf_op jit(solution)/shard_map/ppermute | solution.py:34
  143.1 2.3 collective-permute-done.9
  147.5 1.6 copy-done.2
  149.1 6.1 %fusion.3 = bf16[40,128,256]{2,1,0:T(8,128)(2,1)S(1)} fusion(f32[40,128,128]{2,1,0:T(8,128)S(1)} %get-tuple-element.14, f32[40,128,128]{2,1,0:T(8,128)S(1)} %copy-done.2, pred[40]{0:T(512)(128)(4,1)S(1)} %get-tuple-element.18, f32[40,64,128]{2,1,0:T(8,128)S(1)} %bitcast.68, f32[64,1024]{1,0:T(8,128)S(1)} %copy-done, s32[]{:T(128)S(6)} %select_n.256, ...), kind=kOutput, calls=%fused_computation.9 | convolution fusion | flops 512491520 | bytes 19726852 | tf_op jit(solution)/shard_map/skb,kq->sbq/dot_general | solution.py:166
  155.3 1.5 fusion.19
  157.8 4.2 %collective-permute-start.10 = (bf16[40,16,128]{2,1,0:T(8,128)(2,1)S(1)}, bf16[40,16,128]{2,1,0:T(8,128)(2,1)S(1)}, u32[]{:S(2)}, u32[]{:S(2)}) collective-permute-start(bf16[40,16,128]{2,1,0:T(8,128)(2,1)S(1)} %get-tuple-element.43), channel_id=1, source_target_pairs={{0,1},{1,2},{2,3},{3,4},{4,5},{5,6},{6,7},{7,0},{8,9},{9,10},{10,1... | collective-permute-start | bytes 491528 | tf_op jit(solution)/shard_map/ppermute | solution.py:177
  162.0 6.1 %collective-permute-start.11 = (bf16[40,16,128]{2,1,0:T(8,128)(2,1)S(1)}, bf16[40,16,128]{2,1,0:T(8,128)(2,1)S(1)}, u32[]{:S(2)}, u32[]{:S(2)}) collective-permute-start(bf16[40,16,128]{2,1,0:T(8,128)(2,1)S(1)} %get-tuple-element.42), channel_id=1, source_target_pairs={{0,2},{1,3},{2,4},{3,5},{4,6},{5,7},{6,0},{7,1},{8,10},{9,11},{10,... | collective-permute-start | bytes 491528 | tf_op jit(solution)/shard_map/ppermute | solution.py:177
  168.1 1.5 collective-permute-start.12
  169.7 1.8 collective-permute-start.13
  171.4 3.4 %collective-permute-start.14 = (bf16[40,16,128]{2,1,0:T(8,128)(2,1)S(1)}, bf16[40,16,128]{2,1,0:T(8,128)(2,1)S(1)}, u32[]{:S(2)}, u32[]{:S(2)}) collective-permute-start(bf16[40,16,128]{2,1,0:T(8,128)(2,1)S(1)} %get-tuple-element.39), channel_id=1, source_target_pairs={{0,5},{1,6},{2,7},{3,0},{4,1},{5,2},{6,3},{7,4},{8,13},{9,14},{10,... | collective-permute-start | bytes 491528 | tf_op jit(solution)/shard_map/ppermute | solution.py:177
  176.2 2.4 collective-permute-start.16
  179.3 9.2 %collective-permute-done.12 = bf16[40,16,128]{2,1,0:T(8,128)(2,1)S(1)} collective-permute-done((bf16[40,16,128]{2,1,0:T(8,128)(2,1)S(1)}, bf16[40,16,128]{2,1,0:T(8,128)(2,1)S(1)}, u32[]{:S(2)}, u32[]{:S(2)}) %collective-permute-start.12) | collective-permute-done | bytes 163872 | tf_op jit(solution)/shard_map/ppermute | solution.py:177
  191.9 2.9 %gather_fusion.2 = bf16[160,16,128]{2,1,0:T(8,128)(2,1)} fusion(bf16[320,16,128]{2,1,0:T(8,128)(2,1)} %constant_dynamic-update-slice_fusion, s32[1024]{0:T(1024)S(1)} %pad_clamp_fusion), kind=kCustom, calls=%fused_computation.2 | custom fusion | bytes 1311360 | tf_op jit(solution)/shard_map/jit(_take)/gather | solution.py:180
  195.1 2.3 constant_dynamic-slice_fusion
  197.5 3.9 %collective-permute-start.17 = (bf16[40,16,128]{2,1,0:T(8,128)(2,1)S(1)}, bf16[40,16,128]{2,1,0:T(8,128)(2,1)S(1)}, u32[]{:S(2)}, u32[]{:S(2)}) collective-permute-start(bf16[40,16,128]{2,1,0:T(8,128)(2,1)S(1)} %get-tuple-element.35), channel_id=1, source_target_pairs={{0,1},{1,2},{2,3},{3,4},{4,5},{5,6},{6,7},{7,0},{8,9},{9,10},{10,1... | collective-permute-start | bytes 491528 | tf_op jit(solution)/shard_map/ppermute | solution.py:177
  201.3 6.1 %collective-permute-start.18 = (bf16[40,16,128]{2,1,0:T(8,128)(2,1)S(1)}, bf16[40,16,128]{2,1,0:T(8,128)(2,1)S(1)}, u32[]{:S(2)}, u32[]{:S(2)}) collective-permute-start(bf16[40,16,128]{2,1,0:T(8,128)(2,1)S(1)} %get-tuple-element.34), channel_id=1, source_target_pairs={{0,2},{1,3},{2,4},{3,5},{4,6},{5,7},{6,0},{7,1},{8,10},{9,11},{10,... | collective-permute-start | bytes 491528 | tf_op jit(solution)/shard_map/ppermute | solution.py:177
  207.4 1.9 collective-permute-start.20
  209.3 3.4 %collective-permute-start.21 = (bf16[40,16,128]{2,1,0:T(8,128)(2,1)S(1)}, bf16[40,16,128]{2,1,0:T(8,128)(2,1)S(1)}, u32[]{:S(2)}, u32[]{:S(2)}) collective-permute-start(bf16[40,16,128]{2,1,0:T(8,128)(2,1)S(1)} %get-tuple-element.31), channel_id=1, source_target_pairs={{0,5},{1,6},{2,7},{3,0},{4,1},{5,2},{6,3},{7,4},{8,13},{9,14},{10,... | collective-permute-start | bytes 491528 | tf_op jit(solution)/shard_map/ppermute | solution.py:177
  214.3 1.7 collective-permute-start.23
  216.6 8.9 %collective-permute-done.19 = bf16[40,16,128]{2,1,0:T(8,128)(2,1)S(1)} collective-permute-done((bf16[40,16,128]{2,1,0:T(8,128)(2,1)S(1)}, bf16[40,16,128]{2,1,0:T(8,128)(2,1)S(1)}, u32[]{:S(2)}, u32[]{:S(2)}) %collective-permute-start.19) | collective-permute-done | bytes 163872 | tf_op jit(solution)/shard_map/ppermute | solution.py:177
  229.1 2.9 %gather_fusion.3 = bf16[160,16,128]{2,1,0:T(8,128)(2,1)} fusion(bf16[320,16,128]{2,1,0:T(8,128)(2,1)} %constant_dynamic-update-slice_fusion.7, s32[1024]{0:T(1024)S(1)} %pad_clamp_fusion), kind=kCustom, calls=%fused_computation.3 | custom fusion | bytes 1311360 | tf_op jit(solution)/shard_map/jit(_take)/gather | solution.py:180
  233.5 4.0 %shard_map.121.base_ref = bf16[160,16,1024]{2,1,0:T(8,128)(2,1)} custom-call(bf16[160,16,512]{2,1,0:T(8,128)(2,1)} %all-gather.5.cloned.1.call-done.x_ref), custom_call_target="tpu_custom_call" | custom-call | tf_op jit(solution)/shard_map/pallas_call | solution.py:77
  237.5 13.9 %select_bitcast_fusion = (f32[1,40,128,256]{3,2,1,0:T(8,128)}, f32[1,40,128,256]{3,2,1,0:T(8,128)}) fusion(f32[40,128,256]{2,1,0:T(8,128)} %bitcast.67, pred[40]{0:T(512)(128)(4,1)S(1)} %get-tuple-element.17, f32[40,128,256]{2,1,0:T(8,128)} %bitcast.64, f32[40,128,128]{2,1,0:T(8,128)S(1)} %get-tuple-element.14, f32[40,128,128]{2,1,0:T(8,128)} %copy-done.1, ...), kind=kOutput, calls=%fused_computation.11 | convolution fusion | flops 516423680 | bytes 27591684 | tf_op jit(solution)/shard_map/skb,kq->sbq/dot_general | solution.py:158
  251.4 14.7 %all-gather.7.cloned.1.call-done.a_ref = bf16[160,16,512]{2,1,0:T(8,128)(2,1)} async-done(((bf16[160,16,128]{2,1,0:T(8,128)(2,1)}), bf16[160,16,512]{2,1,0:T(8,128)(2,1)}) %all-gather.7.cloned.1.call-update) | async-done | bytes 2621456 | tf_op jit(solution)/shard_map/all_gather | solution.py:184
  266.1 4.0 %shard_map.122 = bf16[160,16,1024]{2,1,0:T(8,128)(2,1)} custom-call(bf16[160,16,512]{2,1,0:T(8,128)(2,1)} %all-gather.7.cloned.1.call-done.a_ref, bf16[160,16,1024]{2,1,0:T(8,128)(2,1)} %shard_map.121.base_ref), custom_call_target="tpu_custom_call", output_to_operand_aliasing={{}: (1, {})} | custom-call | tf_op jit(solution)/shard_map/pallas_call | solution.py:80
  (95 shorter events, 28.4 us)
Async XLA Ops:
  7.2 116.9 %copy-start = (f32[64,1024]{1,0:T(8,128)S(1)}, f32[64,1024]{1,0:T(8,128)}, u32[]{:S(2)}) copy-start(f32[64,1024]{1,0:T(8,128)} %param.12) | copy-start | bytes 786436
  7.2 42.3 %reduce-scatter.3.cloned.1.call-start = ((), (), s32[]{:S(2)}) async-start(), calls=%async_computation.3 | async-start | bytes 3276800 | tf_op jit(solution)/shard_map/reduce_scatter | solution.py:120
  12.0 75.5 %reduce-scatter.5.cloned.1.call-start = ((), (), s32[]{:S(2)}) async-start(), calls=%async_computation.4 | async-start | bytes 3276800 | tf_op jit(solution)/shard_map/reduce_scatter | solution.py:120
  16.7 0.7 copy-start.9
  52.5 66.9 %all-to-all-start = ((bf16[8,40,16,128]{3,2,1,0:T(8,128)(2,1)}), bf16[8,40,16,128]{3,2,1,0:T(8,128)(2,1)S(1)}, u32[]{:S(2)}, u32[]{:S(2)}) async-start(bf16[8,40,16,128]{3,2,1,0:T(8,128)(2,1)} %bitcast.4), calls=%async_computation.1 | async-start | bytes 2621440 | tf_op jit(solution)/shard_map/all_to_all | solution.py:133
  58.0 175.5 %all-gather.5.cloned.1.call-start = ((), (), s32[]{:S(2)}) async-start(), calls=%async_computation.5 | async-start | bytes 3276800 | tf_op jit(solution)/shard_map/all_gather | solution.py:184
  90.5 14.0 %collective-permute-start = (bf16[40,16,128]{2,1,0:T(8,128)(2,1)}, bf16[40,16,128]{2,1,0:T(8,128)(2,1)S(1)}, u32[]{:S(2)}, u32[]{:S(2)}) collective-permute-start(bf16[40,16,128]{2,1,0:T(8,128)(2,1)} %get-tuple-element.51), channel_id=1, source_target_pairs={{0,1},{1,2},{2,3},{3,4},{4,5},{5,6},{6,7},{7,0},{8,9},{9,10},{10,1... | collective-permute-start | bytes 491528 | tf_op jit(solution)/shard_map/ppermute | solution.py:129
  94.7 11.9 %collective-permute-start.1 = (bf16[40,16,128]{2,1,0:T(8,128)(2,1)}, bf16[40,16,128]{2,1,0:T(8,128)(2,1)S(1)}, u32[]{:S(2)}, u32[]{:S(2)}) collective-permute-start(bf16[40,16,128]{2,1,0:T(8,128)(2,1)} %get-tuple-element.50), channel_id=1, source_target_pairs={{0,2},{1,3},{2,4},{3,5},{4,6},{5,7},{6,0},{7,1},{8,10},{9,11},{10,... | collective-permute-start | bytes 491528 | tf_op jit(solution)/shard_map/ppermute | solution.py:129
  96.2 17.8 %collective-permute-start.2 = (bf16[40,16,128]{2,1,0:T(8,128)(2,1)}, bf16[40,16,128]{2,1,0:T(8,128)(2,1)S(1)}, u32[]{:S(2)}, u32[]{:S(2)}) collective-permute-start(bf16[40,16,128]{2,1,0:T(8,128)(2,1)} %get-tuple-element.49), channel_id=1, source_target_pairs={{0,3},{1,4},{2,5},{3,6},{4,7},{5,0},{6,1},{7,2},{8,11},{9,12},{10,... | collective-permute-start | bytes 491528 | tf_op jit(solution)/shard_map/ppermute | solution.py:129
  98.6 18.0 %collective-permute-start.3 = (bf16[40,16,128]{2,1,0:T(8,128)(2,1)}, bf16[40,16,128]{2,1,0:T(8,128)(2,1)S(1)}, u32[]{:S(2)}, u32[]{:S(2)}) collective-permute-start(bf16[40,16,128]{2,1,0:T(8,128)(2,1)} %get-tuple-element.48), channel_id=1, source_target_pairs={{0,4},{1,5},{2,6},{3,7},{4,0},{5,1},{6,2},{7,3},{8,12},{9,13},{10,... | collective-permute-start | bytes 491528 | tf_op jit(solution)/shard_map/ppermute | solution.py:129
  100.0 17.3 %collective-permute-start.4 = (bf16[40,16,128]{2,1,0:T(8,128)(2,1)S(1)}, bf16[40,16,128]{2,1,0:T(8,128)(2,1)S(1)}, u32[]{:S(2)}, u32[]{:S(2)}) collective-permute-start(bf16[40,16,128]{2,1,0:T(8,128)(2,1)S(1)} %get-tuple-element.47), channel_id=1, source_target_pairs={{0,5},{1,6},{2,7},{3,0},{4,1},{5,2},{6,3},{7,4},{8,13},{9,14},{10,... | collective-permute-start | bytes 491528 | tf_op jit(solution)/shard_map/ppermute | solution.py:129
  104.5 13.5 %collective-permute-start.5 = (bf16[40,16,128]{2,1,0:T(8,128)(2,1)S(1)}, bf16[40,16,128]{2,1,0:T(8,128)(2,1)S(1)}, u32[]{:S(2)}, u32[]{:S(2)}) collective-permute-start(bf16[40,16,128]{2,1,0:T(8,128)(2,1)S(1)} %get-tuple-element.46), channel_id=1, source_target_pairs={{0,6},{1,7},{2,0},{3,1},{4,2},{5,3},{6,4},{7,5},{8,14},{9,15},{10,... | collective-permute-start | bytes 491528 | tf_op jit(solution)/shard_map/ppermute | solution.py:129
  106.6 12.1 %collective-permute-start.6 = (bf16[40,16,128]{2,1,0:T(8,128)(2,1)S(1)}, bf16[40,16,128]{2,1,0:T(8,128)(2,1)S(1)}, u32[]{:S(2)}, u32[]{:S(2)}) collective-permute-start(bf16[40,16,128]{2,1,0:T(8,128)(2,1)S(1)} %get-tuple-element.45), channel_id=1, source_target_pairs={{0,7},{1,0},{2,1},{3,2},{4,3},{5,4},{6,5},{7,6},{8,15},{9,8},{10,9... | collective-permute-start | bytes 491528 | tf_op jit(solution)/shard_map/ppermute | solution.py:129
  124.0 1.5 copy-start.1
  125.5 1.5 copy-start.6
  128.0 2.5 collective-permute-start.7
  131.7 10.2 %copy-start.4 = (bf16[2688,128]{1,0:T(8,128)(2,1)}, bf16[2688,128]{1,0:T(8,128)(2,1)S(1)}, u32[]{:S(2)}) copy-start(bf16[2688,128]{1,0:T(8,128)(2,1)S(1)} %add_convert_fusion) | copy-start | bytes 2064388
  131.8 10.2 %collective-permute-start.8 = (bf16[1344,128]{1,0:T(8,128)(2,1)S(1)}, bf16[1344,128]{1,0:T(8,128)(2,1)S(1)}, u32[]{:S(2)}, u32[]{:S(2)}) collective-permute-start(bf16[1344,128]{1,0:T(8,128)(2,1)S(1)} %dynamic-slice_bitcast_fusion), channel_id=1, source_target_pairs={{0,16},{8,24},{16,0},{24,8},{1,17},{9,25},{17,1},{25,9},{2,18},{10... | collective-permute-start | bytes 1032200 | tf_op jit(solution)/shard_map/ppermute | solution.py:34
  142.9 2.5 collective-permute-start.9
  146.7 0.8 copy-start.5
  146.7 2.4 copy-start.2
  147.5 7.7 %copy-start.3 = (f32[2560,128]{1,0:T(8,128)}, f32[2560,128]{1,0:T(8,128)S(1)}, u32[]{:S(2)}) copy-start(f32[2560,128]{1,0:T(8,128)S(1)} %pad_maximum_fusion) | copy-start | bytes 3932164
  157.8 17.2 %collective-permute-start.10 = (bf16[40,16,128]{2,1,0:T(8,128)(2,1)S(1)}, bf16[40,16,128]{2,1,0:T(8,128)(2,1)S(1)}, u32[]{:S(2)}, u32[]{:S(2)}) collective-permute-start(bf16[40,16,128]{2,1,0:T(8,128)(2,1)S(1)} %get-tuple-element.43), channel_id=1, source_target_pairs={{0,1},{1,2},{2,3},{3,4},{4,5},{5,6},{6,7},{7,0},{8,9},{9,10},{10,1... | collective-permute-start | bytes 491528 | tf_op jit(solution)/shard_map/ppermute | solution.py:177
  162.0 14.2 %collective-permute-start.11 = (bf16[40,16,128]{2,1,0:T(8,128)(2,1)S(1)}, bf16[40,16,128]{2,1,0:T(8,128)(2,1)S(1)}, u32[]{:S(2)}, u32[]{:S(2)}) collective-permute-start(bf16[40,16,128]{2,1,0:T(8,128)(2,1)S(1)} %get-tuple-element.42), channel_id=1, source_target_pairs={{0,2},{1,3},{2,4},{3,5},{4,6},{5,7},{6,0},{7,1},{8,10},{9,11},{10,... | collective-permute-start | bytes 491528 | tf_op jit(solution)/shard_map/ppermute | solution.py:177
  168.1 20.4 %collective-permute-start.12 = (bf16[40,16,128]{2,1,0:T(8,128)(2,1)S(1)}, bf16[40,16,128]{2,1,0:T(8,128)(2,1)S(1)}, u32[]{:S(2)}, u32[]{:S(2)}) collective-permute-start(bf16[40,16,128]{2,1,0:T(8,128)(2,1)S(1)} %get-tuple-element.41), channel_id=1, source_target_pairs={{0,3},{1,4},{2,5},{3,6},{4,7},{5,0},{6,1},{7,2},{8,11},{9,12},{10,... | collective-permute-start | bytes 491528 | tf_op jit(solution)/shard_map/ppermute | solution.py:177
  169.7 19.6 %collective-permute-start.13 = (bf16[40,16,128]{2,1,0:T(8,128)(2,1)S(1)}, bf16[40,16,128]{2,1,0:T(8,128)(2,1)S(1)}, u32[]{:S(2)}, u32[]{:S(2)}) collective-permute-start(bf16[40,16,128]{2,1,0:T(8,128)(2,1)S(1)} %get-tuple-element.40), channel_id=1, source_target_pairs={{0,4},{1,5},{2,6},{3,7},{4,0},{5,1},{6,2},{7,3},{8,12},{9,13},{10,... | collective-permute-start | bytes 491528 | tf_op jit(solution)/shard_map/ppermute | solution.py:177
  171.4 18.5 %collective-permute-start.14 = (bf16[40,16,128]{2,1,0:T(8,128)(2,1)S(1)}, bf16[40,16,128]{2,1,0:T(8,128)(2,1)S(1)}, u32[]{:S(2)}, u32[]{:S(2)}) collective-permute-start(bf16[40,16,128]{2,1,0:T(8,128)(2,1)S(1)} %get-tuple-element.39), channel_id=1, source_target_pairs={{0,5},{1,6},{2,7},{3,0},{4,1},{5,2},{6,3},{7,4},{8,13},{9,14},{10,... | collective-permute-start | bytes 491528 | tf_op jit(solution)/shard_map/ppermute | solution.py:177
  175.0 15.5 %collective-permute-start.15 = (bf16[40,16,128]{2,1,0:T(8,128)(2,1)S(1)}, bf16[40,16,128]{2,1,0:T(8,128)(2,1)S(1)}, u32[]{:S(2)}, u32[]{:S(2)}) collective-permute-start(bf16[40,16,128]{2,1,0:T(8,128)(2,1)S(1)} %get-tuple-element.38), channel_id=1, source_target_pairs={{0,6},{1,7},{2,0},{3,1},{4,2},{5,3},{6,4},{7,5},{8,14},{9,15},{10,... | collective-permute-start | bytes 491528 | tf_op jit(solution)/shard_map/ppermute | solution.py:177
  176.2 15.0 %collective-permute-start.16 = (bf16[40,16,128]{2,1,0:T(8,128)(2,1)S(1)}, bf16[40,16,128]{2,1,0:T(8,128)(2,1)S(1)}, u32[]{:S(2)}, u32[]{:S(2)}) collective-permute-start(bf16[40,16,128]{2,1,0:T(8,128)(2,1)S(1)} %get-tuple-element.37), channel_id=1, source_target_pairs={{0,7},{1,0},{2,1},{3,2},{4,3},{5,4},{6,5},{7,6},{8,15},{9,8},{10,9... | collective-permute-start | bytes 491528 | tf_op jit(solution)/shard_map/ppermute | solution.py:177
  194.9 71.2 %all-gather.7.cloned.1.call-start = ((), (), s32[]{:S(2)}) async-start(), calls=%async_computation.6 | async-start | bytes 3276800 | tf_op jit(solution)/shard_map/all_gather | solution.py:184
  197.5 15.6 %collective-permute-start.17 = (bf16[40,16,128]{2,1,0:T(8,128)(2,1)S(1)}, bf16[40,16,128]{2,1,0:T(8,128)(2,1)S(1)}, u32[]{:S(2)}, u32[]{:S(2)}) collective-permute-start(bf16[40,16,128]{2,1,0:T(8,128)(2,1)S(1)} %get-tuple-element.35), channel_id=1, source_target_pairs={{0,1},{1,2},{2,3},{3,4},{4,5},{5,6},{6,7},{7,0},{8,9},{9,10},{10,1... | collective-permute-start | bytes 491528 | tf_op jit(solution)/shard_map/ppermute | solution.py:177
  201.3 13.0 %collective-permute-start.18 = (bf16[40,16,128]{2,1,0:T(8,128)(2,1)S(1)}, bf16[40,16,128]{2,1,0:T(8,128)(2,1)S(1)}, u32[]{:S(2)}, u32[]{:S(2)}) collective-permute-start(bf16[40,16,128]{2,1,0:T(8,128)(2,1)S(1)} %get-tuple-element.34), channel_id=1, source_target_pairs={{0,2},{1,3},{2,4},{3,5},{4,6},{5,7},{6,0},{7,1},{8,10},{9,11},{10,... | collective-permute-start | bytes 491528 | tf_op jit(solution)/shard_map/ppermute | solution.py:177
  207.4 18.1 %collective-permute-start.19 = (bf16[40,16,128]{2,1,0:T(8,128)(2,1)S(1)}, bf16[40,16,128]{2,1,0:T(8,128)(2,1)S(1)}, u32[]{:S(2)}, u32[]{:S(2)}) collective-permute-start(bf16[40,16,128]{2,1,0:T(8,128)(2,1)S(1)} %get-tuple-element.33), channel_id=1, source_target_pairs={{0,3},{1,4},{2,5},{3,6},{4,7},{5,0},{6,1},{7,2},{8,11},{9,12},{10,... | collective-permute-start | bytes 491528 | tf_op jit(solution)/shard_map/ppermute | solution.py:177
  207.4 18.8 %collective-permute-start.20 = (bf16[40,16,128]{2,1,0:T(8,128)(2,1)S(1)}, bf16[40,16,128]{2,1,0:T(8,128)(2,1)S(1)}, u32[]{:S(2)}, u32[]{:S(2)}) collective-permute-start(bf16[40,16,128]{2,1,0:T(8,128)(2,1)S(1)} %get-tuple-element.32), channel_id=1, source_target_pairs={{0,4},{1,5},{2,6},{3,7},{4,0},{5,1},{6,2},{7,3},{8,12},{9,13},{10,... | collective-permute-start | bytes 491528 | tf_op jit(solution)/shard_map/ppermute | solution.py:177
  209.3 17.6 %collective-permute-start.21 = (bf16[40,16,128]{2,1,0:T(8,128)(2,1)S(1)}, bf16[40,16,128]{2,1,0:T(8,128)(2,1)S(1)}, u32[]{:S(2)}, u32[]{:S(2)}) collective-permute-start(bf16[40,16,128]{2,1,0:T(8,128)(2,1)S(1)} %get-tuple-element.31), channel_id=1, source_target_pairs={{0,5},{1,6},{2,7},{3,0},{4,1},{5,2},{6,3},{7,4},{8,13},{9,14},{10,... | collective-permute-start | bytes 491528 | tf_op jit(solution)/shard_map/ppermute | solution.py:177
  213.0 14.6 %collective-permute-start.22 = (bf16[40,16,128]{2,1,0:T(8,128)(2,1)S(1)}, bf16[40,16,128]{2,1,0:T(8,128)(2,1)S(1)}, u32[]{:S(2)}, u32[]{:S(2)}) collective-permute-start(bf16[40,16,128]{2,1,0:T(8,128)(2,1)S(1)} %get-tuple-element.30), channel_id=1, source_target_pairs={{0,6},{1,7},{2,0},{3,1},{4,2},{5,3},{6,4},{7,5},{8,14},{9,15},{10,... | collective-permute-start | bytes 491528 | tf_op jit(solution)/shard_map/ppermute | solution.py:177
  214.3 14.1 %collective-permute-start.23 = (bf16[40,16,128]{2,1,0:T(8,128)(2,1)S(1)}, bf16[40,16,128]{2,1,0:T(8,128)(2,1)S(1)}, u32[]{:S(2)}, u32[]{:S(2)}) collective-permute-start(bf16[40,16,128]{2,1,0:T(8,128)(2,1)S(1)} %get-tuple-element.29), channel_id=1, source_target_pairs={{0,7},{1,0},{2,1},{3,2},{4,3},{5,4},{6,5},{7,6},{8,15},{9,8},{10,9... | collective-permute-start | bytes 491528 | tf_op jit(solution)/shard_map/ppermute | solution.py:177
  228.3 4.5 %copy-start.7 = (f32[13,1024]{1,0:T(8,128)S(1)}, f32[13,1024]{1,0:T(8,128)}, u32[]{:S(2)}) copy-start(f32[13,1024]{1,0:T(8,128)} %param.14) | copy-start | bytes 159748
  228.3 4.5 %copy-start.8 = (f32[13,1024]{1,0:T(8,128)S(1)}, f32[13,1024]{1,0:T(8,128)}, u32[]{:S(2)}) copy-start(f32[13,1024]{1,0:T(8,128)} %param.15) | copy-start | bytes 159748
Sparse Core Ops, SparseCore 0:
  12.1 37.3 reduce-scatter.2
  52.8 34.6 reduce-scatter.4
  195.0 31.9 all-gather.4
  232.1 33.9 all-gather.6

commit v17 on v15

--- a/solution.py
+++ b/solution.py
@@ -118,6 +118,8 @@
                 block = lax.dynamic_index_in_dim(picked, (me + k) % dev_count, 0, keepdims=False)
                 if k:
                     block = lax.ppermute(block, "dev", [(i, (i + k) % dev_count) for i in range(dev_count)])
+                if k == 1:
+                    coeff_terms, block = lax.optimization_barrier((coeff_terms, block))
                 arrived = lax.dynamic_update_slice_in_dim(arrived, block, ((me - k) % dev_count) * part_rows, 1)
         else:
             picked = jnp.take(summed, source_unit, axis=0, mode="clip")

time: 277 us -> 262 us (0.946)
  local copies, waits for them, and re-layouts: 39.3 us -> 23.3 us
  matrix products: 23 us -> 14.6 us
  other arithmetic: 10.7 us -> 17.8 us
  waiting for transfers between devices: 117 us -> 120 us
    dot_general x1, matrix products: 13.9 us -> 5.46 us  [fresh(): jnp.einsum('skb,kq->sbq', coeffs, basis_cols, precision=lax.Precision.HIGH)]
    unnamed x32 -> x50, local copies, waits for them, and re-layouts: 11.2 us -> 3.88 us
    broadcast_in_dim x0 -> x1, other arithmetic: none -> 6.72 us  [body(): new_momentum[None]]
    ppermute x14, waiting for transfers between devices: 18.8 us -> 23.7 us  [body(): lax.ppermute(out_rows, 'dev', [(i, (i + k) % dev_count) for i in range(de...]
  transfers between devices with their start and end apart: 29 -> 29, of which waited for: 13 -> 17; matrix products, arithmetic and copies ran while one was open for 17% -> 13% of each run, Pallas kernels for 3% -> 3%
where the time goes in v17:
time: 262 us; the launch traced here: 261 us
  waiting for transfers between devices  120 us (46%)
  starting transfers between devices  54.7 us (21%)
  local copies, waits for them, and re-layouts  23.3 us (9%)
  other arithmetic  17.8 us (7%)
  Pallas kernels  16.1 us (6%)
  matrix products  14.6 us (6%)
  between operations  14.5 us (6%)
    reduce_scatter x2, waiting for transfers between devices, body(): summed = lax.psum_scatter(half, 'rep', scatter_dimension=0, tiled=True)[0]  60.8 us
    ppermute x14, starting transfers between devices, body(): lax.ppermute(out_rows, 'dev', [(i, (i + k) % dev_count) for i in range(de...  36 us
    ppermute x14, waiting for transfers between devices, body(): lax.ppermute(out_rows, 'dev', [(i, (i + k) % dev_count) for i in range(de...  23.7 us
    all_gather x2, waiting for transfers between devices, body(): gathered = lax.all_gather(picked, 'rep', axis=2, tiled=True)  15 us
    ppermute x7, starting transfers between devices, body(): lax.ppermute(block, 'dev', [(i, (i + k) % dev_count) for i in range(dev_c...  12.1 us
    ppermute x1, waiting for transfers between devices, rep_sum(): across = lax.ppermute(part, 'rep', [(i, i ^ 2) for i in range(4)])  9.58 us
    pallas_call x2, Pallas kernels, take_half(): pl.pallas_call(_copy_kernel, grid=(quarters,), in_specs=[pl.BlockSpec((un...  8.02 us
    broadcast_in_dim x1, other arithmetic, body(): new_momentum[None]  6.72 us
  transfers between devices with their start and end apart: 29, of which 17 were waited for; matrix products, arithmetic and copies ran while one was open for 13% of the time, Pallas kernels for 3%

profile of v17, /device:TPU:0, one launch (start us, length us, event | category | flops | bytes accessed | tf_op | source)
XLA Modules:
  0.0 260.9 jit_solution(10528485746929876658)
XLA Ops:
  7.2 4.0 %shard_map.119 = bf16[4,160,16,128]{3,2,1,0:T(8,128)(2,1)} custom-call(bf16[160,16,1024]{2,1,0:T(8,128)(2,1)} %bitcast.70), custom_call_target="tpu_custom_call" | custom-call | tf_op jit(solution)/shard_map/pallas_call | solution.py:47
  11.3 4.0 %shard_map.120 = bf16[4,160,16,128]{3,2,1,0:T(8,128)(2,1)} custom-call(bf16[160,16,1024]{2,1,0:T(8,128)(2,1)} %bitcast.71), custom_call_target="tpu_custom_call" | custom-call | tf_op jit(solution)/shard_map/pallas_call | solution.py:47
  16.3 32.4 %reduce-scatter.3.cloned.1.call-done = bf16[1,160,16,128]{3,2,1,0:T(8,128)(2,1)} async-done(((bf16[4,160,16,128]{3,2,1,0:T(8,128)(2,1)}), bf16[1,160,16,128]{3,2,1,0:T(8,128)(2,1)}) %reduce-scatter.3.cloned.1.call-update) | async-done | bytes 655376 | tf_op jit(solution)/shard_map/reduce_scatter | solution.py:111
  48.8 3.0 %gather_fusion = bf16[320,16,128]{2,1,0:T(8,128)(2,1)} fusion(bf16[160,16,128]{2,1,0:T(8,128)(2,1)} %bitcast.84, s32[1024]{0:T(1024)S(1)} %pad_clamp_fusion.1), kind=kCustom, calls=%fused_computation | custom fusion | bytes 2622720 | tf_op jit(solution)/shard_map/jit(_take)/gather | solution.py:125
  51.8 5.6 %all-to-all-start = ((bf16[8,40,16,128]{3,2,1,0:T(8,128)(2,1)}), bf16[8,40,16,128]{3,2,1,0:T(8,128)(2,1)S(1)}, u32[]{:S(2)}, u32[]{:S(2)}) async-start(bf16[8,40,16,128]{3,2,1,0:T(8,128)(2,1)} %bitcast.4), calls=%async_computation.1 | async-start | bytes 2621440 | tf_op jit(solution)/shard_map/all_to_all | solution.py:126
  58.4 28.3 %reduce-scatter.5.cloned.1.call-done = bf16[1,160,16,128]{3,2,1,0:T(8,128)(2,1)} async-done(((bf16[4,160,16,128]{3,2,1,0:T(8,128)(2,1)}), bf16[1,160,16,128]{3,2,1,0:T(8,128)(2,1)}) %reduce-scatter.5.cloned.1.call-update) | async-done | bytes 655376 | tf_op jit(solution)/shard_map/reduce_scatter | solution.py:111
  86.7 2.0 gather_fusion.1
  89.9 1.5 collective-permute-start
  91.3 1.5 collective-permute-start.1
  92.8 2.4 collective-permute-start.2
  95.2 1.4 collective-permute-start.3
  96.6 2.4 collective-permute-start.4
  99.1 1.4 broadcast_in_dim.66
  101.7 2.4 slice_subtract_fusion.1
  104.1 1.5 convolution_bitcast_fusion.1
  105.7 1.5 collective-permute-start.5
  107.2 1.6 constant_dynamic-update-slice_fusion.20
  108.8 1.4 collective-permute-start.6
  110.9 2.1 collective-permute-done.2
  115.1 4.0 %collective-permute-done.5 = bf16[40,16,128]{2,1,0:T(8,128)(2,1)S(1)} collective-permute-done((bf16[40,16,128]{2,1,0:T(8,128)(2,1)S(1)}, bf16[40,16,128]{2,1,0:T(8,128)(2,1)S(1)}, u32[]{:S(2)}, u32[]{:S(2)}) %collective-permute-start.5) | collective-permute-done | bytes 163872 | tf_op jit(solution)/shard_map/ppermute | solution.py:120
  120.5 1.7 slice_subtract_fusion
  122.2 1.5 convolution_bitcast_fusion
  125.4 2.5 collective-permute-done.7
  129.8 9.6 %collective-permute-done.8 = bf16[1344,128]{1,0:T(8,128)(2,1)S(1)} collective-permute-done((bf16[1344,128]{1,0:T(8,128)(2,1)S(1)}, bf16[1344,128]{1,0:T(8,128)(2,1)S(1)}, u32[]{:S(2)}, u32[]{:S(2)}) %collective-permute-start.8) | collective-permute-done | bytes 344096 | tf_op jit(solution)/shard_map/ppermute | solution.py:32
  140.5 2.3 collective-permute-done.9
  144.9 1.6 copy-done.3
  146.6 6.1 %fusion.3 = bf16[40,128,256]{2,1,0:T(8,128)(2,1)S(1)} fusion(f32[40,128,128]{2,1,0:T(8,128)S(1)} %slice_subtract_fusion, f32[40,128,128]{2,1,0:T(8,128)S(1)} %copy-done.3, pred[40]{0:T(512)(128)(4,1)S(1)} %get-tuple-element.22, f32[40,64,128]{2,1,0:T(8,128)S(1)} %bitcast.73, f32[64,1024]{1,0:T(8,128)S(1)} %copy-done, s32[]{:T(128)S(6)} %select_n.226, ...), kind=kOutput, calls=%fused_computation.9 | convolution fusion | flops 512491520 | bytes 19726852 | tf_op jit(solution)/shard_map/skb,kq->sbq/dot_general | solution.py:159
  153.5 2.7 %collective-permute-start.10 = (bf16[40,16,128]{2,1,0:T(8,128)(2,1)S(1)}, bf16[40,16,128]{2,1,0:T(8,128)(2,1)S(1)}, u32[]{:S(2)}, u32[]{:S(2)}) collective-permute-start(bf16[40,16,128]{2,1,0:T(8,128)(2,1)S(1)} %get-tuple-element.45), channel_id=1, source_target_pairs={{0,1},{1,2},{2,3},{3,4},{4,5},{5,6},{6,7},{7,0},{8,9},{9,10},{10,1... | collective-permute-start | bytes 491528 | tf_op jit(solution)/shard_map/ppermute | solution.py:170
  156.2 3.2 %collective-permute-start.11 = (bf16[40,16,128]{2,1,0:T(8,128)(2,1)S(1)}, bf16[40,16,128]{2,1,0:T(8,128)(2,1)S(1)}, u32[]{:S(2)}, u32[]{:S(2)}) collective-permute-start(bf16[40,16,128]{2,1,0:T(8,128)(2,1)S(1)} %get-tuple-element.44), channel_id=1, source_target_pairs={{0,2},{1,3},{2,4},{3,5},{4,6},{5,7},{6,0},{7,1},{8,10},{9,11},{10,... | collective-permute-start | bytes 491528 | tf_op jit(solution)/shard_map/ppermute | solution.py:170
  159.4 1.6 collective-permute-start.12
  161.0 1.8 collective-permute-start.13
  162.9 3.3 %collective-permute-start.14 = (bf16[40,16,128]{2,1,0:T(8,128)(2,1)S(1)}, bf16[40,16,128]{2,1,0:T(8,128)(2,1)S(1)}, u32[]{:S(2)}, u32[]{:S(2)}) collective-permute-start(bf16[40,16,128]{2,1,0:T(8,128)(2,1)S(1)} %get-tuple-element.41), channel_id=1, source_target_pairs={{0,5},{1,6},{2,7},{3,0},{4,1},{5,2},{6,3},{7,4},{8,13},{9,14},{10,... | collective-permute-start | bytes 491528 | tf_op jit(solution)/shard_map/ppermute | solution.py:170
  167.0 3.1 %collective-permute-start.16 = (bf16[40,16,128]{2,1,0:T(8,128)(2,1)S(1)}, bf16[40,16,128]{2,1,0:T(8,128)(2,1)S(1)}, u32[]{:S(2)}, u32[]{:S(2)}) collective-permute-start(bf16[40,16,128]{2,1,0:T(8,128)(2,1)S(1)} %get-tuple-element.39), channel_id=1, source_target_pairs={{0,7},{1,0},{2,1},{3,2},{4,3},{5,4},{6,5},{7,6},{8,15},{9,8},{10,9... | collective-permute-start | bytes 491528 | tf_op jit(solution)/shard_map/ppermute | solution.py:170
  170.1 9.7 %collective-permute-done.12 = bf16[40,16,128]{2,1,0:T(8,128)(2,1)S(1)} collective-permute-done((bf16[40,16,128]{2,1,0:T(8,128)(2,1)S(1)}, bf16[40,16,128]{2,1,0:T(8,128)(2,1)S(1)}, u32[]{:S(2)}, u32[]{:S(2)}) %collective-permute-start.12) | collective-permute-done | bytes 163872 | tf_op jit(solution)/shard_map/ppermute | solution.py:170
  180.5 1.6 gather_fusion.2
  182.8 4.7 %collective-permute-start.17 = (bf16[40,16,128]{2,1,0:T(8,128)(2,1)S(1)}, bf16[40,16,128]{2,1,0:T(8,128)(2,1)S(1)}, u32[]{:S(2)}, u32[]{:S(2)}) collective-permute-start(bf16[40,16,128]{2,1,0:T(8,128)(2,1)S(1)} %get-tuple-element.37), channel_id=1, source_target_pairs={{0,1},{1,2},{2,3},{3,4},{4,5},{5,6},{6,7},{7,0},{8,9},{9,10},{10,1... | collective-permute-start | bytes 491528 | tf_op jit(solution)/shard_map/ppermute | solution.py:170
  187.5 7.4 %collective-permute-start.18 = (bf16[40,16,128]{2,1,0:T(8,128)(2,1)S(1)}, bf16[40,16,128]{2,1,0:T(8,128)(2,1)S(1)}, u32[]{:S(2)}, u32[]{:S(2)}) collective-permute-start(bf16[40,16,128]{2,1,0:T(8,128)(2,1)S(1)} %get-tuple-element.36), channel_id=1, source_target_pairs={{0,2},{1,3},{2,4},{3,5},{4,6},{5,7},{6,0},{7,1},{8,10},{9,11},{10,... | collective-permute-start | bytes 491528 | tf_op jit(solution)/shard_map/ppermute | solution.py:170
  195.5 3.4 %collective-permute-start.21 = (bf16[40,16,128]{2,1,0:T(8,128)(2,1)S(1)}, bf16[40,16,128]{2,1,0:T(8,128)(2,1)S(1)}, u32[]{:S(2)}, u32[]{:S(2)}) collective-permute-start(bf16[40,16,128]{2,1,0:T(8,128)(2,1)S(1)} %get-tuple-element.33), channel_id=1, source_target_pairs={{0,5},{1,6},{2,7},{3,0},{4,1},{5,2},{6,3},{7,4},{8,13},{9,14},{10,... | collective-permute-start | bytes 491528 | tf_op jit(solution)/shard_map/ppermute | solution.py:170
  199.0 2.0 collective-permute-start.22
  201.1 1.6 collective-permute-start.23
  202.7 9.0 %collective-permute-done.19 = bf16[40,16,128]{2,1,0:T(8,128)(2,1)S(1)} collective-permute-done((bf16[40,16,128]{2,1,0:T(8,128)(2,1)S(1)}, bf16[40,16,128]{2,1,0:T(8,128)(2,1)S(1)}, u32[]{:S(2)}, u32[]{:S(2)}) %collective-permute-start.19) | collective-permute-done | bytes 163872 | tf_op jit(solution)/shard_map/ppermute | solution.py:170
  213.6 2.2 collective-permute-done.23
  215.9 1.6 gather_fusion.3
  219.0 4.1 %shard_map.121.base_ref = bf16[160,16,1024]{2,1,0:T(8,128)(2,1)} custom-call(bf16[160,16,512]{2,1,0:T(8,128)(2,1)} %all-gather.5.cloned.1.call-done.x_ref), custom_call_target="tpu_custom_call" | custom-call | tf_op jit(solution)/shard_map/pallas_call | solution.py:68
  223.1 5.5 %maximum_select_fusion.1 = f32[40,128,256]{2,1,0:T(8,128)S(1)} fusion(f32[40,128,128]{2,1,0:T(8,128)} %copy-done.1, f32[40,128,128]{2,1,0:T(8,128)} %copy-done.2, pred[40]{0:T(512)(128)(4,1)S(1)} %get-tuple-element.22, f32[40,64,128]{2,1,0:T(8,128)S(1)} %bitcast.74, f32[64,1024]{1,0:T(8,128)S(1)} %copy-done, s32[]{:T(128)S(6)} %select_n.226), kind=kOutput, calls=%fused_computation.10 | convolution fusion | flops 505937920 | bytes 11862532 | tf_op jit(solution)/shard_map/skb,kq->sbq/dot_general | solution.py:151
  228.6 6.7 %select_bitcast_fusion = (f32[1,40,128,256]{3,2,1,0:T(8,128)}, f32[1,40,128,256]{3,2,1,0:T(8,128)}) fusion(f32[40,128,256]{2,1,0:T(8,128)} %bitcast.72, f32[40,128,256]{2,1,0:T(8,128)S(1)} %maximum_select_fusion.1, pred[40]{0:T(512)(128)(4,1)S(1)} %get-tuple-element.21, f32[40,128,256]{2,1,0:T(8,128)S(1)} %bitcast.69), kind=kLoop, calls=%fused_computation.11 | loop fusion | flops 10485760 | bytes 26214440 | tf_op jit(solution)/shard_map/broadcast_in_dim | solution.py:190
  235.4 15.0 %all-gather.7.cloned.1.call-done.a_ref = bf16[160,16,512]{2,1,0:T(8,128)(2,1)} async-done(((bf16[160,16,128]{2,1,0:T(8,128)(2,1)}), bf16[160,16,512]{2,1,0:T(8,128)(2,1)}) %all-gather.7.cloned.1.call-update) | async-done | bytes 2621456 | tf_op jit(solution)/shard_map/all_gather | solution.py:177
  250.4 4.0 %shard_map.122 = bf16[160,16,1024]{2,1,0:T(8,128)(2,1)} custom-call(bf16[160,16,512]{2,1,0:T(8,128)(2,1)} %all-gather.7.cloned.1.call-done.a_ref, bf16[160,16,1024]{2,1,0:T(8,128)(2,1)} %shard_map.121.base_ref), custom_call_target="tpu_custom_call", output_to_operand_aliasing={{}: (1, {})} | custom-call | tf_op jit(solution)/shard_map/pallas_call | solution.py:71
  (118 shorter events, 22.2 us)
Async XLA Ops:
  7.2 96.9 %copy-start = (f32[64,1024]{1,0:T(8,128)S(1)}, f32[64,1024]{1,0:T(8,128)}, u32[]{:S(2)}) copy-start(f32[64,1024]{1,0:T(8,128)} %param.12) | copy-start | bytes 786436
  7.2 41.6 %reduce-scatter.3.cloned.1.call-start = ((), (), s32[]{:S(2)}) async-start(), calls=%async_computation.3 | async-start | bytes 3276800 | tf_op jit(solution)/shard_map/reduce_scatter | solution.py:111
  11.3 75.5 %reduce-scatter.5.cloned.1.call-start = ((), (), s32[]{:S(2)}) async-start(), calls=%async_computation.4 | async-start | bytes 3276800 | tf_op jit(solution)/shard_map/reduce_scatter | solution.py:111
  15.3 0.7 copy-start.14
  51.8 5.9 %copy-start.13 = (bf16[1,13,1024]{2,1,0:T(8,128)(2,1)S(1)}, bf16[1,13,1024]{2,1,0:T(8,128)(2,1)}, u32[]{:S(2)}) copy-start(bf16[1,13,1024]{2,1,0:T(8,128)(2,1)} %param.13) | copy-start | bytes 79876
  51.8 49.3 %all-to-all-start = ((bf16[8,40,16,128]{3,2,1,0:T(8,128)(2,1)}), bf16[8,40,16,128]{3,2,1,0:T(8,128)(2,1)S(1)}, u32[]{:S(2)}, u32[]{:S(2)}) async-start(bf16[8,40,16,128]{3,2,1,0:T(8,128)(2,1)} %bitcast.4), calls=%async_computation.1 | async-start | bytes 2621440 | tf_op jit(solution)/shard_map/all_to_all | solution.py:126
  57.5 161.5 %all-gather.5.cloned.1.call-start = ((), (), s32[]{:S(2)}) async-start(), calls=%async_computation.5 | async-start | bytes 3276800 | tf_op jit(solution)/shard_map/all_gather | solution.py:177
  89.9 15.8 %collective-permute-start = (bf16[40,16,128]{2,1,0:T(8,128)(2,1)}, bf16[40,16,128]{2,1,0:T(8,128)(2,1)}, u32[]{:S(2)}, u32[]{:S(2)}) collective-permute-start(bf16[40,16,128]{2,1,0:T(8,128)(2,1)} %get-tuple-element.53), channel_id=1, source_target_pairs={{0,1},{1,2},{2,3},{3,4},{4,5},{5,6},{6,7},{7,0},{8,9},{9,10},{10,1... | collective-permute-start | bytes 491528 | tf_op jit(solution)/shard_map/ppermute | solution.py:120
  91.3 17.5 %collective-permute-start.1 = (bf16[40,16,128]{2,1,0:T(8,128)(2,1)}, bf16[40,16,128]{2,1,0:T(8,128)(2,1)S(1)}, u32[]{:S(2)}, u32[]{:S(2)}) collective-permute-start(bf16[40,16,128]{2,1,0:T(8,128)(2,1)} %get-tuple-element.52), channel_id=1, source_target_pairs={{0,2},{1,3},{2,4},{3,5},{4,6},{5,7},{6,0},{7,1},{8,10},{9,11},{10,... | collective-permute-start | bytes 491528 | tf_op jit(solution)/shard_map/ppermute | solution.py:120
  92.8 20.2 %collective-permute-start.2 = (bf16[40,16,128]{2,1,0:T(8,128)(2,1)}, bf16[40,16,128]{2,1,0:T(8,128)(2,1)S(1)}, u32[]{:S(2)}, u32[]{:S(2)}) collective-permute-start(bf16[40,16,128]{2,1,0:T(8,128)(2,1)} %get-tuple-element.51), channel_id=1, source_target_pairs={{0,3},{1,4},{2,5},{3,6},{4,7},{5,0},{6,1},{7,2},{8,11},{9,12},{10,... | collective-permute-start | bytes 491528 | tf_op jit(solution)/shard_map/ppermute | solution.py:120
  95.2 18.5 %collective-permute-start.3 = (bf16[40,16,128]{2,1,0:T(8,128)(2,1)}, bf16[40,16,128]{2,1,0:T(8,128)(2,1)S(1)}, u32[]{:S(2)}, u32[]{:S(2)}) collective-permute-start(bf16[40,16,128]{2,1,0:T(8,128)(2,1)} %get-tuple-element.50), channel_id=1, source_target_pairs={{0,4},{1,5},{2,6},{3,7},{4,0},{5,1},{6,2},{7,3},{8,12},{9,13},{10,... | collective-permute-start | bytes 491528 | tf_op jit(solution)/shard_map/ppermute | solution.py:120
  96.6 17.8 %collective-permute-start.4 = (bf16[40,16,128]{2,1,0:T(8,128)(2,1)}, bf16[40,16,128]{2,1,0:T(8,128)(2,1)S(1)}, u32[]{:S(2)}, u32[]{:S(2)}) collective-permute-start(bf16[40,16,128]{2,1,0:T(8,128)(2,1)} %get-tuple-element.49), channel_id=1, source_target_pairs={{0,5},{1,6},{2,7},{3,0},{4,1},{5,2},{6,3},{7,4},{8,13},{9,14},{10,... | collective-permute-start | bytes 491528 | tf_op jit(solution)/shard_map/ppermute | solution.py:120
  101.7 18.8 %slice-start = ((s8[5242880]{0:T(1024)(128)(4,1)}), s8[4194304]{0:T(1024)(128)(4,1)S(1)}, s32[]{:S(2)}) async-start(s8[5242880]{0:T(1024)(128)(4,1)} %bitcast.64), calls=%async_computation.7 | async-start | bytes 8388608
  101.7 18.8 %slice-start.1 = ((s8[5242880]{0:T(1024)(128)(4,1)}), s8[1048576]{0:T(1024)(128)(4,1)S(1)}, s32[]{:S(2)}) async-start(s8[5242880]{0:T(1024)(128)(4,1)} %bitcast.64), calls=%async_computation.8 | async-start | bytes 2097152
  104.1 1.6 copy-start.2
  104.1 1.6 copy-start.10
  104.1 4.7 %copy-start.9 = (bf16[40,16,128]{2,1,0:T(8,128)(2,1)S(1)}, bf16[40,16,128]{2,1,0:T(8,128)(2,1)}, u32[]{:S(2)}) copy-start(bf16[40,16,128]{2,1,0:T(8,128)(2,1)} %get-tuple-element.47) | copy-start | bytes 491524
  105.7 13.4 %collective-permute-start.5 = (bf16[40,16,128]{2,1,0:T(8,128)(2,1)S(1)}, bf16[40,16,128]{2,1,0:T(8,128)(2,1)S(1)}, u32[]{:S(2)}, u32[]{:S(2)}) collective-permute-start(bf16[40,16,128]{2,1,0:T(8,128)(2,1)S(1)} %copy-done.10), channel_id=1, source_target_pairs={{0,6},{1,7},{2,0},{3,1},{4,2},{5,3},{6,4},{7,5},{8,14},{9,15},{10,... | collective-permute-start | bytes 491528 | tf_op jit(solution)/shard_map/ppermute | solution.py:120
  108.8 11.0 %collective-permute-start.6 = (bf16[40,16,128]{2,1,0:T(8,128)(2,1)S(1)}, bf16[40,16,128]{2,1,0:T(8,128)(2,1)S(1)}, u32[]{:S(2)}, u32[]{:S(2)}) collective-permute-start(bf16[40,16,128]{2,1,0:T(8,128)(2,1)S(1)} %copy-done.9), channel_id=1, source_target_pairs={{0,7},{1,0},{2,1},{3,2},{4,3},{5,4},{6,5},{7,6},{8,15},{9,8},{10,9... | collective-permute-start | bytes 491528 | tf_op jit(solution)/shard_map/ppermute | solution.py:120
  122.2 22.7 %copy-start.1 = (f32[40,128,128]{2,1,0:T(8,128)}, f32[40,128,128]{2,1,0:T(8,128)S(1)}, u32[]{:S(2)}) copy-start(f32[40,128,128]{2,1,0:T(8,128)S(1)} %slice_subtract_fusion) | copy-start | bytes 7864324
  123.7 0.8 copy-start.8
  125.4 2.5 collective-permute-start.7
  129.1 10.2 %copy-start.6 = (bf16[2688,128]{1,0:T(8,128)(2,1)}, bf16[2688,128]{1,0:T(8,128)(2,1)S(1)}, u32[]{:S(2)}) copy-start(bf16[2688,128]{1,0:T(8,128)(2,1)S(1)} %add_convert_fusion) | copy-start | bytes 2064388
  129.2 10.2 %collective-permute-start.8 = (bf16[1344,128]{1,0:T(8,128)(2,1)S(1)}, bf16[1344,128]{1,0:T(8,128)(2,1)S(1)}, u32[]{:S(2)}, u32[]{:S(2)}) collective-permute-start(bf16[1344,128]{1,0:T(8,128)(2,1)S(1)} %dynamic-slice_bitcast_fusion), channel_id=1, source_target_pairs={{0,16},{8,24},{16,0},{24,8},{1,17},{9,25},{17,1},{25,9},{2,18},{10... | collective-permute-start | bytes 1032200 | tf_op jit(solution)/shard_map/ppermute | solution.py:32
  140.3 2.5 collective-permute-start.9
  144.1 0.8 copy-start.7
  144.1 2.5 copy-start.3
  144.9 7.8 %copy-start.4 = (f32[2560,128]{1,0:T(8,128)}, f32[2560,128]{1,0:T(8,128)S(1)}, u32[]{:S(2)}) copy-start(f32[2560,128]{1,0:T(8,128)S(1)} %pad_maximum_fusion) | copy-start | bytes 3932164
  153.5 12.8 %collective-permute-start.10 = (bf16[40,16,128]{2,1,0:T(8,128)(2,1)S(1)}, bf16[40,16,128]{2,1,0:T(8,128)(2,1)S(1)}, u32[]{:S(2)}, u32[]{:S(2)}) collective-permute-start(bf16[40,16,128]{2,1,0:T(8,128)(2,1)S(1)} %get-tuple-element.45), channel_id=1, source_target_pairs={{0,1},{1,2},{2,3},{3,4},{4,5},{5,6},{6,7},{7,0},{8,9},{9,10},{10,1... | collective-permute-start | bytes 491528 | tf_op jit(solution)/shard_map/ppermute | solution.py:170
  156.2 10.7 %collective-permute-start.11 = (bf16[40,16,128]{2,1,0:T(8,128)(2,1)S(1)}, bf16[40,16,128]{2,1,0:T(8,128)(2,1)S(1)}, u32[]{:S(2)}, u32[]{:S(2)}) collective-permute-start(bf16[40,16,128]{2,1,0:T(8,128)(2,1)S(1)} %get-tuple-element.44), channel_id=1, source_target_pairs={{0,2},{1,3},{2,4},{3,5},{4,6},{5,7},{6,0},{7,1},{8,10},{9,11},{10,... | collective-permute-start | bytes 491528 | tf_op jit(solution)/shard_map/ppermute | solution.py:170
  159.4 20.4 %collective-permute-start.12 = (bf16[40,16,128]{2,1,0:T(8,128)(2,1)S(1)}, bf16[40,16,128]{2,1,0:T(8,128)(2,1)S(1)}, u32[]{:S(2)}, u32[]{:S(2)}) collective-permute-start(bf16[40,16,128]{2,1,0:T(8,128)(2,1)S(1)} %get-tuple-element.43), channel_id=1, source_target_pairs={{0,3},{1,4},{2,5},{3,6},{4,7},{5,0},{6,1},{7,2},{8,11},{9,12},{10,... | collective-permute-start | bytes 491528 | tf_op jit(solution)/shard_map/ppermute | solution.py:170
  161.0 19.1 %collective-permute-start.13 = (bf16[40,16,128]{2,1,0:T(8,128)(2,1)S(1)}, bf16[40,16,128]{2,1,0:T(8,128)(2,1)S(1)}, u32[]{:S(2)}, u32[]{:S(2)}) collective-permute-start(bf16[40,16,128]{2,1,0:T(8,128)(2,1)S(1)} %get-tuple-element.42), channel_id=1, source_target_pairs={{0,4},{1,5},{2,6},{3,7},{4,0},{5,1},{6,2},{7,3},{8,12},{9,13},{10,... | collective-permute-start | bytes 491528 | tf_op jit(solution)/shard_map/ppermute | solution.py:170
  162.9 17.3 %collective-permute-start.14 = (bf16[40,16,128]{2,1,0:T(8,128)(2,1)S(1)}, bf16[40,16,128]{2,1,0:T(8,128)(2,1)S(1)}, u32[]{:S(2)}, u32[]{:S(2)}) collective-permute-start(bf16[40,16,128]{2,1,0:T(8,128)(2,1)S(1)} %get-tuple-element.41), channel_id=1, source_target_pairs={{0,5},{1,6},{2,7},{3,0},{4,1},{5,2},{6,3},{7,4},{8,13},{9,14},{10,... | collective-permute-start | bytes 491528 | tf_op jit(solution)/shard_map/ppermute | solution.py:170
  166.4 13.8 %collective-permute-start.15 = (bf16[40,16,128]{2,1,0:T(8,128)(2,1)S(1)}, bf16[40,16,128]{2,1,0:T(8,128)(2,1)S(1)}, u32[]{:S(2)}, u32[]{:S(2)}) collective-permute-start(bf16[40,16,128]{2,1,0:T(8,128)(2,1)S(1)} %get-tuple-element.40), channel_id=1, source_target_pairs={{0,6},{1,7},{2,0},{3,1},{4,2},{5,3},{6,4},{7,5},{8,14},{9,15},{10,... | collective-permute-start | bytes 491528 | tf_op jit(solution)/shard_map/ppermute | solution.py:170
  167.0 13.5 %collective-permute-start.16 = (bf16[40,16,128]{2,1,0:T(8,128)(2,1)S(1)}, bf16[40,16,128]{2,1,0:T(8,128)(2,1)S(1)}, u32[]{:S(2)}, u32[]{:S(2)}) collective-permute-start(bf16[40,16,128]{2,1,0:T(8,128)(2,1)S(1)} %get-tuple-element.39), channel_id=1, source_target_pairs={{0,7},{1,0},{2,1},{3,2},{4,3},{5,4},{6,5},{7,6},{8,15},{9,8},{10,9... | collective-permute-start | bytes 491528 | tf_op jit(solution)/shard_map/ppermute | solution.py:170
  182.2 68.2 %all-gather.7.cloned.1.call-start = ((), (), s32[]{:S(2)}) async-start(), calls=%async_computation.6 | async-start | bytes 3276800 | tf_op jit(solution)/shard_map/all_gather | solution.py:177
  182.8 16.3 %collective-permute-start.17 = (bf16[40,16,128]{2,1,0:T(8,128)(2,1)S(1)}, bf16[40,16,128]{2,1,0:T(8,128)(2,1)S(1)}, u32[]{:S(2)}, u32[]{:S(2)}) collective-permute-start(bf16[40,16,128]{2,1,0:T(8,128)(2,1)S(1)} %get-tuple-element.37), channel_id=1, source_target_pairs={{0,1},{1,2},{2,3},{3,4},{4,5},{5,6},{6,7},{7,0},{8,9},{9,10},{10,1... | collective-permute-start | bytes 491528 | tf_op jit(solution)/shard_map/ppermute | solution.py:170
  187.5 13.6 %collective-permute-start.18 = (bf16[40,16,128]{2,1,0:T(8,128)(2,1)S(1)}, bf16[40,16,128]{2,1,0:T(8,128)(2,1)S(1)}, u32[]{:S(2)}, u32[]{:S(2)}) collective-permute-start(bf16[40,16,128]{2,1,0:T(8,128)(2,1)S(1)} %get-tuple-element.36), channel_id=1, source_target_pairs={{0,2},{1,3},{2,4},{3,5},{4,6},{5,7},{6,0},{7,1},{8,10},{9,11},{10,... | collective-permute-start | bytes 491528 | tf_op jit(solution)/shard_map/ppermute | solution.py:170
  194.9 16.9 %collective-permute-start.19 = (bf16[40,16,128]{2,1,0:T(8,128)(2,1)S(1)}, bf16[40,16,128]{2,1,0:T(8,128)(2,1)S(1)}, u32[]{:S(2)}, u32[]{:S(2)}) collective-permute-start(bf16[40,16,128]{2,1,0:T(8,128)(2,1)S(1)} %get-tuple-element.35), channel_id=1, source_target_pairs={{0,3},{1,4},{2,5},{3,6},{4,7},{5,0},{6,1},{7,2},{8,11},{9,12},{10,... | collective-permute-start | bytes 491528 | tf_op jit(solution)/shard_map/ppermute | solution.py:170
  194.9 17.8 %collective-permute-start.20 = (bf16[40,16,128]{2,1,0:T(8,128)(2,1)S(1)}, bf16[40,16,128]{2,1,0:T(8,128)(2,1)S(1)}, u32[]{:S(2)}, u32[]{:S(2)}) collective-permute-start(bf16[40,16,128]{2,1,0:T(8,128)(2,1)S(1)} %get-tuple-element.34), channel_id=1, source_target_pairs={{0,4},{1,5},{2,6},{3,7},{4,0},{5,1},{6,2},{7,3},{8,12},{9,13},{10,... | collective-permute-start | bytes 491528 | tf_op jit(solution)/shard_map/ppermute | solution.py:170
  195.5 17.3 %collective-permute-start.21 = (bf16[40,16,128]{2,1,0:T(8,128)(2,1)S(1)}, bf16[40,16,128]{2,1,0:T(8,128)(2,1)S(1)}, u32[]{:S(2)}, u32[]{:S(2)}) collective-permute-start(bf16[40,16,128]{2,1,0:T(8,128)(2,1)S(1)} %get-tuple-element.33), channel_id=1, source_target_pairs={{0,5},{1,6},{2,7},{3,0},{4,1},{5,2},{6,3},{7,4},{8,13},{9,14},{10,... | collective-permute-start | bytes 491528 | tf_op jit(solution)/shard_map/ppermute | solution.py:170
  199.0 14.6 %collective-permute-start.22 = (bf16[40,16,128]{2,1,0:T(8,128)(2,1)S(1)}, bf16[40,16,128]{2,1,0:T(8,128)(2,1)S(1)}, u32[]{:S(2)}, u32[]{:S(2)}) collective-permute-start(bf16[40,16,128]{2,1,0:T(8,128)(2,1)S(1)} %get-tuple-element.32), channel_id=1, source_target_pairs={{0,6},{1,7},{2,0},{3,1},{4,2},{5,3},{6,4},{7,5},{8,14},{9,15},{10,... | collective-permute-start | bytes 491528 | tf_op jit(solution)/shard_map/ppermute | solution.py:170
  201.1 14.7 %collective-permute-start.23 = (bf16[40,16,128]{2,1,0:T(8,128)(2,1)S(1)}, bf16[40,16,128]{2,1,0:T(8,128)(2,1)S(1)}, u32[]{:S(2)}, u32[]{:S(2)}) collective-permute-start(bf16[40,16,128]{2,1,0:T(8,128)(2,1)S(1)} %get-tuple-element.31), channel_id=1, source_target_pairs={{0,7},{1,0},{2,1},{3,2},{4,3},{5,4},{6,5},{7,6},{8,15},{9,8},{10,9... | collective-permute-start | bytes 491528 | tf_op jit(solution)/shard_map/ppermute | solution.py:170
  213.6 4.7 %copy-start.11 = (f32[13,1024]{1,0:T(8,128)S(1)}, f32[13,1024]{1,0:T(8,128)}, u32[]{:S(2)}) copy-start(f32[13,1024]{1,0:T(8,128)} %param.14) | copy-start | bytes 159748
  213.6 4.7 %copy-start.12 = (f32[13,1024]{1,0:T(8,128)S(1)}, f32[13,1024]{1,0:T(8,128)}, u32[]{:S(2)}) copy-start(f32[13,1024]{1,0:T(8,128)} %param.15) | copy-start | bytes 159748
  219.0 4.1 %copy-start.5 = (f32[2560,128]{1,0:T(8,128)S(1)}, f32[2560,128]{1,0:T(8,128)}, u32[]{:S(2)}) copy-start(f32[2560,128]{1,0:T(8,128)} %copy-done.4) | copy-start | bytes 3932164
  219.0 9.6 %slice-start.2 = ((s8[5242880]{0:T(1024)(128)(4,1)}), s8[1048576]{0:T(1024)(128)(4,1)S(1)}, s32[]{:S(2)}) async-start(s8[5242880]{0:T(1024)(128)(4,1)} %bitcast.67), calls=%async_computation.9 | async-start | bytes 2097152
  223.1 5.5 %slice-start.3 = ((s8[5242880]{0:T(1024)(128)(4,1)}), s8[4194304]{0:T(1024)(128)(4,1)S(1)}, s32[]{:S(2)}) async-start(s8[5242880]{0:T(1024)(128)(4,1)} %bitcast.67), calls=%async_computation.10 | async-start | bytes 8388608
Sparse Core Ops, SparseCore 0:
  11.4 37.3 reduce-scatter.2
  52.0 34.6 reduce-scatter.4
  182.3 33.1 all-gather.4
  217.6 32.7 all-gather.6
